TPU v7x, 32 devices: a whole 2x2x4 slice. The times are simulated.
32 devices in a mesh: ch: 8 (over y, x, core), row: 4 (over z).
Axes of the slice: x: 2, y: 2, z: 4, core: 2. Of those that a mesh axis runs over, the one named last changes fastest.
Arguments:
- eta_pp: bfloat16 [32, 1024, 1024], P('ch', 'row'), as said below
- gamma_pp: bfloat16 [32, 1024, 1024], P('ch', 'row'), as said below
- pp_factor: int32 [32, 1024], P('ch'), may hold values from -1 to 1
- ph_factor: int32 [32, 1024], P(('ch', 'row')), may hold values from -1 to 1
- recouple: float32 [32, 1024], P(('ch', 'row')), may hold values from -1.5 to 1.5
- src_slot: int32 [32, 8], replicated, may hold values from 0 to 3
Outputs:
- dgamma: bfloat16 [32, 1024, 1024], P('ch', 'row')
Inputs may be any that keep to these rules, and one draw needn't show every extreme that they name: Every block eta_pp[c] is antisymmetric: eta_pp[c][i, k] = -eta_pp[c][k, i]. Every block gamma_pp[c] is symmetric.
All inputs are finite; a program needn't handle non-finite values.
Results may differ from a plain program's by a relative error of at most 0.0033.
Values may be sent and summed in bfloat16 or wider, within the bound.
No kernel may reach another device: no remote copies, remote signals or barrier semaphores. Data moves between devices by JAX's collectives and lax.ppermute only.
A program may use at most 128 MiB of HBM per device.

v0:
```python
import jax
import jax.numpy as jnp
from jax import lax
from jax.sharding import PartitionSpec as P


def per_device(eta_pp, gamma_pp, pp_factor, ph_factor, recouple, src_slot):
    f32 = jnp.float32
    bf16 = jnp.bfloat16
    n_chan = lax.axis_size("ch")
    n_rows = lax.axis_size("row")
    ch_dev, rows, width = eta_pp.shape
    slab = width // n_chan
    ph_dev = ph_factor.shape[0]
    n_total = ch_dev * n_chan
    factor = pp_factor.astype(bf16)[:, None, :]
    eta_w = eta_pp * factor
    product = jnp.einsum(
        "cik,ckj->cij",
        eta_w,
        lax.all_gather(gamma_pp, "row", axis=1, tiled=True),
        preferred_element_type=f32,
    )
    mirrored = lax.all_to_all(product, "row", split_axis=2, concat_axis=1, tiled=True)
    ladder = product + jnp.swapaxes(mirrored, 1, 2)
    mine = lax.axis_index("ch")
    slots = lax.dynamic_slice_in_dim(src_slot, mine, 1, 1)[:, 0]
    groups = jnp.arange(n_total, dtype=jnp.int32) // ch_dev
    stacked = jnp.stack([eta_pp, gamma_pp]).reshape(2, ch_dev, rows, n_chan, slab)
    by_group = stacked.transpose(0, 3, 1, 2, 4)
    picked = by_group[:, groups, slots]
    outgoing = picked.reshape(2, n_chan * n_rows, ph_dev, rows, slab)
    arrived = lax.all_to_all(outgoing, ("ch", "row"), split_axis=1, concat_axis=1, tiled=True)
    arrived = arrived.reshape(2, n_chan, n_rows, ph_dev, rows, slab)
    blocks = arrived.transpose(0, 3, 2, 4, 1, 5).reshape(2, ph_dev, width, width)
    eta_ph = blocks[0]
    gamma_ph = blocks[1]
    ph_weight = ph_factor.astype(bf16)[:, None, :]
    ph_out = jnp.einsum("uik,ukj->uij", eta_ph * ph_weight, gamma_ph, preferred_element_type=f32)
    ph_out = ph_out - jnp.einsum(
        "uik,ukj->uij", gamma_ph * ph_weight, eta_ph, preferred_element_type=f32
    )
    ph_term = (ph_out * recouple[:, None, :]).astype(bf16)
    returning = ph_term.reshape(ph_dev, n_rows, rows, n_chan, slab).transpose(3, 1, 0, 2, 4)
    landed = lax.all_to_all(
        returning.reshape(n_chan * n_rows, ph_dev, rows, slab),
        ("ch", "row"),
        split_axis=0,
        concat_axis=0,
        tiled=True,
    )
    landed = landed.reshape(n_chan, n_rows * ph_dev, rows, slab)
    chosen = slots.reshape(n_chan, ch_dev)
    onehot = (chosen[:, :, None] == jnp.arange(ch_dev, dtype=jnp.int32)[None, None, :]).astype(bf16)
    back = jnp.einsum("gqs,gqiw->sigw", onehot, landed, preferred_element_type=f32)
    back = back.reshape(ch_dev, rows, width)
    return (ladder + back).astype(bf16)


def solution(mesh):
    placed = (
        P("ch", "row", None),
        P("ch", "row", None),
        P("ch", None),
        P(("ch", "row"), None),
        P(("ch", "row"), None),
        P(),
    )
    return jax.shard_map(
        per_device, mesh=mesh, in_specs=placed, out_specs=P("ch", "row", None), check_vma=False
    )
```

profile of v0, /device:TPU:8, one launch (start us, length us, event | category | flops | bytes accessed | tf_op | source)
XLA Modules:
  0.0 436.3 jit_solution(13192371335472725662)
XLA Ops:
  6.5 3.9 copy.25
  10.5 4.1 copy.27
  14.6 2.5 copy.26
  17.1 4.1 copy.28
  21.9 3.9 maximum_bitcast_fusion
  25.8 5.2 %gather_fusion = bf16[32,2,256,128]{3,2,1,0:T(8,128)(2,1)} fusion(bf16[2,8,4,256,128]{4,3,2,1,0:T(8,128)(2,1)} %maximum_bitcast_fusion, s32[32]{0:T(128)S(1)} %get-tuple-element.10), kind=kCustom, calls=%fused_computation | custom fusion | bytes 8388864 | tf_op jit(solution)/shard_map/gather | solution.py:31
  31.0 6.1 %all-to-all-start.1 = ((bf16[2,32,1,256,128]{4,3,0,2,1:T(8,128)(2,1)}), bf16[2,32,1,256,128]{4,3,0,2,1:T(8,128)(2,1)}, u32[]{:S(2)}, u32[]{:S(2)}) async-start(bf16[2,32,1,256,128]{4,3,0,2,1:T(8,128)(2,1)} %bitcast.73), calls=%async_computation.1 | async-start | bytes 8388608 | tf_op jit(solution)/shard_map/all_to_all | solution.py:33
  37.9 193.5 %all-to-all-done.1 = bf16[2,32,1,256,128]{4,3,0,2,1:T(8,128)(2,1)} async-done(((bf16[2,32,1,256,128]{4,3,0,2,1:T(8,128)(2,1)}), bf16[2,32,1,256,128]{4,3,0,2,1:T(8,128)(2,1)}, u32[]{:S(2)}, u32[]{:S(2)}) %all-to-all-start.1) | async-done | bytes 4194336 | tf_op jit(solution)/shard_map/all_to_all | solution.py:33
  231.4 4.9 %copy.65 = bf16[2,8,4,1,256,128]{5,1,4,2,3,0:T(8,128)(2,1)S(1)} copy(bf16[2,8,4,1,256,128]{5,4,0,2,1,3:T(8,128)(2,1)} %bitcast.10) | data formatting | bytes 8388608 | tf_op jit(solution)/shard_map/reshape | solution.py:34
  236.9 2.3 fusion.3
  239.2 2.3 fusion.2
  242.2 1.8 copy.31
  244.1 4.7 %all-to-all-start.2 = ((bf16[32,1,256,128]{3,2,1,0:T(8,128)(2,1)}), bf16[32,1,256,128]{3,2,1,0:T(8,128)(2,1)}, u32[]{:S(2)}, u32[]{:S(2)}) async-start(bf16[32,1,256,128]{3,2,1,0:T(8,128)(2,1)} %bitcast.76), calls=%async_computation.2 | async-start | bytes 4194304 | tf_op jit(solution)/shard_map/all_to_all | solution.py:45
  248.8 51.2 %all-gather.2.cloned.1.call-done = bf16[4,1024,1024]{2,1,0:T(8,128)(2,1)} async-done(((bf16[4,256,1024]{2,1,0:T(8,128)(2,1)}), bf16[4,1024,1024]{2,1,0:T(8,128)(2,1)}) %all-gather.2.cloned.1.call-update) | async-done | bytes 8388624 | tf_op jit(solution)/shard_map/all_gather | solution.py:21
  300.0 7.7 %fusion.14 = f32[4,256,1024]{2,1,0:T(8,128)} fusion(bf16[4,1024,1024]{2,1,0:T(8,128)(2,1)} %all-gather.2.cloned.1.call-done, bf16[4,256,1024]{2,1,0:T(8,128)(2,1)S(1)} %copy-done, bf16[4,1024]{1,0:T(4,128)(2,1)S(1)} %convert_element_type.14), kind=kOutput, calls=%fused_computation.21 | convolution fusion | flops 2148532224 | bytes 14688256 | tf_op jit(solution)/shard_map/cik,ckj->cij/dot_general | solution.py:18
  307.7 5.2 %copy.23 = f32[4,256,1024]{1,0,2:T(4,128)} copy(f32[4,256,1024]{2,1,0:T(8,128)} %fusion.14) | data formatting | bytes 8388608 | tf_op jit(solution)/shard_map/cik,ckj->cij/dot_general | solution.py:18
  312.9 6.3 %all-to-all-start = ((f32[4,256,1024]{1,0,2:T(4,128)}), f32[4,256,1024]{1,0,2:T(4,128)}, u32[]{:S(2)}, u32[]{:S(2)}) async-start(f32[4,256,1024]{1,0,2:T(4,128)} %copy.23), calls=%async_computation | async-start | bytes 8388608 | tf_op jit(solution)/shard_map/all_to_all | solution.py:24
  319.3 3.3 convolution_bitcast_fusion
  322.7 4.4 %copy.34 = f32[4,256,8,128]{3,2,1,0:T(8,128)} copy(f32[4,256,8,128]{3,0,1,2:T(4,128)S(1)} %convolution_bitcast_fusion) | data formatting | bytes 8388608 | tf_op jit(solution)/shard_map/gqs,gqiw->sigw/transpose | solution.py:55
  327.0 4.9 %reshape.140 = f32[4,256,1024]{2,1,0:T(8,128)} reshape(f32[4,256,8,128]{3,2,1,0:T(8,128)} %copy.34) | data formatting | bytes 8388608 | tf_op jit(solution)/shard_map/reshape | solution.py:56
  331.9 77.7 %all-to-all-done = f32[4,256,1024]{1,0,2:T(4,128)} async-done(((f32[4,256,1024]{1,0,2:T(4,128)}), f32[4,256,1024]{1,0,2:T(4,128)}, u32[]{:S(2)}, u32[]{:S(2)}) %all-to-all-start) | async-done | bytes 4194336 | tf_op jit(solution)/shard_map/all_to_all | solution.py:24
  409.6 6.8 %copy.66 = f32[4,256,4,256]{1,2,3,0:T(4,128)} copy(f32[4,256,4,256]{1,0,3,2:T(4,128)} %bitcast) | data formatting | bytes 8388608 | tf_op jit(solution)/shard_map/all_to_all | solution.py:24
  416.4 5.8 %all_to_all.22 = f32[4,1024,256]{1,2,0:T(8,128)} reshape(f32[4,4,256,256]{2,1,3,0:T(4,128)} %bitcast.75) | data formatting | bytes 8388608 | tf_op jit(solution)/shard_map/all_to_all | solution.py:24
  422.2 7.2 %fusion.1 = bf16[4,256,1024]{2,1,0:T(8,128)(2,1)} fusion(f32[4,256,1024]{2,1,0:T(8,128)} %reshape.140, f32[4,256,1024]{2,1,0:T(8,128)} %fusion.14, f32[4,1024,256]{1,2,0:T(8,128)} %all_to_all.22), kind=kLoop, calls=%fused_computation.4 | loop fusion | flops 3145728 | bytes 14680064 | tf_op jit(solution)/shard_map/convert_element_type | solution.py:57
  (21 shorter events, 2.7 us)
Async XLA Ops:
  10.5 4.1 copy-start.1
  17.1 4.8 %copy-start.2 = (bf16[1,4,256,8,128]{4,2,1,3,0:T(8,128)(2,1)S(1)}, bf16[1,4,256,8,128]{4,2,1,3,0:T(8,128)(2,1)}, u32[]{:S(2)}) copy-start(bf16[1,4,256,8,128]{4,2,1,3,0:T(8,128)(2,1)} %copy.27) | copy-start | bytes 6291460
  31.0 200.4 %all-to-all-start.1 = ((bf16[2,32,1,256,128]{4,3,0,2,1:T(8,128)(2,1)}), bf16[2,32,1,256,128]{4,3,0,2,1:T(8,128)(2,1)}, u32[]{:S(2)}, u32[]{:S(2)}) async-start(bf16[2,32,1,256,128]{4,3,0,2,1:T(8,128)(2,1)} %bitcast.73), calls=%async_computation.1 | async-start | bytes 8388608 | tf_op jit(solution)/shard_map/all_to_all | solution.py:33
  37.2 0.8 copy-start.4
  37.2 262.8 %all-gather.2.cloned.1.call-start = ((), (), s32[]{:S(2)}) async-start(), calls=%async_computation.3 | async-start | bytes 10485760 | tf_op jit(solution)/shard_map/all_gather | solution.py:21
  236.9 2.3 copy-start.5
  244.0 4.7 %copy-start.3 = (s32[4,1024]{1,0:T(4,128)S(1)}, s32[4,1024]{1,0:T(4,128)}, u32[]{:S(2)}) copy-start(s32[4,1024]{1,0:T(4,128)} %param.8) | copy-start | bytes 49156
  244.0 56.0 %copy-start = (bf16[4,256,1024]{2,1,0:T(8,128)(2,1)S(1)}, bf16[4,256,1024]{2,1,0:T(8,128)(2,1)}, u32[]{:S(2)}) copy-start(bf16[4,256,1024]{2,1,0:T(8,128)(2,1)} %param.6) | copy-start | bytes 6291460
  244.1 68.9 %all-to-all-start.2 = ((bf16[32,1,256,128]{3,2,1,0:T(8,128)(2,1)}), bf16[32,1,256,128]{3,2,1,0:T(8,128)(2,1)}, u32[]{:S(2)}, u32[]{:S(2)}) async-start(bf16[32,1,256,128]{3,2,1,0:T(8,128)(2,1)} %bitcast.76), calls=%async_computation.2 | async-start | bytes 4194304 | tf_op jit(solution)/shard_map/all_to_all | solution.py:45
  312.9 96.7 %all-to-all-start = ((f32[4,256,1024]{1,0,2:T(4,128)}), f32[4,256,1024]{1,0,2:T(4,128)}, u32[]{:S(2)}, u32[]{:S(2)}) async-start(f32[4,256,1024]{1,0,2:T(4,128)} %copy.23), calls=%async_computation | async-start | bytes 8388608 | tf_op jit(solution)/shard_map/all_to_all | solution.py:24
Sparse Core Ops, SparseCore 0:
  39.6 260.3 all-gather.1
where the time goes:
time: 442 us; the launch traced here: 436 us
  waiting for transfers between devices  323 us (73%)
  local copies, waits for them, and re-layouts  54.4 us (12%)
  starting transfers between devices  17.2 us (4%)
  matrix products  15.7 us (4%)
  between operations  13.5 us (3%)
  other arithmetic  12.4 us (3%)
    all_to_all x1, waiting for transfers between devices, per_device(): lax.all_to_all(outgoing, ('ch', 'row'), split_axis=1, concat_axis=1, tile...  193 us
    all_to_all x1, waiting for transfers between devices, per_device(): lax.all_to_all(product, 'row', split_axis=2, concat_axis=1, tiled=True)  77.7 us
    all_gather x1, waiting for transfers between devices, per_device(): lax.all_gather(gamma_pp, 'row', axis=1, tiled=True)  51.2 us
    all_to_all x2, local copies, waits for them, and re-layouts, per_device(): lax.all_to_all(product, 'row', split_axis=2, concat_axis=1, tiled=True)  12.6 us
  transfers between devices with their start and end apart: 4, of which 3 were waited for; matrix products, arithmetic and copies ran while one was open for 9% of the time, Pallas kernels for 0%

commit v1 on v0

v1 whole, which is shorter than its diff:
```python
import jax
import jax.numpy as jnp
from jax import lax
from jax.sharding import PartitionSpec as P


def per_device(eta_pp, gamma_pp, pp_factor, ph_factor, recouple, src_slot):
    f32 = jnp.float32
    bf16 = jnp.bfloat16
    n_chan = lax.axis_size("ch")
    n_rows = lax.axis_size("row")
    ch_dev, rows, width = eta_pp.shape
    slab = width // n_chan
    n_total = ch_dev * n_chan
    assert ch_dev == n_rows and rows % slab == 0 and n_chan * slab == width
    mine = lax.axis_index("ch")
    level = lax.axis_index("row")

    stacked = jnp.stack([eta_pp, gamma_pp])
    whole = lax.all_to_all(stacked, "row", split_axis=1, concat_axis=2, tiled=True)
    eta_c = whole[0, 0]
    gamma_c = whole[1, 0]

    dest = jnp.arange(n_chan, dtype=jnp.int32)
    q_dest = level * n_chan + dest
    slot_dest = src_slot[q_dest, mine]
    part_dest = q_dest // ch_dev - level * (rows // slab)
    five = stacked.reshape(2, ch_dev, rows // slab, slab, width)
    outgoing = five[:, slot_dest, part_dest]
    arrived = lax.all_to_all(outgoing, "ch", split_axis=1, concat_axis=1, tiled=True)
    a_eta = arrived[0].reshape(width, width)
    b_gamma = arrived[1].reshape(width, width)

    perm = [(q, (q % n_chan) * n_rows + q // n_chan) for q in range(n_total)]
    coefs = lax.ppermute(
        jnp.concatenate([ph_factor.astype(f32), recouple], axis=0), ("ch", "row"), perm
    )
    weight = coefs[0].astype(bf16)[None, :]
    coef = coefs[1]

    ph_t = jnp.dot(a_eta * weight, b_gamma, preferred_element_type=f32)
    ph_t = ph_t - jnp.dot(b_gamma * weight, a_eta, preferred_element_type=f32)
    term_t = (ph_t * coef[:, None]).astype(bf16)
    returning = term_t.reshape(n_chan, slab, n_rows, rows).transpose(0, 2, 1, 3)
    landed = lax.all_to_all(
        returning.reshape(n_chan * n_rows, slab, rows),
        ("ch", "row"),
        split_axis=0,
        concat_axis=0,
        tiled=True,
    )
    landed = landed.reshape(n_chan, n_rows, slab, rows).transpose(1, 0, 2, 3)
    landed = landed.reshape(n_chan, ch_dev, slab, rows)
    chosen = src_slot[:, mine].reshape(n_chan, ch_dev)
    onehot = (chosen[:, :, None] == jnp.arange(ch_dev, dtype=jnp.int32)[None, None, :]).astype(bf16)
    back = jnp.einsum("gts,gtwi->sigw", onehot, landed, preferred_element_type=f32)
    back = back.reshape(ch_dev, rows, width)

    factor = lax.dynamic_index_in_dim(pp_factor, level, 0, False).astype(bf16)
    product = jnp.dot(eta_c * factor[None, :], gamma_c, preferred_element_type=f32)
    ladder_c = product + product.T
    ladder = lax.all_to_all(
        ladder_c.reshape(n_rows, rows, width), "row", split_axis=0, concat_axis=0, tiled=True
    )
    return (ladder + back).astype(bf16)


def solution(mesh):
    placed = (
        P("ch", "row", None),
        P("ch", "row", None),
        P("ch", None),
        P(("ch", "row"), None),
        P(("ch", "row"), None),
        P(),
    )
    return jax.shard_map(
        per_device, mesh=mesh, in_specs=placed, out_specs=P("ch", "row", None), check_vma=False
    )
```

time: 442 us -> 333 us (0.75)
  waiting for transfers between devices: 323 us -> 226 us
  local copies, waits for them, and re-layouts: 54.4 us -> 22.3 us
  starting transfers between devices: 17.2 us -> 38.4 us
  other arithmetic: 12.4 us -> 26.9 us
  between operations: 13.5 us -> 0.11 us
    all_to_all x3 -> x4, waiting for transfers between devices: 271 us -> 160 us  [the longest x1 80.8 us: per_device(): lax.all_to_all(ladder_c.reshape(n_rows, rows, width), 'row', split_axis=0...]
    ppermute x0 -> x1, waiting for transfers between devices: none -> 66.5 us  [per_device(): lax.ppermute(jnp.concatenate([ph_factor.astype(f32), recouple], axis=0),...]
    all_gather x1 -> x0, waiting for transfers between devices: 51.2 us -> none  [per_device(): lax.all_gather(gamma_pp, 'row', axis=1, tiled=True)]
    all_to_all x3 -> x4, starting transfers between devices: 17.1 us -> 36.5 us  [the longest x1 21.4 us: per_device(): lax.all_to_all(returning.reshape(n_chan * n_rows, slab, rows), ('ch', 'ro...]
    all_to_all x2 -> x0, local copies, waits for them, and re-layouts: 12.6 us -> none  [per_device(): lax.all_to_all(product, 'row', split_axis=2, concat_axis=1, tiled=True)]
    another operation x0 -> x2, other arithmetic: none -> 8.5 us  [per_device(): stacked = jnp.stack([eta_pp, gamma_pp])]
    another operation x2 -> x0, local copies, waits for them, and re-layouts: 8.16 us -> none  [per_device(): jnp.stack([eta_pp, gamma_pp]).reshape(2, ch_dev, rows, n_chan, slab)]
    add x0 -> x1, other arithmetic: none -> 6.8 us  [per_device(): ladder_c = product + product.T]
  transfers between devices with their start and end apart: 4 -> 5, of which waited for: 3 -> 5; matrix products, arithmetic and copies ran while one was open for 9% -> 14% of each run, Pallas kernels for 0% -> 0%
where the time goes in v1:
time: 333 us; the launch traced here: 328 us
  waiting for transfers between devices  226 us (68%)
  starting transfers between devices  38.4 us (12%)
  other arithmetic  26.9 us (8%)
  local copies, waits for them, and re-layouts  22.3 us (7%)
  matrix products  14 us (4%)
    all_to_all x1, waiting for transfers between devices, per_device(): lax.all_to_all(ladder_c.reshape(n_rows, rows, width), 'row', split_axis=0...  80.8 us
    ppermute x1, waiting for transfers between devices, per_device(): lax.ppermute(jnp.concatenate([ph_factor.astype(f32), recouple], axis=0),...  66.5 us
    all_to_all x1, waiting for transfers between devices, per_device(): lax.all_to_all(outgoing, 'ch', split_axis=1, concat_axis=1, tiled=True)  45.2 us
    all_to_all x1, waiting for transfers between devices, per_device(): lax.all_to_all(returning.reshape(n_chan * n_rows, slab, rows), ('ch', 'ro...  29.1 us
    all_to_all x1, starting transfers between devices, per_device(): lax.all_to_all(returning.reshape(n_chan * n_rows, slab, rows), ('ch', 'ro...  21.4 us
    another operation x2, other arithmetic, per_device(): stacked = jnp.stack([eta_pp, gamma_pp])  8.5 us
    add x1, other arithmetic, per_device(): ladder_c = product + product.T  6.8 us
  transfers between devices with their start and end apart: 5, of which 5 were waited for; matrix products, arithmetic and copies ran while one was open for 14% of the time, Pallas kernels for 0%

profile of v1, /device:TPU:8, one launch (start us, length us, event | category | flops | bytes accessed | tf_op | source)
XLA Modules:
  0.0 327.8 jit_solution(15456066500167216902)
XLA Ops:
  1.3 4.6 %pad_maximum_fusion.1 = bf16[2,4,2,128,1024]{4,3,2,1,0:T(8,128)(2,1)} fusion(bf16[1,4,2,128,1024]{4,3,2,1,0:T(8,128)(2,1)} %bitcast.50, bf16[1,4,2,128,1024]{4,3,2,1,0:T(8,128)(2,1)} %bitcast.52), kind=kLoop, calls=%fused_computation.3 | loop fusion | flops 2097152 | bytes 8388608 | tf_op jit(solution)/shard_map/stack | solution.py:19
  5.9 5.0 %gather_fusion.1 = bf16[8,2,128,1024]{3,2,1,0:T(8,128)(2,1)} fusion(bf16[2,4,2,128,1024]{4,3,2,1,0:T(8,128)(2,1)} %pad_maximum_fusion.1, s32[8]{0:T(128)S(1)} %fusion.15), kind=kCustom, calls=%fused_computation.1 | custom fusion | bytes 8388672 | tf_op jit(solution)/shard_map/gather | solution.py:29
  10.9 4.7 %all-to-all-start.2 = ((bf16[2,8,128,1024]{3,2,0,1:T(8,128)(2,1)}), bf16[2,8,128,1024]{3,2,0,1:T(8,128)(2,1)}, u32[]{:S(2)}, u32[]{:S(2)}) async-start(bf16[2,8,128,1024]{3,2,0,1:T(8,128)(2,1)} %bitcast.46), calls=%async_computation.2 | async-start | bytes 8388608 | tf_op jit(solution)/shard_map/all_to_all | solution.py:30
  15.6 4.0 %pad_maximum_fusion = bf16[2,4,256,1024]{3,2,0,1:T(8,128)(2,1)} fusion(bf16[1,4,256,1024]{3,2,0,1:T(8,128)(2,1)S(1)} %bitcast.51, bf16[1,4,256,1024]{3,2,0,1:T(8,128)(2,1)} %bitcast.53), kind=kLoop, calls=%fused_computation.2 | loop fusion | flops 2097152 | bytes 8388608 | tf_op jit(solution)/shard_map/stack | solution.py:19
  19.5 45.2 %all-to-all-done.2 = bf16[2,8,128,1024]{3,2,0,1:T(8,128)(2,1)} async-done(((bf16[2,8,128,1024]{3,2,0,1:T(8,128)(2,1)}), bf16[2,8,128,1024]{3,2,0,1:T(8,128)(2,1)}, u32[]{:S(2)}, u32[]{:S(2)}) %all-to-all-start.2) | async-done | bytes 4194336 | tf_op jit(solution)/shard_map/all_to_all | solution.py:30
  64.7 5.3 %all-to-all-start = ((bf16[2,4,256,1024]{3,2,0,1:T(8,128)(2,1)}), bf16[2,4,256,1024]{3,2,0,1:T(8,128)(2,1)}, u32[]{:S(2)}, u32[]{:S(2)}) async-start(bf16[2,4,256,1024]{3,2,0,1:T(8,128)(2,1)} %pad_maximum_fusion), calls=%async_computation | async-start | bytes 8388608 | tf_op jit(solution)/shard_map/all_to_all | solution.py:20
  70.0 1.9 collective-permute-start
  72.0 66.5 %collective-permute-done = f32[2,1024]{1,0:T(2,128)S(1)} collective-permute-done((f32[2,1024]{1,0:T(2,128)S(1)}, f32[2,1024]{1,0:T(2,128)S(1)}, u32[]{:S(2)}, u32[]{:S(2)}) %collective-permute-start) | collective-permute-done | bytes 8224 | tf_op jit(solution)/shard_map/ppermute | solution.py:35
  138.5 2.8 broadcast_multiply_fusion
  141.2 2.3 fusion.18
  143.6 3.7 %multiply_convert_fusion = bf16[1024,1024]{1,0:T(8,128)(2,1)} fusion(f32[1024,1024]{1,0:T(8,128)S(1)} %fusion.18, f32[1024]{0:T(1024)S(1)} %bitcast.60, bf16[1024,1024]{1,0:T(8,128)(2,1)S(1)} %bitcast.56, bf16[1024,1024]{1,0:T(8,128)(2,1)S(1)} %bitcast.57), kind=kOutput, calls=%fused_computation.6 | convolution fusion | flops 2150629376 | bytes 10489856 | tf_op jit(solution)/shard_map/dot_general | solution.py:42
  147.2 3.3 %reshape.146 = bf16[8,128,4,256]{3,2,1,0:T(4,128)(2,1)S(1)} reshape(bf16[1024,1024]{1,0:T(8,128)(2,1)} %multiply_convert_fusion) | data formatting | bytes 4194304 | tf_op jit(solution)/shard_map/reshape | solution.py:44
  152.3 4.7 %all-to-all-done = bf16[2,4,256,1024]{3,2,0,1:T(8,128)(2,1)} async-done(((bf16[2,4,256,1024]{3,2,0,1:T(8,128)(2,1)}), bf16[2,4,256,1024]{3,2,0,1:T(8,128)(2,1)}, u32[]{:S(2)}, u32[]{:S(2)}) %all-to-all-start) | async-done | bytes 4194336 | tf_op jit(solution)/shard_map/all_to_all | solution.py:20
  156.9 21.4 %all-to-all-start.3 = ((bf16[32,128,256]{2,1,0:T(8,128)(2,1)}), bf16[32,128,256]{2,1,0:T(8,128)(2,1)S(1)}, u32[]{:S(2)}, u32[]{:S(2)}) async-start(bf16[32,128,256]{2,1,0:T(8,128)(2,1)} %bitcast.48), calls=%async_computation.3 | async-start | bytes 4194304 | tf_op jit(solution)/shard_map/all_to_all | solution.py:45
  179.1 2.5 fusion.16
  181.6 4.3 %fusion.17 = f32[1024,1024]{1,0:T(8,128)} fusion(bf16[1024,1024]{1,0:T(8,128)(2,1)S(1)} %bitcast.55, bf16[1024,1024]{1,0:T(8,128)(2,1)S(1)} %bitcast.54), kind=kOutput, calls=%fused_computation.39 | convolution fusion | flops 2147483648 | bytes 8388608 | tf_op jit(solution)/shard_map/dot_general | solution.py:60
  185.9 5.4 %copy.14 = f32[1024,1024]{0,1:T(8,128)} copy(f32[1024,1024]{1,0:T(8,128)} %fusion.17) | data formatting | bytes 8388608 | tf_op jit(solution)/shard_map/dot_general | solution.py:60
  191.3 6.8 %bitcast_add_fusion = f32[1024,1024]{1,0:T(8,128)} fusion(f32[1024,1024]{1,0:T(8,128)} %fusion.17, f32[1024,1024]{0,1:T(8,128)} %copy.14), kind=kLoop, calls=%fused_computation.4 | loop fusion | flops 1048576 | bytes 12582912 | tf_op jit(solution)/shard_map/add | solution.py:61
  198.1 29.1 %all-to-all-done.3 = bf16[32,128,256]{2,1,0:T(8,128)(2,1)S(1)} async-done(((bf16[32,128,256]{2,1,0:T(8,128)(2,1)}), bf16[32,128,256]{2,1,0:T(8,128)(2,1)S(1)}, u32[]{:S(2)}, u32[]{:S(2)}) %all-to-all-start.3) | async-done | bytes 2097184 | tf_op jit(solution)/shard_map/all_to_all | solution.py:45
  227.2 5.1 %all-to-all-start.1 = ((f32[4,256,1024]{2,1,0:T(8,128)}), f32[4,256,1024]{2,1,0:T(8,128)}, u32[]{:S(2)}, u32[]{:S(2)}) async-start(f32[4,256,1024]{2,1,0:T(8,128)} %bitcast.44), calls=%async_computation.1 | async-start | bytes 8388608 | tf_op jit(solution)/shard_map/all_to_all | solution.py:62
  232.6 3.7 %fusion = f32[8,128,256,4]{2,3,1,0:T(4,128)} fusion(bf16[8,4,128,256]{3,2,1,0:T(8,128)(2,1)S(1)} %bitcast.49, s32[8,4]{1,0:T(8,128)S(1)} %eq.15), kind=kOutput, calls=%fused_computation.8 | convolution fusion | flops 8388736 | bytes 6291584 | tf_op jit(solution)/shard_map/gts,gtwi->sigw/dot_general | solution.py:56
  236.2 5.3 %copy.18 = f32[4,256,1024]{2,1,0:T(8,128)} copy(f32[4,256,1024]{1,0,2:T(4,128)} %bitcast.45) | data formatting | bytes 8388608 | tf_op jit(solution)/shard_map/reshape | solution.py:57
  241.5 80.8 %all-to-all-done.1 = f32[4,256,1024]{2,1,0:T(8,128)} async-done(((f32[4,256,1024]{2,1,0:T(8,128)}), f32[4,256,1024]{2,1,0:T(8,128)}, u32[]{:S(2)}, u32[]{:S(2)}) %all-to-all-start.1) | async-done | bytes 4194336 | tf_op jit(solution)/shard_map/all_to_all | solution.py:62
  322.3 5.5 %add_convert_fusion = bf16[4,256,1024]{2,1,0:T(8,128)(2,1)} fusion(f32[4,256,1024]{2,1,0:T(8,128)} %all-to-all-done.1, f32[4,256,1024]{2,1,0:T(8,128)} %copy.18), kind=kLoop, calls=%fused_computation.5 | loop fusion | flops 2097152 | bytes 10485760 | tf_op jit(solution)/shard_map/convert_element_type | solution.py:65
  (20 shorter events, 4.1 us)
Async XLA Ops:
  0.0 0.7 copy-start
  10.9 4.7 %copy-start.1 = (bf16[4,256,1024]{2,1,0:T(8,128)(2,1)S(1)}, bf16[4,256,1024]{2,1,0:T(8,128)(2,1)}, u32[]{:S(2)}) copy-start(bf16[4,256,1024]{2,1,0:T(8,128)(2,1)} %param.7) | copy-start | bytes 6291460
  10.9 53.8 %all-to-all-start.2 = ((bf16[2,8,128,1024]{3,2,0,1:T(8,128)(2,1)}), bf16[2,8,128,1024]{3,2,0,1:T(8,128)(2,1)}, u32[]{:S(2)}, u32[]{:S(2)}) async-start(bf16[2,8,128,1024]{3,2,0,1:T(8,128)(2,1)} %bitcast.46), calls=%async_computation.2 | async-start | bytes 8388608 | tf_op jit(solution)/shard_map/all_to_all | solution.py:30
  19.5 50.5 %copy-start.2 = (s32[1,1024]{1,0:T(1,128)S(1)}, s32[1,1024]{1,0:T(1,128)}, u32[]{:S(2)}) copy-start(s32[1,1024]{1,0:T(1,128)} %param.9) | copy-start | bytes 12292
  19.5 50.5 %copy-start.3 = (f32[1,1024]{1,0:T(1,128)S(1)}, f32[1,1024]{1,0:T(1,128)}, u32[]{:S(2)}) copy-start(f32[1,1024]{1,0:T(1,128)} %param.10) | copy-start | bytes 12292
  64.7 92.3 %all-to-all-start = ((bf16[2,4,256,1024]{3,2,0,1:T(8,128)(2,1)}), bf16[2,4,256,1024]{3,2,0,1:T(8,128)(2,1)}, u32[]{:S(2)}, u32[]{:S(2)}) async-start(bf16[2,4,256,1024]{3,2,0,1:T(8,128)(2,1)} %pad_maximum_fusion), calls=%async_computation | async-start | bytes 8388608 | tf_op jit(solution)/shard_map/all_to_all | solution.py:20
  70.0 68.4 %collective-permute-start = (f32[2,1024]{1,0:T(2,128)S(1)}, f32[2,1024]{1,0:T(2,128)S(1)}, u32[]{:S(2)}, u32[]{:S(2)}) collective-permute-start(f32[2,1024]{1,0:T(2,128)S(1)} %pad_maximum_fusion.2), channel_id=1, source_target_pairs={{0,0},{1,4},{2,8},{3,12},{4,16},{5,20},{6,24},{7,28},{8,1},{9,5},{... | collective-permute-start | bytes 24584 | tf_op jit(solution)/shard_map/ppermute | solution.py:35
  156.9 70.3 %all-to-all-start.3 = ((bf16[32,128,256]{2,1,0:T(8,128)(2,1)}), bf16[32,128,256]{2,1,0:T(8,128)(2,1)S(1)}, u32[]{:S(2)}, u32[]{:S(2)}) async-start(bf16[32,128,256]{2,1,0:T(8,128)(2,1)} %bitcast.48), calls=%async_computation.3 | async-start | bytes 4194304 | tf_op jit(solution)/shard_map/all_to_all | solution.py:45
  227.2 95.1 %all-to-all-start.1 = ((f32[4,256,1024]{2,1,0:T(8,128)}), f32[4,256,1024]{2,1,0:T(8,128)}, u32[]{:S(2)}, u32[]{:S(2)}) async-start(f32[4,256,1024]{2,1,0:T(8,128)} %bitcast.44), calls=%async_computation.1 | async-start | bytes 8388608 | tf_op jit(solution)/shard_map/all_to_all | solution.py:62

commit v2 on v1

--- a/solution.py
+++ b/solution.py
@@ -2,6 +2,10 @@
 import jax.numpy as jnp
 from jax import lax
 from jax.sharding import PartitionSpec as P
+
+
+def skip_block(x, b, size):
+    return jnp.concatenate([x[..., (b + 1) * size :], x[..., : b * size]], axis=-1)
 
 
 def per_device(eta_pp, gamma_pp, pp_factor, ph_factor, recouple, src_slot):
@@ -17,9 +21,17 @@
     level = lax.axis_index("row")
 
     stacked = jnp.stack([eta_pp, gamma_pp])
-    whole = lax.all_to_all(stacked, "row", split_axis=1, concat_axis=2, tiled=True)
-    eta_c = whole[0, 0]
-    gamma_c = whole[1, 0]
+    sending = jnp.stack(
+        [skip_block(stacked[:, s], s, rows) for s in range(n_rows)], axis=1
+    )
+    whole = lax.all_to_all(sending, "row", split_axis=1, concat_axis=1, tiled=True)
+    own = lax.dynamic_index_in_dim(stacked, level, 1, False)
+    own_t = own.reshape(2, rows, n_rows, rows).transpose(0, 2, 3, 1)
+    own_t = own_t * jnp.array([-1, 1], bf16)[:, None, None, None]
+    whole = jnp.concatenate([whole, own_t], axis=-1)
+    whole = jnp.roll(whole, (level + 1) * rows, axis=-1).reshape(2, width, width)
+    eta_c = whole[0]
+    gamma_c = whole[1]
 
     dest = jnp.arange(n_chan, dtype=jnp.int32)
     q_dest = level * n_chan + dest
@@ -27,7 +39,12 @@
     part_dest = q_dest // ch_dev - level * (rows // slab)
     five = stacked.reshape(2, ch_dev, rows // slab, slab, width)
     outgoing = five[:, slot_dest, part_dest]
-    arrived = lax.all_to_all(outgoing, "ch", split_axis=1, concat_axis=1, tiled=True)
+    pieces = [lax.dynamic_index_in_dim(outgoing, mine, 1, False)]
+    for shift in range(1, n_chan):
+        piece = lax.dynamic_index_in_dim(outgoing, (mine + shift) % n_chan, 1, False)
+        pairs = [(a, (a + shift) % n_chan) for a in range(n_chan)]
+        pieces.append(lax.ppermute(piece, "ch", pairs))
+    arrived = jnp.stack(pieces, axis=1)[:, (mine - dest) % n_chan]
     a_eta = arrived[0].reshape(width, width)
     b_gamma = arrived[1].reshape(width, width)
 
@@ -58,10 +75,14 @@
 
     factor = lax.dynamic_index_in_dim(pp_factor, level, 0, False).astype(bf16)
     product = jnp.dot(eta_c * factor[None, :], gamma_c, preferred_element_type=f32)
-    ladder_c = product + product.T
-    ladder = lax.all_to_all(
-        ladder_c.reshape(n_rows, rows, width), "row", split_axis=0, concat_axis=0, tiled=True
-    )
+    ladder_c = (product + product.T).reshape(n_rows, rows, width)
+    sending = jnp.stack([skip_block(ladder_c[a], a, rows) for a in range(n_rows)])
+    ladder = lax.all_to_all(sending, "row", split_axis=0, concat_axis=0, tiled=True)
+    weighted = eta_pp * pp_factor.astype(bf16)[:, None, :]
+    diag = jnp.einsum("sik,sjk->sij", weighted, gamma_pp, preferred_element_type=f32)
+    diag = diag + jnp.swapaxes(diag, 1, 2)
+    ladder = jnp.concatenate([ladder, diag], axis=-1)
+    ladder = jnp.roll(ladder, (level + 1) * rows, axis=-1)
     return (ladder + back).astype(bf16)
 
 

time: 333 us -> 275 us (0.83)
  waiting for transfers between devices: 226 us -> 104 us
  local copies, waits for them, and re-layouts: 22.3 us -> 59.7 us
  starting transfers between devices: 38.4 us -> 49.9 us
  other arithmetic: 26.9 us -> 35.5 us
  matrix products: 14 us -> 20.1 us
    all_to_all x3 -> x2, waiting for transfers between devices: 131 us -> 47.7 us  [the longest x1 47.7 us: per_device(): lax.all_to_all(sending, 'row', split_axis=0, concat_axis=0, tiled=True)]
    ppermute x1, waiting for transfers between devices: 66.5 us -> 29.2 us  [per_device(): lax.ppermute(jnp.concatenate([ph_factor.astype(f32), recouple], axis=0),...]
    ppermute x0 -> x7, starting transfers between devices: none -> 26.6 us  [per_device(): pieces.append(lax.ppermute(piece, 'ch', pairs))]
    all_to_all x1, waiting for transfers between devices: 29.1 us -> 11.7 us  [per_device(): lax.all_to_all(returning.reshape(n_chan * n_rows, slab, rows), ('ch', 'ro...]
    ppermute x0 -> x7, waiting for transfers between devices: none -> 15.4 us  [per_device(): pieces.append(lax.ppermute(piece, 'ch', pairs))]
    unnamed x8 -> x19, local copies, waits for them, and re-layouts: 0.69 us -> 13.7 us
    all_to_all x1, starting transfers between devices: 21.4 us -> 11 us  [per_device(): lax.all_to_all(returning.reshape(n_chan * n_rows, slab, rows), ('ch', 'ro...]
    mul x0 -> x2, local copies, waits for them, and re-layouts: none -> 6.31 us  [the longest x1 4.01 us: per_device(): eta_c * factor[None, :]]
  transfers between devices with their start and end apart: 5 -> 11, of which waited for: 5 -> 5; matrix products, arithmetic and copies ran while one was open for 14% -> 37% of each run, Pallas kernels for 0% -> 0%
where the time goes in v2:
time: 275 us; the launch traced here: 270 us
  waiting for transfers between devices  104 us (38%)
  local copies, waits for them, and re-layouts  59.7 us (22%)
  starting transfers between devices  49.9 us (18%)
  other arithmetic  35.5 us (13%)
  matrix products  20.1 us (7%)
    all_to_all x1, waiting for transfers between devices, per_device(): lax.all_to_all(sending, 'row', split_axis=0, concat_axis=0, tiled=True)  47.7 us
    ppermute x1, waiting for transfers between devices, per_device(): lax.ppermute(jnp.concatenate([ph_factor.astype(f32), recouple], axis=0),...  29.2 us
    ppermute x7, starting transfers between devices, per_device(): pieces.append(lax.ppermute(piece, 'ch', pairs))  26.6 us
    ppermute x7, waiting for transfers between devices, per_device(): pieces.append(lax.ppermute(piece, 'ch', pairs))  15.4 us
    unnamed x19, local copies, waits for them, and re-layouts  13.7 us
    all_to_all x1, waiting for transfers between devices, per_device(): lax.all_to_all(returning.reshape(n_chan * n_rows, slab, rows), ('ch', 'ro...  11.7 us
    all_to_all x1, starting transfers between devices, per_device(): lax.all_to_all(returning.reshape(n_chan * n_rows, slab, rows), ('ch', 'ro...  11 us
    reshape x2, local copies, waits for them, and re-layouts, per_device(): returning = term_t.reshape(n_chan, slab, n_rows, rows).transpose(0, 2, 1, 3)  7.85 us
  transfers between devices with their start and end apart: 11, of which 5 were waited for; matrix products, arithmetic and copies ran while one was open for 37% of the time, Pallas kernels for 0%

profile of v2, /device:TPU:8, one launch (start us, length us, event | category | flops | bytes accessed | tf_op | source)
XLA Modules:
  0.0 269.5 jit_solution(5553025176230618551)
XLA Ops:
  2.9 3.9 %copy.25 = bf16[4,256,1024]{1,2,0:T(8,128)(2,1)} copy(bf16[4,256,1024]{2,1,0:T(8,128)(2,1)} %param.8) | data formatting | bytes 4194304 | tf_op args[1]
  11.8 5.6 %all-to-all-start = ((bf16[2,4,256,768]{2,3,0,1:T(8,128)(2,1)}), bf16[2,4,256,768]{2,3,0,1:T(8,128)(2,1)S(1)}, u32[]{:S(2)}, u32[]{:S(2)}) async-start(bf16[2,4,256,768]{2,3,0,1:T(8,128)(2,1)} %pad_maximum_fusion.1), calls=%async_computation | async-start | bytes 6291456 | tf_op jit(solution)/shard_map/all_to_all | solution.py:27
  18.0 4.6 %pad_maximum_fusion = bf16[2,4,2,128,1024]{4,3,2,1,0:T(8,128)(2,1)} fusion(bf16[1,4,2,128,1024]{4,3,2,1,0:T(8,128)(2,1)} %bitcast.110, bf16[1,4,2,128,1024]{4,3,2,1,0:T(8,128)(2,1)} %bitcast.111), kind=kLoop, calls=%fused_computation.29 | loop fusion | flops 2097152 | bytes 8388608 | tf_op jit(solution)/shard_map/stack | solution.py:23
  22.7 5.0 %gather_fusion.1 = bf16[8,2,128,1024]{3,2,1,0:T(8,128)(2,1)} fusion(bf16[2,4,2,128,1024]{4,3,2,1,0:T(8,128)(2,1)} %pad_maximum_fusion, s32[8]{0:T(128)S(1)} %fusion.40), kind=kCustom, calls=%fused_computation.1 | custom fusion | bytes 8388672 | tf_op jit(solution)/shard_map/gather | solution.py:41
  40.5 29.2 %collective-permute-done.7 = f32[2,1024]{1,0:T(2,128)S(1)} collective-permute-done((f32[2,1024]{1,0:T(2,128)S(1)}, f32[2,1024]{1,0:T(2,128)S(1)}, u32[]{:S(2)}, u32[]{:S(2)}) %collective-permute-start.7) | collective-permute-done | bytes 8224 | tf_op jit(solution)/shard_map/ppermute | solution.py:52
  69.7 15.1 %collective-permute-start.4 = (bf16[2,128,1024]{2,1,0:T(8,128)(2,1)S(1)}, bf16[2,128,1024]{2,1,0:T(8,128)(2,1)S(1)}, u32[]{:S(2)}, u32[]{:S(2)}) collective-permute-start(bf16[2,128,1024]{2,1,0:T(8,128)(2,1)S(1)} %get-tuple-element.24), channel_id=1, source_target_pairs={{0,20},{4,24},{8,28},{12,0},{16,4},{20,8},{24,12},{28,16},{1,21},{... | collective-permute-start | bytes 1572872 | tf_op jit(solution)/shard_map/ppermute | solution.py:46
  95.1 5.6 %collective-permute-done.5 = bf16[2,128,1024]{2,1,0:T(8,128)(2,1)S(1)} collective-permute-done((bf16[2,128,1024]{2,1,0:T(8,128)(2,1)S(1)}, bf16[2,128,1024]{2,1,0:T(8,128)(2,1)S(1)}, u32[]{:S(2)}, u32[]{:S(2)}) %collective-permute-start.5) | collective-permute-done | bytes 524320 | tf_op jit(solution)/shard_map/ppermute | solution.py:46
  101.5 9.8 %collective-permute-done.6 = bf16[2,128,1024]{2,1,0:T(8,128)(2,1)S(1)} collective-permute-done((bf16[2,128,1024]{2,1,0:T(8,128)(2,1)S(1)}, bf16[2,128,1024]{2,1,0:T(8,128)(2,1)S(1)}, u32[]{:S(2)}, u32[]{:S(2)}) %collective-permute-start.6) | collective-permute-done | bytes 524320 | tf_op jit(solution)/shard_map/ppermute | solution.py:46
  112.2 5.0 %gather_fusion.2 = bf16[8,2,128,1024]{3,2,1,0:T(8,128)(2,1)} fusion(bf16[2,8,128,1024]{3,2,0,1:T(8,128)(2,1)} %bitcast_dynamic-update-slice_fusion, s32[1024]{0:T(1024)S(1)} %pad_clamp_fusion), kind=kCustom, calls=%fused_computation.2 | custom fusion | bytes 8388640 | tf_op jit(solution)/shard_map/gather | solution.py:47
  122.2 3.7 %multiply_convert_fusion = bf16[1024,1024]{1,0:T(8,128)(2,1)} fusion(f32[1024,1024]{1,0:T(8,128)S(1)} %fusion.45, f32[1024]{0:T(1024)S(1)} %bitcast.120, bf16[1024,1024]{1,0:T(8,128)(2,1)S(1)} %bitcast.116, bf16[1024,1024]{1,0:T(8,128)(2,1)S(1)} %bitcast.117), kind=kOutput, calls=%fused_computation.31 | convolution fusion | flops 2150629376 | bytes 10489856 | tf_op jit(solution)/shard_map/dot_general | solution.py:59
  125.9 4.5 %reshape.194 = bf16[8,128,4,256]{3,2,1,0:T(4,128)(2,1)} reshape(bf16[1024,1024]{1,0:T(8,128)(2,1)} %multiply_convert_fusion) | data formatting | bytes 4194304 | tf_op jit(solution)/shard_map/reshape | solution.py:61
  133.8 11.0 %all-to-all-start.2 = ((bf16[32,128,256]{2,1,0:T(8,128)(2,1)}), bf16[32,128,256]{2,1,0:T(8,128)(2,1)}, u32[]{:S(2)}, u32[]{:S(2)}) async-start(bf16[32,128,256]{2,1,0:T(8,128)(2,1)} %bitcast.109), calls=%async_computation.2 | async-start | bytes 4194304 | tf_op jit(solution)/shard_map/all_to_all | solution.py:62
  149.4 5.6 %fusion.7 = bf16[2,4,256,1024]{2,3,0,1:T(8,128)(2,1)S(1)} fusion(s32[]{:T(128)S(6)} %select_n.149, bf16[2,4,256,768]{2,3,0,1:T(8,128)(2,1)S(1)} %all-to-all-done, bf16[2,4,256,256]{2,3,0,1:T(8,128)(2,1)} %copy.26), kind=kLoop, calls=%fused_computation.28 | loop fusion | flops 16777216 | bytes 8388612 | tf_op jit(solution)/shard_map/jit(_roll_dynamic)/concatenate | solution.py:32
  156.7 4.0 %copy.28 = bf16[1,4,256,1024]{3,2,1,0:T(8,128)(2,1)} copy(bf16[1,4,256,1024]{2,3,0,1:T(8,128)(2,1)} %get-tuple-element.14) | data formatting | bytes 4194304 | tf_op jit(solution)/shard_map/mul | solution.py:77
  163.2 6.5 %fusion.44 = f32[1024,1024]{1,0:T(8,128)} fusion(bf16[1024,1024]{1,0:T(8,128)(2,1)} %bitcast.114, bf16[1024,1024]{1,0:T(8,128)(2,1)} %bitcast.115), kind=kOutput, calls=%fused_computation.115 | convolution fusion | flops 2147483648 | bytes 8388608 | tf_op jit(solution)/shard_map/dot_general | solution.py:77
  169.7 5.4 %copy.30 = f32[1024,1024]{0,1:T(8,128)} copy(f32[1024,1024]{1,0:T(8,128)} %fusion.44) | data formatting | bytes 8388608 | tf_op jit(solution)/shard_map/dot_general | solution.py:77
  175.1 4.4 %bitcast_add_fusion = f32[1024,1024]{1,0:T(8,128)S(1)} fusion(f32[1024,1024]{1,0:T(8,128)} %fusion.44, f32[1024,1024]{0,1:T(8,128)} %copy.30), kind=kLoop, calls=%fused_computation.30 | loop fusion | flops 1048576 | bytes 12582912 | tf_op jit(solution)/shard_map/add | solution.py:78
  181.9 11.7 %all-to-all-done.2 = bf16[32,128,256]{2,1,0:T(8,128)(2,1)} async-done(((bf16[32,128,256]{2,1,0:T(8,128)(2,1)}), bf16[32,128,256]{2,1,0:T(8,128)(2,1)}, u32[]{:S(2)}, u32[]{:S(2)}) %all-to-all-start.2) | async-done | bytes 2097184 | tf_op jit(solution)/shard_map/all_to_all | solution.py:62
  193.6 3.7 %all-to-all-start.1 = ((f32[4,256,768]{2,1,0:T(8,128)}), f32[4,256,768]{2,1,0:T(8,128)S(1)}, u32[]{:S(2)}, u32[]{:S(2)}) async-start(f32[4,256,768]{2,1,0:T(8,128)} %pad_maximum_fusion.2), calls=%async_computation.1 | async-start | bytes 6291456 | tf_op jit(solution)/shard_map/all_to_all | solution.py:80
  197.4 3.9 %fusion.10 = f32[4,256,256]{2,1,0:T(8,128)} fusion(bf16[4,256,1024]{2,1,0:T(8,128)(2,1)} %param.8, bf16[4,256,1024]{2,1,0:T(8,128)(2,1)} %param.7, bf16[4,1024]{1,0:T(4,128)(2,1)S(1)} %convert_element_type.20), kind=kOutput, calls=%fused_computation.37 | convolution fusion | flops 537919488 | bytes 5251072 | tf_op jit(solution)/shard_map/sik,sjk->sij/dot_general | solution.py:82
  208.3 3.7 %fusion.8 = f32[8,128,256,4]{2,3,1,0:T(4,128)} fusion(bf16[8,4,128,256]{3,2,1,0:T(8,128)(2,1)S(1)} %bitcast.112, s32[8,4]{1,0:T(8,128)S(1)} %eq.30), kind=kOutput, calls=%fused_computation.35 | convolution fusion | flops 8388736 | bytes 6291584 | tf_op jit(solution)/shard_map/gts,gtwi->sigw/dot_general | solution.py:73
  212.0 5.3 %copy.37 = f32[4,256,1024]{2,1,0:T(8,128)} copy(f32[4,256,1024]{1,0,2:T(4,128)} %bitcast.106) | data formatting | bytes 8388608 | tf_op jit(solution)/shard_map/reshape | solution.py:74
  217.3 47.7 %all-to-all-done.1 = f32[4,256,768]{2,1,0:T(8,128)S(1)} async-done(((f32[4,256,768]{2,1,0:T(8,128)}), f32[4,256,768]{2,1,0:T(8,128)S(1)}, u32[]{:S(2)}, u32[]{:S(2)}) %all-to-all-start.1) | async-done | bytes 3145760 | tf_op jit(solution)/shard_map/all_to_all | solution.py:80
  265.0 4.5 %fusion.4 = bf16[4,256,1024]{2,1,0:T(8,128)(2,1)} fusion(f32[4,256,1024]{2,1,0:T(8,128)} %copy.37, s32[]{:T(128)S(6)} %select_n.149, f32[4,256,768]{2,1,0:T(8,128)S(1)} %all-to-all-done.1, f32[4,256,256]{2,1,0:T(8,128)} %bitcast_add_fusion.1), kind=kLoop, calls=%fused_computation.25 | loop fusion | flops 5242880 | bytes 10485764 | tf_op jit(solution)/shard_map/convert_element_type | solution.py:86
  (70 shorter events, 59.9 us)
Async XLA Ops:
  0.0 17.4 %copy-start = (s32[32,8]{0,1:T(8,128)S(1)}, s32[32,8]{0,1:T(8,128)}, u32[]{:S(2)}) copy-start(s32[32,8]{0,1:T(8,128)} %param.12) | copy-start | bytes 3076
  11.8 121.9 %all-to-all-start = ((bf16[2,4,256,768]{2,3,0,1:T(8,128)(2,1)}), bf16[2,4,256,768]{2,3,0,1:T(8,128)(2,1)S(1)}, u32[]{:S(2)}, u32[]{:S(2)}) async-start(bf16[2,4,256,768]{2,3,0,1:T(8,128)(2,1)} %pad_maximum_fusion.1), calls=%async_computation | async-start | bytes 6291456 | tf_op jit(solution)/shard_map/all_to_all | solution.py:27
  27.6 2.5 copy-start.2
  27.6 2.5 copy-start.3
  30.0 54.8 %collective-permute-start = (bf16[2,128,1024]{2,1,0:T(8,128)(2,1)S(1)}, bf16[2,128,1024]{2,1,0:T(8,128)(2,1)S(1)}, u32[]{:S(2)}, u32[]{:S(2)}) collective-permute-start(bf16[2,128,1024]{2,1,0:T(8,128)(2,1)S(1)} %get-tuple-element.28), channel_id=1, source_target_pairs={{0,4},{4,8},{8,12},{12,16},{16,20},{20,24},{24,28},{28,0},{1,5},{5... | collective-permute-start | bytes 1572872 | tf_op jit(solution)/shard_map/ppermute | solution.py:46
  30.1 39.6 %collective-permute-start.7 = (f32[2,1024]{1,0:T(2,128)S(1)}, f32[2,1024]{1,0:T(2,128)S(1)}, u32[]{:S(2)}, u32[]{:S(2)}) collective-permute-start(f32[2,1024]{1,0:T(2,128)S(1)} %pad_maximum_fusion.3), channel_id=1, source_target_pairs={{0,0},{1,4},{2,8},{3,12},{4,16},{5,20},{6,24},{7,28},{8,1},{9,5},{... | collective-permute-start | bytes 24584 | tf_op jit(solution)/shard_map/ppermute | solution.py:52
  33.2 56.0 %collective-permute-start.1 = (bf16[2,128,1024]{2,1,0:T(8,128)(2,1)S(1)}, bf16[2,128,1024]{2,1,0:T(8,128)(2,1)S(1)}, u32[]{:S(2)}, u32[]{:S(2)}) collective-permute-start(bf16[2,128,1024]{2,1,0:T(8,128)(2,1)S(1)} %get-tuple-element.27), channel_id=1, source_target_pairs={{0,8},{4,12},{8,16},{12,20},{16,24},{20,28},{24,0},{28,4},{1,9},{5... | collective-permute-start | bytes 1572872 | tf_op jit(solution)/shard_map/ppermute | solution.py:46
  35.3 57.3 %collective-permute-start.2 = (bf16[2,128,1024]{2,1,0:T(8,128)(2,1)S(1)}, bf16[2,128,1024]{2,1,0:T(8,128)(2,1)S(1)}, u32[]{:S(2)}, u32[]{:S(2)}) collective-permute-start(bf16[2,128,1024]{2,1,0:T(8,128)(2,1)S(1)} %get-tuple-element.26), channel_id=1, source_target_pairs={{0,12},{4,16},{8,20},{12,24},{16,28},{20,0},{24,4},{28,8},{1,13},{... | collective-permute-start | bytes 1572872 | tf_op jit(solution)/shard_map/ppermute | solution.py:46
  37.2 56.3 %collective-permute-start.3 = (bf16[2,128,1024]{2,1,0:T(8,128)(2,1)S(1)}, bf16[2,128,1024]{2,1,0:T(8,128)(2,1)S(1)}, u32[]{:S(2)}, u32[]{:S(2)}) collective-permute-start(bf16[2,128,1024]{2,1,0:T(8,128)(2,1)S(1)} %get-tuple-element.25), channel_id=1, source_target_pairs={{0,16},{4,20},{8,24},{12,28},{16,0},{20,4},{24,8},{28,12},{1,17},{... | collective-permute-start | bytes 1572872 | tf_op jit(solution)/shard_map/ppermute | solution.py:46
  69.7 24.6 %collective-permute-start.4 = (bf16[2,128,1024]{2,1,0:T(8,128)(2,1)S(1)}, bf16[2,128,1024]{2,1,0:T(8,128)(2,1)S(1)}, u32[]{:S(2)}, u32[]{:S(2)}) collective-permute-start(bf16[2,128,1024]{2,1,0:T(8,128)(2,1)S(1)} %get-tuple-element.24), channel_id=1, source_target_pairs={{0,20},{4,24},{8,28},{12,0},{16,4},{20,8},{24,12},{28,16},{1,21},{... | collective-permute-start | bytes 1572872 | tf_op jit(solution)/shard_map/ppermute | solution.py:46
  84.8 15.9 %collective-permute-start.5 = (bf16[2,128,1024]{2,1,0:T(8,128)(2,1)S(1)}, bf16[2,128,1024]{2,1,0:T(8,128)(2,1)S(1)}, u32[]{:S(2)}, u32[]{:S(2)}) collective-permute-start(bf16[2,128,1024]{2,1,0:T(8,128)(2,1)S(1)} %get-tuple-element.23), channel_id=1, source_target_pairs={{0,24},{4,28},{8,0},{12,4},{16,8},{20,12},{24,16},{28,20},{1,25},{... | collective-permute-start | bytes 1572872 | tf_op jit(solution)/shard_map/ppermute | solution.py:46
  89.2 22.1 %collective-permute-start.6 = (bf16[2,128,1024]{2,1,0:T(8,128)(2,1)S(1)}, bf16[2,128,1024]{2,1,0:T(8,128)(2,1)S(1)}, u32[]{:S(2)}, u32[]{:S(2)}) collective-permute-start(bf16[2,128,1024]{2,1,0:T(8,128)(2,1)S(1)} %get-tuple-element.22), channel_id=1, source_target_pairs={{0,28},{4,0},{8,4},{12,8},{16,12},{20,16},{24,20},{28,24},{1,29},{... | collective-permute-start | bytes 1572872 | tf_op jit(solution)/shard_map/ppermute | solution.py:46
  130.4 14.3 %copy-start.4 = (bf16[2]{0:T(256)(128)(2,1)S(1)}, bf16[2]{0:T(256)(128)(2,1)}, u32[]{:S(2)}) copy-start(bf16[2]{0:T(256)(128)(2,1)} %constant.146.clone) | copy-start | bytes 16
  133.8 15.6 %copy-start.1 = (s32[4,1024]{1,0:T(4,128)S(1)}, s32[4,1024]{1,0:T(4,128)}, u32[]{:S(2)}) copy-start(s32[4,1024]{1,0:T(4,128)} %param.9) | copy-start | bytes 49156
  133.8 59.9 %all-to-all-start.2 = ((bf16[32,128,256]{2,1,0:T(8,128)(2,1)}), bf16[32,128,256]{2,1,0:T(8,128)(2,1)}, u32[]{:S(2)}, u32[]{:S(2)}) async-start(bf16[32,128,256]{2,1,0:T(8,128)(2,1)} %bitcast.109), calls=%async_computation.2 | async-start | bytes 4194304 | tf_op jit(solution)/shard_map/all_to_all | solution.py:62
  193.6 71.4 %all-to-all-start.1 = ((f32[4,256,768]{2,1,0:T(8,128)}), f32[4,256,768]{2,1,0:T(8,128)S(1)}, u32[]{:S(2)}, u32[]{:S(2)}) async-start(f32[4,256,768]{2,1,0:T(8,128)} %pad_maximum_fusion.2), calls=%async_computation.1 | async-start | bytes 6291456 | tf_op jit(solution)/shard_map/all_to_all | solution.py:80

commit v3 on v2

--- a/solution.py
+++ b/solution.py
@@ -25,14 +25,6 @@
         [skip_block(stacked[:, s], s, rows) for s in range(n_rows)], axis=1
     )
     whole = lax.all_to_all(sending, "row", split_axis=1, concat_axis=1, tiled=True)
-    own = lax.dynamic_index_in_dim(stacked, level, 1, False)
-    own_t = own.reshape(2, rows, n_rows, rows).transpose(0, 2, 3, 1)
-    own_t = own_t * jnp.array([-1, 1], bf16)[:, None, None, None]
-    whole = jnp.concatenate([whole, own_t], axis=-1)
-    whole = jnp.roll(whole, (level + 1) * rows, axis=-1).reshape(2, width, width)
-    eta_c = whole[0]
-    gamma_c = whole[1]
-
     dest = jnp.arange(n_chan, dtype=jnp.int32)
     q_dest = level * n_chan + dest
     slot_dest = src_slot[q_dest, mine]
@@ -44,10 +36,24 @@
         piece = lax.dynamic_index_in_dim(outgoing, (mine + shift) % n_chan, 1, False)
         pairs = [(a, (a + shift) % n_chan) for a in range(n_chan)]
         pieces.append(lax.ppermute(piece, "ch", pairs))
+    whole, pieces = lax.optimization_barrier((whole, pieces))
     arrived = jnp.stack(pieces, axis=1)[:, (mine - dest) % n_chan]
     a_eta = arrived[0].reshape(width, width)
     b_gamma = arrived[1].reshape(width, width)
 
+    own = lax.dynamic_index_in_dim(stacked, level, 1, False)
+    own_t = own.reshape(2, rows, n_rows, rows).transpose(0, 2, 3, 1)
+    own_t = own_t * jnp.array([-1, 1], bf16)[:, None, None, None]
+    whole = jnp.concatenate([whole, own_t], axis=-1)
+    whole = jnp.roll(whole, (level + 1) * rows, axis=-1).reshape(2, width, width)
+    eta_c = whole[0]
+    gamma_c = whole[1]
+
+    factor = lax.dynamic_index_in_dim(pp_factor, level, 0, False).astype(bf16)
+    product = jnp.dot(eta_c * factor[None, :], gamma_c, preferred_element_type=f32)
+    ladder_c = (product + product.T).reshape(n_rows, rows, width)
+    sending = jnp.stack([skip_block(ladder_c[a], a, rows) for a in range(n_rows)])
+    ladder = lax.all_to_all(sending, "row", split_axis=0, concat_axis=0, tiled=True)
     perm = [(q, (q % n_chan) * n_rows + q // n_chan) for q in range(n_total)]
     coefs = lax.ppermute(
         jnp.concatenate([ph_factor.astype(f32), recouple], axis=0), ("ch", "row"), perm
@@ -58,6 +64,7 @@
     ph_t = jnp.dot(a_eta * weight, b_gamma, preferred_element_type=f32)
     ph_t = ph_t - jnp.dot(b_gamma * weight, a_eta, preferred_element_type=f32)
     term_t = (ph_t * coef[:, None]).astype(bf16)
+    ladder, term_t = lax.optimization_barrier((ladder, term_t))
     returning = term_t.reshape(n_chan, slab, n_rows, rows).transpose(0, 2, 1, 3)
     landed = lax.all_to_all(
         returning.reshape(n_chan * n_rows, slab, rows),
@@ -73,11 +80,6 @@
     back = jnp.einsum("gts,gtwi->sigw", onehot, landed, preferred_element_type=f32)
     back = back.reshape(ch_dev, rows, width)
 
-    factor = lax.dynamic_index_in_dim(pp_factor, level, 0, False).astype(bf16)
-    product = jnp.dot(eta_c * factor[None, :], gamma_c, preferred_element_type=f32)
-    ladder_c = (product + product.T).reshape(n_rows, rows, width)
-    sending = jnp.stack([skip_block(ladder_c[a], a, rows) for a in range(n_rows)])
-    ladder = lax.all_to_all(sending, "row", split_axis=0, concat_axis=0, tiled=True)
     weighted = eta_pp * pp_factor.astype(bf16)[:, None, :]
     diag = jnp.einsum("sik,sjk->sij", weighted, gamma_pp, preferred_element_type=f32)
     diag = diag + jnp.swapaxes(diag, 1, 2)

time: 275 us -> 300 us (1.091); the launches traced: 270 us -> 298 us
  waiting for transfers between devices: 104 us -> 121 us
  local copies, waits for them, and re-layouts: 59.7 us -> 68.2 us
  starting transfers between devices: 49.9 us -> 53.1 us
    all_to_all x1, waiting for transfers between devices: 47.7 us -> 0.01 us  [per_device(): lax.all_to_all(sending, 'row', split_axis=0, concat_axis=0, tiled=True)]
    all_to_all x1, waiting for transfers between devices: 11.7 us -> 39.4 us  [per_device(): lax.all_to_all(returning.reshape(n_chan * n_rows, slab, rows), ('ch', 'ro...]
    ppermute x1, waiting for transfers between devices: 29.2 us -> 49.7 us  [per_device(): lax.ppermute(jnp.concatenate([ph_factor.astype(f32), recouple], axis=0),...]
    ppermute x7, waiting for transfers between devices: 15.4 us -> 26.4 us  [per_device(): pieces.append(lax.ppermute(piece, 'ch', pairs))]
    all_to_all x1, starting transfers between devices: 11 us -> 21.6 us  [per_device(): lax.all_to_all(returning.reshape(n_chan * n_rows, slab, rows), ('ch', 'ro...]
    ppermute x7, starting transfers between devices: 26.6 us -> 16.9 us  [per_device(): pieces.append(lax.ppermute(piece, 'ch', pairs))]
    unnamed x19, local copies, waits for them, and re-layouts: 13.7 us -> 19.9 us
    all_to_all x1, waiting for transfers between devices: 0.01 us -> 5.33 us  [per_device(): lax.all_to_all(sending, 'row', split_axis=1, concat_axis=1, tiled=True)]
  transfers between devices with their start and end apart: 11 -> 11, of which waited for: 5 -> 7; matrix products, arithmetic and copies ran while one was open for 37% -> 19% of each run, Pallas kernels for 0% -> 0%
where the time goes in v3:
time: 300 us; the launch traced here: 298 us
  waiting for transfers between devices  121 us (40%)
  local copies, waits for them, and re-layouts  68.2 us (23%)
  starting transfers between devices  53.1 us (18%)
  other arithmetic  35.5 us (12%)
  matrix products  20.2 us (7%)
    ppermute x1, waiting for transfers between devices, per_device(): lax.ppermute(jnp.concatenate([ph_factor.astype(f32), recouple], axis=0),...  49.7 us
    all_to_all x1, waiting for transfers between devices, per_device(): lax.all_to_all(returning.reshape(n_chan * n_rows, slab, rows), ('ch', 'ro...  39.4 us
    ppermute x7, waiting for transfers between devices, per_device(): pieces.append(lax.ppermute(piece, 'ch', pairs))  26.4 us
    all_to_all x1, starting transfers between devices, per_device(): lax.all_to_all(returning.reshape(n_chan * n_rows, slab, rows), ('ch', 'ro...  21.6 us
    unnamed x19, local copies, waits for them, and re-layouts  19.9 us
    ppermute x7, starting transfers between devices, per_device(): pieces.append(lax.ppermute(piece, 'ch', pairs))  16.9 us
    reshape x2, local copies, waits for them, and re-layouts, per_device(): returning = term_t.reshape(n_chan, slab, n_rows, rows).transpose(0, 2, 1, 3)  7.83 us
    another operation x2, other arithmetic, per_device(): stacked = jnp.stack([eta_pp, gamma_pp])  7.3 us
  transfers between devices with their start and end apart: 11, of which 7 were waited for; matrix products, arithmetic and copies ran while one was open for 19% of the time, Pallas kernels for 0%

profile of v3, /device:TPU:8, one launch (start us, length us, event | category | flops | bytes accessed | tf_op | source)
XLA Modules:
  0.0 298.2 jit_solution(16958147779324406163)
XLA Ops:
  2.9 3.9 %copy.25 = bf16[4,256,1024]{1,2,0:T(8,128)(2,1)} copy(bf16[4,256,1024]{2,1,0:T(8,128)(2,1)} %param.8) | data formatting | bytes 4194304 | tf_op args[1]
  11.8 5.3 %all-to-all-start = ((bf16[2,4,256,768]{2,3,0,1:T(8,128)(2,1)}), bf16[2,4,256,768]{2,3,0,1:T(8,128)(2,1)S(1)}, u32[]{:S(2)}, u32[]{:S(2)}) async-start(bf16[2,4,256,768]{2,3,0,1:T(8,128)(2,1)} %pad_maximum_fusion.1), calls=%async_computation | async-start | bytes 6291456 | tf_op jit(solution)/shard_map/all_to_all | solution.py:27
  17.8 4.6 %pad_maximum_fusion = bf16[2,4,2,128,1024]{4,3,2,1,0:T(8,128)(2,1)} fusion(bf16[1,4,2,128,1024]{4,3,2,1,0:T(8,128)(2,1)} %bitcast.112, bf16[1,4,2,128,1024]{4,3,2,1,0:T(8,128)(2,1)} %bitcast.113), kind=kLoop, calls=%fused_computation.29 | loop fusion | flops 2097152 | bytes 8388608 | tf_op jit(solution)/shard_map/stack | solution.py:23
  22.4 5.0 %gather_fusion.1 = bf16[8,2,128,1024]{3,2,1,0:T(8,128)(2,1)} fusion(bf16[2,4,2,128,1024]{4,3,2,1,0:T(8,128)(2,1)} %pad_maximum_fusion, s32[8]{0:T(128)S(1)} %fusion.40), kind=kCustom, calls=%fused_computation.1 | custom fusion | bytes 8388672 | tf_op jit(solution)/shard_map/gather | solution.py:33
  27.4 3.9 %dynamic-slice_bitcast_fusion = (bf16[2,128,1024]{2,1,0:T(8,128)(2,1)}, bf16[2,128,1024]{2,1,0:T(8,128)(2,1)}, bf16[2,128,1024]{2,1,0:T(8,128)(2,1)}, bf16[2,128...) fusion(bf16[8,2,128,1024]{3,2,1,0:T(8,128)(2,1)} %gather_fusion, ...), kind=kLoop, calls=%fused_computation.69 | loop fusion | bytes 8388640 | tf_op jit(solution)/shard_map/jit(dynamic_index_in_dim)/squeeze | solution.py:36
  35.8 10.2 %collective-permute-done = bf16[2,128,1024]{2,1,0:T(8,128)(2,1)} collective-permute-done((bf16[2,128,1024]{2,1,0:T(8,128)(2,1)S(1)}, bf16[2,128,1024]{2,1,0:T(8,128)(2,1)}, u32[]{:S(2)}, u32[]{:S(2)}) %collective-permute-start) | collective-permute-done | bytes 524320 | tf_op jit(solution)/shard_map/ppermute | solution.py:38
  47.4 11.0 %collective-permute-start.6 = (bf16[2,128,1024]{2,1,0:T(8,128)(2,1)}, bf16[2,128,1024]{2,1,0:T(8,128)(2,1)}, u32[]{:S(2)}, u32[]{:S(2)}) collective-permute-start(bf16[2,128,1024]{2,1,0:T(8,128)(2,1)} %get-tuple-element.44), channel_id=1, source_target_pairs={{0,28},{4,0},{8,4},{12,8},{16,12},{20,16},{24,20},{28,24},{1,29},{... | collective-permute-start | bytes 1572872 | tf_op jit(solution)/shard_map/ppermute | solution.py:38
  63.0 5.8 %collective-permute-done.2 = bf16[2,128,1024]{2,1,0:T(8,128)(2,1)} collective-permute-done((bf16[2,128,1024]{2,1,0:T(8,128)(2,1)}, bf16[2,128,1024]{2,1,0:T(8,128)(2,1)}, u32[]{:S(2)}, u32[]{:S(2)}) %collective-permute-start.2) | collective-permute-done | bytes 524320 | tf_op jit(solution)/shard_map/ppermute | solution.py:38
  69.0 10.2 %collective-permute-done.4 = bf16[2,128,1024]{2,1,0:T(8,128)(2,1)} collective-permute-done((bf16[2,128,1024]{2,1,0:T(8,128)(2,1)}, bf16[2,128,1024]{2,1,0:T(8,128)(2,1)}, u32[]{:S(2)}, u32[]{:S(2)}) %collective-permute-start.4) | collective-permute-done | bytes 524320 | tf_op jit(solution)/shard_map/ppermute | solution.py:38
  79.2 5.3 %all-to-all-done = bf16[2,4,256,768]{2,3,0,1:T(8,128)(2,1)S(1)} async-done(((bf16[2,4,256,768]{2,3,0,1:T(8,128)(2,1)}), bf16[2,4,256,768]{2,3,0,1:T(8,128)(2,1)S(1)}, u32[]{:S(2)}, u32[]{:S(2)}) %all-to-all-start) | async-done | bytes 3145760 | tf_op jit(solution)/shard_map/all_to_all | solution.py:27
  84.6 5.6 %fusion.7 = bf16[2,4,256,1024]{2,3,0,1:T(8,128)(2,1)S(1)} fusion(s32[]{:T(128)S(6)} %select_n.168, bf16[2,4,256,768]{2,3,0,1:T(8,128)(2,1)S(1)} %all-to-all-done, bf16[2,4,256,256]{2,3,0,1:T(8,128)(2,1)} %copy.26), kind=kLoop, calls=%fused_computation.28 | loop fusion | flops 16777216 | bytes 8388612 | tf_op jit(solution)/shard_map/jit(_roll_dynamic)/concatenate | solution.py:48
  91.8 4.0 %copy.28 = bf16[1,4,256,1024]{3,2,1,0:T(8,128)(2,1)} copy(bf16[1,4,256,1024]{2,3,0,1:T(8,128)(2,1)} %get-tuple-element.38) | data formatting | bytes 4194304 | tf_op jit(solution)/shard_map/mul | solution.py:53
  98.2 6.5 %fusion.44 = f32[1024,1024]{1,0:T(8,128)} fusion(bf16[1024,1024]{1,0:T(8,128)(2,1)} %bitcast.116, bf16[1024,1024]{1,0:T(8,128)(2,1)} %bitcast.117), kind=kOutput, calls=%fused_computation.116 | convolution fusion | flops 2147483648 | bytes 8388608 | tf_op jit(solution)/shard_map/dot_general | solution.py:53
  104.7 5.4 %copy.30 = f32[1024,1024]{0,1:T(8,128)} copy(f32[1024,1024]{1,0:T(8,128)} %fusion.44) | data formatting | bytes 8388608 | tf_op jit(solution)/shard_map/dot_general | solution.py:53
  110.1 4.4 %bitcast_add_fusion = f32[1024,1024]{1,0:T(8,128)S(1)} fusion(f32[1024,1024]{1,0:T(8,128)} %fusion.44, f32[1024,1024]{0,1:T(8,128)} %copy.30), kind=kLoop, calls=%fused_computation.30 | loop fusion | flops 1048576 | bytes 12582912 | tf_op jit(solution)/shard_map/add | solution.py:54
  116.9 7.1 %all-to-all-start.1 = ((f32[4,256,768]{2,1,0:T(8,128)}), f32[4,256,768]{2,1,0:T(8,128)S(1)}, u32[]{:S(2)}, u32[]{:S(2)}) async-start(f32[4,256,768]{2,1,0:T(8,128)} %pad_maximum_fusion.2), calls=%async_computation.1 | async-start | bytes 6291456 | tf_op jit(solution)/shard_map/all_to_all | solution.py:56
  126.2 49.7 %collective-permute-done.7 = f32[2,1024]{1,0:T(2,128)S(1)} collective-permute-done((f32[2,1024]{1,0:T(2,128)S(1)}, f32[2,1024]{1,0:T(2,128)S(1)}, u32[]{:S(2)}, u32[]{:S(2)}) %collective-permute-start.7) | collective-permute-done | bytes 8224 | tf_op jit(solution)/shard_map/ppermute | solution.py:58
  190.9 5.0 %gather_fusion.2 = bf16[8,2,128,1024]{3,2,1,0:T(8,128)(2,1)} fusion(bf16[2,8,128,1024]{3,2,0,1:T(8,128)(2,1)} %bitcast_dynamic-update-slice_fusion, s32[1024]{0:T(1024)S(1)} %pad_clamp_fusion), kind=kCustom, calls=%fused_computation.2 | custom fusion | bytes 8388640 | tf_op jit(solution)/shard_map/gather | solution.py:40
  204.6 4.5 %reshape.194 = bf16[8,128,4,256]{3,2,1,0:T(4,128)(2,1)} reshape(bf16[1024,1024]{1,0:T(8,128)(2,1)} %multiply_convert_fusion) | data formatting | bytes 4194304 | tf_op jit(solution)/shard_map/reshape | solution.py:68
  212.4 21.6 %all-to-all-start.2 = ((bf16[32,128,256]{2,1,0:T(8,128)(2,1)}), bf16[32,128,256]{2,1,0:T(8,128)(2,1)}, u32[]{:S(2)}, u32[]{:S(2)}) async-start(bf16[32,128,256]{2,1,0:T(8,128)(2,1)} %bitcast.111), calls=%async_computation.2 | async-start | bytes 4194304 | tf_op jit(solution)/shard_map/all_to_all | solution.py:69
  234.2 4.0 %fusion.10 = f32[4,256,256]{2,1,0:T(8,128)} fusion(bf16[4,256,1024]{2,1,0:T(8,128)(2,1)} %param.8, bf16[4,256,1024]{2,1,0:T(8,128)(2,1)} %param.7, bf16[4,1024]{1,0:T(4,128)(2,1)S(1)} %convert_element_type.22), kind=kOutput, calls=%fused_computation.37 | convolution fusion | flops 537919488 | bytes 5251072 | tf_op jit(solution)/shard_map/sik,sjk->sij/dot_general | solution.py:84
  243.5 39.4 %all-to-all-done.2 = bf16[32,128,256]{2,1,0:T(8,128)(2,1)} async-done(((bf16[32,128,256]{2,1,0:T(8,128)(2,1)}), bf16[32,128,256]{2,1,0:T(8,128)(2,1)}, u32[]{:S(2)}, u32[]{:S(2)}) %all-to-all-start.2) | async-done | bytes 2097184 | tf_op jit(solution)/shard_map/all_to_all | solution.py:69
  288.4 5.3 %copy.37 = f32[4,256,1024]{2,1,0:T(8,128)} copy(f32[4,256,1024]{1,0,2:T(4,128)} %bitcast.108) | data formatting | bytes 8388608 | tf_op jit(solution)/shard_map/reshape | solution.py:81
  293.7 4.5 %fusion.4 = bf16[4,256,1024]{2,1,0:T(8,128)(2,1)} fusion(f32[4,256,1024]{2,1,0:T(8,128)} %copy.37, s32[]{:T(128)S(6)} %select_n.168, f32[4,256,768]{2,1,0:T(8,128)S(1)} %all-to-all-done.1, f32[4,256,256]{2,1,0:T(8,128)} %bitcast_add_fusion.1), kind=kLoop, calls=%fused_computation.25 | loop fusion | flops 5242880 | bytes 10485764 | tf_op jit(solution)/shard_map/convert_element_type | solution.py:88
  (69 shorter events, 65.7 us)
Async XLA Ops:
  0.0 17.2 %copy-start = (s32[32,8]{0,1:T(8,128)S(1)}, s32[32,8]{0,1:T(8,128)}, u32[]{:S(2)}) copy-start(s32[32,8]{0,1:T(8,128)} %param.12) | copy-start | bytes 3076
  11.8 72.7 %all-to-all-start = ((bf16[2,4,256,768]{2,3,0,1:T(8,128)(2,1)}), bf16[2,4,256,768]{2,3,0,1:T(8,128)(2,1)S(1)}, u32[]{:S(2)}, u32[]{:S(2)}) async-start(bf16[2,4,256,768]{2,3,0,1:T(8,128)(2,1)} %pad_maximum_fusion.1), calls=%async_computation | async-start | bytes 6291456 | tf_op jit(solution)/shard_map/all_to_all | solution.py:27
  27.4 31.0 %copy-start.4 = (bf16[2]{0:T(256)(128)(2,1)S(1)}, bf16[2]{0:T(256)(128)(2,1)}, u32[]{:S(2)}) copy-start(bf16[2]{0:T(256)(128)(2,1)} %constant.146.clone) | copy-start | bytes 16
  31.2 31.8 %copy-start.1 = (s32[4,1024]{1,0:T(4,128)S(1)}, s32[4,1024]{1,0:T(4,128)}, u32[]{:S(2)}) copy-start(s32[4,1024]{1,0:T(4,128)} %param.9) | copy-start | bytes 49156
  31.3 14.7 %collective-permute-start = (bf16[2,128,1024]{2,1,0:T(8,128)(2,1)S(1)}, bf16[2,128,1024]{2,1,0:T(8,128)(2,1)}, u32[]{:S(2)}, u32[]{:S(2)}) collective-permute-start(bf16[2,128,1024]{2,1,0:T(8,128)(2,1)S(1)} %get-tuple-element.50), channel_id=1, source_target_pairs={{0,4},{4,8},{8,12},{12,16},{16,20},{20,24},{24,28},{28,0},{1,5},{5... | collective-permute-start | bytes 1572872 | tf_op jit(solution)/shard_map/ppermute | solution.py:38
  31.3 16.2 %collective-permute-start.1 = (bf16[2,128,1024]{2,1,0:T(8,128)(2,1)S(1)}, bf16[2,128,1024]{2,1,0:T(8,128)(2,1)}, u32[]{:S(2)}, u32[]{:S(2)}) collective-permute-start(bf16[2,128,1024]{2,1,0:T(8,128)(2,1)S(1)} %get-tuple-element.49), channel_id=1, source_target_pairs={{0,8},{4,12},{8,16},{12,20},{16,24},{20,28},{24,0},{28,4},{1,9},{5... | collective-permute-start | bytes 1572872 | tf_op jit(solution)/shard_map/ppermute | solution.py:38
  32.8 36.0 %collective-permute-start.2 = (bf16[2,128,1024]{2,1,0:T(8,128)(2,1)}, bf16[2,128,1024]{2,1,0:T(8,128)(2,1)}, u32[]{:S(2)}, u32[]{:S(2)}) collective-permute-start(bf16[2,128,1024]{2,1,0:T(8,128)(2,1)} %get-tuple-element.48), channel_id=1, source_target_pairs={{0,12},{4,16},{8,20},{12,24},{16,28},{20,0},{24,4},{28,8},{1,13},{... | collective-permute-start | bytes 1572872 | tf_op jit(solution)/shard_map/ppermute | solution.py:38
  35.2 33.9 %collective-permute-start.3 = (bf16[2,128,1024]{2,1,0:T(8,128)(2,1)}, bf16[2,128,1024]{2,1,0:T(8,128)(2,1)}, u32[]{:S(2)}, u32[]{:S(2)}) collective-permute-start(bf16[2,128,1024]{2,1,0:T(8,128)(2,1)} %get-tuple-element.47), channel_id=1, source_target_pairs={{0,16},{4,20},{8,24},{12,28},{16,0},{20,4},{24,8},{28,12},{1,17},{... | collective-permute-start | bytes 1572872 | tf_op jit(solution)/shard_map/ppermute | solution.py:38
  35.7 43.6 %collective-permute-start.4 = (bf16[2,128,1024]{2,1,0:T(8,128)(2,1)}, bf16[2,128,1024]{2,1,0:T(8,128)(2,1)}, u32[]{:S(2)}, u32[]{:S(2)}) collective-permute-start(bf16[2,128,1024]{2,1,0:T(8,128)(2,1)} %get-tuple-element.46), channel_id=1, source_target_pairs={{0,20},{4,24},{8,28},{12,0},{16,4},{20,8},{24,12},{28,16},{1,21},{... | collective-permute-start | bytes 1572872 | tf_op jit(solution)/shard_map/ppermute | solution.py:38
  46.0 33.2 %collective-permute-start.5 = (bf16[2,128,1024]{2,1,0:T(8,128)(2,1)}, bf16[2,128,1024]{2,1,0:T(8,128)(2,1)}, u32[]{:S(2)}, u32[]{:S(2)}) collective-permute-start(bf16[2,128,1024]{2,1,0:T(8,128)(2,1)} %get-tuple-element.45), channel_id=1, source_target_pairs={{0,24},{4,28},{8,0},{12,4},{16,8},{20,12},{24,16},{28,20},{1,25},{... | collective-permute-start | bytes 1572872 | tf_op jit(solution)/shard_map/ppermute | solution.py:38
  47.4 31.8 %collective-permute-start.6 = (bf16[2,128,1024]{2,1,0:T(8,128)(2,1)}, bf16[2,128,1024]{2,1,0:T(8,128)(2,1)}, u32[]{:S(2)}, u32[]{:S(2)}) collective-permute-start(bf16[2,128,1024]{2,1,0:T(8,128)(2,1)} %get-tuple-element.44), channel_id=1, source_target_pairs={{0,28},{4,0},{8,4},{12,8},{16,12},{20,16},{24,20},{28,24},{1,29},{... | collective-permute-start | bytes 1572872 | tf_op jit(solution)/shard_map/ppermute | solution.py:38
  116.9 7.1 %copy-start.2 = (s32[1,1024]{1,0:T(1,128)S(1)}, s32[1,1024]{1,0:T(1,128)}, u32[]{:S(2)}) copy-start(s32[1,1024]{1,0:T(1,128)} %param.10) | copy-start | bytes 12292
  116.9 7.1 %copy-start.3 = (f32[1,1024]{1,0:T(1,128)S(1)}, f32[1,1024]{1,0:T(1,128)}, u32[]{:S(2)}) copy-start(f32[1,1024]{1,0:T(1,128)} %param.11) | copy-start | bytes 12292
  116.9 87.7 %all-to-all-start.1 = ((f32[4,256,768]{2,1,0:T(8,128)}), f32[4,256,768]{2,1,0:T(8,128)S(1)}, u32[]{:S(2)}, u32[]{:S(2)}) async-start(f32[4,256,768]{2,1,0:T(8,128)} %pad_maximum_fusion.2), calls=%async_computation.1 | async-start | bytes 6291456 | tf_op jit(solution)/shard_map/all_to_all | solution.py:56
  124.0 51.8 %collective-permute-start.7 = (f32[2,1024]{1,0:T(2,128)S(1)}, f32[2,1024]{1,0:T(2,128)S(1)}, u32[]{:S(2)}, u32[]{:S(2)}) collective-permute-start(f32[2,1024]{1,0:T(2,128)S(1)} %pad_maximum_fusion.3), channel_id=1, source_target_pairs={{0,0},{1,4},{2,8},{3,12},{4,16},{5,20},{6,24},{7,28},{8,1},{9,5},{... | collective-permute-start | bytes 24584 | tf_op jit(solution)/shard_map/ppermute | solution.py:58
  212.4 70.5 %all-to-all-start.2 = ((bf16[32,128,256]{2,1,0:T(8,128)(2,1)}), bf16[32,128,256]{2,1,0:T(8,128)(2,1)}, u32[]{:S(2)}, u32[]{:S(2)}) async-start(bf16[32,128,256]{2,1,0:T(8,128)(2,1)} %bitcast.111), calls=%async_computation.2 | async-start | bytes 4194304 | tf_op jit(solution)/shard_map/all_to_all | solution.py:69

commit v4 on v3

--- a/solution.py
+++ b/solution.py
@@ -31,16 +31,27 @@
     part_dest = q_dest // ch_dev - level * (rows // slab)
     five = stacked.reshape(2, ch_dev, rows // slab, slab, width)
     outgoing = five[:, slot_dest, part_dest]
-    pieces = [lax.dynamic_index_in_dim(outgoing, mine, 1, False)]
+    pieces = [lax.dynamic_index_in_dim(outgoing, mine, 1, True)]
     for shift in range(1, n_chan):
-        piece = lax.dynamic_index_in_dim(outgoing, (mine + shift) % n_chan, 1, False)
+        piece = lax.dynamic_index_in_dim(outgoing, (mine + shift) % n_chan, 1, True)
         pairs = [(a, (a + shift) % n_chan) for a in range(n_chan)]
         pieces.append(lax.ppermute(piece, "ch", pairs))
     whole, pieces = lax.optimization_barrier((whole, pieces))
-    arrived = jnp.stack(pieces, axis=1)[:, (mine - dest) % n_chan]
+    arrived = jnp.concatenate(pieces, axis=1)[:, (mine - dest) % n_chan]
     a_eta = arrived[0].reshape(width, width)
     b_gamma = arrived[1].reshape(width, width)
 
+    perm = [(q, (q % n_chan) * n_rows + q // n_chan) for q in range(n_total)]
+    coefs = lax.ppermute(
+        jnp.concatenate([ph_factor.astype(f32), recouple], axis=0), ("ch", "row"), perm
+    )
+    weight = coefs[0].astype(bf16)[None, :]
+    coef = coefs[1]
+
+    ph_t = jnp.dot(a_eta * weight, b_gamma, preferred_element_type=f32)
+    ph_t = ph_t - jnp.dot(b_gamma * weight, a_eta, preferred_element_type=f32)
+    term_t = (ph_t * coef[:, None]).astype(bf16)
+    whole, term_t = lax.optimization_barrier((whole, term_t))
     own = lax.dynamic_index_in_dim(stacked, level, 1, False)
     own_t = own.reshape(2, rows, n_rows, rows).transpose(0, 2, 3, 1)
     own_t = own_t * jnp.array([-1, 1], bf16)[:, None, None, None]
@@ -53,18 +64,6 @@
     product = jnp.dot(eta_c * factor[None, :], gamma_c, preferred_element_type=f32)
     ladder_c = (product + product.T).reshape(n_rows, rows, width)
     sending = jnp.stack([skip_block(ladder_c[a], a, rows) for a in range(n_rows)])
-    ladder = lax.all_to_all(sending, "row", split_axis=0, concat_axis=0, tiled=True)
-    perm = [(q, (q % n_chan) * n_rows + q // n_chan) for q in range(n_total)]
-    coefs = lax.ppermute(
-        jnp.concatenate([ph_factor.astype(f32), recouple], axis=0), ("ch", "row"), perm
-    )
-    weight = coefs[0].astype(bf16)[None, :]
-    coef = coefs[1]
-
-    ph_t = jnp.dot(a_eta * weight, b_gamma, preferred_element_type=f32)
-    ph_t = ph_t - jnp.dot(b_gamma * weight, a_eta, preferred_element_type=f32)
-    term_t = (ph_t * coef[:, None]).astype(bf16)
-    ladder, term_t = lax.optimization_barrier((ladder, term_t))
     returning = term_t.reshape(n_chan, slab, n_rows, rows).transpose(0, 2, 1, 3)
     landed = lax.all_to_all(
         returning.reshape(n_chan * n_rows, slab, rows),
@@ -75,6 +74,8 @@
     )
     landed = landed.reshape(n_chan, n_rows, slab, rows).transpose(1, 0, 2, 3)
     landed = landed.reshape(n_chan, ch_dev, slab, rows)
+    sending, landed = lax.optimization_barrier((sending, landed))
+    ladder = lax.all_to_all(sending, "row", split_axis=0, concat_axis=0, tiled=True)
     chosen = src_slot[:, mine].reshape(n_chan, ch_dev)
     onehot = (chosen[:, :, None] == jnp.arange(ch_dev, dtype=jnp.int32)[None, None, :]).astype(bf16)
     back = jnp.einsum("gts,gtwi->sigw", onehot, landed, preferred_element_type=f32)

time: 300 us -> 290 us (0.967); the launches traced: 298 us -> 284 us
  waiting for transfers between devices: 121 us -> 109 us
  starting transfers between devices: 53.1 us -> 49.8 us
    all_to_all x1, waiting for transfers between devices: 0.01 us -> 47.8 us  [per_device(): lax.all_to_all(sending, 'row', split_axis=0, concat_axis=0, tiled=True)]
    all_to_all x1, waiting for transfers between devices: 39.4 us -> 11.7 us  [per_device(): lax.all_to_all(returning.reshape(n_chan * n_rows, slab, rows), ('ch', 'ro...]
    ppermute x1, waiting for transfers between devices: 49.7 us -> 30 us  [per_device(): lax.ppermute(jnp.concatenate([ph_factor.astype(f32), recouple], axis=0),...]
    all_to_all x1, starting transfers between devices: 21.6 us -> 11 us  [per_device(): lax.all_to_all(returning.reshape(n_chan * n_rows, slab, rows), ('ch', 'ro...]
    ppermute x7, starting transfers between devices: 16.9 us -> 26.7 us  [per_device(): pieces.append(lax.ppermute(piece, 'ch', pairs))]
    ppermute x7, waiting for transfers between devices: 26.4 us -> 19.6 us  [per_device(): pieces.append(lax.ppermute(piece, 'ch', pairs))]
    all_to_all x1, waiting for transfers between devices: 5.33 us -> 0.01 us  [per_device(): lax.all_to_all(sending, 'row', split_axis=1, concat_axis=1, tiled=True)]
    squeeze x1 -> x0, local copies, waits for them, and re-layouts: 3.86 us -> none  [per_device(): lax.dynamic_index_in_dim(outgoing, (mine + shift) % n_chan, 1, False)]
  transfers between devices with their start and end apart: 11 -> 11, of which waited for: 7 -> 6; matrix products, arithmetic and copies ran while one was open for 19% -> 25% of each run, Pallas kernels for 0% -> 0%
where the time goes in v4:
time: 290 us; the launch traced here: 284 us
  waiting for transfers between devices  109 us (38%)
  local copies, waits for them, and re-layouts  67.5 us (23%)
  starting transfers between devices  49.8 us (17%)
  other arithmetic  35.4 us (12%)
  matrix products  21.8 us (8%)
    all_to_all x1, waiting for transfers between devices, per_device(): lax.all_to_all(sending, 'row', split_axis=0, concat_axis=0, tiled=True)  47.8 us
    ppermute x1, waiting for transfers between devices, per_device(): lax.ppermute(jnp.concatenate([ph_factor.astype(f32), recouple], axis=0),...  30 us
    ppermute x7, starting transfers between devices, per_device(): pieces.append(lax.ppermute(piece, 'ch', pairs))  26.7 us
    ppermute x7, waiting for transfers between devices, per_device(): pieces.append(lax.ppermute(piece, 'ch', pairs))  19.6 us
    unnamed x37, local copies, waits for them, and re-layouts  17.8 us
    all_to_all x1, waiting for transfers between devices, per_device(): lax.all_to_all(returning.reshape(n_chan * n_rows, slab, rows), ('ch', 'ro...  11.7 us
    all_to_all x1, starting transfers between devices, per_device(): lax.all_to_all(returning.reshape(n_chan * n_rows, slab, rows), ('ch', 'ro...  11 us
    reshape x2, local copies, waits for them, and re-layouts, per_device(): returning = term_t.reshape(n_chan, slab, n_rows, rows).transpose(0, 2, 1, 3)  7.83 us
  transfers between devices with their start and end apart: 11, of which 6 were waited for; matrix products, arithmetic and copies ran while one was open for 25% of the time, Pallas kernels for 0%

profile of v4, /device:TPU:8, one launch (start us, length us, event | category | flops | bytes accessed | tf_op | source)
XLA Modules:
  0.0 283.8 jit_solution(17860554486160112857)
XLA Ops:
  2.9 3.9 %copy.25 = bf16[4,256,1024]{1,2,0:T(8,128)(2,1)} copy(bf16[4,256,1024]{2,1,0:T(8,128)(2,1)} %param.8) | data formatting | bytes 4194304 | tf_op args[1]
  11.8 5.6 %all-to-all-start = ((bf16[2,4,256,768]{2,3,0,1:T(8,128)(2,1)}), bf16[2,4,256,768]{2,3,0,1:T(8,128)(2,1)S(1)}, u32[]{:S(2)}, u32[]{:S(2)}) async-start(bf16[2,4,256,768]{2,3,0,1:T(8,128)(2,1)} %pad_maximum_fusion.1), calls=%async_computation | async-start | bytes 6291456 | tf_op jit(solution)/shard_map/all_to_all | solution.py:27
  18.0 4.6 %pad_maximum_fusion = bf16[2,4,2,128,1024]{4,3,2,1,0:T(8,128)(2,1)} fusion(bf16[1,4,2,128,1024]{4,3,2,1,0:T(8,128)(2,1)} %bitcast.96, bf16[1,4,2,128,1024]{4,3,2,1,0:T(8,128)(2,1)} %bitcast.97), kind=kLoop, calls=%fused_computation.29 | loop fusion | flops 2097152 | bytes 8388608 | tf_op jit(solution)/shard_map/stack | solution.py:23
  22.6 5.0 %gather_fusion.1 = bf16[8,2,128,1024]{3,2,1,0:T(8,128)(2,1)} fusion(bf16[2,4,2,128,1024]{4,3,2,1,0:T(8,128)(2,1)} %pad_maximum_fusion, s32[8]{0:T(128)S(1)} %fusion.40), kind=kCustom, calls=%fused_computation.1 | custom fusion | bytes 8388672 | tf_op jit(solution)/shard_map/gather | solution.py:33
  39.7 30.0 %collective-permute-done.7 = f32[2,1024]{1,0:T(2,128)S(1)} collective-permute-done((f32[2,1024]{1,0:T(2,128)S(1)}, f32[2,1024]{1,0:T(2,128)S(1)}, u32[]{:S(2)}, u32[]{:S(2)}) %collective-permute-start.7) | collective-permute-done | bytes 8224 | tf_op jit(solution)/shard_map/ppermute | solution.py:45
  69.7 15.1 %collective-permute-start.4 = (bf16[2,1,128,1024]{3,2,0,1:T(8,128)(2,1)S(1)}, bf16[2,1,128,1024]{3,2,0,1:T(8,128)(2,1)S(1)}, u32[]{:S(2)}, u32[]{:S(2)}) collective-permute-start(bf16[2,1,128,1024]{3,2,0,1:T(8,128)(2,1)S(1)} %get-tuple-element.50), channel_id=1, source_target_pairs={{0,20},{4,24},{8,28},{12,0},{16,4},{20,8},{24,12},{28,16},{1,21},{... | collective-permute-start | bytes 1572872 | tf_op jit(solution)/shard_map/ppermute | solution.py:38
  91.5 9.2 %collective-permute-done.5 = bf16[2,1,128,1024]{3,2,0,1:T(8,128)(2,1)S(1)} collective-permute-done((bf16[2,1,128,1024]{3,2,0,1:T(8,128)(2,1)S(1)}, bf16[2,1,128,1024]{3,2,0,1:T(8,128)(2,1)S(1)}, u32[]{:S(2)}, u32[]{:S(2)}) %collective-permute-start.5) | collective-permute-done | bytes 524320 | tf_op jit(solution)/shard_map/ppermute | solution.py:38
  101.5 9.8 %collective-permute-done.6 = bf16[2,1,128,1024]{3,2,0,1:T(8,128)(2,1)} collective-permute-done((bf16[2,1,128,1024]{3,2,0,1:T(8,128)(2,1)S(1)}, bf16[2,1,128,1024]{3,2,0,1:T(8,128)(2,1)}, u32[]{:S(2)}, u32[]{:S(2)}) %collective-permute-start.6) | collective-permute-done | bytes 524320 | tf_op jit(solution)/shard_map/ppermute | solution.py:38
  123.3 5.0 %gather_fusion.2 = bf16[8,2,128,1024]{3,2,1,0:T(8,128)(2,1)} fusion(bf16[2,8,128,1024]{3,2,0,1:T(8,128)(2,1)} %constant_dynamic-update-slice_fusion, s32[1024]{0:T(1024)S(1)} %pad_clamp_fusion), kind=kCustom, calls=%fused_computation.2 | custom fusion | bytes 8388640 | tf_op jit(solution)/shard_map/gather | solution.py:40
  133.4 3.7 %multiply_convert_fusion = bf16[1024,1024]{1,0:T(8,128)(2,1)} fusion(f32[1024,1024]{1,0:T(8,128)S(1)} %fusion.44, f32[1024]{0:T(1024)S(1)} %bitcast.106, bf16[1024,1024]{1,0:T(8,128)(2,1)S(1)} %bitcast.102, bf16[1024,1024]{1,0:T(8,128)(2,1)S(1)} %bitcast.103), kind=kOutput, calls=%fused_computation.31 | convolution fusion | flops 2150629376 | bytes 10489856 | tf_op jit(solution)/shard_map/dot_general | solution.py:52
  137.1 4.5 %reshape.194 = bf16[8,128,4,256]{3,2,1,0:T(4,128)(2,1)} reshape(bf16[1024,1024]{1,0:T(8,128)(2,1)} %multiply_convert_fusion) | data formatting | bytes 4194304 | tf_op jit(solution)/shard_map/reshape | solution.py:67
  144.9 11.0 %all-to-all-start.1 = ((bf16[32,128,256]{2,1,0:T(8,128)(2,1)}), bf16[32,128,256]{2,1,0:T(8,128)(2,1)}, u32[]{:S(2)}, u32[]{:S(2)}) async-start(bf16[32,128,256]{2,1,0:T(8,128)(2,1)} %bitcast.95), calls=%async_computation.1 | async-start | bytes 4194304 | tf_op jit(solution)/shard_map/all_to_all | solution.py:68
  160.6 5.6 %fusion.7 = bf16[2,4,256,1024]{2,3,0,1:T(8,128)(2,1)S(1)} fusion(s32[]{:T(128)S(6)} %select_n.170, bf16[2,4,256,768]{2,3,0,1:T(8,128)(2,1)S(1)} %all-to-all-done, bf16[2,4,256,256]{2,3,0,1:T(8,128)(2,1)} %copy.26), kind=kLoop, calls=%fused_computation.28 | loop fusion | flops 16777216 | bytes 8388612 | tf_op jit(solution)/shard_map/jit(_roll_dynamic)/concatenate | solution.py:59
  167.9 4.0 %copy.28 = bf16[1,4,256,1024]{3,2,1,0:T(8,128)(2,1)} copy(bf16[1,4,256,1024]{2,3,0,1:T(8,128)(2,1)} %get-tuple-element.40) | data formatting | bytes 4194304 | tf_op jit(solution)/shard_map/mul | solution.py:64
  174.4 6.5 %fusion.45 = f32[1024,1024]{1,0:T(8,128)} fusion(bf16[1024,1024]{1,0:T(8,128)(2,1)} %bitcast.100, bf16[1024,1024]{1,0:T(8,128)(2,1)} %bitcast.101), kind=kOutput, calls=%fused_computation.117 | convolution fusion | flops 2147483648 | bytes 8388608 | tf_op jit(solution)/shard_map/dot_general | solution.py:64
  180.9 5.5 %copy.30 = f32[1024,1024]{0,1:T(8,128)} copy(f32[1024,1024]{1,0:T(8,128)} %fusion.45) | data formatting | bytes 8388608 | tf_op jit(solution)/shard_map/dot_general | solution.py:64
  186.4 4.4 %bitcast_add_fusion = f32[1024,1024]{1,0:T(8,128)S(1)} fusion(f32[1024,1024]{1,0:T(8,128)} %fusion.45, f32[1024,1024]{0,1:T(8,128)} %copy.30), kind=kLoop, calls=%fused_computation.30 | loop fusion | flops 1048576 | bytes 12582912 | tf_op jit(solution)/shard_map/add | solution.py:65
  193.1 11.7 %all-to-all-done.1 = bf16[32,128,256]{2,1,0:T(8,128)(2,1)} async-done(((bf16[32,128,256]{2,1,0:T(8,128)(2,1)}), bf16[32,128,256]{2,1,0:T(8,128)(2,1)}, u32[]{:S(2)}, u32[]{:S(2)}) %all-to-all-start.1) | async-done | bytes 2097184 | tf_op jit(solution)/shard_map/all_to_all | solution.py:68
  207.9 3.7 %all-to-all-start.2 = ((f32[4,256,768]{2,1,0:T(8,128)}), f32[4,256,768]{2,1,0:T(8,128)S(1)}, u32[]{:S(2)}, u32[]{:S(2)}) async-start(f32[4,256,768]{2,1,0:T(8,128)} %pad_maximum_fusion.2), calls=%async_computation.2 | async-start | bytes 6291456 | tf_op jit(solution)/shard_map/all_to_all | solution.py:78
  211.8 4.0 %fusion.10 = f32[4,256,256]{2,1,0:T(8,128)} fusion(bf16[4,256,1024]{2,1,0:T(8,128)(2,1)} %param.8, bf16[4,256,1024]{2,1,0:T(8,128)(2,1)} %param.7, bf16[4,1024]{1,0:T(4,128)(2,1)S(1)} %convert_element_type.22), kind=kOutput, calls=%fused_computation.37 | convolution fusion | flops 537919488 | bytes 5251072 | tf_op jit(solution)/shard_map/sik,sjk->sij/dot_general | solution.py:85
  220.9 5.3 %fusion.8 = f32[8,128,256,4]{2,3,1,0:T(4,128)} fusion(bf16[8,4,128,256]{3,2,1,0:T(8,128)(2,1)} %bitcast.98, s32[8,4]{1,0:T(8,128)S(1)} %eq.30), kind=kOutput, calls=%fused_computation.35 | convolution fusion | flops 8388736 | bytes 6291584 | tf_op jit(solution)/shard_map/gts,gtwi->sigw/dot_general | solution.py:81
  226.3 5.3 %copy.37 = f32[4,256,1024]{2,1,0:T(8,128)} copy(f32[4,256,1024]{1,0,2:T(4,128)} %bitcast.92) | data formatting | bytes 8388608 | tf_op jit(solution)/shard_map/reshape | solution.py:82
  231.5 47.8 %all-to-all-done.2 = f32[4,256,768]{2,1,0:T(8,128)S(1)} async-done(((f32[4,256,768]{2,1,0:T(8,128)}), f32[4,256,768]{2,1,0:T(8,128)S(1)}, u32[]{:S(2)}, u32[]{:S(2)}) %all-to-all-start.2) | async-done | bytes 3145760 | tf_op jit(solution)/shard_map/all_to_all | solution.py:78
  279.3 4.5 %fusion.4 = bf16[4,256,1024]{2,1,0:T(8,128)(2,1)} fusion(f32[4,256,1024]{2,1,0:T(8,128)} %copy.37, s32[]{:T(128)S(6)} %select_n.170, f32[4,256,768]{2,1,0:T(8,128)S(1)} %all-to-all-done.2, f32[4,256,256]{2,1,0:T(8,128)} %bitcast_add_fusion.1), kind=kLoop, calls=%fused_computation.25 | loop fusion | flops 5242880 | bytes 10485764 | tf_op jit(solution)/shard_map/convert_element_type | solution.py:89
  (87 shorter events, 68.0 us)
Async XLA Ops:
  0.0 17.4 %copy-start = (s32[32,8]{0,1:T(8,128)S(1)}, s32[32,8]{0,1:T(8,128)}, u32[]{:S(2)}) copy-start(s32[32,8]{0,1:T(8,128)} %param.12) | copy-start | bytes 3076
  11.8 99.5 %all-to-all-start = ((bf16[2,4,256,768]{2,3,0,1:T(8,128)(2,1)}), bf16[2,4,256,768]{2,3,0,1:T(8,128)(2,1)S(1)}, u32[]{:S(2)}, u32[]{:S(2)}) async-start(bf16[2,4,256,768]{2,3,0,1:T(8,128)(2,1)} %pad_maximum_fusion.1), calls=%async_computation | async-start | bytes 6291456 | tf_op jit(solution)/shard_map/all_to_all | solution.py:27
  27.6 5.1 %copy-start.11 = (s32[1,1024]{1,0:T(1,128)S(1)}, s32[1,1024]{1,0:T(1,128)}, u32[]{:S(2)}) copy-start(s32[1,1024]{1,0:T(1,128)} %param.10) | copy-start | bytes 12292
  27.6 5.1 %copy-start.12 = (f32[1,1024]{1,0:T(1,128)S(1)}, f32[1,1024]{1,0:T(1,128)}, u32[]{:S(2)}) copy-start(f32[1,1024]{1,0:T(1,128)} %param.11) | copy-start | bytes 12292
  31.2 53.6 %collective-permute-start = (bf16[2,1,128,1024]{3,2,0,1:T(8,128)(2,1)S(1)}, bf16[2,1,128,1024]{3,2,0,1:T(8,128)(2,1)S(1)}, u32[]{:S(2)}, u32[]{:S(2)}) collective-permute-start(bf16[2,1,128,1024]{3,2,0,1:T(8,128)(2,1)S(1)} %get-tuple-element.54), channel_id=1, source_target_pairs={{0,4},{4,8},{8,12},{12,16},{16,20},{20,24},{24,28},{28,0},{1,5},{5... | collective-permute-start | bytes 1572872 | tf_op jit(solution)/shard_map/ppermute | solution.py:38
  31.2 57.1 %collective-permute-start.1 = (bf16[2,1,128,1024]{3,2,0,1:T(8,128)(2,1)S(1)}, bf16[2,1,128,1024]{3,2,0,1:T(8,128)(2,1)S(1)}, u32[]{:S(2)}, u32[]{:S(2)}) collective-permute-start(bf16[2,1,128,1024]{3,2,0,1:T(8,128)(2,1)S(1)} %get-tuple-element.53), channel_id=1, source_target_pairs={{0,8},{4,12},{8,16},{12,20},{16,24},{20,28},{24,0},{28,4},{1,9},{5... | collective-permute-start | bytes 1572872 | tf_op jit(solution)/shard_map/ppermute | solution.py:38
  32.7 36.9 %collective-permute-start.7 = (f32[2,1024]{1,0:T(2,128)S(1)}, f32[2,1024]{1,0:T(2,128)S(1)}, u32[]{:S(2)}, u32[]{:S(2)}) collective-permute-start(f32[2,1024]{1,0:T(2,128)S(1)} %pad_maximum_fusion.3), channel_id=1, source_target_pairs={{0,0},{1,4},{2,8},{3,12},{4,16},{5,20},{6,24},{7,28},{8,1},{9,5},{... | collective-permute-start | bytes 24584 | tf_op jit(solution)/shard_map/ppermute | solution.py:45
  35.6 55.2 %collective-permute-start.2 = (bf16[2,1,128,1024]{3,2,0,1:T(8,128)(2,1)S(1)}, bf16[2,1,128,1024]{3,2,0,1:T(8,128)(2,1)S(1)}, u32[]{:S(2)}, u32[]{:S(2)}) collective-permute-start(bf16[2,1,128,1024]{3,2,0,1:T(8,128)(2,1)S(1)} %get-tuple-element.52), channel_id=1, source_target_pairs={{0,12},{4,16},{8,20},{12,24},{16,28},{20,0},{24,4},{28,8},{1,13},{... | collective-permute-start | bytes 1572872 | tf_op jit(solution)/shard_map/ppermute | solution.py:38
  37.3 53.5 %collective-permute-start.3 = (bf16[2,1,128,1024]{3,2,0,1:T(8,128)(2,1)S(1)}, bf16[2,1,128,1024]{3,2,0,1:T(8,128)(2,1)S(1)}, u32[]{:S(2)}, u32[]{:S(2)}) collective-permute-start(bf16[2,1,128,1024]{3,2,0,1:T(8,128)(2,1)S(1)} %get-tuple-element.51), channel_id=1, source_target_pairs={{0,16},{4,20},{8,24},{12,28},{16,0},{20,4},{24,8},{28,12},{1,17},{... | collective-permute-start | bytes 1572872 | tf_op jit(solution)/shard_map/ppermute | solution.py:38
  69.7 21.8 %collective-permute-start.4 = (bf16[2,1,128,1024]{3,2,0,1:T(8,128)(2,1)S(1)}, bf16[2,1,128,1024]{3,2,0,1:T(8,128)(2,1)S(1)}, u32[]{:S(2)}, u32[]{:S(2)}) collective-permute-start(bf16[2,1,128,1024]{3,2,0,1:T(8,128)(2,1)S(1)} %get-tuple-element.50), channel_id=1, source_target_pairs={{0,20},{4,24},{8,28},{12,0},{16,4},{20,8},{24,12},{28,16},{1,21},{... | collective-permute-start | bytes 1572872 | tf_op jit(solution)/shard_map/ppermute | solution.py:38
  84.8 15.9 %copy-start.1 = (bf16[2,1,128,1024]{3,2,0,1:T(8,128)(2,1)}, bf16[2,1,128,1024]{3,2,0,1:T(8,128)(2,1)S(1)}, u32[]{:S(2)}) copy-start(bf16[2,1,128,1024]{3,2,0,1:T(8,128)(2,1)S(1)} %collective-permute-done) | copy-start | bytes 1572868
  84.8 15.9 %collective-permute-start.5 = (bf16[2,1,128,1024]{3,2,0,1:T(8,128)(2,1)S(1)}, bf16[2,1,128,1024]{3,2,0,1:T(8,128)(2,1)S(1)}, u32[]{:S(2)}, u32[]{:S(2)}) collective-permute-start(bf16[2,1,128,1024]{3,2,0,1:T(8,128)(2,1)S(1)} %get-tuple-element.49), channel_id=1, source_target_pairs={{0,24},{4,28},{8,0},{12,4},{16,8},{20,12},{24,16},{28,20},{1,25},{... | collective-permute-start | bytes 1572872 | tf_op jit(solution)/shard_map/ppermute | solution.py:38
  88.3 12.3 %copy-start.2 = (bf16[2,1,128,1024]{3,2,0,1:T(8,128)(2,1)}, bf16[2,1,128,1024]{3,2,0,1:T(8,128)(2,1)S(1)}, u32[]{:S(2)}) copy-start(bf16[2,1,128,1024]{3,2,0,1:T(8,128)(2,1)S(1)} %collective-permute-done.1) | copy-start | bytes 1572868
  88.3 23.0 %collective-permute-start.6 = (bf16[2,1,128,1024]{3,2,0,1:T(8,128)(2,1)S(1)}, bf16[2,1,128,1024]{3,2,0,1:T(8,128)(2,1)}, u32[]{:S(2)}, u32[]{:S(2)}) collective-permute-start(bf16[2,1,128,1024]{3,2,0,1:T(8,128)(2,1)S(1)} %get-tuple-element.48), channel_id=1, source_target_pairs={{0,28},{4,0},{8,4},{12,8},{16,12},{20,16},{24,20},{28,24},{1,29},{... | collective-permute-start | bytes 1572872 | tf_op jit(solution)/shard_map/ppermute | solution.py:38
  90.8 9.8 %copy-start.3 = (bf16[2,1,128,1024]{3,2,0,1:T(8,128)(2,1)}, bf16[2,1,128,1024]{3,2,0,1:T(8,128)(2,1)S(1)}, u32[]{:S(2)}) copy-start(bf16[2,1,128,1024]{3,2,0,1:T(8,128)(2,1)S(1)} %collective-permute-done.2) | copy-start | bytes 1572868
  90.8 9.8 %copy-start.4 = (bf16[2,1,128,1024]{3,2,0,1:T(8,128)(2,1)}, bf16[2,1,128,1024]{3,2,0,1:T(8,128)(2,1)S(1)}, u32[]{:S(2)}) copy-start(bf16[2,1,128,1024]{3,2,0,1:T(8,128)(2,1)S(1)} %collective-permute-done.3) | copy-start | bytes 1572868
  91.5 9.2 %copy-start.6 = (bf16[2,1,128,1024]{3,2,0,1:T(8,128)(2,1)}, bf16[2,1,128,1024]{3,2,0,1:T(8,128)(2,1)S(1)}, u32[]{:S(2)}) copy-start(bf16[2,1,128,1024]{3,2,0,1:T(8,128)(2,1)S(1)} %collective-permute-done.4) | copy-start | bytes 1572868
  111.3 7.7 %copy-start.5 = (bf16[2,1,128,1024]{3,2,0,1:T(8,128)(2,1)S(1)}, bf16[2,1,128,1024]{3,2,0,1:T(8,128)(2,1)}, u32[]{:S(2)}) copy-start(bf16[2,1,128,1024]{3,2,0,1:T(8,128)(2,1)} %copy-done.4) | copy-start | bytes 1572868
  111.3 8.5 %copy-start.7 = (bf16[2,1,128,1024]{3,2,0,1:T(8,128)(2,1)S(1)}, bf16[2,1,128,1024]{3,2,0,1:T(8,128)(2,1)}, u32[]{:S(2)}) copy-start(bf16[2,1,128,1024]{3,2,0,1:T(8,128)(2,1)} %copy-done.6) | copy-start | bytes 1572868
  111.3 9.3 %copy-start.9 = (bf16[2,1,128,1024]{3,2,0,1:T(8,128)(2,1)S(1)}, bf16[2,1,128,1024]{3,2,0,1:T(8,128)(2,1)}, u32[]{:S(2)}) copy-start(bf16[2,1,128,1024]{3,2,0,1:T(8,128)(2,1)} %copy-done.8) | copy-start | bytes 1572868
  141.6 14.3 %copy-start.13 = (bf16[2]{0:T(256)(128)(2,1)S(1)}, bf16[2]{0:T(256)(128)(2,1)}, u32[]{:S(2)}) copy-start(bf16[2]{0:T(256)(128)(2,1)} %constant.146.clone) | copy-start | bytes 16
  144.9 15.6 %copy-start.10 = (s32[4,1024]{1,0:T(4,128)S(1)}, s32[4,1024]{1,0:T(4,128)}, u32[]{:S(2)}) copy-start(s32[4,1024]{1,0:T(4,128)} %param.9) | copy-start | bytes 49156
  144.9 59.9 %all-to-all-start.1 = ((bf16[32,128,256]{2,1,0:T(8,128)(2,1)}), bf16[32,128,256]{2,1,0:T(8,128)(2,1)}, u32[]{:S(2)}, u32[]{:S(2)}) async-start(bf16[32,128,256]{2,1,0:T(8,128)(2,1)} %bitcast.95), calls=%async_computation.1 | async-start | bytes 4194304 | tf_op jit(solution)/shard_map/all_to_all | solution.py:68
  207.9 71.4 %all-to-all-start.2 = ((f32[4,256,768]{2,1,0:T(8,128)}), f32[4,256,768]{2,1,0:T(8,128)S(1)}, u32[]{:S(2)}, u32[]{:S(2)}) async-start(f32[4,256,768]{2,1,0:T(8,128)} %pad_maximum_fusion.2), calls=%async_computation.2 | async-start | bytes 6291456 | tf_op jit(solution)/shard_map/all_to_all | solution.py:78
  (1 other events, 0.8 us)

commit v5 on v4

--- a/solution.py
+++ b/solution.py
@@ -31,13 +31,13 @@
     part_dest = q_dest // ch_dev - level * (rows // slab)
     five = stacked.reshape(2, ch_dev, rows // slab, slab, width)
     outgoing = five[:, slot_dest, part_dest]
-    pieces = [lax.dynamic_index_in_dim(outgoing, mine, 1, True)]
+    pieces = [lax.dynamic_index_in_dim(outgoing, mine, 1, False)]
     for shift in range(1, n_chan):
-        piece = lax.dynamic_index_in_dim(outgoing, (mine + shift) % n_chan, 1, True)
+        piece = lax.dynamic_index_in_dim(outgoing, (mine + shift) % n_chan, 1, False)
         pairs = [(a, (a + shift) % n_chan) for a in range(n_chan)]
         pieces.append(lax.ppermute(piece, "ch", pairs))
     whole, pieces = lax.optimization_barrier((whole, pieces))
-    arrived = jnp.concatenate(pieces, axis=1)[:, (mine - dest) % n_chan]
+    arrived = jnp.stack(pieces, axis=1)[:, (mine - dest) % n_chan]
     a_eta = arrived[0].reshape(width, width)
     b_gamma = arrived[1].reshape(width, width)
 
@@ -55,14 +55,14 @@
     own = lax.dynamic_index_in_dim(stacked, level, 1, False)
     own_t = own.reshape(2, rows, n_rows, rows).transpose(0, 2, 3, 1)
     own_t = own_t * jnp.array([-1, 1], bf16)[:, None, None, None]
-    whole = jnp.concatenate([whole, own_t], axis=-1)
-    whole = jnp.roll(whole, (level + 1) * rows, axis=-1).reshape(2, width, width)
-    eta_c = whole[0]
-    gamma_c = whole[1]
-
+    whole = jnp.concatenate([whole, own_t], axis=-1).reshape(2, width, width)
     factor = lax.dynamic_index_in_dim(pp_factor, level, 0, False).astype(bf16)
-    product = jnp.dot(eta_c * factor[None, :], gamma_c, preferred_element_type=f32)
-    ladder_c = (product + product.T).reshape(n_rows, rows, width)
+    factor = jnp.roll(factor, -(level + 1) * rows)
+    left = jnp.concatenate([whole[0] * factor, whole[1] * factor], axis=-1)
+    right = jnp.concatenate([whole[1], whole[0]], axis=-1)
+    ladder_c = lax.dot_general(
+        left, right, (((1,), (1,)), ((), ())), preferred_element_type=f32
+    ).reshape(n_rows, rows, width)
     sending = jnp.stack([skip_block(ladder_c[a], a, rows) for a in range(n_rows)])
     returning = term_t.reshape(n_chan, slab, n_rows, rows).transpose(0, 2, 1, 3)
     landed = lax.all_to_all(
@@ -81,9 +81,10 @@
     back = jnp.einsum("gts,gtwi->sigw", onehot, landed, preferred_element_type=f32)
     back = back.reshape(ch_dev, rows, width)
 
-    weighted = eta_pp * pp_factor.astype(bf16)[:, None, :]
-    diag = jnp.einsum("sik,sjk->sij", weighted, gamma_pp, preferred_element_type=f32)
-    diag = diag + jnp.swapaxes(diag, 1, 2)
+    local_d = pp_factor.astype(bf16)[:, None, :]
+    left = jnp.concatenate([eta_pp * local_d, gamma_pp * local_d], axis=-1)
+    right = jnp.concatenate([gamma_pp, eta_pp], axis=-1)
+    diag = jnp.einsum("sik,sjk->sij", left, right, preferred_element_type=f32)
     ladder = jnp.concatenate([ladder, diag], axis=-1)
     ladder = jnp.roll(ladder, (level + 1) * rows, axis=-1)
     return (ladder + back).astype(bf16)

time: 290 us -> 294 us (1.014)
  waiting for transfers between devices: 109 us -> 135 us
  matrix products: 21.8 us -> 14.2 us
  other arithmetic: 35.4 us -> 27.8 us
  local copies, waits for them, and re-layouts: 67.5 us -> 63 us
    all_to_all x1, waiting for transfers between devices: 11.7 us -> 24.3 us  [per_device(): lax.all_to_all(returning.reshape(n_chan * n_rows, slab, rows), ('ch', 'ro...]
    all_to_all x1, waiting for transfers between devices: 47.8 us -> 58.9 us  [per_device(): lax.all_to_all(sending, 'row', split_axis=0, concat_axis=0, tiled=True)]
    dot_general x2 -> x0, local copies, waits for them, and re-layouts: 8 us -> none  [the longest x1 5.45 us: per_device(): jnp.dot(eta_c * factor[None, :], gamma_c, preferred_element_type=f32)]
    add x2 -> x0, other arithmetic: 7.07 us -> none  [the longest x1 4.4 us: per_device(): ladder_c = (product + product.T).reshape(n_rows, rows, width)]
    slice x1 -> x2, local copies, waits for them, and re-layouts: 2.49 us -> 7.93 us  [per_device(): left = jnp.concatenate([whole[0] * factor, whole[1] * factor], axis=-1)]
    reshape x1 -> x0, local copies, waits for them, and re-layouts: 5.26 us -> none  [per_device(): back = back.reshape(ch_dev, rows, width)]
    mul x0 -> x2, other arithmetic: none -> 4.74 us  [the longest x1 2.65 us: per_device(): left = jnp.concatenate([whole[0] * factor, whole[1] * factor], axis=-1)]
    mul x1 -> x0, local copies, waits for them, and re-layouts: 4.02 us -> none  [per_device(): eta_c * factor[None, :]]
  transfers between devices with their start and end apart: 11 -> 11, of which waited for: 6 -> 6; matrix products, arithmetic and copies ran while one was open for 25% -> 16% of each run, Pallas kernels for 0% -> 0%
where the time goes in v5:
time: 294 us; the launch traced here: 289 us
  waiting for transfers between devices  135 us (46%)
  local copies, waits for them, and re-layouts  63 us (21%)
  starting transfers between devices  49 us (17%)
  other arithmetic  27.8 us (9%)
  matrix products  14.2 us (5%)
    all_to_all x1, waiting for transfers between devices, per_device(): lax.all_to_all(sending, 'row', split_axis=0, concat_axis=0, tiled=True)  58.9 us
    ppermute x1, waiting for transfers between devices, per_device(): lax.ppermute(jnp.concatenate([ph_factor.astype(f32), recouple], axis=0),...  30.8 us
    ppermute x7, starting transfers between devices, per_device(): pieces.append(lax.ppermute(piece, 'ch', pairs))  26.7 us
    all_to_all x1, waiting for transfers between devices, per_device(): lax.all_to_all(returning.reshape(n_chan * n_rows, slab, rows), ('ch', 'ro...  24.3 us
    unnamed x31, local copies, waits for them, and re-layouts  20.8 us
    ppermute x7, waiting for transfers between devices, per_device(): pieces.append(lax.ppermute(piece, 'ch', pairs))  20.5 us
    all_to_all x1, starting transfers between devices, per_device(): lax.all_to_all(returning.reshape(n_chan * n_rows, slab, rows), ('ch', 'ro...  9.38 us
    slice x2, local copies, waits for them, and re-layouts, per_device(): left = jnp.concatenate([whole[0] * factor, whole[1] * factor], axis=-1)  7.93 us
  transfers between devices with their start and end apart: 11, of which 6 were waited for; matrix products, arithmetic and copies ran while one was open for 16% of the time, Pallas kernels for 0%

profile of v5, /device:TPU:8, one launch (start us, length us, event | category | flops | bytes accessed | tf_op | source)
XLA Modules:
  0.0 288.9 jit_solution(16117169280072780705)
XLA Ops:
  0.0 4.1 %copy.21 = bf16[4,256,1024]{1,2,0:T(8,128)(2,1)} copy(bf16[4,256,1024]{2,1,0:T(8,128)(2,1)} %param.7) | data formatting | bytes 4194304 | tf_op args[0]
  11.9 5.5 %all-to-all-start = ((bf16[2,4,256,768]{2,3,0,1:T(8,128)(2,1)}), bf16[2,4,256,768]{2,3,0,1:T(8,128)(2,1)}, u32[]{:S(2)}, u32[]{:S(2)}) async-start(bf16[2,4,256,768]{2,3,0,1:T(8,128)(2,1)} %pad_maximum_fusion.1), calls=%async_computation | async-start | bytes 6291456 | tf_op jit(solution)/shard_map/all_to_all | solution.py:27
  18.0 3.9 %pad_maximum_fusion = bf16[2,4,2,128,1024]{4,3,2,1,0:T(8,128)(2,1)} fusion(bf16[1,4,2,128,1024]{4,3,2,1,0:T(8,128)(2,1)} %bitcast.104, bf16[1,4,2,128,1024]{4,3,2,1,0:T(8,128)(2,1)S(1)} %bitcast.103), kind=kLoop, calls=%fused_computation.22 | loop fusion | flops 2097152 | bytes 8388608 | tf_op jit(solution)/shard_map/stack | solution.py:23
  21.9 5.0 %gather_fusion.1 = bf16[8,2,128,1024]{3,2,1,0:T(8,128)(2,1)} fusion(bf16[2,4,2,128,1024]{4,3,2,1,0:T(8,128)(2,1)} %pad_maximum_fusion, s32[8]{0:T(128)S(1)} %fusion.47), kind=kCustom, calls=%fused_computation.1 | custom fusion | bytes 8388672 | tf_op jit(solution)/shard_map/gather | solution.py:33
  26.9 3.6 %dynamic-slice_bitcast_fusion = (bf16[2,128,1024]{2,1,0:T(8,128)(2,1)S(1)}, bf16[2,128,1024]{2,1,0:T(8,128)(2,1)S(1)}, bf16[2,128,1024]{2,1,0:T(8,128)(2,1)S(1)}...) fusion(bf16[8,2,128,1024]{3,2,1,0:T(8,128)(2,1)} %gather_fusion, ...), kind=kLoop, calls=%fused_computation.78 | loop fusion | bytes 8388640 | tf_op jit(solution)/shard_map/jit(dynamic_index_in_dim)/squeeze | solution.py:36
  39.0 30.8 %collective-permute-done.7 = f32[2,1024]{1,0:T(2,128)S(1)} collective-permute-done((f32[2,1024]{1,0:T(2,128)S(1)}, f32[2,1024]{1,0:T(2,128)S(1)}, u32[]{:S(2)}, u32[]{:S(2)}) %collective-permute-start.7) | collective-permute-done | bytes 8224 | tf_op jit(solution)/shard_map/ppermute | solution.py:45
  69.8 15.2 %collective-permute-start.4 = (bf16[2,128,1024]{2,1,0:T(8,128)(2,1)S(1)}, bf16[2,128,1024]{2,1,0:T(8,128)(2,1)}, u32[]{:S(2)}, u32[]{:S(2)}) collective-permute-start(bf16[2,128,1024]{2,1,0:T(8,128)(2,1)S(1)} %get-tuple-element.45), channel_id=1, source_target_pairs={{0,20},{4,24},{8,28},{12,0},{16,4},{20,8},{24,12},{28,16},{1,21},{... | collective-permute-start | bytes 1572872 | tf_op jit(solution)/shard_map/ppermute | solution.py:38
  85.0 3.4 %collective-permute-start.5 = (bf16[2,128,1024]{2,1,0:T(8,128)(2,1)S(1)}, bf16[2,128,1024]{2,1,0:T(8,128)(2,1)}, u32[]{:S(2)}, u32[]{:S(2)}) collective-permute-start(bf16[2,128,1024]{2,1,0:T(8,128)(2,1)S(1)} %get-tuple-element.44), channel_id=1, source_target_pairs={{0,24},{4,28},{8,0},{12,4},{16,8},{20,12},{24,16},{28,20},{1,25},{... | collective-permute-start | bytes 1572872 | tf_op jit(solution)/shard_map/ppermute | solution.py:38
  91.7 9.0 %collective-permute-done.5 = bf16[2,128,1024]{2,1,0:T(8,128)(2,1)} collective-permute-done((bf16[2,128,1024]{2,1,0:T(8,128)(2,1)S(1)}, bf16[2,128,1024]{2,1,0:T(8,128)(2,1)}, u32[]{:S(2)}, u32[]{:S(2)}) %collective-permute-start.5) | collective-permute-done | bytes 524320 | tf_op jit(solution)/shard_map/ppermute | solution.py:38
  100.7 10.7 %collective-permute-done.6 = bf16[2,128,1024]{2,1,0:T(8,128)(2,1)} collective-permute-done((bf16[2,128,1024]{2,1,0:T(8,128)(2,1)S(1)}, bf16[2,128,1024]{2,1,0:T(8,128)(2,1)}, u32[]{:S(2)}, u32[]{:S(2)}) %collective-permute-start.6) | collective-permute-done | bytes 524320 | tf_op jit(solution)/shard_map/ppermute | solution.py:38
  126.4 5.0 %gather_fusion.2 = bf16[8,2,128,1024]{3,2,1,0:T(8,128)(2,1)} fusion(bf16[2,8,128,1024]{3,2,0,1:T(8,128)(2,1)} %bitcast_dynamic-update-slice_fusion, s32[1024]{0:T(1024)S(1)} %pad_clamp_fusion), kind=kCustom, calls=%fused_computation.2 | custom fusion | bytes 8388640 | tf_op jit(solution)/shard_map/gather | solution.py:40
  136.6 3.7 %multiply_convert_fusion = bf16[1024,1024]{1,0:T(8,128)(2,1)} fusion(f32[1024,1024]{1,0:T(8,128)S(1)} %fusion.52, f32[1024]{0:T(1024)S(1)} %bitcast.117, bf16[1024,1024]{1,0:T(8,128)(2,1)S(1)} %bitcast.113, bf16[1024,1024]{1,0:T(8,128)(2,1)S(1)} %bitcast.114), kind=kOutput, calls=%fused_computation.39 | convolution fusion | flops 2150629376 | bytes 10489856 | tf_op jit(solution)/shard_map/dot_general | solution.py:52
  140.2 4.5 %reshape.190 = bf16[8,128,4,256]{3,2,1,0:T(4,128)(2,1)} reshape(bf16[1024,1024]{1,0:T(8,128)(2,1)} %multiply_convert_fusion) | data formatting | bytes 4194304 | tf_op jit(solution)/shard_map/reshape | solution.py:67
  144.7 3.3 %copy.26 = bf16[8,128,4,256]{3,1,2,0:T(8,128)(2,1)} copy(bf16[8,128,4,256]{3,2,1,0:T(4,128)(2,1)} %reshape.190) | data formatting | bytes 4194304 | tf_op jit(solution)/shard_map/reshape | solution.py:67
  148.1 9.4 %all-to-all-start.1 = ((bf16[32,128,256]{2,1,0:T(8,128)(2,1)}), bf16[32,128,256]{2,1,0:T(8,128)(2,1)}, u32[]{:S(2)}, u32[]{:S(2)}) async-start(bf16[32,128,256]{2,1,0:T(8,128)(2,1)} %bitcast.110), calls=%async_computation.1 | async-start | bytes 4194304 | tf_op jit(solution)/shard_map/all_to_all | solution.py:68
  160.2 3.5 %fusion.19 = (bf16[1,4,256,1024]{2,3,0,1:T(8,128)(2,1)}, bf16[1,4,256,1024]{2,3,0,1:T(8,128)(2,1)}) fusion(bf16[2,4,256,768]{2,3,0,1:T(8,128)(2,1)} %all-to-all-done, bf16[2,4,256,256]{2,3,0,1:T(8,128)(2,1)S(1)} %copy.23), kind=kLoop, calls=%fused_computation.43 | loop fusion | flops 8388608 | bytes 8388608 | tf_op jit(solution)/shard_map/concatenate | solution.py:58
  163.8 4.0 %copy.24 = bf16[1,4,256,1024]{3,2,1,0:T(8,128)(2,1)} copy(bf16[1,4,256,1024]{2,3,0,1:T(8,128)(2,1)} %get-tuple-element.39) | data formatting | bytes 4194304 | tf_op jit(solution)/shard_map/slice | solution.py:61
  167.7 3.9 %copy.25 = bf16[1,4,256,1024]{3,2,1,0:T(8,128)(2,1)} copy(bf16[1,4,256,1024]{2,3,0,1:T(8,128)(2,1)} %get-tuple-element.40) | data formatting | bytes 4194304 | tf_op jit(solution)/shard_map/slice | solution.py:61
  175.2 4.5 %fusion.5 = f32[1024,1024]{0,1:T(8,128)S(1)} fusion(bf16[1024,1024]{1,0:T(8,128)(2,1)S(1)} %get-tuple-element.59, bf16[1024,1024]{1,0:T(8,128)(2,1)S(1)} %get-tuple-element.58, bf16[1024,1024]{1,0:T(8,128)(2,1)S(1)} %bitcast.108, bf16[1024,1024]{1,0:T(8,128)(2,1)S(1)} %bitcast.109), kind=kOutput, calls=%fused_computation.25 | convolution fusion | flops 4311744512 | bytes 12582912 | tf_op jit(solution)/shard_map/dot_general | solution.py:63
  182.0 24.3 %all-to-all-done.1 = bf16[32,128,256]{2,1,0:T(8,128)(2,1)} async-done(((bf16[32,128,256]{2,1,0:T(8,128)(2,1)}), bf16[32,128,256]{2,1,0:T(8,128)(2,1)}, u32[]{:S(2)}, u32[]{:S(2)}) %all-to-all-start.1) | async-done | bytes 2097184 | tf_op jit(solution)/shard_map/all_to_all | solution.py:68
  206.3 3.1 %copy.27 = bf16[8,4,128,256]{3,2,0,1:T(8,128)(2,1)} copy(bf16[8,4,128,256]{3,2,1,0:T(8,128)(2,1)} %bitcast.48) | data formatting | bytes 4194304 | tf_op jit(solution)/shard_map/reshape | solution.py:75
  209.5 4.7 %all-to-all-start.2 = ((f32[4,256,768]{1,2,0:T(8,128)}), f32[4,256,768]{1,2,0:T(8,128)}, u32[]{:S(2)}, u32[]{:S(2)}) async-start(f32[4,256,768]{1,2,0:T(8,128)} %pad_maximum_fusion.2), calls=%async_computation.2 | async-start | bytes 6291456 | tf_op jit(solution)/shard_map/all_to_all | solution.py:78
  223.0 58.9 %all-to-all-done.2 = f32[4,256,768]{1,2,0:T(8,128)} async-done(((f32[4,256,768]{1,2,0:T(8,128)}), f32[4,256,768]{1,2,0:T(8,128)}, u32[]{:S(2)}, u32[]{:S(2)}) %all-to-all-start.2) | async-done | bytes 3145760 | tf_op jit(solution)/shard_map/all_to_all | solution.py:78
  281.9 4.6 %fusion.4 = bf16[4,256,1024]{1,2,0:T(8,128)(2,1)S(1)} fusion(s32[]{:T(128)S(6)} %select_n.176, f32[4,256,768]{1,2,0:T(8,128)} %all-to-all-done.2, f32[4,256,256]{1,2,0:T(8,128)S(1)} %fusion.12, f32[4,256,8,128]{1,3,2,0:T(8,128)} %copy.29), kind=kLoop, calls=%fused_computation.21 | loop fusion | flops 5242880 | bytes 10485764 | tf_op jit(solution)/shard_map/convert_element_type | solution.py:90
  (80 shorter events, 59.8 us)
Async XLA Ops:
  0.0 17.3 %copy-start = (s32[32,8]{0,1:T(8,128)S(1)}, s32[32,8]{0,1:T(8,128)}, u32[]{:S(2)}) copy-start(s32[32,8]{0,1:T(8,128)} %param.12) | copy-start | bytes 3076
  0.0 4.1 %copy-start.2 = (bf16[4,256,1024]{2,1,0:T(8,128)(2,1)S(1)}, bf16[4,256,1024]{2,1,0:T(8,128)(2,1)}, u32[]{:S(2)}) copy-start(bf16[4,256,1024]{2,1,0:T(8,128)(2,1)} %param.8) | copy-start | bytes 6291460
  11.8 6.1 %copy-start.1 = (bf16[4,256,1024]{2,1,0:T(8,128)(2,1)S(1)}, bf16[4,256,1024]{2,1,0:T(8,128)(2,1)}, u32[]{:S(2)}) copy-start(bf16[4,256,1024]{2,1,0:T(8,128)(2,1)} %param.7) | copy-start | bytes 6291460
  11.9 99.5 %all-to-all-start = ((bf16[2,4,256,768]{2,3,0,1:T(8,128)(2,1)}), bf16[2,4,256,768]{2,3,0,1:T(8,128)(2,1)}, u32[]{:S(2)}, u32[]{:S(2)}) async-start(bf16[2,4,256,768]{2,3,0,1:T(8,128)(2,1)} %pad_maximum_fusion.1), calls=%async_computation | async-start | bytes 6291456 | tf_op jit(solution)/shard_map/all_to_all | solution.py:27
  26.9 5.1 %copy-start.8 = (s32[1,1024]{1,0:T(1,128)S(1)}, s32[1,1024]{1,0:T(1,128)}, u32[]{:S(2)}) copy-start(s32[1,1024]{1,0:T(1,128)} %param.10) | copy-start | bytes 12292
  26.9 5.1 %copy-start.9 = (f32[1,1024]{1,0:T(1,128)S(1)}, f32[1,1024]{1,0:T(1,128)}, u32[]{:S(2)}) copy-start(f32[1,1024]{1,0:T(1,128)} %param.11) | copy-start | bytes 12292
  30.5 54.5 %collective-permute-start = (bf16[2,128,1024]{2,1,0:T(8,128)(2,1)S(1)}, bf16[2,128,1024]{2,1,0:T(8,128)(2,1)}, u32[]{:S(2)}, u32[]{:S(2)}) collective-permute-start(bf16[2,128,1024]{2,1,0:T(8,128)(2,1)S(1)} %get-tuple-element.49), channel_id=1, source_target_pairs={{0,4},{4,8},{8,12},{12,16},{16,20},{20,24},{24,28},{28,0},{1,5},{5... | collective-permute-start | bytes 1572872 | tf_op jit(solution)/shard_map/ppermute | solution.py:38
  30.5 57.9 %collective-permute-start.1 = (bf16[2,128,1024]{2,1,0:T(8,128)(2,1)S(1)}, bf16[2,128,1024]{2,1,0:T(8,128)(2,1)}, u32[]{:S(2)}, u32[]{:S(2)}) collective-permute-start(bf16[2,128,1024]{2,1,0:T(8,128)(2,1)S(1)} %get-tuple-element.48), channel_id=1, source_target_pairs={{0,8},{4,12},{8,16},{12,20},{16,24},{20,28},{24,0},{28,4},{1,9},{5... | collective-permute-start | bytes 1572872 | tf_op jit(solution)/shard_map/ppermute | solution.py:38
  32.1 37.7 %collective-permute-start.7 = (f32[2,1024]{1,0:T(2,128)S(1)}, f32[2,1024]{1,0:T(2,128)S(1)}, u32[]{:S(2)}, u32[]{:S(2)}) collective-permute-start(f32[2,1024]{1,0:T(2,128)S(1)} %pad_maximum_fusion.4), channel_id=1, source_target_pairs={{0,0},{1,4},{2,8},{3,12},{4,16},{5,20},{6,24},{7,28},{8,1},{9,5},{... | collective-permute-start | bytes 24584 | tf_op jit(solution)/shard_map/ppermute | solution.py:45
  34.9 56.0 %collective-permute-start.2 = (bf16[2,128,1024]{2,1,0:T(8,128)(2,1)S(1)}, bf16[2,128,1024]{2,1,0:T(8,128)(2,1)}, u32[]{:S(2)}, u32[]{:S(2)}) collective-permute-start(bf16[2,128,1024]{2,1,0:T(8,128)(2,1)S(1)} %get-tuple-element.47), channel_id=1, source_target_pairs={{0,12},{4,16},{8,20},{12,24},{16,28},{20,0},{24,4},{28,8},{1,13},{... | collective-permute-start | bytes 1572872 | tf_op jit(solution)/shard_map/ppermute | solution.py:38
  36.6 54.3 %collective-permute-start.3 = (bf16[2,128,1024]{2,1,0:T(8,128)(2,1)S(1)}, bf16[2,128,1024]{2,1,0:T(8,128)(2,1)}, u32[]{:S(2)}, u32[]{:S(2)}) collective-permute-start(bf16[2,128,1024]{2,1,0:T(8,128)(2,1)S(1)} %get-tuple-element.46), channel_id=1, source_target_pairs={{0,16},{4,20},{8,24},{12,28},{16,0},{20,4},{24,8},{28,12},{1,17},{... | collective-permute-start | bytes 1572872 | tf_op jit(solution)/shard_map/ppermute | solution.py:38
  69.8 21.9 %collective-permute-start.4 = (bf16[2,128,1024]{2,1,0:T(8,128)(2,1)S(1)}, bf16[2,128,1024]{2,1,0:T(8,128)(2,1)}, u32[]{:S(2)}, u32[]{:S(2)}) collective-permute-start(bf16[2,128,1024]{2,1,0:T(8,128)(2,1)S(1)} %get-tuple-element.45), channel_id=1, source_target_pairs={{0,20},{4,24},{8,28},{12,0},{16,4},{20,8},{24,12},{28,16},{1,21},{... | collective-permute-start | bytes 1572872 | tf_op jit(solution)/shard_map/ppermute | solution.py:38
  85.0 15.7 %collective-permute-start.5 = (bf16[2,128,1024]{2,1,0:T(8,128)(2,1)S(1)}, bf16[2,128,1024]{2,1,0:T(8,128)(2,1)}, u32[]{:S(2)}, u32[]{:S(2)}) collective-permute-start(bf16[2,128,1024]{2,1,0:T(8,128)(2,1)S(1)} %get-tuple-element.44), channel_id=1, source_target_pairs={{0,24},{4,28},{8,0},{12,4},{16,8},{20,12},{24,16},{28,20},{1,25},{... | collective-permute-start | bytes 1572872 | tf_op jit(solution)/shard_map/ppermute | solution.py:38
  88.4 23.0 %collective-permute-start.6 = (bf16[2,128,1024]{2,1,0:T(8,128)(2,1)S(1)}, bf16[2,128,1024]{2,1,0:T(8,128)(2,1)}, u32[]{:S(2)}, u32[]{:S(2)}) collective-permute-start(bf16[2,128,1024]{2,1,0:T(8,128)(2,1)S(1)} %get-tuple-element.43), channel_id=1, source_target_pairs={{0,28},{4,0},{8,4},{12,8},{16,12},{20,16},{24,20},{28,24},{1,29},{... | collective-permute-start | bytes 1572872 | tf_op jit(solution)/shard_map/ppermute | solution.py:38
  144.7 12.8 %copy-start.10 = (bf16[2]{0:T(256)(128)(2,1)S(1)}, bf16[2]{0:T(256)(128)(2,1)}, u32[]{:S(2)}) copy-start(bf16[2]{0:T(256)(128)(2,1)} %constant.149.clone) | copy-start | bytes 16
  148.1 12.0 %copy-start.7 = (s32[4,1024]{1,0:T(4,128)S(1)}, s32[4,1024]{1,0:T(4,128)}, u32[]{:S(2)}) copy-start(s32[4,1024]{1,0:T(4,128)} %param.9) | copy-start | bytes 49156
  148.1 58.3 %all-to-all-start.1 = ((bf16[32,128,256]{2,1,0:T(8,128)(2,1)}), bf16[32,128,256]{2,1,0:T(8,128)(2,1)}, u32[]{:S(2)}, u32[]{:S(2)}) async-start(bf16[32,128,256]{2,1,0:T(8,128)(2,1)} %bitcast.110), calls=%async_computation.1 | async-start | bytes 4194304 | tf_op jit(solution)/shard_map/all_to_all | solution.py:68
  171.7 2.9 copy-start.4
  171.7 3.5 %copy-start.5 = (bf16[1,4,256,1024]{3,2,1,0:T(8,128)(2,1)S(1)}, bf16[1,4,256,1024]{3,2,1,0:T(8,128)(2,1)}, u32[]{:S(2)}) copy-start(bf16[1,4,256,1024]{3,2,1,0:T(8,128)(2,1)} %copy.25) | copy-start | bytes 6291460
  209.5 72.4 %all-to-all-start.2 = ((f32[4,256,768]{1,2,0:T(8,128)}), f32[4,256,768]{1,2,0:T(8,128)}, u32[]{:S(2)}, u32[]{:S(2)}) async-start(f32[4,256,768]{1,2,0:T(8,128)} %pad_maximum_fusion.2), calls=%async_computation.2 | async-start | bytes 6291456 | tf_op jit(solution)/shard_map/all_to_all | solution.py:78
  214.3 2.2 copy-start.3
  216.5 2.0 copy-start.6

commit v6 on v5

--- a/solution.py
+++ b/solution.py
@@ -24,20 +24,18 @@
     sending = jnp.stack(
         [skip_block(stacked[:, s], s, rows) for s in range(n_rows)], axis=1
     )
-    whole = lax.all_to_all(sending, "row", split_axis=1, concat_axis=1, tiled=True)
+    ladder_in = [lax.dynamic_index_in_dim(sending, level, 1, False)]
+    for shift in range(1, n_rows):
+        piece = lax.dynamic_index_in_dim(sending, (level + shift) % n_rows, 1, False)
+        pairs = [(a, (a + shift) % n_rows) for a in range(n_rows)]
+        ladder_in.append(lax.ppermute(piece, "row", pairs))
     dest = jnp.arange(n_chan, dtype=jnp.int32)
     q_dest = level * n_chan + dest
     slot_dest = src_slot[q_dest, mine]
     part_dest = q_dest // ch_dev - level * (rows // slab)
     five = stacked.reshape(2, ch_dev, rows // slab, slab, width)
     outgoing = five[:, slot_dest, part_dest]
-    pieces = [lax.dynamic_index_in_dim(outgoing, mine, 1, False)]
-    for shift in range(1, n_chan):
-        piece = lax.dynamic_index_in_dim(outgoing, (mine + shift) % n_chan, 1, False)
-        pairs = [(a, (a + shift) % n_chan) for a in range(n_chan)]
-        pieces.append(lax.ppermute(piece, "ch", pairs))
-    whole, pieces = lax.optimization_barrier((whole, pieces))
-    arrived = jnp.stack(pieces, axis=1)[:, (mine - dest) % n_chan]
+    arrived = lax.all_to_all(outgoing, "ch", split_axis=1, concat_axis=1, tiled=True)
     a_eta = arrived[0].reshape(width, width)
     b_gamma = arrived[1].reshape(width, width)
 
@@ -51,7 +49,9 @@
     ph_t = jnp.dot(a_eta * weight, b_gamma, preferred_element_type=f32)
     ph_t = ph_t - jnp.dot(b_gamma * weight, a_eta, preferred_element_type=f32)
     term_t = (ph_t * coef[:, None]).astype(bf16)
-    whole, term_t = lax.optimization_barrier((whole, term_t))
+    ladder_in, term_t = lax.optimization_barrier((ladder_in, term_t))
+    sources = (level - jnp.arange(n_rows, dtype=jnp.int32)) % n_rows
+    whole = jnp.stack(ladder_in, axis=1)[:, sources]
     own = lax.dynamic_index_in_dim(stacked, level, 1, False)
     own_t = own.reshape(2, rows, n_rows, rows).transpose(0, 2, 3, 1)
     own_t = own_t * jnp.array([-1, 1], bf16)[:, None, None, None]

time: 294 us -> 261 us (0.89)
  the two profiles are of different devices: /device:TPU:8 before, /device:TPU:0 now
where the time goes in v6:
time: 261 us; the launch traced here: 260 us
  waiting for transfers between devices  126 us (48%)
  local copies, waits for them, and re-layouts  47.7 us (18%)
  starting transfers between devices  42.1 us (16%)
  other arithmetic  29.4 us (11%)
  matrix products  14.2 us (5%)
    all_to_all x1, waiting for transfers between devices, per_device(): lax.all_to_all(sending, 'row', split_axis=0, concat_axis=0, tiled=True)  63.3 us
    all_to_all x1, waiting for transfers between devices, per_device(): lax.all_to_all(returning.reshape(n_chan * n_rows, slab, rows), ('ch', 'ro...  28.8 us
    all_to_all x1, starting transfers between devices, per_device(): lax.all_to_all(returning.reshape(n_chan * n_rows, slab, rows), ('ch', 'ro...  22.7 us
    ppermute x3, waiting for transfers between devices, per_device(): ladder_in.append(lax.ppermute(piece, 'row', pairs))  21 us
    all_to_all x1, waiting for transfers between devices, per_device(): lax.all_to_all(outgoing, 'ch', split_axis=1, concat_axis=1, tiled=True)  13.2 us
    ppermute x3, starting transfers between devices, per_device(): ladder_in.append(lax.ppermute(piece, 'row', pairs))  8.77 us
    dynamic_slice x4, local copies, waits for them, and re-layouts, per_device(): lax.dynamic_index_in_dim(sending, (level + shift) % n_rows, 1, False)  8.7 us
    reshape x2, local copies, waits for them, and re-layouts, per_device(): returning = term_t.reshape(n_chan, slab, n_rows, rows).transpose(0, 2, 1, 3)  7.82 us
  transfers between devices with their start and end apart: 7, of which 4 were waited for; matrix products, arithmetic and copies ran while one was open for 24% of the time, Pallas kernels for 0%

profile of v6, /device:TPU:0, one launch (start us, length us, event | category | flops | bytes accessed | tf_op | source)
XLA Modules:
  0.0 260.0 jit_solution(12641155034997598670)
XLA Ops:
  1.3 4.6 %pad_maximum_fusion = bf16[2,4,2,128,1024]{4,3,2,1,0:T(8,128)(2,1)} fusion(bf16[1,4,2,128,1024]{4,3,2,1,0:T(8,128)(2,1)} %bitcast.81, bf16[1,4,2,128,1024]{4,3,2,1,0:T(8,128)(2,1)} %bitcast.80), kind=kLoop, calls=%fused_computation.22 | loop fusion | flops 2097152 | bytes 8388608 | tf_op jit(solution)/shard_map/stack | solution.py:23
  6.0 4.9 %gather_fusion.1 = bf16[8,2,128,1024]{3,2,1,0:T(8,128)(2,1)} fusion(bf16[2,4,2,128,1024]{4,3,2,1,0:T(8,128)(2,1)} %pad_maximum_fusion, s32[8]{0:T(128)S(1)} %fusion.48), kind=kCustom, calls=%fused_computation.1 | custom fusion | bytes 8388672 | tf_op jit(solution)/shard_map/gather | solution.py:37
  10.9 5.3 %all-to-all-start = ((bf16[2,8,128,1024]{3,2,0,1:T(8,128)(2,1)}), bf16[2,8,128,1024]{3,2,0,1:T(8,128)(2,1)}, u32[]{:S(2)}, u32[]{:S(2)}) async-start(bf16[2,8,128,1024]{3,2,0,1:T(8,128)(2,1)} %bitcast.82), calls=%async_computation | async-start | bytes 8388608 | tf_op jit(solution)/shard_map/all_to_all | solution.py:38
  16.9 2.6 copy.28
  19.5 3.9 %copy.29 = bf16[4,256,1024]{1,2,0:T(8,128)(2,1)} copy(bf16[4,256,1024]{2,1,0:T(8,128)(2,1)} %param.8) | data formatting | bytes 4194304 | tf_op args[1]
  23.4 4.1 %fusion.23 = (bf16[2,256,1024]{1,2,0:T(8,128)(2,1)}, bf16[2,256,1024]{1,2,0:T(8,128)(2,1)S(1)}, bf16[2,256,1024]{1,2,0:T(8,128)(2,1)S(1)}, bf16[2,256,1024]{1,2,0:T(8,128)(2,1)}, bf16[2,1,256,1024]{2,3,0,1:T(8,128)(2,1)S(1)}) fusion(bf16[1,4,256,1024]{2,3,0,1:T(8,128)(2,1)} %bitcast.84, bf16[1,4,256,1024]{2,3,0,1:T(8,128)(2,1)} %bitcast.85, s32[]{:T(128)S(6)} %select_n.123), kind=kLoop, calls=%fused_computation.49 | loop fusion | flops 2621440 | bytes 9437188 | tf_op jit(solution)/shard_map/squeeze | solution.py:25
  36.5 3.7 %collective-permute-start = (bf16[2,256,768]{2,1,0:T(8,128)(2,1)}, bf16[2,256,768]{2,1,0:T(8,128)(2,1)}, u32[]{:S(2)}, u32[]{:S(2)}) collective-permute-start(bf16[2,256,768]{2,1,0:T(8,128)(2,1)} %bitcast.96), channel_id=1, source_target_pairs={{0,1},{1,2},{2,3},{3,0},{4,5},{5,6},{6,7},{7,4},{8,9},{9,10},{10,1... | collective-permute-start | bytes 2359304 | tf_op jit(solution)/shard_map/ppermute | solution.py:31
  42.4 3.2 %collective-permute-start.1 = (bf16[2,256,768]{2,1,0:T(8,128)(2,1)}, bf16[2,256,768]{2,1,0:T(8,128)(2,1)}, u32[]{:S(2)}, u32[]{:S(2)}) collective-permute-start(bf16[2,256,768]{2,1,0:T(8,128)(2,1)} %bitcast.97), channel_id=1, source_target_pairs={{0,2},{1,3},{2,0},{3,1},{4,6},{5,7},{6,4},{7,5},{8,10},{9,11},{10,... | collective-permute-start | bytes 2359304 | tf_op jit(solution)/shard_map/ppermute | solution.py:31
  52.2 13.2 %all-to-all-done = bf16[2,8,128,1024]{3,2,0,1:T(8,128)(2,1)} async-done(((bf16[2,8,128,1024]{3,2,0,1:T(8,128)(2,1)}), bf16[2,8,128,1024]{3,2,0,1:T(8,128)(2,1)}, u32[]{:S(2)}, u32[]{:S(2)}) %all-to-all-start) | async-done | bytes 4194336 | tf_op jit(solution)/shard_map/all_to_all | solution.py:38
  65.4 2.8 %broadcast_multiply_fusion.4 = (bf16[1,8,128,1024]{3,2,0,1:T(8,128)(2,1)S(1)}, bf16[1,8,128,1024]{3,2,0,1:T(8,128)(2,1)S(1)}, bf16[1,8,128,1024]{3,2,0,1:T(8,128)(2,1)S(1)}, bf16[1,8,128,1024]{3,2,0,1:T(8,128)(2,1)S(1)}) fusion(bf16[1024]{0:T(1024)(128)(2,1)S(1)} %fusion.34, bf16[2,8,128,1024]{3,2,0,1:T(8,128)(2,1)} %all-to-all-done), kind=kLoop, calls=%fused_computation.62 | loop fusion | flops 2097152 | bytes 12584960 | tf_op jit(solution)/shard_map/mul | solution.py:50
  70.5 3.7 %multiply_convert_fusion = bf16[1024,1024]{1,0:T(8,128)(2,1)} fusion(f32[1024,1024]{1,0:T(8,128)S(1)} %fusion.53, f32[1024]{0:T(1024)S(1)} %bitcast.99, bf16[1024,1024]{1,0:T(8,128)(2,1)S(1)} %bitcast.92, bf16[1024,1024]{1,0:T(8,128)(2,1)S(1)} %bitcast.93), kind=kOutput, calls=%fused_computation.39 | convolution fusion | flops 2150629376 | bytes 10489856 | tf_op jit(solution)/shard_map/dot_general | solution.py:50
  74.2 21.0 %collective-permute-done.1 = bf16[2,256,768]{2,1,0:T(8,128)(2,1)} collective-permute-done((bf16[2,256,768]{2,1,0:T(8,128)(2,1)}, bf16[2,256,768]{2,1,0:T(8,128)(2,1)}, u32[]{:S(2)}, u32[]{:S(2)}) %collective-permute-start.1) | collective-permute-done | bytes 786464 | tf_op jit(solution)/shard_map/ppermute | solution.py:31
  95.2 4.5 %reshape.190 = bf16[8,128,4,256]{3,2,1,0:T(4,128)(2,1)} reshape(bf16[1024,1024]{1,0:T(8,128)(2,1)} %multiply_convert_fusion) | data formatting | bytes 4194304 | tf_op jit(solution)/shard_map/reshape | solution.py:67
  99.7 3.3 %copy.35 = bf16[8,128,4,256]{3,1,2,0:T(8,128)(2,1)} copy(bf16[8,128,4,256]{3,2,1,0:T(4,128)(2,1)} %reshape.190) | data formatting | bytes 4194304 | tf_op jit(solution)/shard_map/reshape | solution.py:67
  103.0 22.7 %all-to-all-start.1 = ((bf16[32,128,256]{2,1,0:T(8,128)(2,1)}), bf16[32,128,256]{2,1,0:T(8,128)(2,1)}, u32[]{:S(2)}, u32[]{:S(2)}) async-start(bf16[32,128,256]{2,1,0:T(8,128)(2,1)} %bitcast.86), calls=%async_computation.1 | async-start | bytes 4194304 | tf_op jit(solution)/shard_map/all_to_all | solution.py:68
  127.0 3.2 %pad_maximum_fusion.2 = bf16[2,4,256,768]{3,2,1,0:T(8,128)(2,1)} fusion(bf16[2,1,256,768]{3,2,1,0:T(8,128)(2,1)} %bitcast.28, bf16[2,1,256,768]{3,2,1,0:T(8,128)(2,1)} %bitcast.27, bf16[2,1,256,768]{3,2,1,0:T(8,128)(2,1)} %bitcast.26, bf16[2,1,256,768]{3,2,1,0:T(8,128)(2,1)} %bitcast.91), kind=kLoop, calls=%fused_computation.41 | loop fusion | flops 4718592 | bytes 6291456 | tf_op jit(solution)/shard_map/stack | solution.py:54
  130.3 4.4 %gather_fusion.2 = bf16[4,2,256,768]{3,2,1,0:T(8,128)(2,1)} fusion(bf16[2,4,256,768]{3,2,1,0:T(8,128)(2,1)} %pad_maximum_fusion.2, s32[1024]{0:T(1024)S(1)} %pad_clamp_fusion), kind=kCustom, calls=%fused_computation.2 | custom fusion | bytes 6291472 | tf_op jit(solution)/shard_map/gather | solution.py:54
  137.4 4.5 %fusion.5 = f32[1024,1024]{0,1:T(8,128)S(1)} fusion(bf16[1024,1024]{1,0:T(8,128)(2,1)S(1)} %get-tuple-element.43, bf16[1024,1024]{1,0:T(8,128)(2,1)S(1)} %get-tuple-element.42, bf16[1024,1024]{1,0:T(8,128)(2,1)S(1)} %bitcast.87, bf16[1024,1024]{1,0:T(8,128)(2,1)S(1)} %bitcast.88), kind=kOutput, calls=%fused_computation.25 | convolution fusion | flops 4311744512 | bytes 12582912 | tf_op jit(solution)/shard_map/dot_general | solution.py:63
  144.3 28.8 %all-to-all-done.1 = bf16[32,128,256]{2,1,0:T(8,128)(2,1)} async-done(((bf16[32,128,256]{2,1,0:T(8,128)(2,1)}), bf16[32,128,256]{2,1,0:T(8,128)(2,1)}, u32[]{:S(2)}, u32[]{:S(2)}) %all-to-all-start.1) | async-done | bytes 2097184 | tf_op jit(solution)/shard_map/all_to_all | solution.py:68
  173.1 3.1 %copy.36 = bf16[8,4,128,256]{3,2,0,1:T(8,128)(2,1)} copy(bf16[8,4,128,256]{3,2,1,0:T(8,128)(2,1)} %bitcast.41) | data formatting | bytes 4194304 | tf_op jit(solution)/shard_map/reshape | solution.py:75
  176.2 4.6 %all-to-all-start.2 = ((f32[4,256,768]{1,2,0:T(8,128)}), f32[4,256,768]{1,2,0:T(8,128)}, u32[]{:S(2)}, u32[]{:S(2)}) async-start(f32[4,256,768]{1,2,0:T(8,128)} %pad_maximum_fusion.3), calls=%async_computation.2 | async-start | bytes 6291456 | tf_op jit(solution)/shard_map/all_to_all | solution.py:78
  186.9 2.8 %copy.38 = f32[4,256,8,128]{1,3,2,0:T(8,128)} copy(f32[4,256,8,128]{1,0,3,2:T(4,128)S(1)} %convolution_bitcast_fusion) | data formatting | bytes 8388608 | tf_op jit(solution)/shard_map/gts,gtwi->sigw/transpose | solution.py:81
  189.7 63.3 %all-to-all-done.2 = f32[4,256,768]{1,2,0:T(8,128)} async-done(((f32[4,256,768]{1,2,0:T(8,128)}), f32[4,256,768]{1,2,0:T(8,128)}, u32[]{:S(2)}, u32[]{:S(2)}) %all-to-all-start.2) | async-done | bytes 3145760 | tf_op jit(solution)/shard_map/all_to_all | solution.py:78
  253.0 4.6 %fusion.4 = bf16[4,256,1024]{1,2,0:T(8,128)(2,1)S(1)} fusion(s32[]{:T(128)S(6)} %select_n.140, f32[4,256,768]{1,2,0:T(8,128)} %all-to-all-done.2, f32[4,256,256]{1,2,0:T(8,128)S(1)} %fusion.12, f32[4,256,8,128]{1,3,2,0:T(8,128)} %copy.38), kind=kLoop, calls=%fused_computation.21 | loop fusion | flops 5242880 | bytes 10485764 | tf_op jit(solution)/shard_map/convert_element_type | solution.py:90
  (67 shorter events, 36.9 us)
Async XLA Ops:
  0.0 0.7 copy-start
  10.9 5.3 %copy-start.8 = (s32[1,1024]{1,0:T(1,128)S(1)}, s32[1,1024]{1,0:T(1,128)}, u32[]{:S(2)}) copy-start(s32[1,1024]{1,0:T(1,128)} %param.10) | copy-start | bytes 12292
  10.9 5.3 %copy-start.9 = (f32[1,1024]{1,0:T(1,128)S(1)}, f32[1,1024]{1,0:T(1,128)}, u32[]{:S(2)}) copy-start(f32[1,1024]{1,0:T(1,128)} %param.11) | copy-start | bytes 12292
  10.9 6.0 %copy-start.1 = (bf16[4,256,1024]{2,1,0:T(8,128)(2,1)S(1)}, bf16[4,256,1024]{2,1,0:T(8,128)(2,1)}, u32[]{:S(2)}) copy-start(bf16[4,256,1024]{2,1,0:T(8,128)(2,1)} %param.7) | copy-start | bytes 6291460
  10.9 54.5 %all-to-all-start = ((bf16[2,8,128,1024]{3,2,0,1:T(8,128)(2,1)}), bf16[2,8,128,1024]{3,2,0,1:T(8,128)(2,1)}, u32[]{:S(2)}, u32[]{:S(2)}) async-start(bf16[2,8,128,1024]{3,2,0,1:T(8,128)(2,1)} %bitcast.82), calls=%async_computation | async-start | bytes 8388608 | tf_op jit(solution)/shard_map/all_to_all | solution.py:38
  16.2 35.9 %collective-permute-start.3 = (f32[2,1024]{1,0:T(2,128)S(1)}, f32[2,1024]{1,0:T(2,128)S(1)}, u32[]{:S(2)}, u32[]{:S(2)}) collective-permute-start(f32[2,1024]{1,0:T(2,128)S(1)} %pad_maximum_fusion.5), channel_id=1, source_target_pairs={{0,0},{1,4},{2,8},{3,12},{4,16},{5,20},{6,24},{7,28},{8,1},{9,5},{... | collective-permute-start | bytes 24584 | tf_op jit(solution)/shard_map/ppermute | solution.py:43
  29.9 1.6 copy-start.5
  29.9 1.9 copy-start.6
  36.5 37.7 %collective-permute-start = (bf16[2,256,768]{2,1,0:T(8,128)(2,1)}, bf16[2,256,768]{2,1,0:T(8,128)(2,1)}, u32[]{:S(2)}, u32[]{:S(2)}) collective-permute-start(bf16[2,256,768]{2,1,0:T(8,128)(2,1)} %bitcast.96), channel_id=1, source_target_pairs={{0,1},{1,2},{2,3},{3,0},{4,5},{5,6},{6,7},{7,4},{8,9},{9,10},{10,1... | collective-permute-start | bytes 2359304 | tf_op jit(solution)/shard_map/ppermute | solution.py:31
  42.4 52.8 %collective-permute-start.1 = (bf16[2,256,768]{2,1,0:T(8,128)(2,1)}, bf16[2,256,768]{2,1,0:T(8,128)(2,1)}, u32[]{:S(2)}, u32[]{:S(2)}) collective-permute-start(bf16[2,256,768]{2,1,0:T(8,128)(2,1)} %bitcast.97), channel_id=1, source_target_pairs={{0,2},{1,3},{2,0},{3,1},{4,6},{5,7},{6,4},{7,5},{8,10},{9,11},{10,... | collective-permute-start | bytes 2359304 | tf_op jit(solution)/shard_map/ppermute | solution.py:31
  47.9 47.3 %collective-permute-start.2 = (bf16[2,256,768]{2,1,0:T(8,128)(2,1)}, bf16[2,256,768]{2,1,0:T(8,128)(2,1)}, u32[]{:S(2)}, u32[]{:S(2)}) collective-permute-start(bf16[2,256,768]{2,1,0:T(8,128)(2,1)} %bitcast.98), channel_id=1, source_target_pairs={{0,3},{1,0},{2,1},{3,2},{4,7},{5,4},{6,5},{7,6},{8,11},{9,8},{10,9... | collective-permute-start | bytes 2359304 | tf_op jit(solution)/shard_map/ppermute | solution.py:31
  103.0 22.8 %copy-start.7 = (s32[4,1024]{1,0:T(4,128)S(1)}, s32[4,1024]{1,0:T(4,128)}, u32[]{:S(2)}) copy-start(s32[4,1024]{1,0:T(4,128)} %param.9) | copy-start | bytes 49156
  103.0 22.9 %copy-start.10 = (bf16[2]{0:T(256)(128)(2,1)S(1)}, bf16[2]{0:T(256)(128)(2,1)}, u32[]{:S(2)}) copy-start(bf16[2]{0:T(256)(128)(2,1)} %constant.120.clone) | copy-start | bytes 16
  103.0 70.1 %all-to-all-start.1 = ((bf16[32,128,256]{2,1,0:T(8,128)(2,1)}), bf16[32,128,256]{2,1,0:T(8,128)(2,1)}, u32[]{:S(2)}, u32[]{:S(2)}) async-start(bf16[32,128,256]{2,1,0:T(8,128)(2,1)} %bitcast.86), calls=%async_computation.1 | async-start | bytes 4194304 | tf_op jit(solution)/shard_map/all_to_all | solution.py:68
  130.3 4.4 %copy-start.4 = (bf16[2,4,256,256]{3,2,0,1:T(8,128)(2,1)S(1)}, bf16[2,4,256,256]{3,2,0,1:T(8,128)(2,1)}, u32[]{:S(2)}) copy-start(bf16[2,4,256,256]{3,2,0,1:T(8,128)(2,1)} %fusion.30) | copy-start | bytes 3145732
  176.2 76.8 %all-to-all-start.2 = ((f32[4,256,768]{1,2,0:T(8,128)}), f32[4,256,768]{1,2,0:T(8,128)}, u32[]{:S(2)}, u32[]{:S(2)}) async-start(f32[4,256,768]{1,2,0:T(8,128)} %pad_maximum_fusion.3), calls=%async_computation.2 | async-start | bytes 6291456 | tf_op jit(solution)/shard_map/all_to_all | solution.py:78
  181.0 2.2 copy-start.2
  183.2 2.0 copy-start.3

commit v7 on v6

--- a/solution.py
+++ b/solution.py
@@ -49,7 +49,7 @@
     ph_t = jnp.dot(a_eta * weight, b_gamma, preferred_element_type=f32)
     ph_t = ph_t - jnp.dot(b_gamma * weight, a_eta, preferred_element_type=f32)
     term_t = (ph_t * coef[:, None]).astype(bf16)
-    ladder_in, term_t = lax.optimization_barrier((ladder_in, term_t))
+    ladder_in, _ = lax.optimization_barrier((ladder_in, term_t))
     sources = (level - jnp.arange(n_rows, dtype=jnp.int32)) % n_rows
     whole = jnp.stack(ladder_in, axis=1)[:, sources]
     own = lax.dynamic_index_in_dim(stacked, level, 1, False)
@@ -74,8 +74,12 @@
     )
     landed = landed.reshape(n_chan, n_rows, slab, rows).transpose(1, 0, 2, 3)
     landed = landed.reshape(n_chan, ch_dev, slab, rows)
-    sending, landed = lax.optimization_barrier((sending, landed))
-    ladder = lax.all_to_all(sending, "row", split_axis=0, concat_axis=0, tiled=True)
+    returned = [lax.dynamic_index_in_dim(sending, level, 0, False)]
+    for shift in range(1, n_rows):
+        piece = lax.dynamic_index_in_dim(sending, (level + shift) % n_rows, 0, False)
+        pairs = [(a, (a + shift) % n_rows) for a in range(n_rows)]
+        returned.append(lax.ppermute(piece, "row", pairs))
+    ladder = jnp.stack(returned)[sources]
     chosen = src_slot[:, mine].reshape(n_chan, ch_dev)
     onehot = (chosen[:, :, None] == jnp.arange(ch_dev, dtype=jnp.int32)[None, None, :]).astype(bf16)
     back = jnp.einsum("gts,gtwi->sigw", onehot, landed, preferred_element_type=f32)

time: 261 us -> 262 us (level)
  the two profiles are of different devices: /device:TPU:0 before, /device:TPU:8 now
where the time goes in v7:
time: 262 us; the launch traced here: 261 us
  waiting for transfers between devices  137 us (52%)
  local copies, waits for them, and re-layouts  49 us (19%)
  starting transfers between devices  34.1 us (13%)
  other arithmetic  26.6 us (10%)
  matrix products  14.2 us (5%)
    ppermute x3, waiting for transfers between devices, per_device(): returned.append(lax.ppermute(piece, 'row', pairs))  93.2 us
    ppermute x1, waiting for transfers between devices, per_device(): lax.ppermute(jnp.concatenate([ph_factor.astype(f32), recouple], axis=0),...  40.4 us
    all_to_all x1, starting transfers between devices, per_device(): lax.all_to_all(returning.reshape(n_chan * n_rows, slab, rows), ('ch', 'ro...  17.9 us
    dynamic_slice x4, local copies, waits for them, and re-layouts, per_device(): lax.dynamic_index_in_dim(sending, (level + shift) % n_rows, 1, False)  8.73 us
    unnamed x26, local copies, waits for them, and re-layouts  8.67 us
    reshape x2, local copies, waits for them, and re-layouts, per_device(): returning = term_t.reshape(n_chan, slab, n_rows, rows).transpose(0, 2, 1, 3)  7.8 us
  transfers between devices with their start and end apart: 9, of which 6 were waited for; matrix products, arithmetic and copies ran while one was open for 24% of the time, Pallas kernels for 0%

profile of v7, /device:TPU:8, one launch (start us, length us, event | category | flops | bytes accessed | tf_op | source)
XLA Modules:
  0.0 261.4 jit_solution(9565064490801638166)
XLA Ops:
  1.3 4.6 %pad_maximum_fusion = bf16[2,4,2,128,1024]{4,3,2,1,0:T(8,128)(2,1)} fusion(bf16[1,4,2,128,1024]{4,3,2,1,0:T(8,128)(2,1)} %bitcast.90, bf16[1,4,2,128,1024]{4,3,2,1,0:T(8,128)(2,1)} %bitcast.89), kind=kLoop, calls=%fused_computation.23 | loop fusion | flops 2097152 | bytes 8388608 | tf_op jit(solution)/shard_map/stack | solution.py:23
  6.0 4.9 %gather_fusion.1 = bf16[8,2,128,1024]{3,2,1,0:T(8,128)(2,1)} fusion(bf16[2,4,2,128,1024]{4,3,2,1,0:T(8,128)(2,1)} %pad_maximum_fusion, s32[8]{0:T(128)S(1)} %fusion.48), kind=kCustom, calls=%fused_computation.1 | custom fusion | bytes 8388672 | tf_op jit(solution)/shard_map/gather | solution.py:37
  10.9 4.7 %all-to-all-start = ((bf16[2,8,128,1024]{3,2,0,1:T(8,128)(2,1)}), bf16[2,8,128,1024]{3,2,0,1:T(8,128)(2,1)}, u32[]{:S(2)}, u32[]{:S(2)}) async-start(bf16[2,8,128,1024]{3,2,0,1:T(8,128)(2,1)} %bitcast.91), calls=%async_computation | async-start | bytes 8388608 | tf_op jit(solution)/shard_map/all_to_all | solution.py:38
  15.6 2.6 copy.28
  18.2 4.0 %copy.29 = bf16[4,256,1024]{1,2,0:T(8,128)(2,1)} copy(bf16[4,256,1024]{2,1,0:T(8,128)(2,1)} %param.8) | data formatting | bytes 4194304 | tf_op args[1]
  22.1 3.9 %fusion.23 = (bf16[2,256,1024]{1,2,0:T(8,128)(2,1)}, bf16[2,256,1024]{1,2,0:T(8,128)(2,1)S(1)}, bf16[2,256,1024]{1,2,0:T(8,128)(2,1)S(1)}, bf16[2,256,1024]{1,2,0:T(8,128)(2,1)}, bf16[2,1,256,1024]{2,3,0,1:T(8,128)(2,1)S(1)}) fusion(bf16[1,4,256,1024]{2,3,0,1:T(8,128)(2,1)} %bitcast.93, bf16[1,4,256,1024]{2,3,0,1:T(8,128)(2,1)} %bitcast.94, s32[]{:T(128)S(6)} %select_n.135), kind=kLoop, calls=%fused_computation.51 | loop fusion | flops 2621440 | bytes 9437188 | tf_op jit(solution)/shard_map/squeeze | solution.py:25
  32.7 2.3 copy.31
  36.7 2.4 copy.32
  49.7 40.4 %collective-permute-done.3 = f32[2,1024]{1,0:T(2,128)S(1)} collective-permute-done((f32[2,1024]{1,0:T(2,128)S(1)}, f32[2,1024]{1,0:T(2,128)S(1)}, u32[]{:S(2)}, u32[]{:S(2)}) %collective-permute-start.3) | collective-permute-done | bytes 8224 | tf_op jit(solution)/shard_map/ppermute | solution.py:43
  90.2 2.8 %broadcast_multiply_fusion.4 = (bf16[1,8,128,1024]{3,2,0,1:T(8,128)(2,1)S(1)}, bf16[1,8,128,1024]{3,2,0,1:T(8,128)(2,1)S(1)}, bf16[1,8,128,1024]{3,2,0,1:T(8,128)(2,1)S(1)}, bf16[1,8,128,1024]{3,2,0,1:T(8,128)(2,1)S(1)}) fusion(bf16[1024]{0:T(1024)(128)(2,1)S(1)} %fusion.34, bf16[2,8,128,1024]{3,2,0,1:T(8,128)(2,1)} %all-to-all-done), kind=kLoop, calls=%fused_computation.64 | loop fusion | flops 2097152 | bytes 12584960 | tf_op jit(solution)/shard_map/mul | solution.py:50
  92.9 2.3 fusion.53
  95.3 3.7 %multiply_convert_fusion = bf16[1024,1024]{1,0:T(8,128)(2,1)} fusion(f32[1024,1024]{1,0:T(8,128)S(1)} %fusion.53, f32[1024]{0:T(1024)S(1)} %bitcast.111, bf16[1024,1024]{1,0:T(8,128)(2,1)S(1)} %bitcast.101, bf16[1024,1024]{1,0:T(8,128)(2,1)S(1)} %bitcast.102), kind=kOutput, calls=%fused_computation.40 | convolution fusion | flops 2150629376 | bytes 10489856 | tf_op jit(solution)/shard_map/dot_general | solution.py:50
  98.9 4.5 %reshape.190 = bf16[8,128,4,256]{3,2,1,0:T(4,128)(2,1)} reshape(bf16[1024,1024]{1,0:T(8,128)(2,1)} %multiply_convert_fusion) | data formatting | bytes 4194304 | tf_op jit(solution)/shard_map/reshape | solution.py:67
  107.0 3.3 %copy.35 = bf16[8,128,4,256]{3,1,2,0:T(8,128)(2,1)} copy(bf16[8,128,4,256]{3,2,1,0:T(4,128)(2,1)} %reshape.190) | data formatting | bytes 4194304 | tf_op jit(solution)/shard_map/reshape | solution.py:67
  110.4 17.9 %all-to-all-start.1 = ((bf16[32,128,256]{2,1,0:T(8,128)(2,1)}), bf16[32,128,256]{2,1,0:T(8,128)(2,1)}, u32[]{:S(2)}, u32[]{:S(2)}) async-start(bf16[32,128,256]{2,1,0:T(8,128)(2,1)} %bitcast.95), calls=%async_computation.1 | async-start | bytes 4194304 | tf_op jit(solution)/shard_map/all_to_all | solution.py:68
  128.3 3.1 %pad_maximum_fusion.2 = bf16[2,4,256,768]{3,2,1,0:T(8,128)(2,1)} fusion(bf16[2,1,256,768]{3,2,1,0:T(8,128)(2,1)} %bitcast.28, bf16[2,1,256,768]{3,2,1,0:T(8,128)(2,1)} %bitcast.27, bf16[2,1,256,768]{3,2,1,0:T(8,128)(2,1)} %bitcast.26, bf16[2,1,256,768]{3,2,1,0:T(8,128)(2,1)S(1)} %bitcast.100), kind=kLoop, calls=%fused_computation.42 | loop fusion | flops 4718592 | bytes 6291456 | tf_op jit(solution)/shard_map/stack | solution.py:54
  131.3 4.4 %gather_fusion.2 = bf16[4,2,256,768]{3,2,1,0:T(8,128)(2,1)} fusion(bf16[2,4,256,768]{3,2,1,0:T(8,128)(2,1)} %pad_maximum_fusion.2, s32[1024]{0:T(1024)S(1)} %pad_clamp_fusion), kind=kCustom, calls=%fused_computation.2 | custom fusion | bytes 6291472 | tf_op jit(solution)/shard_map/gather | solution.py:54
  138.4 4.5 %fusion.5 = f32[1024,1024]{0,1:T(8,128)S(1)} fusion(bf16[1024,1024]{1,0:T(8,128)(2,1)S(1)} %get-tuple-element.41, bf16[1024,1024]{1,0:T(8,128)(2,1)S(1)} %get-tuple-element.40, bf16[1024,1024]{1,0:T(8,128)(2,1)S(1)} %bitcast.96, bf16[1024,1024]{1,0:T(8,128)(2,1)S(1)} %bitcast.97), kind=kOutput, calls=%fused_computation.26 | convolution fusion | flops 4311744512 | bytes 12582912 | tf_op jit(solution)/shard_map/dot_general | solution.py:63
  150.6 74.2 %collective-permute-done.4 = f32[256,768]{0,1:T(8,128)S(1)} collective-permute-done((f32[256,768]{0,1:T(8,128)S(1)}, f32[256,768]{0,1:T(8,128)S(1)}, u32[]{:S(2)}, u32[]{:S(2)}) %collective-permute-start.4) | collective-permute-done | bytes 786464 | tf_op jit(solution)/shard_map/ppermute | solution.py:81
  224.8 16.4 %collective-permute-done.5 = f32[256,768]{0,1:T(8,128)S(1)} collective-permute-done((f32[256,768]{0,1:T(8,128)S(1)}, f32[256,768]{0,1:T(8,128)S(1)}, u32[]{:S(2)}, u32[]{:S(2)}) %collective-permute-start.5) | collective-permute-done | bytes 786464 | tf_op jit(solution)/shard_map/ppermute | solution.py:81
  241.2 2.6 collective-permute-done.6
  245.7 4.3 %gather_fusion.3 = f32[4,256,768]{1,2,0:T(8,128)} fusion(f32[4,256,768]{1,2,0:T(8,128)} %pad_maximum_fusion.4, s32[1024]{0:T(1024)S(1)} %pad_clamp_fusion), kind=kCustom, calls=%fused_computation.3 | custom fusion | bytes 6291472 | tf_op jit(solution)/shard_map/gather | solution.py:82
  255.4 3.6 %fusion.4 = bf16[4,256,1024]{1,2,0:T(8,128)(2,1)S(1)} fusion(s32[]{:T(128)S(6)} %select_n.152, f32[4,256,768]{1,2,0:T(8,128)S(1)} %copy-done.4, f32[4,256,256]{1,2,0:T(8,128)S(1)} %fusion.12, f32[4,256,8,128]{1,3,2,0:T(8,128)S(1)} %copy.38), kind=kLoop, calls=%fused_computation.22 | loop fusion | flops 5242880 | bytes 10485764 | tf_op jit(solution)/shard_map/convert_element_type | solution.py:94
  259.0 2.4 copy.39
  (76 shorter events, 41.4 us)
Async XLA Ops:
  0.0 0.7 copy-start
  10.9 4.7 %copy-start.2 = (bf16[4,256,1024]{2,1,0:T(8,128)(2,1)S(1)}, bf16[4,256,1024]{2,1,0:T(8,128)(2,1)}, u32[]{:S(2)}) copy-start(bf16[4,256,1024]{2,1,0:T(8,128)(2,1)} %param.7) | copy-start | bytes 6291460
  10.9 79.2 %all-to-all-start = ((bf16[2,8,128,1024]{3,2,0,1:T(8,128)(2,1)}), bf16[2,8,128,1024]{3,2,0,1:T(8,128)(2,1)}, u32[]{:S(2)}, u32[]{:S(2)}) async-start(bf16[2,8,128,1024]{3,2,0,1:T(8,128)(2,1)} %bitcast.91), calls=%async_computation | async-start | bytes 8388608 | tf_op jit(solution)/shard_map/all_to_all | solution.py:38
  28.5 1.6 copy-start.6
  28.5 1.9 copy-start.7
  32.7 11.8 %copy-start.9 = (s32[1,1024]{1,0:T(1,128)S(1)}, s32[1,1024]{1,0:T(1,128)}, u32[]{:S(2)}) copy-start(s32[1,1024]{1,0:T(1,128)} %param.10) | copy-start | bytes 12292
  32.7 11.8 %copy-start.10 = (f32[1,1024]{1,0:T(1,128)S(1)}, f32[1,1024]{1,0:T(1,128)}, u32[]{:S(2)}) copy-start(f32[1,1024]{1,0:T(1,128)} %param.11) | copy-start | bytes 12292
  32.7 14.1 %copy-start.8 = (s32[4,1024]{1,0:T(4,128)S(1)}, s32[4,1024]{1,0:T(4,128)}, u32[]{:S(2)}) copy-start(s32[4,1024]{1,0:T(4,128)} %param.9) | copy-start | bytes 49156
  32.7 14.2 %copy-start.11 = (bf16[2]{0:T(256)(128)(2,1)S(1)}, bf16[2]{0:T(256)(128)(2,1)}, u32[]{:S(2)}) copy-start(bf16[2]{0:T(256)(128)(2,1)} %constant.136.clone) | copy-start | bytes 16
  35.1 68.4 %collective-permute-start = (bf16[2,256,768]{2,1,0:T(8,128)(2,1)}, bf16[2,256,768]{2,1,0:T(8,128)(2,1)}, u32[]{:S(2)}, u32[]{:S(2)}) collective-permute-start(bf16[2,256,768]{2,1,0:T(8,128)(2,1)} %bitcast.108), channel_id=1, source_target_pairs={{0,1},{1,2},{2,3},{3,0},{4,5},{5,6},{6,7},{7,4},{8,9},{9,10},{10,1... | collective-permute-start | bytes 2359304 | tf_op jit(solution)/shard_map/ppermute | solution.py:31
  39.1 65.8 %collective-permute-start.1 = (bf16[2,256,768]{2,1,0:T(8,128)(2,1)}, bf16[2,256,768]{2,1,0:T(8,128)(2,1)}, u32[]{:S(2)}, u32[]{:S(2)}) collective-permute-start(bf16[2,256,768]{2,1,0:T(8,128)(2,1)} %bitcast.109), channel_id=1, source_target_pairs={{0,2},{1,3},{2,0},{3,1},{4,6},{5,7},{6,4},{7,5},{8,10},{9,11},{10,... | collective-permute-start | bytes 2359304 | tf_op jit(solution)/shard_map/ppermute | solution.py:31
  42.5 64.6 %collective-permute-start.2 = (bf16[2,256,768]{2,1,0:T(8,128)(2,1)}, bf16[2,256,768]{2,1,0:T(8,128)(2,1)}, u32[]{:S(2)}, u32[]{:S(2)}) collective-permute-start(bf16[2,256,768]{2,1,0:T(8,128)(2,1)} %bitcast.110), channel_id=1, source_target_pairs={{0,3},{1,0},{2,1},{3,2},{4,7},{5,4},{6,5},{7,6},{8,11},{9,8},{10,9... | collective-permute-start | bytes 2359304 | tf_op jit(solution)/shard_map/ppermute | solution.py:31
  44.5 45.6 %collective-permute-start.3 = (f32[2,1024]{1,0:T(2,128)S(1)}, f32[2,1024]{1,0:T(2,128)S(1)}, u32[]{:S(2)}, u32[]{:S(2)}) collective-permute-start(f32[2,1024]{1,0:T(2,128)S(1)} %pad_maximum_fusion.6), channel_id=1, source_target_pairs={{0,0},{1,4},{2,8},{3,12},{4,16},{5,20},{6,24},{7,28},{8,1},{9,5},{... | collective-permute-start | bytes 24584 | tf_op jit(solution)/shard_map/ppermute | solution.py:43
  110.4 139.6 %all-to-all-start.1 = ((bf16[32,128,256]{2,1,0:T(8,128)(2,1)}), bf16[32,128,256]{2,1,0:T(8,128)(2,1)}, u32[]{:S(2)}, u32[]{:S(2)}) async-start(bf16[32,128,256]{2,1,0:T(8,128)(2,1)} %bitcast.95), calls=%async_computation.1 | async-start | bytes 4194304 | tf_op jit(solution)/shard_map/all_to_all | solution.py:68
  131.3 4.4 %copy-start.5 = (bf16[2,4,256,256]{3,2,0,1:T(8,128)(2,1)S(1)}, bf16[2,4,256,256]{3,2,0,1:T(8,128)(2,1)}, u32[]{:S(2)}) copy-start(bf16[2,4,256,256]{3,2,0,1:T(8,128)(2,1)} %fusion.30) | copy-start | bytes 3145732
  143.6 4.7 %copy-start.3 = (bf16[4,256,1024]{2,1,0:T(8,128)(2,1)S(1)}, bf16[4,256,1024]{2,1,0:T(8,128)(2,1)}, u32[]{:S(2)}) copy-start(bf16[4,256,1024]{2,1,0:T(8,128)(2,1)} %param.8) | copy-start | bytes 6291460
  143.8 81.0 %collective-permute-start.4 = (f32[256,768]{0,1:T(8,128)S(1)}, f32[256,768]{0,1:T(8,128)S(1)}, u32[]{:S(2)}, u32[]{:S(2)}) collective-permute-start(f32[256,768]{0,1:T(8,128)S(1)} %get-tuple-element.33), channel_id=1, source_target_pairs={{0,1},{1,2},{2,3},{3,0},{4,5},{5,6},{6,7},{7,4},{8,9},{9,10},{10,1... | collective-permute-start | bytes 2359304 | tf_op jit(solution)/shard_map/ppermute | solution.py:81
  145.4 95.9 %collective-permute-start.5 = (f32[256,768]{0,1:T(8,128)S(1)}, f32[256,768]{0,1:T(8,128)S(1)}, u32[]{:S(2)}, u32[]{:S(2)}) collective-permute-start(f32[256,768]{0,1:T(8,128)S(1)} %get-tuple-element.32), channel_id=1, source_target_pairs={{0,2},{1,3},{2,0},{3,1},{4,6},{5,7},{6,4},{7,5},{8,10},{9,11},{10,... | collective-permute-start | bytes 2359304 | tf_op jit(solution)/shard_map/ppermute | solution.py:81
  146.7 97.0 %collective-permute-start.6 = (f32[256,768]{0,1:T(8,128)S(1)}, f32[256,768]{0,1:T(8,128)S(1)}, u32[]{:S(2)}, u32[]{:S(2)}) collective-permute-start(f32[256,768]{0,1:T(8,128)S(1)} %get-tuple-element.31), channel_id=1, source_target_pairs={{0,3},{1,0},{2,1},{3,2},{4,7},{5,4},{6,5},{7,6},{8,11},{9,8},{10,9... | collective-permute-start | bytes 2359304 | tf_op jit(solution)/shard_map/ppermute | solution.py:81
  253.5 1.9 copy-start.4
  255.3 6.0 %copy-start.1 = (s32[32,8]{0,1:T(8,128)S(1)}, s32[32,8]{0,1:T(8,128)}, u32[]{:S(2)}) copy-start(s32[32,8]{0,1:T(8,128)} %param.12) | copy-start | bytes 3076

commit v8 on v7

--- a/solution.py
+++ b/solution.py
@@ -20,15 +20,21 @@
     mine = lax.axis_index("ch")
     level = lax.axis_index("row")
 
+    assert n_rows == 4
     stacked = jnp.stack([eta_pp, gamma_pp])
-    sending = jnp.stack(
-        [skip_block(stacked[:, s], s, rows) for s in range(n_rows)], axis=1
-    )
-    ladder_in = [lax.dynamic_index_in_dim(sending, level, 1, False)]
+    ladder_in = []
     for shift in range(1, n_rows):
-        piece = lax.dynamic_index_in_dim(sending, (level + shift) % n_rows, 1, False)
+        block = lax.dynamic_index_in_dim(stacked, (level + shift) % n_rows, 1, False)
+        d = n_rows - shift
+        hop = (d % (n_rows - 1) + 1 - d) % n_rows
+        own_blk = lax.dynamic_slice_in_dim(block, level * rows, rows, axis=-1)
+        next_blk = lax.dynamic_slice_in_dim(
+            block, ((level + hop) % n_rows) * rows, rows, axis=-1
+        )
         pairs = [(a, (a + shift) % n_rows) for a in range(n_rows)]
-        ladder_in.append(lax.ppermute(piece, "row", pairs))
+        ladder_in.append(
+            lax.ppermute(jnp.concatenate([own_blk, next_blk], axis=-1), "row", pairs)
+        )
     dest = jnp.arange(n_chan, dtype=jnp.int32)
     q_dest = level * n_chan + dest
     slot_dest = src_slot[q_dest, mine]
@@ -50,14 +56,22 @@
     ph_t = ph_t - jnp.dot(b_gamma * weight, a_eta, preferred_element_type=f32)
     term_t = (ph_t * coef[:, None]).astype(bf16)
     ladder_in, _ = lax.optimization_barrier((ladder_in, term_t))
-    sources = (level - jnp.arange(n_rows, dtype=jnp.int32)) % n_rows
-    whole = jnp.stack(ladder_in, axis=1)[:, sources]
+    sign = jnp.array([-1, 1], bf16)[:, None, None]
     own = lax.dynamic_index_in_dim(stacked, level, 1, False)
-    own_t = own.reshape(2, rows, n_rows, rows).transpose(0, 2, 3, 1)
-    own_t = own_t * jnp.array([-1, 1], bf16)[:, None, None, None]
-    whole = jnp.concatenate([whole, own_t], axis=-1).reshape(2, width, width)
+    own = jnp.roll(own, -level * rows, axis=-1)
+    grid = [[None] * n_rows for _ in range(n_rows)]
+    for d in range(n_rows):
+        grid[0][d] = own[..., d * rows : (d + 1) * rows]
+    for d in range(1, n_rows):
+        piece = ladder_in[n_rows - d - 1]
+        succ = d % (n_rows - 1) + 1
+        grid[d][0] = sign * jnp.swapaxes(grid[0][d], -1, -2)
+        grid[d][d] = piece[..., :rows]
+        grid[d][succ] = piece[..., rows:]
+        grid[succ][d] = sign * jnp.swapaxes(piece[..., rows:], -1, -2)
+    whole = jnp.concatenate([jnp.concatenate(line, axis=-1) for line in grid], axis=-2)
     factor = lax.dynamic_index_in_dim(pp_factor, level, 0, False).astype(bf16)
-    factor = jnp.roll(factor, -(level + 1) * rows)
+    factor = jnp.roll(factor, -level * rows)
     left = jnp.concatenate([whole[0] * factor, whole[1] * factor], axis=-1)
     right = jnp.concatenate([whole[1], whole[0]], axis=-1)
     ladder_c = lax.dot_general(
@@ -74,11 +88,11 @@
     )
     landed = landed.reshape(n_chan, n_rows, slab, rows).transpose(1, 0, 2, 3)
     landed = landed.reshape(n_chan, ch_dev, slab, rows)
-    returned = [lax.dynamic_index_in_dim(sending, level, 0, False)]
+    returned = [sending[0]]
     for shift in range(1, n_rows):
-        piece = lax.dynamic_index_in_dim(sending, (level + shift) % n_rows, 0, False)
         pairs = [(a, (a + shift) % n_rows) for a in range(n_rows)]
-        returned.append(lax.ppermute(piece, "row", pairs))
+        returned.append(lax.ppermute(sending[shift], "row", pairs))
+    sources = (level - jnp.arange(n_rows, dtype=jnp.int32)) % n_rows
     ladder = jnp.stack(returned)[sources]
     chosen = src_slot[:, mine].reshape(n_chan, ch_dev)
     onehot = (chosen[:, :, None] == jnp.arange(ch_dev, dtype=jnp.int32)[None, None, :]).astype(bf16)

time: 262 us -> 238 us (0.908)
  local copies, waits for them, and re-layouts: 49 us -> 34.8 us
  starting transfers between devices: 34.1 us -> 25.1 us
  waiting for transfers between devices: 137 us -> 133 us
  other arithmetic: 26.6 us -> 29.7 us
    ppermute x1, waiting for transfers between devices: 40.4 us -> 26.3 us  [per_device(): lax.ppermute(jnp.concatenate([ph_factor.astype(f32), recouple], axis=0),...]
    all_to_all x1, starting transfers between devices: 17.9 us -> 9.04 us  [per_device(): lax.all_to_all(returning.reshape(n_chan * n_rows, slab, rows), ('ch', 'ro...]
    dynamic_slice x6 -> x3, local copies, waits for them, and re-layouts: 10.3 us -> 1.57 us  [the longest x1 1.31 us: per_device(): own = lax.dynamic_index_in_dim(stacked, level, 1, False)]
    unnamed x26 -> x18, local copies, waits for them, and re-layouts: 8.67 us -> 1.78 us
    all_to_all x1, waiting for transfers between devices: 0.01 us -> 6.59 us  [per_device(): lax.all_to_all(outgoing, 'ch', split_axis=1, concat_axis=1, tiled=True)]
    concatenate x2 -> x9, other arithmetic: 2.24 us -> 8.76 us  [the longest x3 2.52 us: per_device(): jnp.concatenate([own_blk, next_blk], axis=-1)]
    another operation x6 -> x0, other arithmetic: 5.37 us -> none  [the longest x1 3.06 us: per_device(): whole = jnp.stack(ladder_in, axis=1)[:, sources]]
    gather x1 -> x0, local copies, waits for them, and re-layouts: 4.4 us -> none  [per_device(): whole = jnp.stack(ladder_in, axis=1)[:, sources]]
  transfers between devices with their start and end apart: 9 -> 9, of which waited for: 6 -> 5; matrix products, arithmetic and copies ran while one was open for 24% -> 17% of each run, Pallas kernels for 0% -> 0%
where the time goes in v8:
time: 238 us
  waiting for transfers between devices  133 us (56%)
  local copies, waits for them, and re-layouts  34.8 us (15%)
  other arithmetic  29.7 us (12%)
  starting transfers between devices  25.1 us (11%)
  matrix products  14.4 us (6%)
    ppermute x3, waiting for transfers between devices, per_device(): returned.append(lax.ppermute(sending[shift], 'row', pairs))  100 us
    ppermute x1, waiting for transfers between devices, per_device(): lax.ppermute(jnp.concatenate([ph_factor.astype(f32), recouple], axis=0),...  26.3 us
    all_to_all x1, starting transfers between devices, per_device(): lax.all_to_all(returning.reshape(n_chan * n_rows, slab, rows), ('ch', 'ro...  9.04 us
    reshape x2, local copies, waits for them, and re-layouts, per_device(): returning = term_t.reshape(n_chan, slab, n_rows, rows).transpose(0, 2, 1, 3)  7.85 us
    all_to_all x1, waiting for transfers between devices, per_device(): lax.all_to_all(outgoing, 'ch', split_axis=1, concat_axis=1, tiled=True)  6.59 us
    another operation x2, other arithmetic, per_device(): stacked = jnp.stack([eta_pp, gamma_pp])  5.75 us
    gather x1, local copies, waits for them, and re-layouts, per_device(): outgoing = five[:, slot_dest, part_dest]  4.95 us
    ppermute x3, starting transfers between devices, per_device(): returned.append(lax.ppermute(sending[shift], 'row', pairs))  4.83 us
  transfers between devices with their start and end apart: 9, of which 5 were waited for; matrix products, arithmetic and copies ran while one was open for 17% of the time, Pallas kernels for 0%

profile of v8, /device:TPU:8, one launch (start us, length us, event | category | flops | bytes accessed | tf_op | source)
XLA Modules:
  0.0 237.6 jit_solution(6702350837329304800)
XLA Ops:
  1.3 4.6 %pad_maximum_fusion = bf16[2,4,2,128,1024]{4,3,2,1,0:T(8,128)(2,1)} fusion(bf16[1,4,2,128,1024]{4,3,2,1,0:T(8,128)(2,1)} %bitcast.79, bf16[1,4,2,128,1024]{4,3,2,1,0:T(8,128)(2,1)} %bitcast.76), kind=kLoop, calls=%fused_computation.26 | loop fusion | flops 2097152 | bytes 8388608 | tf_op jit(solution)/shard_map/stack | solution.py:24
  5.9 4.9 %gather_fusion.1 = bf16[8,2,128,1024]{3,2,1,0:T(8,128)(2,1)} fusion(bf16[2,4,2,128,1024]{4,3,2,1,0:T(8,128)(2,1)} %pad_maximum_fusion, s32[8]{0:T(128)S(1)} %fusion.54), kind=kCustom, calls=%fused_computation.1 | custom fusion | bytes 8388672 | tf_op jit(solution)/shard_map/gather | solution.py:43
  10.9 4.7 %all-to-all-start = ((bf16[2,8,128,1024]{3,2,0,1:T(8,128)(2,1)}), bf16[2,8,128,1024]{3,2,0,1:T(8,128)(2,1)}, u32[]{:S(2)}, u32[]{:S(2)}) async-start(bf16[2,8,128,1024]{3,2,0,1:T(8,128)(2,1)} %bitcast.82), calls=%async_computation | async-start | bytes 8388608 | tf_op jit(solution)/shard_map/all_to_all | solution.py:44
  15.7 2.3 fusion.31
  18.8 2.5 %collective-permute-start.1 = (bf16[2,256,512]{2,1,0:T(8,128)(2,1)}, bf16[2,256,512]{2,1,0:T(8,128)(2,1)}, u32[]{:S(2)}, u32[]{:S(2)}) collective-permute-start(bf16[2,256,512]{2,1,0:T(8,128)(2,1)} %pad_maximum_fusion.6), channel_id=1, source_target_pairs={{0,2},{1,3},{2,0},{3,1},{4,6},{5,7},{6,4},{7,5},{8,10},{9,11},{10,... | collective-permute-start | bytes 1572872 | tf_op jit(solution)/shard_map/ppermute | solution.py:36
  31.8 26.3 %collective-permute-done.3 = f32[2,1024]{1,0:T(2,128)S(1)} collective-permute-done((f32[2,1024]{1,0:T(2,128)S(1)}, f32[2,1024]{1,0:T(2,128)S(1)}, u32[]{:S(2)}, u32[]{:S(2)}) %collective-permute-start.3) | collective-permute-done | bytes 8224 | tf_op jit(solution)/shard_map/ppermute | solution.py:49
  58.1 6.6 %all-to-all-done = bf16[2,8,128,1024]{3,2,0,1:T(8,128)(2,1)} async-done(((bf16[2,8,128,1024]{3,2,0,1:T(8,128)(2,1)}), bf16[2,8,128,1024]{3,2,0,1:T(8,128)(2,1)}, u32[]{:S(2)}, u32[]{:S(2)}) %all-to-all-start) | async-done | bytes 4194336 | tf_op jit(solution)/shard_map/all_to_all | solution.py:44
  64.7 2.8 %broadcast_multiply_fusion.4 = (bf16[1,8,128,1024]{3,2,0,1:T(8,128)(2,1)S(1)}, bf16[1,8,128,1024]{3,2,0,1:T(8,128)(2,1)S(1)}, bf16[1,8,128,1024]{3,2,0,1:T(8,128)(2,1)S(1)}, bf16[1,8,128,1024]{3,2,0,1:T(8,128)(2,1)S(1)}) fusion(bf16[1024]{0:T(1024)(128)(2,1)S(1)} %fusion.40, bf16[2,8,128,1024]{3,2,0,1:T(8,128)(2,1)} %all-to-all-done), kind=kLoop, calls=%fused_computation.57 | loop fusion | flops 2097152 | bytes 12584960 | tf_op jit(solution)/shard_map/mul | solution.py:56
  67.5 2.3 fusion.59
  69.8 3.7 %multiply_convert_fusion = bf16[1024,1024]{1,0:T(8,128)(2,1)} fusion(f32[1024,1024]{1,0:T(8,128)S(1)} %fusion.59, f32[1024]{0:T(1024)S(1)} %bitcast.95, bf16[1024,1024]{1,0:T(8,128)(2,1)S(1)} %bitcast.86, bf16[1024,1024]{1,0:T(8,128)(2,1)S(1)} %bitcast.87), kind=kOutput, calls=%fused_computation.42 | convolution fusion | flops 2150629376 | bytes 10489856 | tf_op jit(solution)/shard_map/dot_general | solution.py:56
  73.5 4.5 %reshape.186 = bf16[8,128,4,256]{3,2,1,0:T(4,128)(2,1)} reshape(bf16[1024,1024]{1,0:T(8,128)(2,1)} %multiply_convert_fusion) | data formatting | bytes 4194304 | tf_op jit(solution)/shard_map/reshape | solution.py:81
  78.0 2.0 copy.20
  84.0 2.2 pad_maximum_fusion.2
  86.2 2.3 copy.23
  92.0 3.3 %copy.24 = bf16[8,128,4,256]{3,1,2,0:T(8,128)(2,1)} copy(bf16[8,128,4,256]{3,2,1,0:T(4,128)(2,1)} %reshape.186) | data formatting | bytes 4194304 | tf_op jit(solution)/shard_map/reshape | solution.py:81
  95.3 9.0 %all-to-all-start.1 = ((bf16[32,128,256]{2,1,0:T(8,128)(2,1)}), bf16[32,128,256]{2,1,0:T(8,128)(2,1)}, u32[]{:S(2)}, u32[]{:S(2)}) async-start(bf16[32,128,256]{2,1,0:T(8,128)(2,1)} %bitcast.83), calls=%async_computation.1 | async-start | bytes 4194304 | tf_op jit(solution)/shard_map/all_to_all | solution.py:82
  104.4 2.1 maximum_maximum_fusion
  107.3 4.7 %fusion.5 = f32[1024,1024]{0,1:T(8,128)S(1)} fusion(bf16[1024,1024]{0,1:T(8,128)(2,1)S(1)} %get-tuple-element.12, bf16[1024,1024]{0,1:T(8,128)(2,1)S(1)} %get-tuple-element.11, bf16[1024,1024]{0,1:T(8,128)(2,1)S(1)} %get-tuple-element.22, bf16[1024,1024]{0,1:T(8,128)(2,1)S(1)} %get-tuple-element.21), kind=kOutput, calls=%fused_computation.28 | convolution fusion | flops 4311744512 | bytes 12582912 | tf_op jit(solution)/shard_map/dot_general | solution.py:77
  119.6 81.3 %collective-permute-done.4 = f32[256,768]{0,1:T(8,128)S(1)} collective-permute-done((f32[256,768]{0,1:T(8,128)S(1)}, f32[256,768]{0,1:T(8,128)S(1)}, u32[]{:S(2)}, u32[]{:S(2)}) %collective-permute-start.4) | collective-permute-done | bytes 786464 | tf_op jit(solution)/shard_map/ppermute | solution.py:94
  201.0 16.4 %collective-permute-done.5 = f32[256,768]{0,1:T(8,128)S(1)} collective-permute-done((f32[256,768]{0,1:T(8,128)S(1)}, f32[256,768]{0,1:T(8,128)S(1)}, u32[]{:S(2)}, u32[]{:S(2)}) %collective-permute-start.5) | collective-permute-done | bytes 786464 | tf_op jit(solution)/shard_map/ppermute | solution.py:94
  217.4 2.6 %collective-permute-done.6 = f32[256,768]{0,1:T(8,128)S(1)} collective-permute-done((f32[256,768]{0,1:T(8,128)S(1)}, f32[256,768]{0,1:T(8,128)S(1)}, u32[]{:S(2)}, u32[]{:S(2)}) %collective-permute-start.6) | collective-permute-done | bytes 786464 | tf_op jit(solution)/shard_map/ppermute | solution.py:94
  221.8 4.3 %gather_fusion.2 = f32[4,256,768]{1,2,0:T(8,128)} fusion(f32[4,256,768]{1,2,0:T(8,128)} %pad_maximum_fusion.1, s32[1024]{0:T(1024)S(1)} %pad_clamp_fusion), kind=kCustom, calls=%fused_computation.2 | custom fusion | bytes 6291472 | tf_op jit(solution)/shard_map/gather | solution.py:96
  231.5 3.6 %fusion.4 = bf16[4,256,1024]{1,2,0:T(8,128)(2,1)S(1)} fusion(s32[]{:T(128)S(6)} %select_n.183, f32[4,256,768]{1,2,0:T(8,128)S(1)} %copy-done.4, f32[4,256,256]{1,2,0:T(8,128)S(1)} %fusion.12, f32[4,256,8,128]{1,3,2,0:T(8,128)S(1)} %copy.27), kind=kLoop, calls=%fused_computation.25 | loop fusion | flops 5242880 | bytes 10485764 | tf_op jit(solution)/shard_map/convert_element_type | solution.py:108
  235.2 2.4 %copy.28 = bf16[4,256,1024]{2,1,0:T(8,128)(2,1)} copy(bf16[4,256,1024]{1,2,0:T(8,128)(2,1)S(1)} %fusion.4) | data formatting | bytes 4194304 | tf_op jit(solution)/shard_map/convert_element_type | solution.py:108
  (67 shorter events, 35.7 us)
Async XLA Ops:
  0.0 0.7 copy-start
  10.9 4.8 %copy-start.2 = (bf16[4,256,1024]{2,1,0:T(8,128)(2,1)S(1)}, bf16[4,256,1024]{2,1,0:T(8,128)(2,1)}, u32[]{:S(2)}) copy-start(bf16[4,256,1024]{2,1,0:T(8,128)(2,1)} %param.7) | copy-start | bytes 6291460
  10.9 53.8 %all-to-all-start = ((bf16[2,8,128,1024]{3,2,0,1:T(8,128)(2,1)}), bf16[2,8,128,1024]{3,2,0,1:T(8,128)(2,1)}, u32[]{:S(2)}, u32[]{:S(2)}) async-start(bf16[2,8,128,1024]{3,2,0,1:T(8,128)(2,1)} %bitcast.82), calls=%async_computation | async-start | bytes 8388608 | tf_op jit(solution)/shard_map/all_to_all | solution.py:44
  15.7 9.7 %copy-start.6 = (s32[1,1024]{1,0:T(1,128)S(1)}, s32[1,1024]{1,0:T(1,128)}, u32[]{:S(2)}) copy-start(s32[1,1024]{1,0:T(1,128)} %param.10) | copy-start | bytes 12292
  15.7 9.7 %copy-start.7 = (f32[1,1024]{1,0:T(1,128)S(1)}, f32[1,1024]{1,0:T(1,128)}, u32[]{:S(2)}) copy-start(f32[1,1024]{1,0:T(1,128)} %param.11) | copy-start | bytes 12292
  18.8 59.2 %collective-permute-start.1 = (bf16[2,256,512]{2,1,0:T(8,128)(2,1)}, bf16[2,256,512]{2,1,0:T(8,128)(2,1)}, u32[]{:S(2)}, u32[]{:S(2)}) collective-permute-start(bf16[2,256,512]{2,1,0:T(8,128)(2,1)} %pad_maximum_fusion.6), channel_id=1, source_target_pairs={{0,2},{1,3},{2,0},{3,1},{4,6},{5,7},{6,4},{7,5},{8,10},{9,11},{10,... | collective-permute-start | bytes 1572872 | tf_op jit(solution)/shard_map/ppermute | solution.py:36
  22.2 55.8 %collective-permute-start.2 = (bf16[2,256,512]{2,1,0:T(8,128)(2,1)}, bf16[2,256,512]{2,1,0:T(8,128)(2,1)}, u32[]{:S(2)}, u32[]{:S(2)}) collective-permute-start(bf16[2,256,512]{2,1,0:T(8,128)(2,1)} %pad_maximum_fusion.7), channel_id=1, source_target_pairs={{0,3},{1,0},{2,1},{3,2},{4,7},{5,4},{6,5},{7,6},{8,11},{9,8},{10,9... | collective-permute-start | bytes 1572872 | tf_op jit(solution)/shard_map/ppermute | solution.py:36
  23.0 6.8 %copy-start.5 = (s32[4,1024]{1,0:T(4,128)S(1)}, s32[4,1024]{1,0:T(4,128)}, u32[]{:S(2)}) copy-start(s32[4,1024]{1,0:T(4,128)} %param.9) | copy-start | bytes 49156
  23.8 54.2 %collective-permute-start = (bf16[2,256,512]{1,2,0:T(8,128)(2,1)}, bf16[2,256,512]{1,2,0:T(8,128)(2,1)}, u32[]{:S(2)}, u32[]{:S(2)}) collective-permute-start(bf16[2,256,512]{1,2,0:T(8,128)(2,1)} %pad_maximum_fusion.5), channel_id=1, source_target_pairs={{0,1},{1,2},{2,3},{3,0},{4,5},{5,6},{6,7},{7,4},{8,9},{9,10},{10,1... | collective-permute-start | bytes 1572872 | tf_op jit(solution)/shard_map/ppermute | solution.py:36
  25.4 32.7 %collective-permute-start.3 = (f32[2,1024]{1,0:T(2,128)S(1)}, f32[2,1024]{1,0:T(2,128)S(1)}, u32[]{:S(2)}, u32[]{:S(2)}) collective-permute-start(f32[2,1024]{1,0:T(2,128)S(1)} %pad_maximum_fusion.8), channel_id=1, source_target_pairs={{0,0},{1,4},{2,8},{3,12},{4,16},{5,20},{6,24},{7,28},{8,1},{9,5},{... | collective-permute-start | bytes 24584 | tf_op jit(solution)/shard_map/ppermute | solution.py:49
  73.5 6.6 %copy-start.8 = (bf16[2]{0:T(256)(128)(2,1)S(1)}, bf16[2]{0:T(256)(128)(2,1)}, u32[]{:S(2)}) copy-start(bf16[2]{0:T(256)(128)(2,1)} %constant.254.clone) | copy-start | bytes 16
  95.3 130.8 %all-to-all-start.1 = ((bf16[32,128,256]{2,1,0:T(8,128)(2,1)}), bf16[32,128,256]{2,1,0:T(8,128)(2,1)}, u32[]{:S(2)}, u32[]{:S(2)}) async-start(bf16[32,128,256]{2,1,0:T(8,128)(2,1)} %bitcast.83), calls=%async_computation.1 | async-start | bytes 4194304 | tf_op jit(solution)/shard_map/all_to_all | solution.py:82
  112.1 5.2 %copy-start.3 = (bf16[4,256,1024]{2,1,0:T(8,128)(2,1)S(1)}, bf16[4,256,1024]{2,1,0:T(8,128)(2,1)}, u32[]{:S(2)}) copy-start(bf16[4,256,1024]{2,1,0:T(8,128)(2,1)} %param.8) | copy-start | bytes 6291460
  112.3 88.7 %collective-permute-start.4 = (f32[256,768]{0,1:T(8,128)S(1)}, f32[256,768]{0,1:T(8,128)S(1)}, u32[]{:S(2)}, u32[]{:S(2)}) collective-permute-start(f32[256,768]{0,1:T(8,128)S(1)} %pad_maximum_fusion.3), channel_id=1, source_target_pairs={{0,1},{1,2},{2,3},{3,0},{4,5},{5,6},{6,7},{7,4},{8,9},{9,10},{10,1... | collective-permute-start | bytes 2359304 | tf_op jit(solution)/shard_map/ppermute | solution.py:94
  113.9 103.5 %collective-permute-start.5 = (f32[256,768]{0,1:T(8,128)S(1)}, f32[256,768]{0,1:T(8,128)S(1)}, u32[]{:S(2)}, u32[]{:S(2)}) collective-permute-start(f32[256,768]{0,1:T(8,128)S(1)} %pad_maximum_fusion.4), channel_id=1, source_target_pairs={{0,2},{1,3},{2,0},{3,1},{4,6},{5,7},{6,4},{7,5},{8,10},{9,11},{10,... | collective-permute-start | bytes 2359304 | tf_op jit(solution)/shard_map/ppermute | solution.py:94
  115.5 104.5 %collective-permute-start.6 = (f32[256,768]{0,1:T(8,128)S(1)}, f32[256,768]{0,1:T(8,128)S(1)}, u32[]{:S(2)}, u32[]{:S(2)}) collective-permute-start(f32[256,768]{0,1:T(8,128)S(1)} %get-tuple-element.16), channel_id=1, source_target_pairs={{0,3},{1,0},{2,1},{3,2},{4,7},{5,4},{6,5},{7,6},{8,11},{9,8},{10,9... | collective-permute-start | bytes 2359304 | tf_op jit(solution)/shard_map/ppermute | solution.py:94
  229.6 1.9 copy-start.4
  231.5 6.0 %copy-start.1 = (s32[32,8]{0,1:T(8,128)S(1)}, s32[32,8]{0,1:T(8,128)}, u32[]{:S(2)}) copy-start(s32[32,8]{0,1:T(8,128)} %param.12) | copy-start | bytes 3076

commit v9 on v8

--- a/solution.py
+++ b/solution.py
@@ -22,6 +22,8 @@
 
     assert n_rows == 4
     stacked = jnp.stack([eta_pp, gamma_pp])
+    upper = jnp.arange(rows)[:, None] < jnp.arange(rows)[None, :]
+    lower = jnp.arange(rows)[:, None] > jnp.arange(rows)[None, :]
     ladder_in = []
     for shift in range(1, n_rows):
         block = lax.dynamic_index_in_dim(stacked, (level + shift) % n_rows, 1, False)
@@ -31,9 +33,10 @@
         next_blk = lax.dynamic_slice_in_dim(
             block, ((level + hop) % n_rows) * rows, rows, axis=-1
         )
+        packed = jnp.where(upper, own_blk[0], own_blk[1])
         pairs = [(a, (a + shift) % n_rows) for a in range(n_rows)]
         ladder_in.append(
-            lax.ppermute(jnp.concatenate([own_blk, next_blk], axis=-1), "row", pairs)
+            lax.ppermute(jnp.concatenate([packed[None], next_blk]), "row", pairs)
         )
     dest = jnp.arange(n_chan, dtype=jnp.int32)
     q_dest = level * n_chan + dest
@@ -66,9 +69,12 @@
         piece = ladder_in[n_rows - d - 1]
         succ = d % (n_rows - 1) + 1
         grid[d][0] = sign * jnp.swapaxes(grid[0][d], -1, -2)
-        grid[d][d] = piece[..., :rows]
-        grid[d][succ] = piece[..., rows:]
-        grid[succ][d] = sign * jnp.swapaxes(piece[..., rows:], -1, -2)
+        packed = piece[0]
+        eta_d = jnp.where(upper, packed, jnp.where(lower, -packed.T, jnp.zeros_like(packed)))
+        gamma_d = jnp.where(lower | upper, jnp.where(upper, packed.T, packed), packed)
+        grid[d][d] = jnp.stack([eta_d, gamma_d])
+        grid[d][succ] = piece[1:]
+        grid[succ][d] = sign * jnp.swapaxes(piece[1:], -1, -2)
     whole = jnp.concatenate([jnp.concatenate(line, axis=-1) for line in grid], axis=-2)
     factor = lax.dynamic_index_in_dim(pp_factor, level, 0, False).astype(bf16)
     factor = jnp.roll(factor, -level * rows)

time: 238 us -> 242 us (1.017)
  waiting for transfers between devices: 133 us -> 109 us
  other arithmetic: 29.7 us -> 47.7 us
  local copies, waits for them, and re-layouts: 34.8 us -> 46.1 us
    ppermute x3, waiting for transfers between devices: 100 us -> 82.2 us  [per_device(): returned.append(lax.ppermute(sending[shift], 'row', pairs))]
    concatenate x1, other arithmetic: 2.15 us -> 18.8 us  [per_device(): jnp.concatenate([jnp.concatenate(line, axis=-1) for line in grid], axis=-2)]
    ppermute x1, waiting for transfers between devices: 26.3 us -> 15.2 us  [per_device(): lax.ppermute(jnp.concatenate([ph_factor.astype(f32), recouple], axis=0),...]
    slice x0 -> x5, local copies, waits for them, and re-layouts: none -> 8.59 us  [the longest x2 3.58 us: per_device(): grid[d][succ] = piece[1:]]
    squeeze x0 -> x4, local copies, waits for them, and re-layouts: none -> 6.46 us  [per_device(): packed = piece[0]]
    all_to_all x1, waiting for transfers between devices: 6.59 us -> 11.9 us  [per_device(): lax.all_to_all(outgoing, 'ch', split_axis=1, concat_axis=1, tiled=True)]
    mul x2 -> x0, other arithmetic: 3.95 us -> none  [the longest x1 2.03 us: per_device(): grid[d][0] = sign * jnp.swapaxes(grid[0][d], -1, -2)]
    mul x2 -> x0, local copies, waits for them, and re-layouts: 3.6 us -> none  [per_device(): grid[d][0] = sign * jnp.swapaxes(grid[0][d], -1, -2)]
  transfers between devices with their start and end apart: 9 -> 9, of which waited for: 5 -> 5; matrix products, arithmetic and copies ran while one was open for 17% -> 26% of each run, Pallas kernels for 0% -> 0%
where the time goes in v9:
time: 242 us; the launch traced here: 241 us
  waiting for transfers between devices  109 us (45%)
  other arithmetic  47.7 us (20%)
  local copies, waits for them, and re-layouts  46.1 us (19%)
  starting transfers between devices  22.9 us (9%)
  matrix products  14.4 us (6%)
    ppermute x3, waiting for transfers between devices, per_device(): returned.append(lax.ppermute(sending[shift], 'row', pairs))  82.2 us
    concatenate x1, other arithmetic, per_device(): jnp.concatenate([jnp.concatenate(line, axis=-1) for line in grid], axis=-2)  18.8 us
    ppermute x1, waiting for transfers between devices, per_device(): lax.ppermute(jnp.concatenate([ph_factor.astype(f32), recouple], axis=0),...  15.2 us
    all_to_all x1, waiting for transfers between devices, per_device(): lax.all_to_all(outgoing, 'ch', split_axis=1, concat_axis=1, tiled=True)  11.9 us
    reshape x2, local copies, waits for them, and re-layouts, per_device(): returning = term_t.reshape(n_chan, slab, n_rows, rows).transpose(0, 2, 1, 3)  7.93 us
    another operation x2, other arithmetic, per_device(): stacked = jnp.stack([eta_pp, gamma_pp])  6.91 us
    squeeze x4, local copies, waits for them, and re-layouts, per_device(): packed = piece[0]  6.46 us
    all_to_all x1, starting transfers between devices, per_device(): lax.all_to_all(returning.reshape(n_chan * n_rows, slab, rows), ('ch', 'ro...  6 us
  transfers between devices with their start and end apart: 9, of which 5 were waited for; matrix products, arithmetic and copies ran while one was open for 26% of the time, Pallas kernels for 0%

profile of v9, /device:TPU:8, one launch (start us, length us, event | category | flops | bytes accessed | tf_op | source)
XLA Modules:
  0.0 240.9 jit_solution(12250166035008499544)
XLA Ops:
  1.3 4.6 %pad_maximum_fusion = bf16[2,4,2,128,1024]{4,3,2,1,0:T(8,128)(2,1)} fusion(bf16[1,4,2,128,1024]{4,3,2,1,0:T(8,128)(2,1)} %bitcast.141, bf16[1,4,2,128,1024]{4,3,2,1,0:T(8,128)(2,1)} %bitcast.138), kind=kLoop, calls=%fused_computation.26 | loop fusion | flops 2097152 | bytes 8388608 | tf_op jit(solution)/shard_map/stack | solution.py:24
  6.0 4.9 %gather_fusion.1 = bf16[8,2,128,1024]{3,2,1,0:T(8,128)(2,1)} fusion(bf16[2,4,2,128,1024]{4,3,2,1,0:T(8,128)(2,1)} %pad_maximum_fusion, s32[8]{0:T(128)S(1)} %fusion.76), kind=kCustom, calls=%fused_computation.1 | custom fusion | bytes 8388672 | tf_op jit(solution)/shard_map/gather | solution.py:46
  10.9 4.7 %all-to-all-start = ((bf16[2,8,128,1024]{3,2,0,1:T(8,128)(2,1)}), bf16[2,8,128,1024]{3,2,0,1:T(8,128)(2,1)}, u32[]{:S(2)}, u32[]{:S(2)}) async-start(bf16[2,8,128,1024]{3,2,0,1:T(8,128)(2,1)} %bitcast.144), calls=%async_computation | async-start | bytes 8388608 | tf_op jit(solution)/shard_map/all_to_all | solution.py:47
  15.7 2.3 fusion.28
  19.7 3.0 %collective-permute-start.1 = (bf16[3,256,256]{2,1,0:T(8,128)(2,1)}, bf16[3,256,256]{2,1,0:T(8,128)(2,1)}, u32[]{:S(2)}, u32[]{:S(2)}) collective-permute-start(bf16[3,256,256]{2,1,0:T(8,128)(2,1)} %pad_maximum_fusion.5), channel_id=1, source_target_pairs={{0,2},{1,3},{2,0},{3,1},{4,6},{5,7},{6,4},{7,5},{8,10},{9,11},{10,... | collective-permute-start | bytes 1179656 | tf_op jit(solution)/shard_map/ppermute | solution.py:39
  23.5 2.5 %collective-permute-start = (bf16[3,256,256]{2,1,0:T(8,128)(2,1)}, bf16[3,256,256]{2,1,0:T(8,128)(2,1)}, u32[]{:S(2)}, u32[]{:S(2)}) collective-permute-start(bf16[3,256,256]{2,1,0:T(8,128)(2,1)} %pad_maximum_fusion.4), channel_id=1, source_target_pairs={{0,1},{1,2},{2,3},{3,0},{4,5},{5,6},{6,7},{7,4},{8,9},{9,10},{10,1... | collective-permute-start | bytes 1179656 | tf_op jit(solution)/shard_map/ppermute | solution.py:39
  35.6 15.2 %collective-permute-done.3 = f32[2,1024]{1,0:T(2,128)} collective-permute-done((f32[2,1024]{1,0:T(2,128)}, f32[2,1024]{1,0:T(2,128)}, u32[]{:S(2)}, u32[]{:S(2)}) %collective-permute-start.3) | collective-permute-done | bytes 8224 | tf_op jit(solution)/shard_map/ppermute | solution.py:52
  52.8 11.9 %all-to-all-done = bf16[2,8,128,1024]{3,2,0,1:T(8,128)(2,1)} async-done(((bf16[2,8,128,1024]{3,2,0,1:T(8,128)(2,1)}), bf16[2,8,128,1024]{3,2,0,1:T(8,128)(2,1)}, u32[]{:S(2)}, u32[]{:S(2)}) %all-to-all-start) | async-done | bytes 4194336 | tf_op jit(solution)/shard_map/all_to_all | solution.py:47
  64.7 2.8 %broadcast_multiply_fusion.4 = (bf16[1,8,128,1024]{3,2,0,1:T(8,128)(2,1)S(1)}, bf16[1,8,128,1024]{3,2,0,1:T(8,128)(2,1)S(1)}, bf16[1,8,128,1024]{3,2,0,1:T(8,128)(2,1)S(1)}, bf16[1,8,128,1024]{3,2,0,1:T(8,128)(2,1)S(1)}) fusion(bf16[1024]{0:T(1024)(128)(2,1)S(1)} %fusion.62, bf16[2,8,128,1024]{3,2,0,1:T(8,128)(2,1)} %all-to-all-done), kind=kLoop, calls=%fused_computation.57 | loop fusion | flops 2097152 | bytes 12584960 | tf_op jit(solution)/shard_map/mul | solution.py:59
  67.5 2.3 fusion.83
  69.9 3.7 %multiply_convert_fusion = bf16[1024,1024]{1,0:T(8,128)(2,1)} fusion(f32[1024,1024]{1,0:T(8,128)S(1)} %fusion.83, f32[1024]{0:T(1024)S(1)} %bitcast.154, bf16[1024,1024]{1,0:T(8,128)(2,1)S(1)} %bitcast.147, bf16[1024,1024]{1,0:T(8,128)(2,1)S(1)} %bitcast.148), kind=kOutput, calls=%fused_computation.42 | convolution fusion | flops 2150629376 | bytes 10489856 | tf_op jit(solution)/shard_map/dot_general | solution.py:59
  73.5 4.5 %reshape.279 = bf16[8,128,4,256]{3,2,1,0:T(4,128)(2,1)} reshape(bf16[1024,1024]{1,0:T(8,128)(2,1)} %multiply_convert_fusion) | data formatting | bytes 4194304 | tf_op jit(solution)/shard_map/reshape | solution.py:87
  87.1 2.4 %fusion.81 = (bf16[2,256,256]{2,1,0:T(8,128)(2,1)}, bf16[2,256,256]{1,2,0:T(8,128)(2,1)}, bf16[2,256,256]{1,2,0:T(8,128)(2,1)}, bf16[2,256,256]{2,1,0:T(8,128)(2...) fusion(bf16[3,256,256]{2,1,0:T(8,128)(2,1)S(1)} %collective-per, ...), kind=kLoop, calls=%fused_computation.162 | loop fusion | flops 786432 | bytes 3932164 | tf_op jit(solution)/shard_map/slice | solution.py:76
  98.2 3.4 %copy.32 = bf16[8,128,4,256]{3,1,2,0:T(8,128)(2,1)} copy(bf16[8,128,4,256]{3,2,1,0:T(4,128)(2,1)} %reshape.279) | data formatting | bytes 4194304 | tf_op jit(solution)/shard_map/reshape | solution.py:87
  101.6 6.0 %all-to-all-start.1 = ((bf16[32,128,256]{2,1,0:T(8,128)(2,1)}), bf16[32,128,256]{2,1,0:T(8,128)(2,1)}, u32[]{:S(2)}, u32[]{:S(2)}) async-start(bf16[32,128,256]{2,1,0:T(8,128)(2,1)} %bitcast.145), calls=%async_computation.1 | async-start | bytes 4194304 | tf_op jit(solution)/shard_map/all_to_all | solution.py:88
  108.9 18.8 %maximum_maximum_fusion = bf16[2,1024,1024]{1,2,0:T(8,128)(2,1)S(1)} fusion(bf16[1,256,256]{1,2,0:T(8,128)(2,1)S(1)} %get-tuple-element.53, bf16[1,256,256]{1,2,0:T(8,128)(2,1)S(1)} %get-tuple-element.54, bf16[2,256,256]{1,2,0:T(8,128)(2,1)} %get-tuple-element.60, bf16[2,256,256]{1,2,0:T(8,128)(2,1)} %copy.30, bf16[2,256,256]{1,2,0:T(8,128)(2,1)} %get-tuple-element.58, ...), kind=kLoop, calls=%fused_computation.27 | loop fusion | flops 67108864 | bytes 8388608 | tf_op jit(solution)/shard_map/concatenate | solution.py:78
  128.7 4.7 %fusion.5 = f32[1024,1024]{0,1:T(8,128)S(1)} fusion(bf16[1024,1024]{0,1:T(8,128)(2,1)S(1)} %get-tuple-element.12, bf16[1024,1024]{0,1:T(8,128)(2,1)S(1)} %get-tuple-element.11, bf16[1024,1024]{0,1:T(8,128)(2,1)S(1)} %get-tuple-element.22, bf16[1024,1024]{0,1:T(8,128)(2,1)S(1)} %get-tuple-element.21), kind=kOutput, calls=%fused_computation.28 | convolution fusion | flops 4311744512 | bytes 12582912 | tf_op jit(solution)/shard_map/dot_general | solution.py:83
  139.0 2.0 fusion.12
  141.0 63.3 %collective-permute-done.4 = f32[256,768]{0,1:T(8,128)S(1)} collective-permute-done((f32[256,768]{0,1:T(8,128)S(1)}, f32[256,768]{0,1:T(8,128)S(1)}, u32[]{:S(2)}, u32[]{:S(2)}) %collective-permute-start.4) | collective-permute-done | bytes 786464 | tf_op jit(solution)/shard_map/ppermute | solution.py:100
  204.2 16.4 %collective-permute-done.5 = f32[256,768]{0,1:T(8,128)S(1)} collective-permute-done((f32[256,768]{0,1:T(8,128)S(1)}, f32[256,768]{0,1:T(8,128)S(1)}, u32[]{:S(2)}, u32[]{:S(2)}) %collective-permute-start.5) | collective-permute-done | bytes 786464 | tf_op jit(solution)/shard_map/ppermute | solution.py:100
  220.6 2.6 %collective-permute-done.6 = f32[256,768]{0,1:T(8,128)S(1)} collective-permute-done((f32[256,768]{0,1:T(8,128)S(1)}, f32[256,768]{0,1:T(8,128)S(1)}, u32[]{:S(2)}, u32[]{:S(2)}) %collective-permute-start.6) | collective-permute-done | bytes 786464 | tf_op jit(solution)/shard_map/ppermute | solution.py:100
  225.1 4.4 %gather_fusion.2 = f32[4,256,768]{1,2,0:T(8,128)} fusion(f32[4,256,768]{1,2,0:T(8,128)} %pad_maximum_fusion.1, s32[1024]{0:T(1024)} %pad_clamp_fusion), kind=kCustom, calls=%fused_computation.2 | custom fusion | bytes 6291472 | tf_op jit(solution)/shard_map/gather | solution.py:102
  234.9 3.6 %fusion.4 = bf16[4,256,1024]{1,2,0:T(8,128)(2,1)S(1)} fusion(s32[]{:T(128)S(6)} %select_n.265, f32[4,256,768]{1,2,0:T(8,128)S(1)} %copy-done.4, f32[4,256,256]{1,2,0:T(8,128)S(1)} %fusion.12, f32[4,256,8,128]{1,3,2,0:T(8,128)S(1)} %copy.35), kind=kLoop, calls=%fused_computation.25 | loop fusion | flops 5242880 | bytes 10485764 | tf_op jit(solution)/shard_map/convert_element_type | solution.py:114
  238.5 2.4 copy.36
  (82 shorter events, 48.1 us)
Async XLA Ops:
  0.0 0.7 copy-start
  10.9 4.8 %copy-start.2 = (bf16[4,256,1024]{2,1,0:T(8,128)(2,1)S(1)}, bf16[4,256,1024]{2,1,0:T(8,128)(2,1)}, u32[]{:S(2)}) copy-start(bf16[4,256,1024]{2,1,0:T(8,128)(2,1)} %param.7) | copy-start | bytes 6291460
  10.9 53.8 %all-to-all-start = ((bf16[2,8,128,1024]{3,2,0,1:T(8,128)(2,1)}), bf16[2,8,128,1024]{3,2,0,1:T(8,128)(2,1)}, u32[]{:S(2)}, u32[]{:S(2)}) async-start(bf16[2,8,128,1024]{3,2,0,1:T(8,128)(2,1)} %bitcast.144), calls=%async_computation | async-start | bytes 8388608 | tf_op jit(solution)/shard_map/all_to_all | solution.py:47
  15.7 10.3 %copy-start.9 = (s32[1,1024]{1,0:T(1,128)S(1)}, s32[1,1024]{1,0:T(1,128)}, u32[]{:S(2)}) copy-start(s32[1,1024]{1,0:T(1,128)} %param.10) | copy-start | bytes 12292
  15.7 10.3 %copy-start.11 = (f32[1,1024]{1,0:T(1,128)S(1)}, f32[1,1024]{1,0:T(1,128)}, u32[]{:S(2)}) copy-start(f32[1,1024]{1,0:T(1,128)} %param.11) | copy-start | bytes 12292
  18.9 59.2 %collective-permute-start.2 = (bf16[3,256,256]{2,1,0:T(8,128)(2,1)}, bf16[3,256,256]{2,1,0:T(8,128)(2,1)S(1)}, u32[]{:S(2)}, u32[]{:S(2)}) collective-permute-start(bf16[3,256,256]{2,1,0:T(8,128)(2,1)} %pad_maximum_fusion.6), channel_id=1, source_target_pairs={{0,3},{1,0},{2,1},{3,2},{4,7},{5,4},{6,5},{7,6},{8,11},{9,8},{10,9... | collective-permute-start | bytes 1179656 | tf_op jit(solution)/shard_map/ppermute | solution.py:39
  19.7 58.3 %collective-permute-start.1 = (bf16[3,256,256]{2,1,0:T(8,128)(2,1)}, bf16[3,256,256]{2,1,0:T(8,128)(2,1)}, u32[]{:S(2)}, u32[]{:S(2)}) collective-permute-start(bf16[3,256,256]{2,1,0:T(8,128)(2,1)} %pad_maximum_fusion.5), channel_id=1, source_target_pairs={{0,2},{1,3},{2,0},{3,1},{4,6},{5,7},{6,4},{7,5},{8,10},{9,11},{10,... | collective-permute-start | bytes 1179656 | tf_op jit(solution)/shard_map/ppermute | solution.py:39
  23.5 54.5 %collective-permute-start = (bf16[3,256,256]{2,1,0:T(8,128)(2,1)}, bf16[3,256,256]{2,1,0:T(8,128)(2,1)}, u32[]{:S(2)}, u32[]{:S(2)}) collective-permute-start(bf16[3,256,256]{2,1,0:T(8,128)(2,1)} %pad_maximum_fusion.4), channel_id=1, source_target_pairs={{0,1},{1,2},{2,3},{3,0},{4,5},{5,6},{6,7},{7,4},{8,9},{9,10},{10,1... | collective-permute-start | bytes 1179656 | tf_op jit(solution)/shard_map/ppermute | solution.py:39
  26.6 24.2 %collective-permute-start.3 = (f32[2,1024]{1,0:T(2,128)}, f32[2,1024]{1,0:T(2,128)}, u32[]{:S(2)}, u32[]{:S(2)}) collective-permute-start(f32[2,1024]{1,0:T(2,128)} %pad_maximum_fusion.7), channel_id=1, source_target_pairs={{0,0},{1,4},{2,8},{3,12},{4,16},{5,20},{6,24},{7,28},{8,1},{9,5},{... | collective-permute-start | bytes 24584 | tf_op jit(solution)/shard_map/ppermute | solution.py:52
  67.5 2.4 copy-start.10
  73.5 13.6 %copy-start.12 = (bf16[2]{0:T(256)(128)(2,1)S(1)}, bf16[2]{0:T(256)(128)(2,1)}, u32[]{:S(2)}) copy-start(bf16[2]{0:T(256)(128)(2,1)} %constant.256.clone) | copy-start | bytes 16
  98.2 10.7 %copy-start.5 = (bf16[2,256,1024]{1,2,0:T(8,128)(2,1)S(1)}, bf16[2,256,1024]{1,2,0:T(8,128)(2,1)}, u32[]{:S(2)}) copy-start(bf16[2,256,1024]{1,2,0:T(8,128)(2,1)} %copy.31) | copy-start | bytes 3145732
  98.2 10.7 %copy-start.6 = (bf16[2,256,256]{1,2,0:T(8,128)(2,1)S(1)}, bf16[2,256,256]{1,2,0:T(8,128)(2,1)}, u32[]{:S(2)}) copy-start(bf16[2,256,256]{1,2,0:T(8,128)(2,1)} %get-tuple-element.41) | copy-start | bytes 786436
  98.2 10.7 %copy-start.7 = (bf16[1,256,256]{1,2,0:T(8,128)(2,1)S(1)}, bf16[1,256,256]{1,2,0:T(8,128)(2,1)}, u32[]{:S(2)}) copy-start(bf16[1,256,256]{1,2,0:T(8,128)(2,1)} %get-tuple-element.34) | copy-start | bytes 393220
  101.6 127.8 %all-to-all-start.1 = ((bf16[32,128,256]{2,1,0:T(8,128)(2,1)}), bf16[32,128,256]{2,1,0:T(8,128)(2,1)}, u32[]{:S(2)}, u32[]{:S(2)}) async-start(bf16[32,128,256]{2,1,0:T(8,128)(2,1)} %bitcast.145), calls=%async_computation.1 | async-start | bytes 4194304 | tf_op jit(solution)/shard_map/all_to_all | solution.py:88
  127.7 0.6 copy-start.8
  133.5 5.2 %copy-start.3 = (bf16[4,256,1024]{2,1,0:T(8,128)(2,1)S(1)}, bf16[4,256,1024]{2,1,0:T(8,128)(2,1)}, u32[]{:S(2)}) copy-start(bf16[4,256,1024]{2,1,0:T(8,128)(2,1)} %param.8) | copy-start | bytes 6291460
  133.6 70.6 %collective-permute-start.4 = (f32[256,768]{0,1:T(8,128)S(1)}, f32[256,768]{0,1:T(8,128)S(1)}, u32[]{:S(2)}, u32[]{:S(2)}) collective-permute-start(f32[256,768]{0,1:T(8,128)S(1)} %pad_maximum_fusion.2), channel_id=1, source_target_pairs={{0,1},{1,2},{2,3},{3,0},{4,5},{5,6},{6,7},{7,4},{8,9},{9,10},{10,1... | collective-permute-start | bytes 2359304 | tf_op jit(solution)/shard_map/ppermute | solution.py:100
  135.2 85.4 %collective-permute-start.5 = (f32[256,768]{0,1:T(8,128)S(1)}, f32[256,768]{0,1:T(8,128)S(1)}, u32[]{:S(2)}, u32[]{:S(2)}) collective-permute-start(f32[256,768]{0,1:T(8,128)S(1)} %pad_maximum_fusion.3), channel_id=1, source_target_pairs={{0,2},{1,3},{2,0},{3,1},{4,6},{5,7},{6,4},{7,5},{8,10},{9,11},{10,... | collective-permute-start | bytes 2359304 | tf_op jit(solution)/shard_map/ppermute | solution.py:100
  136.8 86.4 %collective-permute-start.6 = (f32[256,768]{0,1:T(8,128)S(1)}, f32[256,768]{0,1:T(8,128)S(1)}, u32[]{:S(2)}, u32[]{:S(2)}) collective-permute-start(f32[256,768]{0,1:T(8,128)S(1)} %get-tuple-element.16), channel_id=1, source_target_pairs={{0,3},{1,0},{2,1},{3,2},{4,7},{5,4},{6,5},{7,6},{8,11},{9,8},{10,9... | collective-permute-start | bytes 2359304 | tf_op jit(solution)/shard_map/ppermute | solution.py:100
  233.0 1.9 copy-start.4
  234.9 6.0 %copy-start.1 = (s32[32,8]{0,1:T(8,128)S(1)}, s32[32,8]{0,1:T(8,128)}, u32[]{:S(2)}) copy-start(s32[32,8]{0,1:T(8,128)} %param.12) | copy-start | bytes 3076

commit v10 on v8

--- a/solution.py
+++ b/solution.py
@@ -42,20 +42,7 @@
     five = stacked.reshape(2, ch_dev, rows // slab, slab, width)
     outgoing = five[:, slot_dest, part_dest]
     arrived = lax.all_to_all(outgoing, "ch", split_axis=1, concat_axis=1, tiled=True)
-    a_eta = arrived[0].reshape(width, width)
-    b_gamma = arrived[1].reshape(width, width)
 
-    perm = [(q, (q % n_chan) * n_rows + q // n_chan) for q in range(n_total)]
-    coefs = lax.ppermute(
-        jnp.concatenate([ph_factor.astype(f32), recouple], axis=0), ("ch", "row"), perm
-    )
-    weight = coefs[0].astype(bf16)[None, :]
-    coef = coefs[1]
-
-    ph_t = jnp.dot(a_eta * weight, b_gamma, preferred_element_type=f32)
-    ph_t = ph_t - jnp.dot(b_gamma * weight, a_eta, preferred_element_type=f32)
-    term_t = (ph_t * coef[:, None]).astype(bf16)
-    ladder_in, _ = lax.optimization_barrier((ladder_in, term_t))
     sign = jnp.array([-1, 1], bf16)[:, None, None]
     own = lax.dynamic_index_in_dim(stacked, level, 1, False)
     own = jnp.roll(own, -level * rows, axis=-1)
@@ -78,6 +65,25 @@
         left, right, (((1,), (1,)), ((), ())), preferred_element_type=f32
     ).reshape(n_rows, rows, width)
     sending = jnp.stack([skip_block(ladder_c[a], a, rows) for a in range(n_rows)])
+    sending, arrived = lax.optimization_barrier((sending, arrived))
+    returned = [sending[0]]
+    for shift in range(1, n_rows):
+        pairs = [(a, (a + shift) % n_rows) for a in range(n_rows)]
+        returned.append(lax.ppermute(sending[shift], "row", pairs))
+    sources = (level - jnp.arange(n_rows, dtype=jnp.int32)) % n_rows
+    ladder = jnp.stack(returned)[sources]
+    a_eta = arrived[0].reshape(width, width)
+    b_gamma = arrived[1].reshape(width, width)
+    perm = [(q, (q % n_chan) * n_rows + q // n_chan) for q in range(n_total)]
+    coefs = lax.ppermute(
+        jnp.concatenate([ph_factor.astype(f32), recouple], axis=0), ("ch", "row"), perm
+    )
+    weight = coefs[0].astype(bf16)[None, :]
+    coef = coefs[1]
+
+    ph_t = jnp.dot(a_eta * weight, b_gamma, preferred_element_type=f32)
+    ph_t = ph_t - jnp.dot(b_gamma * weight, a_eta, preferred_element_type=f32)
+    term_t = (ph_t * coef[:, None]).astype(bf16)
     returning = term_t.reshape(n_chan, slab, n_rows, rows).transpose(0, 2, 1, 3)
     landed = lax.all_to_all(
         returning.reshape(n_chan * n_rows, slab, rows),
@@ -88,12 +94,6 @@
     )
     landed = landed.reshape(n_chan, n_rows, slab, rows).transpose(1, 0, 2, 3)
     landed = landed.reshape(n_chan, ch_dev, slab, rows)
-    returned = [sending[0]]
-    for shift in range(1, n_rows):
-        pairs = [(a, (a + shift) % n_rows) for a in range(n_rows)]
-        returned.append(lax.ppermute(sending[shift], "row", pairs))
-    sources = (level - jnp.arange(n_rows, dtype=jnp.int32)) % n_rows
-    ladder = jnp.stack(returned)[sources]
     chosen = src_slot[:, mine].reshape(n_chan, ch_dev)
     onehot = (chosen[:, :, None] == jnp.arange(ch_dev, dtype=jnp.int32)[None, None, :]).astype(bf16)
     back = jnp.einsum("gts,gtwi->sigw", onehot, landed, preferred_element_type=f32)

time: 238 us -> 249 us (1.046)
  starting transfers between devices: 25.1 us -> 42.6 us
  waiting for transfers between devices: 133 us -> 127 us
    all_to_all x1, starting transfers between devices: 9.04 us -> 24.5 us  [per_device(): lax.all_to_all(returning.reshape(n_chan * n_rows, slab, rows), ('ch', 'ro...]
    ppermute x1, waiting for transfers between devices: 26.3 us -> 11.8 us  [per_device(): lax.ppermute(jnp.concatenate([ph_factor.astype(f32), recouple], axis=0),...]
    ppermute x3, waiting for transfers between devices: 0.01 us -> 8.71 us  [per_device(): lax.ppermute(jnp.concatenate([own_blk, next_blk], axis=-1), 'row', pairs)]
    all_to_all x1, waiting for transfers between devices: 6.59 us -> 0.01 us  [per_device(): lax.all_to_all(outgoing, 'ch', split_axis=1, concat_axis=1, tiled=True)]
    ppermute x3, waiting for transfers between devices: 100 us -> 106 us  [per_device(): returned.append(lax.ppermute(sending[shift], 'row', pairs))]
  transfers between devices with their start and end apart: 9 -> 9, of which waited for: 5 -> 5; matrix products, arithmetic and copies ran while one was open for 17% -> 19% of each run, Pallas kernels for 0% -> 0%
where the time goes in v10:
time: 249 us; the launch traced here: 248 us
  waiting for transfers between devices  127 us (51%)
  starting transfers between devices  42.6 us (17%)
  local copies, waits for them, and re-layouts  34.7 us (14%)
  other arithmetic  29.4 us (12%)
  matrix products  14.2 us (6%)
    ppermute x3, waiting for transfers between devices, per_device(): returned.append(lax.ppermute(sending[shift], 'row', pairs))  106 us
    all_to_all x1, starting transfers between devices, per_device(): lax.all_to_all(returning.reshape(n_chan * n_rows, slab, rows), ('ch', 'ro...  24.5 us
    ppermute x1, waiting for transfers between devices, per_device(): lax.ppermute(jnp.concatenate([ph_factor.astype(f32), recouple], axis=0),...  11.8 us
    ppermute x3, waiting for transfers between devices, per_device(): lax.ppermute(jnp.concatenate([own_blk, next_blk], axis=-1), 'row', pairs)  8.71 us
    reshape x2, local copies, waits for them, and re-layouts, per_device(): returning = term_t.reshape(n_chan, slab, n_rows, rows).transpose(0, 2, 1, 3)  7.83 us
    another operation x2, other arithmetic, per_device(): stacked = jnp.stack([eta_pp, gamma_pp])  6.73 us
  transfers between devices with their start and end apart: 9, of which 5 were waited for; matrix products, arithmetic and copies ran while one was open for 19% of the time, Pallas kernels for 0%

profile of v10, /device:TPU:8, one launch (start us, length us, event | category | flops | bytes accessed | tf_op | source)
XLA Modules:
  0.0 248.1 jit_solution(4453422994160022759)
XLA Ops:
  0.0 2.8 %fusion.24 = (bf16[2,1,256,256]{3,2,0,1:T(8,128)(2,1)S(1)}, bf16[2,256,256]{2,1,0:T(8,128)(2,1)S(1)}, bf16[2,256,256]{2,1,0:T(8,128)(2,1)S(1)}, bf16[2,256,256]{...) fusion(s32[]{:T(128)S(6)} %select_n.162, s32[]{:T(128)S(6)} %select_n.164, ...), kind=kLoop, calls=%fused_computation.72 | loop fusion | flops 3145728 | bytes 5767192 | tf_op jit(solution)/shard_map/stack | solution.py:24
  3.6 2.5 %collective-permute-start.2 = (bf16[2,256,512]{2,1,0:T(8,128)(2,1)}, bf16[2,256,512]{2,1,0:T(8,128)(2,1)}, u32[]{:S(2)}, u32[]{:S(2)}) collective-permute-start(bf16[2,256,512]{2,1,0:T(8,128)(2,1)} %pad_maximum_fusion.6), channel_id=1, source_target_pairs={{0,2},{1,3},{2,0},{3,1},{4,6},{5,7},{6,4},{7,5},{8,10},{9,11},{10,... | collective-permute-start | bytes 1572872 | tf_op jit(solution)/shard_map/ppermute | solution.py:36
  10.8 4.0 %pad_maximum_fusion = bf16[2,4,2,128,1024]{4,3,2,1,0:T(8,128)(2,1)} fusion(bf16[1,4,2,128,1024]{4,3,2,1,0:T(8,128)(2,1)} %bitcast.93, bf16[1,4,2,128,1024]{4,3,2,1,0:T(8,128)(2,1)S(1)} %bitcast.90), kind=kLoop, calls=%fused_computation.34 | loop fusion | flops 2097152 | bytes 8388608 | tf_op jit(solution)/shard_map/stack | solution.py:24
  14.7 4.9 %gather_fusion.1 = bf16[8,2,128,1024]{3,2,1,0:T(8,128)(2,1)} fusion(bf16[2,4,2,128,1024]{4,3,2,1,0:T(8,128)(2,1)} %pad_maximum_fusion, s32[8]{0:T(128)S(1)} %fusion.56), kind=kCustom, calls=%fused_computation.1 | custom fusion | bytes 8388672 | tf_op jit(solution)/shard_map/gather | solution.py:43
  19.7 4.7 %all-to-all-start = ((bf16[2,8,128,1024]{3,2,0,1:T(8,128)(2,1)}), bf16[2,8,128,1024]{3,2,0,1:T(8,128)(2,1)}, u32[]{:S(2)}, u32[]{:S(2)}) async-start(bf16[2,8,128,1024]{3,2,0,1:T(8,128)(2,1)} %bitcast.95), calls=%async_computation | async-start | bytes 8388608 | tf_op jit(solution)/shard_map/all_to_all | solution.py:44
  24.5 4.3 %collective-permute-start.6 = (f32[2,1024]{1,0:T(2,128)S(1)}, f32[2,1024]{1,0:T(2,128)S(1)}, u32[]{:S(2)}, u32[]{:S(2)}) collective-permute-start(f32[2,1024]{1,0:T(2,128)S(1)} %pad_maximum_fusion.7), channel_id=1, source_target_pairs={{0,0},{1,4},{2,8},{3,12},{4,16},{5,20},{6,24},{7,28},{8,1},{9,5},{... | collective-permute-start | bytes 24584 | tf_op jit(solution)/shard_map/ppermute | solution.py:78
  30.7 11.8 %collective-permute-done.6 = f32[2,1024]{1,0:T(2,128)S(1)} collective-permute-done((f32[2,1024]{1,0:T(2,128)S(1)}, f32[2,1024]{1,0:T(2,128)S(1)}, u32[]{:S(2)}, u32[]{:S(2)}) %collective-permute-start.6) | collective-permute-done | bytes 8224 | tf_op jit(solution)/shard_map/ppermute | solution.py:78
  42.6 8.7 %collective-permute-done.1 = bf16[2,256,512]{2,1,0:T(8,128)(2,1)} collective-permute-done((bf16[2,256,512]{2,1,0:T(8,128)(2,1)}, bf16[2,256,512]{2,1,0:T(8,128)(2,1)}, u32[]{:S(2)}, u32[]{:S(2)}) %collective-permute-start.1) | collective-permute-done | bytes 524320 | tf_op jit(solution)/shard_map/ppermute | solution.py:36
  51.3 2.2 fusion.32
  53.5 2.1 pad_maximum_fusion.3
  55.5 2.3 copy.23
  67.1 4.5 %fusion.5 = f32[1024,1024]{0,1:T(8,128)S(1)} fusion(bf16[1024,1024]{1,0:T(8,128)(2,1)S(1)} %get-tuple-element.12, bf16[1024,1024]{1,0:T(8,128)(2,1)S(1)} %get-tuple-element.11, bf16[1024,1024]{1,0:T(8,128)(2,1)S(1)} %get-tuple-element.22, bf16[1024,1024]{1,0:T(8,128)(2,1)S(1)} %get-tuple-element.21), kind=kOutput, calls=%fused_computation.27 | convolution fusion | flops 4311744512 | bytes 12582912 | tf_op jit(solution)/shard_map/dot_general | solution.py:64
  73.9 2.8 %broadcast_multiply_fusion = (bf16[1,8,128,1024]{3,2,0,1:T(8,128)(2,1)S(1)}, bf16[1,8,128,1024]{3,2,0,1:T(8,128)(2,1)S(1)}, bf16[1,8,128,1024]{3,2,0,1:T(8,128)(2,1)S(1)}, bf16[1,8,128,1024]{3,2,0,1:T(8,128)(2,1)S(1)}) fusion(bf16[1024]{0:T(1024)(128)(2,1)S(1)} %fusion.42, bf16[2,8,128,1024]{3,2,0,1:T(8,128)(2,1)} %all-to-all-done), kind=kLoop, calls=%fused_computation.55 | loop fusion | flops 2097152 | bytes 12584960 | tf_op jit(solution)/shard_map/mul | solution.py:85
  76.7 2.3 fusion.62
  79.0 3.7 %multiply_convert_fusion = bf16[1024,1024]{1,0:T(8,128)(2,1)} fusion(f32[1024,1024]{1,0:T(8,128)S(1)} %fusion.62, f32[1024]{0:T(1024)S(1)} %bitcast.107, bf16[1024,1024]{1,0:T(8,128)(2,1)S(1)} %bitcast.98, bf16[1024,1024]{1,0:T(8,128)(2,1)S(1)} %bitcast.99), kind=kOutput, calls=%fused_computation.42 | convolution fusion | flops 2150629376 | bytes 10489856 | tf_op jit(solution)/shard_map/dot_general | solution.py:85
  82.7 4.5 %reshape.186 = bf16[8,128,4,256]{3,2,1,0:T(4,128)(2,1)} reshape(bf16[1024,1024]{1,0:T(8,128)(2,1)} %multiply_convert_fusion) | data formatting | bytes 4194304 | tf_op jit(solution)/shard_map/reshape | solution.py:87
  87.2 3.3 %copy.24 = bf16[8,128,4,256]{3,1,2,0:T(8,128)(2,1)} copy(bf16[8,128,4,256]{3,2,1,0:T(4,128)(2,1)} %reshape.186) | data formatting | bytes 4194304 | tf_op jit(solution)/shard_map/reshape | solution.py:87
  90.5 24.5 %all-to-all-start.1 = ((bf16[32,128,256]{2,1,0:T(8,128)(2,1)}), bf16[32,128,256]{2,1,0:T(8,128)(2,1)}, u32[]{:S(2)}, u32[]{:S(2)}) async-start(bf16[32,128,256]{2,1,0:T(8,128)(2,1)} %bitcast.96), calls=%async_computation.1 | async-start | bytes 4194304 | tf_op jit(solution)/shard_map/all_to_all | solution.py:88
  115.2 2.2 fusion.61
  124.2 87.8 %collective-permute-done.3 = f32[256,768]{0,1:T(8,128)S(1)} collective-permute-done((f32[256,768]{0,1:T(8,128)S(1)}, f32[256,768]{0,1:T(8,128)S(1)}, u32[]{:S(2)}, u32[]{:S(2)}) %collective-permute-start.3) | collective-permute-done | bytes 786464 | tf_op jit(solution)/shard_map/ppermute | solution.py:72
  212.0 16.7 %collective-permute-done.4 = f32[256,768]{0,1:T(8,128)S(1)} collective-permute-done((f32[256,768]{0,1:T(8,128)S(1)}, f32[256,768]{0,1:T(8,128)S(1)}, u32[]{:S(2)}, u32[]{:S(2)}) %collective-permute-start.4) | collective-permute-done | bytes 786464 | tf_op jit(solution)/shard_map/ppermute | solution.py:72
  232.4 4.3 %gather_fusion.2 = f32[4,256,768]{1,2,0:T(8,128)} fusion(f32[4,256,768]{1,2,0:T(8,128)} %pad_maximum_fusion.2, s32[1024]{0:T(1024)S(1)} %pad_clamp_fusion), kind=kCustom, calls=%fused_computation.2 | custom fusion | bytes 6291472 | tf_op jit(solution)/shard_map/gather | solution.py:74
  242.1 3.6 %fusion.4 = bf16[4,256,1024]{1,2,0:T(8,128)(2,1)S(1)} fusion(s32[]{:T(128)S(6)} %select_n.183, f32[4,256,768]{1,2,0:T(8,128)S(1)} %copy-done.3, f32[4,256,256]{1,2,0:T(8,128)S(1)} %fusion.12, f32[4,256,8,128]{1,3,2,0:T(8,128)S(1)} %copy.27), kind=kLoop, calls=%fused_computation.25 | loop fusion | flops 5242880 | bytes 10485764 | tf_op jit(solution)/shard_map/convert_element_type | solution.py:108
  245.7 2.4 copy.28
  (65 shorter events, 34.8 us)
Async XLA Ops:
  0.0 10.1 %copy-start = (s32[32,8]{0,1:T(8,128)S(1)}, s32[32,8]{0,1:T(8,128)}, u32[]{:S(2)}) copy-start(s32[32,8]{0,1:T(8,128)} %param.12) | copy-start | bytes 3076
  0.0 10.8 %copy-start.1 = (bf16[4,256,1024]{2,1,0:T(8,128)(2,1)S(1)}, bf16[4,256,1024]{2,1,0:T(8,128)(2,1)}, u32[]{:S(2)}) copy-start(bf16[4,256,1024]{2,1,0:T(8,128)(2,1)} %param.7) | copy-start | bytes 6291460
  3.6 39.0 %collective-permute-start.2 = (bf16[2,256,512]{2,1,0:T(8,128)(2,1)}, bf16[2,256,512]{2,1,0:T(8,128)(2,1)}, u32[]{:S(2)}, u32[]{:S(2)}) collective-permute-start(bf16[2,256,512]{2,1,0:T(8,128)(2,1)} %pad_maximum_fusion.6), channel_id=1, source_target_pairs={{0,2},{1,3},{2,0},{3,1},{4,6},{5,7},{6,4},{7,5},{8,10},{9,11},{10,... | collective-permute-start | bytes 1572872 | tf_op jit(solution)/shard_map/ppermute | solution.py:36
  6.9 44.3 %collective-permute-start.1 = (bf16[2,256,512]{2,1,0:T(8,128)(2,1)}, bf16[2,256,512]{2,1,0:T(8,128)(2,1)}, u32[]{:S(2)}, u32[]{:S(2)}) collective-permute-start(bf16[2,256,512]{2,1,0:T(8,128)(2,1)} %pad_maximum_fusion.5), channel_id=1, source_target_pairs={{0,1},{1,2},{2,3},{3,0},{4,5},{5,6},{6,7},{7,4},{8,9},{9,10},{10,1... | collective-permute-start | bytes 1572872 | tf_op jit(solution)/shard_map/ppermute | solution.py:36
  8.1 45.4 %collective-permute-start = (bf16[2,256,512]{1,2,0:T(8,128)(2,1)}, bf16[2,256,512]{1,2,0:T(8,128)(2,1)}, u32[]{:S(2)}, u32[]{:S(2)}) collective-permute-start(bf16[2,256,512]{1,2,0:T(8,128)(2,1)} %pad_maximum_fusion.4), channel_id=1, source_target_pairs={{0,3},{1,0},{2,1},{3,2},{4,7},{5,4},{6,5},{7,6},{8,11},{9,8},{10,9... | collective-permute-start | bytes 1572872 | tf_op jit(solution)/shard_map/ppermute | solution.py:36
  19.7 4.7 %copy-start.5 = (s32[1,1024]{1,0:T(1,128)S(1)}, s32[1,1024]{1,0:T(1,128)}, u32[]{:S(2)}) copy-start(s32[1,1024]{1,0:T(1,128)} %param.10) | copy-start | bytes 12292
  19.7 4.8 %copy-start.6 = (f32[1,1024]{1,0:T(1,128)S(1)}, f32[1,1024]{1,0:T(1,128)}, u32[]{:S(2)}) copy-start(f32[1,1024]{1,0:T(1,128)} %param.11) | copy-start | bytes 12292
  19.7 54.2 %all-to-all-start = ((bf16[2,8,128,1024]{3,2,0,1:T(8,128)(2,1)}), bf16[2,8,128,1024]{3,2,0,1:T(8,128)(2,1)}, u32[]{:S(2)}, u32[]{:S(2)}) async-start(bf16[2,8,128,1024]{3,2,0,1:T(8,128)(2,1)} %bitcast.95), calls=%async_computation | async-start | bytes 8388608 | tf_op jit(solution)/shard_map/all_to_all | solution.py:44
  24.4 6.2 %copy-start.4 = (s32[4,1024]{1,0:T(4,128)S(1)}, s32[4,1024]{1,0:T(4,128)}, u32[]{:S(2)}) copy-start(s32[4,1024]{1,0:T(4,128)} %param.9) | copy-start | bytes 49156
  24.4 26.9 %copy-start.7 = (bf16[2]{0:T(256)(128)(2,1)S(1)}, bf16[2]{0:T(256)(128)(2,1)}, u32[]{:S(2)}) copy-start(bf16[2]{0:T(256)(128)(2,1)} %constant.254.clone) | copy-start | bytes 16
  24.5 18.1 %collective-permute-start.6 = (f32[2,1024]{1,0:T(2,128)S(1)}, f32[2,1024]{1,0:T(2,128)S(1)}, u32[]{:S(2)}, u32[]{:S(2)}) collective-permute-start(f32[2,1024]{1,0:T(2,128)S(1)} %pad_maximum_fusion.7), channel_id=1, source_target_pairs={{0,0},{1,4},{2,8},{3,12},{4,16},{5,20},{6,24},{7,28},{8,1},{9,5},{... | collective-permute-start | bytes 24584 | tf_op jit(solution)/shard_map/ppermute | solution.py:78
  90.5 146.1 %all-to-all-start.1 = ((bf16[32,128,256]{2,1,0:T(8,128)(2,1)}), bf16[32,128,256]{2,1,0:T(8,128)(2,1)}, u32[]{:S(2)}, u32[]{:S(2)}) async-start(bf16[32,128,256]{2,1,0:T(8,128)(2,1)} %bitcast.96), calls=%async_computation.1 | async-start | bytes 4194304 | tf_op jit(solution)/shard_map/all_to_all | solution.py:88
  115.2 6.7 %copy-start.2 = (bf16[4,256,1024]{2,1,0:T(8,128)(2,1)S(1)}, bf16[4,256,1024]{2,1,0:T(8,128)(2,1)}, u32[]{:S(2)}) copy-start(bf16[4,256,1024]{2,1,0:T(8,128)(2,1)} %param.8) | copy-start | bytes 6291460
  117.4 94.6 %collective-permute-start.3 = (f32[256,768]{0,1:T(8,128)S(1)}, f32[256,768]{0,1:T(8,128)S(1)}, u32[]{:S(2)}, u32[]{:S(2)}) collective-permute-start(f32[256,768]{0,1:T(8,128)S(1)} %get-tuple-element.32), channel_id=1, source_target_pairs={{0,1},{1,2},{2,3},{3,0},{4,5},{5,6},{6,7},{7,4},{8,9},{9,10},{10,1... | collective-permute-start | bytes 2359304 | tf_op jit(solution)/shard_map/ppermute | solution.py:72
  118.9 109.8 %collective-permute-start.4 = (f32[256,768]{0,1:T(8,128)S(1)}, f32[256,768]{0,1:T(8,128)S(1)}, u32[]{:S(2)}, u32[]{:S(2)}) collective-permute-start(f32[256,768]{0,1:T(8,128)S(1)} %get-tuple-element.31), channel_id=1, source_target_pairs={{0,2},{1,3},{2,0},{3,1},{4,6},{5,7},{6,4},{7,5},{8,10},{9,11},{10,... | collective-permute-start | bytes 2359304 | tf_op jit(solution)/shard_map/ppermute | solution.py:72
  120.4 110.2 %collective-permute-start.5 = (f32[256,768]{0,1:T(8,128)S(1)}, f32[256,768]{0,1:T(8,128)S(1)}, u32[]{:S(2)}, u32[]{:S(2)}) collective-permute-start(f32[256,768]{0,1:T(8,128)S(1)} %get-tuple-element.30), channel_id=1, source_target_pairs={{0,3},{1,0},{2,1},{3,2},{4,7},{5,4},{6,5},{7,6},{8,11},{9,8},{10,9... | collective-permute-start | bytes 2359304 | tf_op jit(solution)/shard_map/ppermute | solution.py:72
  240.2 1.9 copy-start.3

commit v11 on v8

--- a/solution.py
+++ b/solution.py
@@ -21,10 +21,10 @@
     level = lax.axis_index("row")
 
     assert n_rows == 4
-    stacked = jnp.stack([eta_pp, gamma_pp])
+    pair = lambda f: jnp.stack([f(eta_pp), f(gamma_pp)])
     ladder_in = []
     for shift in range(1, n_rows):
-        block = lax.dynamic_index_in_dim(stacked, (level + shift) % n_rows, 1, False)
+        block = pair(lambda x: lax.dynamic_index_in_dim(x, (level + shift) % n_rows, 0, False))
         d = n_rows - shift
         hop = (d % (n_rows - 1) + 1 - d) % n_rows
         own_blk = lax.dynamic_slice_in_dim(block, level * rows, rows, axis=-1)
@@ -39,8 +39,7 @@
     q_dest = level * n_chan + dest
     slot_dest = src_slot[q_dest, mine]
     part_dest = q_dest // ch_dev - level * (rows // slab)
-    five = stacked.reshape(2, ch_dev, rows // slab, slab, width)
-    outgoing = five[:, slot_dest, part_dest]
+    outgoing = pair(lambda x: x.reshape(ch_dev, rows // slab, slab, width)[slot_dest, part_dest])
     arrived = lax.all_to_all(outgoing, "ch", split_axis=1, concat_axis=1, tiled=True)
     a_eta = arrived[0].reshape(width, width)
     b_gamma = arrived[1].reshape(width, width)
@@ -57,7 +56,7 @@
     term_t = (ph_t * coef[:, None]).astype(bf16)
     ladder_in, _ = lax.optimization_barrier((ladder_in, term_t))
     sign = jnp.array([-1, 1], bf16)[:, None, None]
-    own = lax.dynamic_index_in_dim(stacked, level, 1, False)
+    own = pair(lambda x: lax.dynamic_index_in_dim(x, level, 0, False))
     own = jnp.roll(own, -level * rows, axis=-1)
     grid = [[None] * n_rows for _ in range(n_rows)]
     for d in range(n_rows):

time: 238 us -> 230 us (0.966)
  other arithmetic: 29.7 us -> 24.4 us
  local copies, waits for them, and re-layouts: 34.8 us -> 40 us
  waiting for transfers between devices: 133 us -> 128 us
  starting transfers between devices: 25.1 us -> 22.2 us
    ppermute x1, waiting for transfers between devices: 26.3 us -> 0.01 us  [per_device(): lax.ppermute(jnp.concatenate([ph_factor.astype(f32), recouple], axis=0),...]
    all_to_all x1, waiting for transfers between devices: 6.59 us -> 27.8 us  [per_device(): lax.all_to_all(outgoing, 'ch', split_axis=1, concat_axis=1, tiled=True)]
    slice x0 -> x4, local copies, waits for them, and re-layouts: none -> 5.4 us  [the longest x2 1.81 us: per_device(): grid[d][succ] = piece[..., rows:]]
    all_to_all x1, starting transfers between devices: 9.04 us -> 4.58 us  [per_device(): lax.all_to_all(returning.reshape(n_chan * n_rows, slab, rows), ('ch', 'ro...]
    dynamic_slice x3, local copies, waits for them, and re-layouts: 1.57 us -> 5.19 us  [the longest x2 3.81 us: per_device(): own = pair(lambda x: lax.dynamic_index_in_dim(x, level, 0, False))]
    mul x2 -> x0, local copies, waits for them, and re-layouts: 3.6 us -> none  [per_device(): grid[d][0] = sign * jnp.swapaxes(grid[0][d], -1, -2)]
    gather x1 -> x2, local copies, waits for them, and re-layouts: 4.95 us -> 5.62 us  [per_device(): x.reshape(ch_dev, rows // slab, slab, width)[slot_dest, part_dest]]
    another operation x2 -> x3, other arithmetic: 5.75 us -> 5.43 us  [per_device(): pair = lambda f: jnp.stack([f(eta_pp), f(gamma_pp)])]
  transfers between devices with their start and end apart: 9 -> 9, of which waited for: 5 -> 4; matrix products, arithmetic and copies ran while one was open for 17% -> 19% of each run, Pallas kernels for 0% -> 0%
where the time goes in v11:
time: 230 us
  waiting for transfers between devices  128 us (56%)
  local copies, waits for them, and re-layouts  40 us (17%)
  other arithmetic  24.4 us (11%)
  starting transfers between devices  22.2 us (10%)
  matrix products  14.4 us (6%)
    ppermute x3, waiting for transfers between devices, per_device(): returned.append(lax.ppermute(sending[shift], 'row', pairs))  100 us
    all_to_all x1, waiting for transfers between devices, per_device(): lax.all_to_all(outgoing, 'ch', split_axis=1, concat_axis=1, tiled=True)  27.8 us
    reshape x2, local copies, waits for them, and re-layouts, per_device(): returning = term_t.reshape(n_chan, slab, n_rows, rows).transpose(0, 2, 1, 3)  7.82 us
    ppermute x3, starting transfers between devices, per_device(): lax.ppermute(jnp.concatenate([own_blk, next_blk], axis=-1), 'row', pairs)  6.07 us
    gather x2, local copies, waits for them, and re-layouts, per_device(): x.reshape(ch_dev, rows // slab, slab, width)[slot_dest, part_dest]  5.62 us
    another operation x3, other arithmetic, per_device(): pair = lambda f: jnp.stack([f(eta_pp), f(gamma_pp)])  5.43 us
    ppermute x3, starting transfers between devices, per_device(): returned.append(lax.ppermute(sending[shift], 'row', pairs))  4.83 us
    dot_general x1, matrix products, per_device(): lax.dot_general(left, right, (((1,), (1,)), ((), ())), preferred_element_...  4.73 us
  transfers between devices with their start and end apart: 9, of which 4 were waited for; matrix products, arithmetic and copies ran while one was open for 19% of the time, Pallas kernels for 0%

profile of v11, /device:TPU:8, one launch (start us, length us, event | category | flops | bytes accessed | tf_op | source)
XLA Modules:
  0.0 229.5 jit_solution(6889827563362007324)
XLA Ops:
  1.3 3.6 %gather_fusion.1 = bf16[8,128,1024]{2,1,0:T(8,128)(2,1)} fusion(bf16[4,2,128,1024]{3,2,1,0:T(8,128)(2,1)} %bitcast.64, s32[8]{0:T(128)S(1)} %fusion.51), kind=kCustom, calls=%fused_computation.1 | custom fusion | bytes 4194368 | tf_op jit(solution)/shard_map/gather | solution.py:42
  7.0 4.5 %pad_maximum_fusion = bf16[2,8,128,1024]{3,2,0,1:T(8,128)(2,1)} fusion(bf16[1,8,128,1024]{3,2,0,1:T(8,128)(2,1)} %bitcast.68, bf16[1,8,128,1024]{3,2,0,1:T(8,128)(2,1)} %bitcast.67), kind=kLoop, calls=%fused_computation.13 | loop fusion | flops 2097152 | bytes 8388608 | tf_op jit(solution)/shard_map/stack | solution.py:24
  11.5 4.7 %all-to-all-start = ((bf16[2,8,128,1024]{3,2,0,1:T(8,128)(2,1)}), bf16[2,8,128,1024]{3,2,0,1:T(8,128)(2,1)}, u32[]{:S(2)}, u32[]{:S(2)}) async-start(bf16[2,8,128,1024]{3,2,0,1:T(8,128)(2,1)} %pad_maximum_fusion), calls=%async_computation | async-start | bytes 8388608 | tf_op jit(solution)/shard_map/all_to_all | solution.py:43
  16.3 2.1 collective-permute-start.3
  18.4 2.6 %constant_dynamic-slice_fusion.8 = (bf16[1,256,1024]{2,1,0:T(8,128)(2,1)}, bf16[1,256,1024]{2,1,0:T(8,128)(2,1)S(1)}, bf16[1,256,1024]{2,1,0:T(8,128)(2,1)S(1)}, bf16[1,256,1024]{2,1,0:T(8,128)(2,1)S(1)}) fusion(bf16[4,256,1024]{2,1,0:T(8,128)(2,1)} %param.8, s32[]{:T(128)S(6)} %select_n.157, s32[]{:T(128)S(6)} %select_n.168, s32[]{:T(128)S(6)} %select_n.165, ...), kind=kLoop, calls=%fused_computation.93 | loop fusion | bytes 4194320 | tf_op jit(solution)/shard_map/jit(dynamic_index_in_dim)/dynamic_slice | solution.py:59
  26.2 4.2 %collective-permute-start.1 = (bf16[2,256,512]{1,2,0:T(8,128)(2,1)}, bf16[2,256,512]{1,2,0:T(8,128)(2,1)}, u32[]{:S(2)}, u32[]{:S(2)}) collective-permute-start(bf16[2,256,512]{1,2,0:T(8,128)(2,1)} %pad_maximum_fusion.5), channel_id=1, source_target_pairs={{0,2},{1,3},{2,0},{3,1},{4,6},{5,7},{6,4},{7,5},{8,10},{9,11},{10,... | collective-permute-start | bytes 1572872 | tf_op jit(solution)/shard_map/ppermute | solution.py:36
  37.5 27.8 %all-to-all-done = bf16[2,8,128,1024]{3,2,0,1:T(8,128)(2,1)} async-done(((bf16[2,8,128,1024]{3,2,0,1:T(8,128)(2,1)}), bf16[2,8,128,1024]{3,2,0,1:T(8,128)(2,1)}, u32[]{:S(2)}, u32[]{:S(2)}) %all-to-all-start) | async-done | bytes 4194336 | tf_op jit(solution)/shard_map/all_to_all | solution.py:43
  65.3 2.8 %broadcast_multiply_fusion.4 = (bf16[1,8,128,1024]{3,2,0,1:T(8,128)(2,1)S(1)}, bf16[1,8,128,1024]{3,2,0,1:T(8,128)(2,1)S(1)}, bf16[1,8,128,1024]{3,2,0,1:T(8,128)(2,1)S(1)}, bf16[1,8,128,1024]{3,2,0,1:T(8,128)(2,1)S(1)}) fusion(bf16[1024]{0:T(1024)(128)(2,1)S(1)} %fusion.37, bf16[2,8,128,1024]{3,2,0,1:T(8,128)(2,1)} %all-to-all-done), kind=kLoop, calls=%fused_computation.58 | loop fusion | flops 2097152 | bytes 12584960 | tf_op jit(solution)/shard_map/mul | solution.py:55
  68.1 2.3 %fusion.56 = f32[1024,1024]{1,0:T(8,128)S(1)} fusion(bf16[1024,1024]{1,0:T(8,128)(2,1)S(1)} %bitcast.72, bf16[1024,1024]{1,0:T(8,128)(2,1)S(1)} %bitcast.73), kind=kOutput, calls=%fused_computation.132 | convolution fusion | flops 2147483648 | bytes 8388608 | tf_op jit(solution)/shard_map/dot_general | solution.py:54
  70.4 3.7 %multiply_convert_fusion = bf16[1024,1024]{1,0:T(8,128)(2,1)} fusion(f32[1024,1024]{1,0:T(8,128)S(1)} %fusion.56, f32[1024]{0:T(1024)S(1)} %bitcast.77, bf16[1024,1024]{1,0:T(8,128)(2,1)S(1)} %bitcast.70, bf16[1024,1024]{1,0:T(8,128)(2,1)S(1)} %bitcast.71), kind=kOutput, calls=%fused_computation.29 | convolution fusion | flops 2150629376 | bytes 10489856 | tf_op jit(solution)/shard_map/dot_general | solution.py:55
  74.1 4.5 %reshape.183 = bf16[8,128,4,256]{3,2,1,0:T(4,128)(2,1)} reshape(bf16[1024,1024]{1,0:T(8,128)(2,1)} %multiply_convert_fusion) | data formatting | bytes 4194304 | tf_op jit(solution)/shard_map/reshape | solution.py:80
  80.5 2.0 copy.31
  82.5 2.4 %fusion.31 = (bf16[2,256,256]{1,2,0:T(8,128)(2,1)S(1)}, bf16[2,256,256]{1,2,0:T(8,128)(2,1)}, bf16[2,256,256]{1,2,0:T(8,128)(2,1)}, bf16[2,256,256]{2,1,0:T(8,12...) fusion(bf16[2,256,1024]{2,1,0:T(8,128)(2,1)S(1)} %fusion.21, ...), kind=kLoop, calls=%fused_computation.77 | loop fusion | flops 786432 | bytes 3932164 | tf_op jit(solution)/shard_map/mul | solution.py:67
  88.5 3.3 %copy.36 = bf16[8,128,4,256]{3,1,2,0:T(8,128)(2,1)} copy(bf16[8,128,4,256]{3,2,1,0:T(4,128)(2,1)} %reshape.183) | data formatting | bytes 4194304 | tf_op jit(solution)/shard_map/reshape | solution.py:80
  91.8 4.6 %all-to-all-start.1 = ((bf16[32,128,256]{2,1,0:T(8,128)(2,1)}), bf16[32,128,256]{2,1,0:T(8,128)(2,1)}, u32[]{:S(2)}, u32[]{:S(2)}) async-start(bf16[32,128,256]{2,1,0:T(8,128)(2,1)} %bitcast.66), calls=%async_computation.1 | async-start | bytes 4194304 | tf_op jit(solution)/shard_map/all_to_all | solution.py:81
  96.4 2.2 maximum_maximum_fusion
  99.4 4.7 %fusion.5 = f32[1024,1024]{0,1:T(8,128)S(1)} fusion(bf16[1024,1024]{0,1:T(8,128)(2,1)S(1)} %get-tuple-element.12, bf16[1024,1024]{0,1:T(8,128)(2,1)S(1)} %get-tuple-element.11, bf16[1024,1024]{0,1:T(8,128)(2,1)S(1)} %get-tuple-element.22, bf16[1024,1024]{0,1:T(8,128)(2,1)S(1)} %get-tuple-element.21), kind=kOutput, calls=%fused_computation.15 | convolution fusion | flops 4311744512 | bytes 12582912 | tf_op jit(solution)/shard_map/dot_general | solution.py:76
  109.7 2.0 fusion.12
  111.7 81.3 %collective-permute-done.4 = f32[256,768]{0,1:T(8,128)S(1)} collective-permute-done((f32[256,768]{0,1:T(8,128)S(1)}, f32[256,768]{0,1:T(8,128)S(1)}, u32[]{:S(2)}, u32[]{:S(2)}) %collective-permute-start.4) | collective-permute-done | bytes 786464 | tf_op jit(solution)/shard_map/ppermute | solution.py:93
  193.0 16.4 %collective-permute-done.5 = f32[256,768]{0,1:T(8,128)S(1)} collective-permute-done((f32[256,768]{0,1:T(8,128)S(1)}, f32[256,768]{0,1:T(8,128)S(1)}, u32[]{:S(2)}, u32[]{:S(2)}) %collective-permute-start.5) | collective-permute-done | bytes 786464 | tf_op jit(solution)/shard_map/ppermute | solution.py:93
  209.4 2.6 %collective-permute-done.6 = f32[256,768]{0,1:T(8,128)S(1)} collective-permute-done((f32[256,768]{0,1:T(8,128)S(1)}, f32[256,768]{0,1:T(8,128)S(1)}, u32[]{:S(2)}, u32[]{:S(2)}) %collective-permute-start.6) | collective-permute-done | bytes 786464 | tf_op jit(solution)/shard_map/ppermute | solution.py:93
  213.8 4.3 %gather_fusion.3 = f32[4,256,768]{1,2,0:T(8,128)} fusion(f32[4,256,768]{1,2,0:T(8,128)} %pad_maximum_fusion.1, s32[1024]{0:T(1024)S(1)} %pad_clamp_fusion), kind=kCustom, calls=%fused_computation.3 | custom fusion | bytes 6291472 | tf_op jit(solution)/shard_map/gather | solution.py:95
  223.5 3.6 %fusion.4 = bf16[4,256,1024]{1,2,0:T(8,128)(2,1)S(1)} fusion(s32[]{:T(128)S(6)} %select_n.177, f32[4,256,768]{1,2,0:T(8,128)S(1)} %copy-done.5, f32[4,256,256]{1,2,0:T(8,128)S(1)} %fusion.12, f32[4,256,8,128]{1,3,2,0:T(8,128)S(1)} %copy.39), kind=kLoop, calls=%fused_computation.12 | loop fusion | flops 5242880 | bytes 10485764 | tf_op jit(solution)/shard_map/convert_element_type | solution.py:107
  227.2 2.4 %copy.40 = bf16[4,256,1024]{2,1,0:T(8,128)(2,1)} copy(bf16[4,256,1024]{1,2,0:T(8,128)(2,1)S(1)} %fusion.4) | data formatting | bytes 4194304 | tf_op jit(solution)/shard_map/convert_element_type | solution.py:107
  (73 shorter events, 34.5 us)
Async XLA Ops:
  0.0 0.7 copy-start
  0.0 5.0 %copy-start.3 = (bf16[4,256,1024]{2,1,0:T(8,128)(2,1)S(1)}, bf16[4,256,1024]{2,1,0:T(8,128)(2,1)}, u32[]{:S(2)}) copy-start(bf16[4,256,1024]{2,1,0:T(8,128)(2,1)} %param.8) | copy-start | bytes 6291460
  11.5 4.7 %copy-start.8 = (s32[1,1024]{1,0:T(1,128)S(1)}, s32[1,1024]{1,0:T(1,128)}, u32[]{:S(2)}) copy-start(s32[1,1024]{1,0:T(1,128)} %param.10) | copy-start | bytes 12292
  11.5 4.7 %copy-start.9 = (f32[1,1024]{1,0:T(1,128)S(1)}, f32[1,1024]{1,0:T(1,128)}, u32[]{:S(2)}) copy-start(f32[1,1024]{1,0:T(1,128)} %param.11) | copy-start | bytes 12292
  11.5 53.8 %all-to-all-start = ((bf16[2,8,128,1024]{3,2,0,1:T(8,128)(2,1)}), bf16[2,8,128,1024]{3,2,0,1:T(8,128)(2,1)}, u32[]{:S(2)}, u32[]{:S(2)}) async-start(bf16[2,8,128,1024]{3,2,0,1:T(8,128)(2,1)} %pad_maximum_fusion), calls=%async_computation | async-start | bytes 8388608 | tf_op jit(solution)/shard_map/all_to_all | solution.py:43
  16.2 4.8 %copy-start.2 = (bf16[4,256,1024]{2,1,0:T(8,128)(2,1)S(1)}, bf16[4,256,1024]{2,1,0:T(8,128)(2,1)}, u32[]{:S(2)}) copy-start(bf16[4,256,1024]{2,1,0:T(8,128)(2,1)} %param.7) | copy-start | bytes 6291460
  16.3 21.2 %collective-permute-start.3 = (f32[2,1024]{1,0:T(2,128)S(1)}, f32[2,1024]{1,0:T(2,128)S(1)}, u32[]{:S(2)}, u32[]{:S(2)}) collective-permute-start(f32[2,1024]{1,0:T(2,128)S(1)} %pad_maximum_fusion.7), channel_id=1, source_target_pairs={{0,0},{1,4},{2,8},{3,12},{4,16},{5,20},{6,24},{7,28},{8,1},{9,5},{... | collective-permute-start | bytes 24584 | tf_op jit(solution)/shard_map/ppermute | solution.py:48
  23.9 10.2 %copy-start.7 = (s32[4,1024]{1,0:T(4,128)S(1)}, s32[4,1024]{1,0:T(4,128)}, u32[]{:S(2)}) copy-start(s32[4,1024]{1,0:T(4,128)} %param.9) | copy-start | bytes 49156
  23.9 54.7 %collective-permute-start.2 = (bf16[2,256,512]{2,1,0:T(8,128)(2,1)}, bf16[2,256,512]{2,1,0:T(8,128)(2,1)}, u32[]{:S(2)}, u32[]{:S(2)}) collective-permute-start(bf16[2,256,512]{2,1,0:T(8,128)(2,1)} %pad_maximum_fusion.6), channel_id=1, source_target_pairs={{0,3},{1,0},{2,1},{3,2},{4,7},{5,4},{6,5},{7,6},{8,11},{9,8},{10,9... | collective-permute-start | bytes 1572872 | tf_op jit(solution)/shard_map/ppermute | solution.py:36
  26.2 52.4 %collective-permute-start.1 = (bf16[2,256,512]{1,2,0:T(8,128)(2,1)}, bf16[2,256,512]{1,2,0:T(8,128)(2,1)}, u32[]{:S(2)}, u32[]{:S(2)}) collective-permute-start(bf16[2,256,512]{1,2,0:T(8,128)(2,1)} %pad_maximum_fusion.5), channel_id=1, source_target_pairs={{0,2},{1,3},{2,0},{3,1},{4,6},{5,7},{6,4},{7,5},{8,10},{9,11},{10,... | collective-permute-start | bytes 1572872 | tf_op jit(solution)/shard_map/ppermute | solution.py:36
  32.2 46.4 %collective-permute-start = (bf16[2,256,512]{2,1,0:T(8,128)(2,1)}, bf16[2,256,512]{2,1,0:T(8,128)(2,1)}, u32[]{:S(2)}, u32[]{:S(2)}) collective-permute-start(bf16[2,256,512]{2,1,0:T(8,128)(2,1)} %pad_maximum_fusion.4), channel_id=1, source_target_pairs={{0,1},{1,2},{2,3},{3,0},{4,5},{5,6},{6,7},{7,4},{8,9},{9,10},{10,1... | collective-permute-start | bytes 1572872 | tf_op jit(solution)/shard_map/ppermute | solution.py:36
  74.1 8.4 %copy-start.10 = (bf16[2]{0:T(256)(128)(2,1)S(1)}, bf16[2]{0:T(256)(128)(2,1)}, u32[]{:S(2)}) copy-start(bf16[2]{0:T(256)(128)(2,1)} %constant.147.clone) | copy-start | bytes 16
  91.8 4.6 %copy-start.6 = (bf16[2,256,1024]{1,2,0:T(8,128)(2,1)S(1)}, bf16[2,256,1024]{1,2,0:T(8,128)(2,1)}, u32[]{:S(2)}) copy-start(bf16[2,256,1024]{1,2,0:T(8,128)(2,1)} %copy.35) | copy-start | bytes 3145732
  91.8 126.3 %all-to-all-start.1 = ((bf16[32,128,256]{2,1,0:T(8,128)(2,1)}), bf16[32,128,256]{2,1,0:T(8,128)(2,1)}, u32[]{:S(2)}, u32[]{:S(2)}) async-start(bf16[32,128,256]{2,1,0:T(8,128)(2,1)} %bitcast.66), calls=%async_computation.1 | async-start | bytes 4194304 | tf_op jit(solution)/shard_map/all_to_all | solution.py:81
  104.3 5.1 %copy-start.4 = (bf16[4,256,1024]{2,1,0:T(8,128)(2,1)S(1)}, bf16[4,256,1024]{2,1,0:T(8,128)(2,1)}, u32[]{:S(2)}) copy-start(bf16[4,256,1024]{2,1,0:T(8,128)(2,1)} %param.8) | copy-start | bytes 6291460
  104.4 88.6 %collective-permute-start.4 = (f32[256,768]{0,1:T(8,128)S(1)}, f32[256,768]{0,1:T(8,128)S(1)}, u32[]{:S(2)}, u32[]{:S(2)}) collective-permute-start(f32[256,768]{0,1:T(8,128)S(1)} %pad_maximum_fusion.2), channel_id=1, source_target_pairs={{0,1},{1,2},{2,3},{3,0},{4,5},{5,6},{6,7},{7,4},{8,9},{9,10},{10,1... | collective-permute-start | bytes 2359304 | tf_op jit(solution)/shard_map/ppermute | solution.py:93
  105.9 103.5 %collective-permute-start.5 = (f32[256,768]{0,1:T(8,128)S(1)}, f32[256,768]{0,1:T(8,128)S(1)}, u32[]{:S(2)}, u32[]{:S(2)}) collective-permute-start(f32[256,768]{0,1:T(8,128)S(1)} %pad_maximum_fusion.3), channel_id=1, source_target_pairs={{0,2},{1,3},{2,0},{3,1},{4,6},{5,7},{6,4},{7,5},{8,10},{9,11},{10,... | collective-permute-start | bytes 2359304 | tf_op jit(solution)/shard_map/ppermute | solution.py:93
  107.5 104.4 %collective-permute-start.6 = (f32[256,768]{0,1:T(8,128)S(1)}, f32[256,768]{0,1:T(8,128)S(1)}, u32[]{:S(2)}, u32[]{:S(2)}) collective-permute-start(f32[256,768]{0,1:T(8,128)S(1)} %get-tuple-element.16), channel_id=1, source_target_pairs={{0,3},{1,0},{2,1},{3,2},{4,7},{5,4},{6,5},{7,6},{8,11},{9,8},{10,9... | collective-permute-start | bytes 2359304 | tf_op jit(solution)/shard_map/ppermute | solution.py:93
  221.6 1.9 copy-start.5
  223.5 6.0 %copy-start.1 = (s32[32,8]{0,1:T(8,128)S(1)}, s32[32,8]{0,1:T(8,128)}, u32[]{:S(2)}) copy-start(s32[32,8]{0,1:T(8,128)} %param.12) | copy-start | bytes 3076

commit v12 on v11

--- a/solution.py
+++ b/solution.py
@@ -51,9 +51,15 @@
     weight = coefs[0].astype(bf16)[None, :]
     coef = coefs[1]
 
-    ph_t = jnp.dot(a_eta * weight, b_gamma, preferred_element_type=f32)
-    ph_t = ph_t - jnp.dot(b_gamma * weight, a_eta, preferred_element_type=f32)
-    term_t = (ph_t * coef[:, None]).astype(bf16)
+    split = lambda x: x.reshape(n_chan, slab, width)
+    cols = lambda x: x.reshape(width, n_rows, rows)
+    ph_t = jnp.einsum(
+        "ewk,kri->erwi", split(a_eta * weight), cols(b_gamma), preferred_element_type=f32
+    )
+    ph_t = ph_t - jnp.einsum(
+        "ewk,kri->erwi", split(b_gamma * weight), cols(a_eta), preferred_element_type=f32
+    )
+    term_t = (ph_t * coef.reshape(n_chan, 1, slab, 1)).astype(bf16)
     ladder_in, _ = lax.optimization_barrier((ladder_in, term_t))
     sign = jnp.array([-1, 1], bf16)[:, None, None]
     own = pair(lambda x: lax.dynamic_index_in_dim(x, level, 0, False))
@@ -77,7 +83,7 @@
         left, right, (((1,), (1,)), ((), ())), preferred_element_type=f32
     ).reshape(n_rows, rows, width)
     sending = jnp.stack([skip_block(ladder_c[a], a, rows) for a in range(n_rows)])
-    returning = term_t.reshape(n_chan, slab, n_rows, rows).transpose(0, 2, 1, 3)
+    returning = term_t
     landed = lax.all_to_all(
         returning.reshape(n_chan * n_rows, slab, rows),
         ("ch", "row"),
@@ -91,8 +97,9 @@
     for shift in range(1, n_rows):
         pairs = [(a, (a + shift) % n_rows) for a in range(n_rows)]
         returned.append(lax.ppermute(sending[shift], "row", pairs))
-    sources = (level - jnp.arange(n_rows, dtype=jnp.int32)) % n_rows
-    ladder = jnp.stack(returned)[sources]
+    ladder = jnp.stack(
+        [lax.select_n((level - s) % n_rows, *returned) for s in range(n_rows)]
+    )
     chosen = src_slot[:, mine].reshape(n_chan, ch_dev)
     onehot = (chosen[:, :, None] == jnp.arange(ch_dev, dtype=jnp.int32)[None, None, :]).astype(bf16)
     back = jnp.einsum("gts,gtwi->sigw", onehot, landed, preferred_element_type=f32)

time: 230 us -> 237 us (1.030)
  local copies, waits for them, and re-layouts: 40 us -> 45.9 us
  matrix products: 14.4 us -> 18.9 us
  other arithmetic: 24.4 us -> 20.4 us
    another operation x1 -> x2, local copies, waits for them, and re-layouts: 0.14 us -> 9.09 us  [per_device(): cols = lambda x: x.reshape(width, n_rows, rows)]
    reshape x2 -> x0, local copies, waits for them, and re-layouts: 7.82 us -> none  [per_device(): returning = term_t.reshape(n_chan, slab, n_rows, rows).transpose(0, 2, 1, 3)]
    slice x0 -> x1, local copies, waits for them, and re-layouts: none -> 4.92 us  [per_device(): b_gamma = arrived[1].reshape(width, width)]
    gather x1 -> x0, local copies, waits for them, and re-layouts: 4.27 us -> none  [per_device(): ladder = jnp.stack(returned)[sources]]
    dot_general x2, matrix products: 6 us -> 10 us  [the longest x1 5.27 us: per_device(): jnp.einsum('ewk,kri->erwi', split(a_eta * weight), cols(b_gamma), preferr...]
    convert_element_type x0 -> x1, local copies, waits for them, and re-layouts: none -> 3.95 us  [per_device(): term_t = (ph_t * coef.reshape(n_chan, 1, slab, 1)).astype(bf16)]
    mul x1 -> x0, other arithmetic: 2.76 us -> none  [per_device(): ph_t = ph_t - jnp.dot(b_gamma * weight, a_eta, preferred_element_type=f32)]
  transfers between devices with their start and end apart: 9 -> 9, of which waited for: 4 -> 4; matrix products, arithmetic and copies ran while one was open for 19% -> 23% of each run, Pallas kernels for 0% -> 0%
where the time goes in v12:
time: 237 us; the launch traced here: 236 us
  waiting for transfers between devices  128 us (54%)
  local copies, waits for them, and re-layouts  45.9 us (19%)
  starting transfers between devices  21.9 us (9%)
  other arithmetic  20.4 us (9%)
  matrix products  18.9 us (8%)
    ppermute x3, waiting for transfers between devices, per_device(): returned.append(lax.ppermute(sending[shift], 'row', pairs))  100 us
    all_to_all x1, waiting for transfers between devices, per_device(): lax.all_to_all(outgoing, 'ch', split_axis=1, concat_axis=1, tiled=True)  27.8 us
    another operation x2, local copies, waits for them, and re-layouts, per_device(): cols = lambda x: x.reshape(width, n_rows, rows)  9.09 us
    ppermute x3, starting transfers between devices, per_device(): lax.ppermute(jnp.concatenate([own_blk, next_blk], axis=-1), 'row', pairs)  6.07 us
    gather x2, local copies, waits for them, and re-layouts, per_device(): x.reshape(ch_dev, rows // slab, slab, width)[slot_dest, part_dest]  5.61 us
    another operation x3, other arithmetic, per_device(): pair = lambda f: jnp.stack([f(eta_pp), f(gamma_pp)])  5.53 us
    dot_general x1, matrix products, per_device(): jnp.einsum('ewk,kri->erwi', split(a_eta * weight), cols(b_gamma), preferr...  5.27 us
    slice x1, local copies, waits for them, and re-layouts, per_device(): b_gamma = arrived[1].reshape(width, width)  4.92 us
  transfers between devices with their start and end apart: 9, of which 4 were waited for; matrix products, arithmetic and copies ran while one was open for 23% of the time, Pallas kernels for 0%

profile of v12, /device:TPU:8, one launch (start us, length us, event | category | flops | bytes accessed | tf_op | source)
XLA Modules:
  0.0 235.6 jit_solution(1474348531151835947)
XLA Ops:
  1.3 3.6 %gather_fusion.1 = bf16[8,128,1024]{2,1,0:T(8,128)(2,1)} fusion(bf16[4,2,128,1024]{3,2,1,0:T(8,128)(2,1)} %bitcast.77, s32[8]{0:T(128)S(1)} %fusion.70), kind=kCustom, calls=%fused_computation.1 | custom fusion | bytes 4194368 | tf_op jit(solution)/shard_map/gather | solution.py:42
  7.0 4.6 %pad_maximum_fusion = bf16[2,8,128,1024]{3,2,0,1:T(8,128)(2,1)} fusion(bf16[1,8,128,1024]{3,2,0,1:T(8,128)(2,1)} %bitcast.81, bf16[1,8,128,1024]{3,2,0,1:T(8,128)(2,1)} %bitcast.80), kind=kLoop, calls=%fused_computation.24 | loop fusion | flops 2097152 | bytes 8388608 | tf_op jit(solution)/shard_map/stack | solution.py:24
  11.6 4.7 %all-to-all-start = ((bf16[2,8,128,1024]{3,2,0,1:T(8,128)(2,1)}), bf16[2,8,128,1024]{3,2,0,1:T(8,128)(2,1)}, u32[]{:S(2)}, u32[]{:S(2)}) async-start(bf16[2,8,128,1024]{3,2,0,1:T(8,128)(2,1)} %pad_maximum_fusion), calls=%async_computation | async-start | bytes 8388608 | tf_op jit(solution)/shard_map/all_to_all | solution.py:43
  16.4 2.1 collective-permute-start.3
  18.5 2.6 %constant_dynamic-slice_fusion.8 = (bf16[1,256,1024]{2,1,0:T(8,128)(2,1)}, bf16[1,256,1024]{2,1,0:T(8,128)(2,1)S(1)}, bf16[1,256,1024]{2,1,0:T(8,128)(2,1)S(1)}, bf16[1,256,1024]{2,1,0:T(8,128)(2,1)S(1)}) fusion(bf16[4,256,1024]{2,1,0:T(8,128)(2,1)} %param.8, s32[]{:T(128)S(6)} %select_n.263, s32[]{:T(128)S(6)} %select_n.274, s32[]{:T(128)S(6)} %select_n.271, ...), kind=kLoop, calls=%fused_computation.113 | loop fusion | bytes 4194320 | tf_op jit(solution)/shard_map/jit(dynamic_index_in_dim)/dynamic_slice | solution.py:65
  26.3 4.2 %collective-permute-start.1 = (bf16[2,256,512]{1,2,0:T(8,128)(2,1)}, bf16[2,256,512]{1,2,0:T(8,128)(2,1)}, u32[]{:S(2)}, u32[]{:S(2)}) collective-permute-start(bf16[2,256,512]{1,2,0:T(8,128)(2,1)} %pad_maximum_fusion.4), channel_id=1, source_target_pairs={{0,2},{1,3},{2,0},{3,1},{4,6},{5,7},{6,4},{7,5},{8,10},{9,11},{10,... | collective-permute-start | bytes 1572872 | tf_op jit(solution)/shard_map/ppermute | solution.py:36
  37.6 27.8 %all-to-all-done = bf16[2,8,128,1024]{3,2,0,1:T(8,128)(2,1)} async-done(((bf16[2,8,128,1024]{3,2,0,1:T(8,128)(2,1)}), bf16[2,8,128,1024]{3,2,0,1:T(8,128)(2,1)}, u32[]{:S(2)}, u32[]{:S(2)}) %all-to-all-start) | async-done | bytes 4194336 | tf_op jit(solution)/shard_map/all_to_all | solution.py:43
  65.4 4.9 %fusion.77 = (bf16[1,8,128,1024]{3,2,0,1:T(8,128)(2,1)}, bf16[1,8,128,1024]{3,2,0,1:T(8,128)(2,1)}) fusion(bf16[2,8,128,1024]{3,2,0,1:T(8,128)(2,1)} %all-to-all-done), kind=kLoop, calls=%fused_computation.149 | loop fusion | bytes 8388608 | tf_op jit(solution)/shard_map/slice | solution.py:45
  70.3 4.5 %reshape.163 = bf16[1024,4,256]{2,1,0:T(4,128)(2,1)} reshape(bf16[1,8,128,1024]{3,2,0,1:T(8,128)(2,1)} %get-tuple-element.24) | data formatting | bytes 4194304 | tf_op jit(solution)/shard_map/reshape;reshape;squeeze | solution.py:55
  74.9 4.6 %reshape.162 = bf16[1024,4,256]{2,1,0:T(4,128)(2,1)} reshape(bf16[1,8,128,1024]{3,2,0,1:T(8,128)(2,1)} %get-tuple-element.23) | data formatting | bytes 4194304 | tf_op jit(solution)/shard_map/reshape;reshape;squeeze | solution.py:55
  79.4 4.8 %fusion.26 = f32[4,256,8,128]{3,1,2,0:T(8,128)S(1)} fusion(bf16[1024,4,256,1]{2,1,0,3:T(4,128)(2,1)} %bitcast.84, bf16[1024]{0:T(1024)(128)(2,1)S(1)} %fusion.58, bf16[2,8,128,1024]{3,2,0,1:T(8,128)(2,1)} %all-to-all-done), kind=kOutput, calls=%fused_computation.49 | convolution fusion | flops 2151677952 | bytes 8390656 | tf_op jit(solution)/shard_map/ewk,kri->erwi/dot_general | solution.py:59
  84.2 5.3 %fusion.25 = bf16[8,4,128,256]{2,3,0,1:T(8,128)(2,1)} fusion(f32[4,256,8,128]{3,1,2,0:T(8,128)S(1)} %fusion.26, f32[8,128]{1,0:T(8,128)S(1)} %bitcast.85, bf16[1024,4,256,1]{2,1,0,3:T(4,128)(2,1)S(1)} %bitcast.83, bf16[1024]{0:T(1024)(128)(2,1)S(1)} %fusion.58, bf16[2,8,128,1024]{3,2,0,1:T(8,128)(2,1)} %all-to-all-done), kind=kOutput, calls=%fused_computation.42 | convolution fusion | flops 2154823680 | bytes 10491904 | tf_op jit(solution)/shard_map/ewk,kri->erwi/dot_general | solution.py:56
  89.5 4.0 %copy.42 = bf16[8,4,128,256]{3,2,1,0:T(8,128)(2,1)} copy(bf16[8,4,128,256]{2,3,0,1:T(8,128)(2,1)} %fusion.25) | data formatting | bytes 4194304 | tf_op jit(solution)/shard_map/convert_element_type | solution.py:62
  95.3 2.0 copy.37
  97.3 2.5 %fusion.52 = (bf16[2,256,256]{1,2,0:T(8,128)(2,1)S(1)}, bf16[2,256,256]{1,2,0:T(8,128)(2,1)}, bf16[2,256,256]{1,2,0:T(8,128)(2,1)}, bf16[2,256,256]{2,1,0:T(8,12...) fusion(bf16[2,256,1024]{2,1,0:T(8,128)(2,1)S(1)} %fusion.40, ...), kind=kLoop, calls=%fused_computation.99 | loop fusion | flops 786432 | bytes 3932164 | tf_op jit(solution)/shard_map/mul | solution.py:73
  103.5 4.6 %all-to-all-start.1 = ((bf16[32,128,256]{2,1,0:T(8,128)(2,1)}), bf16[32,128,256]{2,1,0:T(8,128)(2,1)}, u32[]{:S(2)}, u32[]{:S(2)}) async-start(bf16[32,128,256]{2,1,0:T(8,128)(2,1)} %bitcast.79), calls=%async_computation.1 | async-start | bytes 4194304 | tf_op jit(solution)/shard_map/all_to_all | solution.py:87
  108.1 2.2 maximum_maximum_fusion
  111.1 4.8 %fusion.11 = f32[1024,1024]{0,1:T(8,128)S(1)} fusion(bf16[1024,1024]{0,1:T(8,128)(2,1)S(1)} %get-tuple-element.16, bf16[1024,1024]{0,1:T(8,128)(2,1)S(1)} %get-tuple-element.15, bf16[1024,1024]{0,1:T(8,128)(2,1)S(1)} %get-tuple-element.22, bf16[1024,1024]{0,1:T(8,128)(2,1)S(1)} %get-tuple-element.21), kind=kOutput, calls=%fused_computation.26 | convolution fusion | flops 4311744512 | bytes 12582912 | tf_op jit(solution)/shard_map/dot_general | solution.py:82
  121.1 2.3 fusion.18
  123.4 81.3 %collective-permute-done.4 = f32[256,768]{0,1:T(8,128)S(1)} collective-permute-done((f32[256,768]{0,1:T(8,128)S(1)}, f32[256,768]{0,1:T(8,128)S(1)}, u32[]{:S(2)}, u32[]{:S(2)}) %collective-permute-start.4) | collective-permute-done | bytes 786464 | tf_op jit(solution)/shard_map/ppermute | solution.py:99
  204.7 16.4 %collective-permute-done.5 = f32[256,768]{0,1:T(8,128)S(1)} collective-permute-done((f32[256,768]{0,1:T(8,128)S(1)}, f32[256,768]{0,1:T(8,128)S(1)}, u32[]{:S(2)}, u32[]{:S(2)}) %collective-permute-start.5) | collective-permute-done | bytes 786464 | tf_op jit(solution)/shard_map/ppermute | solution.py:99
  221.1 2.6 %collective-permute-done.6 = f32[256,768]{0,1:T(8,128)S(1)} collective-permute-done((f32[256,768]{0,1:T(8,128)S(1)}, f32[256,768]{0,1:T(8,128)S(1)}, u32[]{:S(2)}, u32[]{:S(2)}) %collective-permute-start.6) | collective-permute-done | bytes 786464 | tf_op jit(solution)/shard_map/ppermute | solution.py:99
  230.7 2.5 %fusion.7 = bf16[4,256,1024]{1,2,0:T(8,128)(2,1)S(1)} fusion(s32[]{:T(128)S(6)} %select_n.316, f32[1,256,768]{1,2,0:T(8,128)S(1)} %copy-done.8, f32[1,256,768]{1,2,0:T(8,128)S(1)} %copy-done.7, f32[1,256,768]{1,2,0:T(8,128)S(1)} %copy-done.6, f32[1,256,768]{1,2,0:T(8,128)S(1)} %get-tuple-element.11, f32[4,256,256]{1,2,0:T(8,128)S(1)} %copy-done.10, ...), kind=kLoop, calls=%fused_computation.20 | loop fusion | flops 11534336 | bytes 10485764 | tf_op jit(solution)/shard_map/convert_element_type | solution.py:114
  233.3 2.4 %copy.46 = bf16[4,256,1024]{2,1,0:T(8,128)(2,1)} copy(bf16[4,256,1024]{1,2,0:T(8,128)(2,1)S(1)} %fusion.7) | data formatting | bytes 4194304 | tf_op jit(solution)/shard_map/convert_element_type | solution.py:114
  (79 shorter events, 34.0 us)
Async XLA Ops:
  0.0 0.7 copy-start
  0.0 5.0 %copy-start.3 = (bf16[4,256,1024]{2,1,0:T(8,128)(2,1)S(1)}, bf16[4,256,1024]{2,1,0:T(8,128)(2,1)}, u32[]{:S(2)}) copy-start(bf16[4,256,1024]{2,1,0:T(8,128)(2,1)} %param.8) | copy-start | bytes 6291460
  11.6 4.7 %copy-start.12 = (s32[1,1024]{1,0:T(1,128)S(1)}, s32[1,1024]{1,0:T(1,128)}, u32[]{:S(2)}) copy-start(s32[1,1024]{1,0:T(1,128)} %param.10) | copy-start | bytes 12292
  11.6 4.7 %copy-start.13 = (f32[1,1024]{1,0:T(1,128)S(1)}, f32[1,1024]{1,0:T(1,128)}, u32[]{:S(2)}) copy-start(f32[1,1024]{1,0:T(1,128)} %param.11) | copy-start | bytes 12292
  11.6 53.8 %all-to-all-start = ((bf16[2,8,128,1024]{3,2,0,1:T(8,128)(2,1)}), bf16[2,8,128,1024]{3,2,0,1:T(8,128)(2,1)}, u32[]{:S(2)}, u32[]{:S(2)}) async-start(bf16[2,8,128,1024]{3,2,0,1:T(8,128)(2,1)} %pad_maximum_fusion), calls=%async_computation | async-start | bytes 8388608 | tf_op jit(solution)/shard_map/all_to_all | solution.py:43
  16.3 4.8 %copy-start.2 = (bf16[4,256,1024]{2,1,0:T(8,128)(2,1)S(1)}, bf16[4,256,1024]{2,1,0:T(8,128)(2,1)}, u32[]{:S(2)}) copy-start(bf16[4,256,1024]{2,1,0:T(8,128)(2,1)} %param.7) | copy-start | bytes 6291460
  16.4 21.2 %collective-permute-start.3 = (f32[2,1024]{1,0:T(2,128)S(1)}, f32[2,1024]{1,0:T(2,128)S(1)}, u32[]{:S(2)}, u32[]{:S(2)}) collective-permute-start(f32[2,1024]{1,0:T(2,128)S(1)} %pad_maximum_fusion.6), channel_id=1, source_target_pairs={{0,0},{1,4},{2,8},{3,12},{4,16},{5,20},{6,24},{7,28},{8,1},{9,5},{... | collective-permute-start | bytes 24584 | tf_op jit(solution)/shard_map/ppermute | solution.py:48
  23.2 11.1 %copy-start.11 = (s32[4,1024]{1,0:T(4,128)S(1)}, s32[4,1024]{1,0:T(4,128)}, u32[]{:S(2)}) copy-start(s32[4,1024]{1,0:T(4,128)} %param.9) | copy-start | bytes 49156
  24.0 69.4 %collective-permute-start.2 = (bf16[2,256,512]{2,1,0:T(8,128)(2,1)}, bf16[2,256,512]{2,1,0:T(8,128)(2,1)}, u32[]{:S(2)}, u32[]{:S(2)}) collective-permute-start(bf16[2,256,512]{2,1,0:T(8,128)(2,1)} %pad_maximum_fusion.5), channel_id=1, source_target_pairs={{0,3},{1,0},{2,1},{3,2},{4,7},{5,4},{6,5},{7,6},{8,11},{9,8},{10,9... | collective-permute-start | bytes 1572872 | tf_op jit(solution)/shard_map/ppermute | solution.py:36
  26.3 67.1 %collective-permute-start.1 = (bf16[2,256,512]{1,2,0:T(8,128)(2,1)}, bf16[2,256,512]{1,2,0:T(8,128)(2,1)}, u32[]{:S(2)}, u32[]{:S(2)}) collective-permute-start(bf16[2,256,512]{1,2,0:T(8,128)(2,1)} %pad_maximum_fusion.4), channel_id=1, source_target_pairs={{0,2},{1,3},{2,0},{3,1},{4,6},{5,7},{6,4},{7,5},{8,10},{9,11},{10,... | collective-permute-start | bytes 1572872 | tf_op jit(solution)/shard_map/ppermute | solution.py:36
  32.4 61.1 %collective-permute-start = (bf16[2,256,512]{2,1,0:T(8,128)(2,1)}, bf16[2,256,512]{2,1,0:T(8,128)(2,1)}, u32[]{:S(2)}, u32[]{:S(2)}) collective-permute-start(bf16[2,256,512]{2,1,0:T(8,128)(2,1)} %pad_maximum_fusion.3), channel_id=1, source_target_pairs={{0,1},{1,2},{2,3},{3,0},{4,5},{5,6},{6,7},{7,4},{8,9},{9,10},{10,1... | collective-permute-start | bytes 1572872 | tf_op jit(solution)/shard_map/ppermute | solution.py:36
  79.4 4.8 %copy-start.9 = (bf16[1024,4,256]{2,1,0:T(4,128)(2,1)S(1)}, bf16[1024,4,256]{2,1,0:T(4,128)(2,1)}, u32[]{:S(2)}) copy-start(bf16[1024,4,256]{2,1,0:T(4,128)(2,1)} %reshape.162) | copy-start | bytes 6291460
  89.5 7.8 %copy-start.14 = (bf16[2]{0:T(256)(128)(2,1)S(1)}, bf16[2]{0:T(256)(128)(2,1)}, u32[]{:S(2)}) copy-start(bf16[2]{0:T(256)(128)(2,1)} %constant.158.clone) | copy-start | bytes 16
  99.8 8.3 %copy-start.5 = (bf16[2,256,1024]{1,2,0:T(8,128)(2,1)S(1)}, bf16[2,256,1024]{1,2,0:T(8,128)(2,1)}, u32[]{:S(2)}) copy-start(bf16[2,256,1024]{1,2,0:T(8,128)(2,1)} %copy.41) | copy-start | bytes 3145732
  103.5 121.8 %all-to-all-start.1 = ((bf16[32,128,256]{2,1,0:T(8,128)(2,1)}), bf16[32,128,256]{2,1,0:T(8,128)(2,1)}, u32[]{:S(2)}, u32[]{:S(2)}) async-start(bf16[32,128,256]{2,1,0:T(8,128)(2,1)} %bitcast.79), calls=%async_computation.1 | async-start | bytes 4194304 | tf_op jit(solution)/shard_map/all_to_all | solution.py:87
  115.9 4.9 %copy-start.4 = (bf16[4,256,1024]{2,1,0:T(8,128)(2,1)S(1)}, bf16[4,256,1024]{2,1,0:T(8,128)(2,1)}, u32[]{:S(2)}) copy-start(bf16[4,256,1024]{2,1,0:T(8,128)(2,1)} %param.8) | copy-start | bytes 6291460
  116.2 88.5 %collective-permute-start.4 = (f32[256,768]{0,1:T(8,128)S(1)}, f32[256,768]{0,1:T(8,128)S(1)}, u32[]{:S(2)}, u32[]{:S(2)}) collective-permute-start(f32[256,768]{0,1:T(8,128)S(1)} %pad_maximum_fusion.1), channel_id=1, source_target_pairs={{0,1},{1,2},{2,3},{3,0},{4,5},{5,6},{6,7},{7,4},{8,9},{9,10},{10,1... | collective-permute-start | bytes 2359304 | tf_op jit(solution)/shard_map/ppermute | solution.py:99
  117.8 103.3 %collective-permute-start.5 = (f32[256,768]{0,1:T(8,128)S(1)}, f32[256,768]{0,1:T(8,128)S(1)}, u32[]{:S(2)}, u32[]{:S(2)}) collective-permute-start(f32[256,768]{0,1:T(8,128)S(1)} %pad_maximum_fusion.2), channel_id=1, source_target_pairs={{0,2},{1,3},{2,0},{3,1},{4,6},{5,7},{6,4},{7,5},{8,10},{9,11},{10,... | collective-permute-start | bytes 2359304 | tf_op jit(solution)/shard_map/ppermute | solution.py:99
  119.2 104.4 %collective-permute-start.6 = (f32[256,768]{0,1:T(8,128)S(1)}, f32[256,768]{0,1:T(8,128)S(1)}, u32[]{:S(2)}, u32[]{:S(2)}) collective-permute-start(f32[256,768]{0,1:T(8,128)S(1)} %slice.122), channel_id=1, source_target_pairs={{0,3},{1,0},{2,1},{3,2},{4,7},{5,4},{6,5},{7,6},{8,11},{9,8},{10,9... | collective-permute-start | bytes 2359304 | tf_op jit(solution)/shard_map/ppermute | solution.py:99
  228.8 1.1 copy-start.6
  228.8 1.4 copy-start.7
  228.8 1.6 copy-start.8
  228.8 1.9 copy-start.10
  230.7 4.9 %copy-start.1 = (s32[32,8]{0,1:T(8,128)S(1)}, s32[32,8]{0,1:T(8,128)}, u32[]{:S(2)}) copy-start(s32[32,8]{0,1:T(8,128)} %param.12) | copy-start | bytes 3076

commit v13 on v11

--- a/solution.py
+++ b/solution.py
@@ -91,8 +91,9 @@
     for shift in range(1, n_rows):
         pairs = [(a, (a + shift) % n_rows) for a in range(n_rows)]
         returned.append(lax.ppermute(sending[shift], "row", pairs))
-    sources = (level - jnp.arange(n_rows, dtype=jnp.int32)) % n_rows
-    ladder = jnp.stack(returned)[sources]
+    ladder = jnp.stack(
+        [lax.select_n((level - s) % n_rows, *returned) for s in range(n_rows)]
+    )
     chosen = src_slot[:, mine].reshape(n_chan, ch_dev)
     onehot = (chosen[:, :, None] == jnp.arange(ch_dev, dtype=jnp.int32)[None, None, :]).astype(bf16)
     back = jnp.einsum("gts,gtwi->sigw", onehot, landed, preferred_element_type=f32)

time: 230 us -> 225 us (0.978)
  local copies, waits for them, and re-layouts: 40 us -> 35.8 us
    gather x1 -> x0, local copies, waits for them, and re-layouts: 4.27 us -> none  [per_device(): ladder = jnp.stack(returned)[sources]]
  transfers between devices with their start and end apart: 9 -> 9, of which waited for: 4 -> 4; matrix products, arithmetic and copies ran while one was open for 19% -> 17% of each run, Pallas kernels for 0% -> 0%
where the time goes in v13:
time: 225 us; the launch traced here: 224 us
  waiting for transfers between devices  128 us (57%)
  local copies, waits for them, and re-layouts  35.8 us (16%)
  other arithmetic  23 us (10%)
  starting transfers between devices  21.9 us (10%)
  matrix products  14.8 us (7%)
    ppermute x3, waiting for transfers between devices, per_device(): returned.append(lax.ppermute(sending[shift], 'row', pairs))  100 us
    all_to_all x1, waiting for transfers between devices, per_device(): lax.all_to_all(outgoing, 'ch', split_axis=1, concat_axis=1, tiled=True)  27.8 us
    reshape x2, local copies, waits for them, and re-layouts, per_device(): returning = term_t.reshape(n_chan, slab, n_rows, rows).transpose(0, 2, 1, 3)  7.91 us
    ppermute x3, starting transfers between devices, per_device(): lax.ppermute(jnp.concatenate([own_blk, next_blk], axis=-1), 'row', pairs)  6.06 us
    gather x2, local copies, waits for them, and re-layouts, per_device(): x.reshape(ch_dev, rows // slab, slab, width)[slot_dest, part_dest]  5.63 us
    another operation x3, other arithmetic, per_device(): pair = lambda f: jnp.stack([f(eta_pp), f(gamma_pp)])  5.45 us
    dot_general x1, matrix products, per_device(): lax.dot_general(left, right, (((1,), (1,)), ((), ())), preferred_element_...  4.81 us
    all_to_all x1, starting transfers between devices, per_device(): lax.all_to_all(outgoing, 'ch', split_axis=1, concat_axis=1, tiled=True)  4.7 us
  transfers between devices with their start and end apart: 9, of which 4 were waited for; matrix products, arithmetic and copies ran while one was open for 17% of the time, Pallas kernels for 0%

profile of v13, /device:TPU:8, one launch (start us, length us, event | category | flops | bytes accessed | tf_op | source)
XLA Modules:
  0.0 224.1 jit_solution(4851265743398638076)
XLA Ops:
  1.3 3.6 %gather_fusion.1 = bf16[8,128,1024]{2,1,0:T(8,128)(2,1)} fusion(bf16[4,2,128,1024]{3,2,1,0:T(8,128)(2,1)} %bitcast.65, s32[8]{0:T(128)S(1)} %fusion.55), kind=kCustom, calls=%fused_computation.1 | custom fusion | bytes 4194368 | tf_op jit(solution)/shard_map/gather | solution.py:42
  5.0 2.0 gather_fusion.2
  7.0 4.6 %pad_maximum_fusion = bf16[2,8,128,1024]{3,2,0,1:T(8,128)(2,1)} fusion(bf16[1,8,128,1024]{3,2,0,1:T(8,128)(2,1)} %bitcast.69, bf16[1,8,128,1024]{3,2,0,1:T(8,128)(2,1)} %bitcast.68), kind=kLoop, calls=%fused_computation.24 | loop fusion | flops 2097152 | bytes 8388608 | tf_op jit(solution)/shard_map/stack | solution.py:24
  11.5 4.7 %all-to-all-start = ((bf16[2,8,128,1024]{3,2,0,1:T(8,128)(2,1)}), bf16[2,8,128,1024]{3,2,0,1:T(8,128)(2,1)}, u32[]{:S(2)}, u32[]{:S(2)}) async-start(bf16[2,8,128,1024]{3,2,0,1:T(8,128)(2,1)} %pad_maximum_fusion), calls=%async_computation | async-start | bytes 8388608 | tf_op jit(solution)/shard_map/all_to_all | solution.py:43
  16.3 2.1 collective-permute-start.3
  18.4 2.6 %constant_dynamic-slice_fusion.8 = (bf16[1,256,1024]{2,1,0:T(8,128)(2,1)}, bf16[1,256,1024]{2,1,0:T(8,128)(2,1)S(1)}, bf16[1,256,1024]{2,1,0:T(8,128)(2,1)S(1)}, bf16[1,256,1024]{2,1,0:T(8,128)(2,1)S(1)}) fusion(bf16[4,256,1024]{2,1,0:T(8,128)(2,1)} %param.8, s32[]{:T(128)S(6)} %select_n.263, s32[]{:T(128)S(6)} %select_n.274, s32[]{:T(128)S(6)} %select_n.271, ...), kind=kLoop, calls=%fused_computation.104 | loop fusion | bytes 4194320 | tf_op jit(solution)/shard_map/jit(dynamic_index_in_dim)/dynamic_slice | solution.py:59
  26.3 4.2 %collective-permute-start.1 = (bf16[2,256,512]{1,2,0:T(8,128)(2,1)}, bf16[2,256,512]{1,2,0:T(8,128)(2,1)}, u32[]{:S(2)}, u32[]{:S(2)}) collective-permute-start(bf16[2,256,512]{1,2,0:T(8,128)(2,1)} %pad_maximum_fusion.4), channel_id=1, source_target_pairs={{0,2},{1,3},{2,0},{3,1},{4,6},{5,7},{6,4},{7,5},{8,10},{9,11},{10,... | collective-permute-start | bytes 1572872 | tf_op jit(solution)/shard_map/ppermute | solution.py:36
  37.5 27.8 %all-to-all-done = bf16[2,8,128,1024]{3,2,0,1:T(8,128)(2,1)} async-done(((bf16[2,8,128,1024]{3,2,0,1:T(8,128)(2,1)}), bf16[2,8,128,1024]{3,2,0,1:T(8,128)(2,1)}, u32[]{:S(2)}, u32[]{:S(2)}) %all-to-all-start) | async-done | bytes 4194336 | tf_op jit(solution)/shard_map/all_to_all | solution.py:43
  65.4 2.8 %broadcast_multiply_fusion.4 = (bf16[1,8,128,1024]{3,2,0,1:T(8,128)(2,1)S(1)}, bf16[1,8,128,1024]{3,2,0,1:T(8,128)(2,1)S(1)}, bf16[1,8,128,1024]{3,2,0,1:T(8,128)(2,1)S(1)}, bf16[1,8,128,1024]{3,2,0,1:T(8,128)(2,1)S(1)}) fusion(bf16[1024]{0:T(1024)(128)(2,1)S(1)} %fusion.43, bf16[2,8,128,1024]{3,2,0,1:T(8,128)(2,1)} %all-to-all-done), kind=kLoop, calls=%fused_computation.68 | loop fusion | flops 2097152 | bytes 12584960 | tf_op jit(solution)/shard_map/mul | solution.py:55
  68.1 2.3 %fusion.60 = f32[1024,1024]{1,0:T(8,128)S(1)} fusion(bf16[1024,1024]{1,0:T(8,128)(2,1)S(1)} %bitcast.73, bf16[1024,1024]{1,0:T(8,128)(2,1)S(1)} %bitcast.74), kind=kOutput, calls=%fused_computation.138 | convolution fusion | flops 2147483648 | bytes 8388608 | tf_op jit(solution)/shard_map/dot_general | solution.py:54
  70.5 3.7 %multiply_convert_fusion = bf16[1024,1024]{1,0:T(8,128)(2,1)} fusion(f32[1024,1024]{1,0:T(8,128)S(1)} %fusion.60, f32[1024]{0:T(1024)S(1)} %bitcast.75, bf16[1024,1024]{1,0:T(8,128)(2,1)S(1)} %bitcast.71, bf16[1024,1024]{1,0:T(8,128)(2,1)S(1)} %bitcast.72), kind=kOutput, calls=%fused_computation.40 | convolution fusion | flops 2150629376 | bytes 10489856 | tf_op jit(solution)/shard_map/dot_general | solution.py:55
  74.1 4.5 %reshape.134 = bf16[8,128,4,256]{3,2,1,0:T(4,128)(2,1)} reshape(bf16[1024,1024]{1,0:T(8,128)(2,1)} %multiply_convert_fusion) | data formatting | bytes 4194304 | tf_op jit(solution)/shard_map/reshape | solution.py:80
  80.5 2.1 copy.31
  82.5 2.4 %fusion.37 = (bf16[2,256,256]{1,2,0:T(8,128)(2,1)S(1)}, bf16[2,256,256]{1,2,0:T(8,128)(2,1)}, bf16[2,256,256]{1,2,0:T(8,128)(2,1)}, bf16[2,256,256]{2,1,0:T(8,12...) fusion(bf16[2,256,1024]{2,1,0:T(8,128)(2,1)S(1)} %fusion.27, ...), kind=kLoop, calls=%fused_computation.90 | loop fusion | flops 786432 | bytes 3932164 | tf_op jit(solution)/shard_map/mul | solution.py:67
  88.5 3.4 %copy.36 = bf16[8,128,4,256]{3,1,2,0:T(8,128)(2,1)} copy(bf16[8,128,4,256]{3,2,1,0:T(4,128)(2,1)} %reshape.134) | data formatting | bytes 4194304 | tf_op jit(solution)/shard_map/reshape | solution.py:80
  91.9 4.6 %all-to-all-start.1 = ((bf16[32,128,256]{2,1,0:T(8,128)(2,1)}), bf16[32,128,256]{2,1,0:T(8,128)(2,1)}, u32[]{:S(2)}, u32[]{:S(2)}) async-start(bf16[32,128,256]{2,1,0:T(8,128)(2,1)} %bitcast.67), calls=%async_computation.1 | async-start | bytes 4194304 | tf_op jit(solution)/shard_map/all_to_all | solution.py:81
  96.5 2.2 maximum_maximum_fusion
  99.5 4.8 %fusion.11 = f32[1024,1024]{0,1:T(8,128)S(1)} fusion(bf16[1024,1024]{0,1:T(8,128)(2,1)S(1)} %get-tuple-element.16, bf16[1024,1024]{0,1:T(8,128)(2,1)S(1)} %get-tuple-element.15, bf16[1024,1024]{0,1:T(8,128)(2,1)S(1)} %get-tuple-element.24, bf16[1024,1024]{0,1:T(8,128)(2,1)S(1)} %get-tuple-element.23), kind=kOutput, calls=%fused_computation.26 | convolution fusion | flops 4311744512 | bytes 12582912 | tf_op jit(solution)/shard_map/dot_general | solution.py:76
  109.5 2.3 %fusion.18 = f32[4,256,256]{1,2,0:T(8,128)} fusion(bf16[4,256,1024]{2,1,0:T(8,128)(2,1)S(1)} %get-tuple-element.48, bf16[4,256,1024]{2,1,0:T(8,128)(2,1)S(1)} %get-tuple-element.47, bf16[4,256,1024]{2,1,0:T(8,128)(2,1)S(1)} %copy-done.2, bf16[4,256,1024]{2,1,0:T(8,128)(2,1)S(1)} %copy-done.4), kind=kOutput, calls=%fused_computation.33 | convolution fusion | flops 1090519040 | bytes 9437184 | tf_op jit(solution)/shard_map/sik,sjk->sij/dot_general | solution.py:105
  111.8 81.3 %collective-permute-done.4 = f32[256,768]{0,1:T(8,128)S(1)} collective-permute-done((f32[256,768]{0,1:T(8,128)S(1)}, f32[256,768]{0,1:T(8,128)S(1)}, u32[]{:S(2)}, u32[]{:S(2)}) %collective-permute-start.4) | collective-permute-done | bytes 786464 | tf_op jit(solution)/shard_map/ppermute | solution.py:93
  193.1 16.4 %collective-permute-done.5 = f32[256,768]{0,1:T(8,128)S(1)} collective-permute-done((f32[256,768]{0,1:T(8,128)S(1)}, f32[256,768]{0,1:T(8,128)S(1)}, u32[]{:S(2)}, u32[]{:S(2)}) %collective-permute-start.5) | collective-permute-done | bytes 786464 | tf_op jit(solution)/shard_map/ppermute | solution.py:93
  209.5 2.6 %collective-permute-done.6 = f32[256,768]{0,1:T(8,128)S(1)} collective-permute-done((f32[256,768]{0,1:T(8,128)S(1)}, f32[256,768]{0,1:T(8,128)S(1)}, u32[]{:S(2)}, u32[]{:S(2)}) %collective-permute-start.6) | collective-permute-done | bytes 786464 | tf_op jit(solution)/shard_map/ppermute | solution.py:93
  219.2 2.5 %fusion.7 = bf16[4,256,1024]{1,2,0:T(8,128)(2,1)S(1)} fusion(s32[]{:T(128)S(6)} %select_n.316, f32[1,256,768]{1,2,0:T(8,128)S(1)} %copy-done.8, f32[1,256,768]{1,2,0:T(8,128)S(1)} %copy-done.7, f32[1,256,768]{1,2,0:T(8,128)S(1)} %copy-done.6, f32[1,256,768]{1,2,0:T(8,128)S(1)} %get-tuple-element.11, f32[4,256,256]{1,2,0:T(8,128)S(1)} %copy-done.9, ...), kind=kLoop, calls=%fused_computation.20 | loop fusion | flops 11534336 | bytes 10485764 | tf_op jit(solution)/shard_map/convert_element_type | solution.py:108
  221.7 2.4 %copy.40 = bf16[4,256,1024]{2,1,0:T(8,128)(2,1)} copy(bf16[4,256,1024]{1,2,0:T(8,128)(2,1)S(1)} %fusion.7) | data formatting | bytes 4194304 | tf_op jit(solution)/shard_map/convert_element_type | solution.py:108
  (76 shorter events, 32.0 us)
Async XLA Ops:
  0.0 0.7 copy-start
  0.0 5.0 %copy-start.3 = (bf16[4,256,1024]{2,1,0:T(8,128)(2,1)S(1)}, bf16[4,256,1024]{2,1,0:T(8,128)(2,1)}, u32[]{:S(2)}) copy-start(bf16[4,256,1024]{2,1,0:T(8,128)(2,1)} %param.8) | copy-start | bytes 6291460
  11.5 4.7 %copy-start.11 = (s32[1,1024]{1,0:T(1,128)S(1)}, s32[1,1024]{1,0:T(1,128)}, u32[]{:S(2)}) copy-start(s32[1,1024]{1,0:T(1,128)} %param.10) | copy-start | bytes 12292
  11.5 4.7 %copy-start.12 = (f32[1,1024]{1,0:T(1,128)S(1)}, f32[1,1024]{1,0:T(1,128)}, u32[]{:S(2)}) copy-start(f32[1,1024]{1,0:T(1,128)} %param.11) | copy-start | bytes 12292
  11.5 53.8 %all-to-all-start = ((bf16[2,8,128,1024]{3,2,0,1:T(8,128)(2,1)}), bf16[2,8,128,1024]{3,2,0,1:T(8,128)(2,1)}, u32[]{:S(2)}, u32[]{:S(2)}) async-start(bf16[2,8,128,1024]{3,2,0,1:T(8,128)(2,1)} %pad_maximum_fusion), calls=%async_computation | async-start | bytes 8388608 | tf_op jit(solution)/shard_map/all_to_all | solution.py:43
  16.2 4.8 %copy-start.2 = (bf16[4,256,1024]{2,1,0:T(8,128)(2,1)S(1)}, bf16[4,256,1024]{2,1,0:T(8,128)(2,1)}, u32[]{:S(2)}) copy-start(bf16[4,256,1024]{2,1,0:T(8,128)(2,1)} %param.7) | copy-start | bytes 6291460
  16.3 21.2 %collective-permute-start.3 = (f32[2,1024]{1,0:T(2,128)S(1)}, f32[2,1024]{1,0:T(2,128)S(1)}, u32[]{:S(2)}, u32[]{:S(2)}) collective-permute-start(f32[2,1024]{1,0:T(2,128)S(1)} %pad_maximum_fusion.6), channel_id=1, source_target_pairs={{0,0},{1,4},{2,8},{3,12},{4,16},{5,20},{6,24},{7,28},{8,1},{9,5},{... | collective-permute-start | bytes 24584 | tf_op jit(solution)/shard_map/ppermute | solution.py:48
  23.1 11.0 %copy-start.10 = (s32[4,1024]{1,0:T(4,128)S(1)}, s32[4,1024]{1,0:T(4,128)}, u32[]{:S(2)}) copy-start(s32[4,1024]{1,0:T(4,128)} %param.9) | copy-start | bytes 49156
  23.9 54.7 %collective-permute-start.2 = (bf16[2,256,512]{2,1,0:T(8,128)(2,1)}, bf16[2,256,512]{2,1,0:T(8,128)(2,1)}, u32[]{:S(2)}, u32[]{:S(2)}) collective-permute-start(bf16[2,256,512]{2,1,0:T(8,128)(2,1)} %pad_maximum_fusion.5), channel_id=1, source_target_pairs={{0,3},{1,0},{2,1},{3,2},{4,7},{5,4},{6,5},{7,6},{8,11},{9,8},{10,9... | collective-permute-start | bytes 1572872 | tf_op jit(solution)/shard_map/ppermute | solution.py:36
  26.3 52.4 %collective-permute-start.1 = (bf16[2,256,512]{1,2,0:T(8,128)(2,1)}, bf16[2,256,512]{1,2,0:T(8,128)(2,1)}, u32[]{:S(2)}, u32[]{:S(2)}) collective-permute-start(bf16[2,256,512]{1,2,0:T(8,128)(2,1)} %pad_maximum_fusion.4), channel_id=1, source_target_pairs={{0,2},{1,3},{2,0},{3,1},{4,6},{5,7},{6,4},{7,5},{8,10},{9,11},{10,... | collective-permute-start | bytes 1572872 | tf_op jit(solution)/shard_map/ppermute | solution.py:36
  32.3 46.3 %collective-permute-start = (bf16[2,256,512]{2,1,0:T(8,128)(2,1)}, bf16[2,256,512]{2,1,0:T(8,128)(2,1)}, u32[]{:S(2)}, u32[]{:S(2)}) collective-permute-start(bf16[2,256,512]{2,1,0:T(8,128)(2,1)} %pad_maximum_fusion.3), channel_id=1, source_target_pairs={{0,1},{1,2},{2,3},{3,0},{4,5},{5,6},{6,7},{7,4},{8,9},{9,10},{10,1... | collective-permute-start | bytes 1572872 | tf_op jit(solution)/shard_map/ppermute | solution.py:36
  74.1 8.4 %copy-start.13 = (bf16[2]{0:T(256)(128)(2,1)S(1)}, bf16[2]{0:T(256)(128)(2,1)}, u32[]{:S(2)}) copy-start(bf16[2]{0:T(256)(128)(2,1)} %constant.158.clone) | copy-start | bytes 16
  88.5 8.0 %copy-start.5 = (bf16[2,256,1024]{1,2,0:T(8,128)(2,1)S(1)}, bf16[2,256,1024]{1,2,0:T(8,128)(2,1)}, u32[]{:S(2)}) copy-start(bf16[2,256,1024]{1,2,0:T(8,128)(2,1)} %copy.35) | copy-start | bytes 3145732
  91.9 121.8 %all-to-all-start.1 = ((bf16[32,128,256]{2,1,0:T(8,128)(2,1)}), bf16[32,128,256]{2,1,0:T(8,128)(2,1)}, u32[]{:S(2)}, u32[]{:S(2)}) async-start(bf16[32,128,256]{2,1,0:T(8,128)(2,1)} %bitcast.67), calls=%async_computation.1 | async-start | bytes 4194304 | tf_op jit(solution)/shard_map/all_to_all | solution.py:81
  104.3 4.9 %copy-start.4 = (bf16[4,256,1024]{2,1,0:T(8,128)(2,1)S(1)}, bf16[4,256,1024]{2,1,0:T(8,128)(2,1)}, u32[]{:S(2)}) copy-start(bf16[4,256,1024]{2,1,0:T(8,128)(2,1)} %param.8) | copy-start | bytes 6291460
  104.6 88.5 %collective-permute-start.4 = (f32[256,768]{0,1:T(8,128)S(1)}, f32[256,768]{0,1:T(8,128)S(1)}, u32[]{:S(2)}, u32[]{:S(2)}) collective-permute-start(f32[256,768]{0,1:T(8,128)S(1)} %pad_maximum_fusion.1), channel_id=1, source_target_pairs={{0,1},{1,2},{2,3},{3,0},{4,5},{5,6},{6,7},{7,4},{8,9},{9,10},{10,1... | collective-permute-start | bytes 2359304 | tf_op jit(solution)/shard_map/ppermute | solution.py:93
  106.2 103.3 %collective-permute-start.5 = (f32[256,768]{0,1:T(8,128)S(1)}, f32[256,768]{0,1:T(8,128)S(1)}, u32[]{:S(2)}, u32[]{:S(2)}) collective-permute-start(f32[256,768]{0,1:T(8,128)S(1)} %pad_maximum_fusion.2), channel_id=1, source_target_pairs={{0,2},{1,3},{2,0},{3,1},{4,6},{5,7},{6,4},{7,5},{8,10},{9,11},{10,... | collective-permute-start | bytes 2359304 | tf_op jit(solution)/shard_map/ppermute | solution.py:93
  107.7 104.4 %collective-permute-start.6 = (f32[256,768]{0,1:T(8,128)S(1)}, f32[256,768]{0,1:T(8,128)S(1)}, u32[]{:S(2)}, u32[]{:S(2)}) collective-permute-start(f32[256,768]{0,1:T(8,128)S(1)} %slice.122), channel_id=1, source_target_pairs={{0,3},{1,0},{2,1},{3,2},{4,7},{5,4},{6,5},{7,6},{8,11},{9,8},{10,9... | collective-permute-start | bytes 2359304 | tf_op jit(solution)/shard_map/ppermute | solution.py:93
  217.3 1.1 copy-start.6
  217.3 1.4 copy-start.7
  217.3 1.6 copy-start.8
  217.3 1.9 copy-start.9
  219.2 4.9 %copy-start.1 = (s32[32,8]{0,1:T(8,128)S(1)}, s32[32,8]{0,1:T(8,128)}, u32[]{:S(2)}) copy-start(s32[32,8]{0,1:T(8,128)} %param.12) | copy-start | bytes 3076

commit v14 on v13

--- a/solution.py
+++ b/solution.py
@@ -41,6 +41,20 @@
     part_dest = q_dest // ch_dev - level * (rows // slab)
     outgoing = pair(lambda x: x.reshape(ch_dev, rows // slab, slab, width)[slot_dest, part_dest])
     arrived = lax.all_to_all(outgoing, "ch", split_axis=1, concat_axis=1, tiled=True)
+
+    sign = jnp.array([-1, 1], bf16)[:, None, None]
+    own = pair(lambda x: lax.dynamic_index_in_dim(x, level, 0, False))
+    own = jnp.roll(own, -level * rows, axis=-1)
+    own_cols = [sign * jnp.swapaxes(own[..., d * rows : (d + 1) * rows], -1, -2) for d in range(1, n_rows)]
+    factor = lax.dynamic_index_in_dim(pp_factor, level, 0, False).astype(bf16)
+    factor = jnp.roll(factor, -level * rows)
+    local_d = pp_factor.astype(bf16)[:, None, :]
+    left = jnp.concatenate([eta_pp * local_d, gamma_pp * local_d], axis=-1)
+    right = jnp.concatenate([gamma_pp, eta_pp], axis=-1)
+    diag = jnp.einsum("sik,sjk->sij", left, right, preferred_element_type=f32)
+    arrived, own, own_cols, factor, diag = lax.optimization_barrier(
+        (arrived, own, own_cols, factor, diag)
+    )
     a_eta = arrived[0].reshape(width, width)
     b_gamma = arrived[1].reshape(width, width)
 
@@ -55,22 +69,17 @@
     ph_t = ph_t - jnp.dot(b_gamma * weight, a_eta, preferred_element_type=f32)
     term_t = (ph_t * coef[:, None]).astype(bf16)
     ladder_in, _ = lax.optimization_barrier((ladder_in, term_t))
-    sign = jnp.array([-1, 1], bf16)[:, None, None]
-    own = pair(lambda x: lax.dynamic_index_in_dim(x, level, 0, False))
-    own = jnp.roll(own, -level * rows, axis=-1)
     grid = [[None] * n_rows for _ in range(n_rows)]
     for d in range(n_rows):
         grid[0][d] = own[..., d * rows : (d + 1) * rows]
     for d in range(1, n_rows):
         piece = ladder_in[n_rows - d - 1]
         succ = d % (n_rows - 1) + 1
-        grid[d][0] = sign * jnp.swapaxes(grid[0][d], -1, -2)
+        grid[d][0] = own_cols[d - 1]
         grid[d][d] = piece[..., :rows]
         grid[d][succ] = piece[..., rows:]
         grid[succ][d] = sign * jnp.swapaxes(piece[..., rows:], -1, -2)
     whole = jnp.concatenate([jnp.concatenate(line, axis=-1) for line in grid], axis=-2)
-    factor = lax.dynamic_index_in_dim(pp_factor, level, 0, False).astype(bf16)
-    factor = jnp.roll(factor, -level * rows)
     left = jnp.concatenate([whole[0] * factor, whole[1] * factor], axis=-1)
     right = jnp.concatenate([whole[1], whole[0]], axis=-1)
     ladder_c = lax.dot_general(
@@ -99,10 +108,6 @@
     back = jnp.einsum("gts,gtwi->sigw", onehot, landed, preferred_element_type=f32)
     back = back.reshape(ch_dev, rows, width)
 
-    local_d = pp_factor.astype(bf16)[:, None, :]
-    left = jnp.concatenate([eta_pp * local_d, gamma_pp * local_d], axis=-1)
-    right = jnp.concatenate([gamma_pp, eta_pp], axis=-1)
-    diag = jnp.einsum("sik,sjk->sij", left, right, preferred_element_type=f32)
     ladder = jnp.concatenate([ladder, diag], axis=-1)
     ladder = jnp.roll(ladder, (level + 1) * rows, axis=-1)
     return (ladder + back).astype(bf16)

time: 225 us -> 231 us (1.027)
  other arithmetic: 23 us -> 40.4 us
  waiting for transfers between devices: 128 us -> 113 us
  starting transfers between devices: 21.9 us -> 25.3 us
    all_to_all x1, waiting for transfers between devices: 27.8 us -> 6.51 us  [per_device(): lax.all_to_all(outgoing, 'ch', split_axis=1, concat_axis=1, tiled=True)]
    ppermute x1, waiting for transfers between devices: 0.01 us -> 19.3 us  [per_device(): lax.ppermute(jnp.concatenate([ph_factor.astype(f32), recouple], axis=0),...]
    ppermute x3, waiting for transfers between devices: 100 us -> 87.7 us  [per_device(): returned.append(lax.ppermute(sending[shift], 'row', pairs))]
    concatenate x1, other arithmetic: 2.17 us -> 12.5 us  [per_device(): jnp.concatenate([jnp.concatenate(line, axis=-1) for line in grid], axis=-2)]
    all_to_all x1, starting transfers between devices: 4.58 us -> 9.17 us  [per_device(): lax.all_to_all(returning.reshape(n_chan * n_rows, slab, rows), ('ch', 'ro...]
    mul x0 -> x2, local copies, waits for them, and re-layouts: none -> 3.59 us  [per_device(): grid[succ][d] = sign * jnp.swapaxes(piece[..., rows:], -1, -2)]
    reshape x2, local copies, waits for them, and re-layouts: 7.91 us -> 5.03 us  [per_device(): returning = term_t.reshape(n_chan, slab, n_rows, rows).transpose(0, 2, 1, 3)]
    optimization_barrier x0 -> x2, local copies, waits for them, and re-layouts: none -> 2.88 us  [per_device(): lax.optimization_barrier((arrived, own, own_cols, factor, diag))]
  transfers between devices with their start and end apart: 9 -> 9, of which waited for: 4 -> 4; matrix products, arithmetic and copies ran while one was open for 17% -> 22% of each run, Pallas kernels for 0% -> 0%
where the time goes in v14:
time: 231 us; the launch traced here: 230 us
  waiting for transfers between devices  113 us (49%)
  other arithmetic  40.4 us (17%)
  local copies, waits for them, and re-layouts  35.9 us (16%)
  starting transfers between devices  25.3 us (11%)
  matrix products  14.5 us (6%)
    ppermute x3, waiting for transfers between devices, per_device(): returned.append(lax.ppermute(sending[shift], 'row', pairs))  87.7 us
    ppermute x1, waiting for transfers between devices, per_device(): lax.ppermute(jnp.concatenate([ph_factor.astype(f32), recouple], axis=0),...  19.3 us
    concatenate x1, other arithmetic, per_device(): jnp.concatenate([jnp.concatenate(line, axis=-1) for line in grid], axis=-2)  12.5 us
    all_to_all x1, starting transfers between devices, per_device(): lax.all_to_all(returning.reshape(n_chan * n_rows, slab, rows), ('ch', 'ro...  9.17 us
    another operation x4, other arithmetic, per_device(): pair = lambda f: jnp.stack([f(eta_pp), f(gamma_pp)])  6.9 us
    all_to_all x1, waiting for transfers between devices, per_device(): lax.all_to_all(outgoing, 'ch', split_axis=1, concat_axis=1, tiled=True)  6.51 us
    gather x2, local copies, waits for them, and re-layouts, per_device(): x.reshape(ch_dev, rows // slab, slab, width)[slot_dest, part_dest]  5.63 us
    reshape x2, local copies, waits for them, and re-layouts, per_device(): returning = term_t.reshape(n_chan, slab, n_rows, rows).transpose(0, 2, 1, 3)  5.03 us
  transfers between devices with their start and end apart: 9, of which 4 were waited for; matrix products, arithmetic and copies ran while one was open for 22% of the time, Pallas kernels for 0%

profile of v14, /device:TPU:8, one launch (start us, length us, event | category | flops | bytes accessed | tf_op | source)
XLA Modules:
  0.0 230.0 jit_solution(3905785851454444615)
XLA Ops:
  1.3 3.6 %gather_fusion.2 = bf16[8,128,1024]{2,1,0:T(8,128)(2,1)} fusion(bf16[4,2,128,1024]{3,2,1,0:T(8,128)(2,1)} %bitcast.65, s32[8]{0:T(128)S(1)} %fusion.55), kind=kCustom, calls=%fused_computation.2 | custom fusion | bytes 4194368 | tf_op jit(solution)/shard_map/gather | solution.py:42
  4.9 2.0 gather_fusion.1
  7.0 4.6 %pad_maximum_fusion = bf16[2,8,128,1024]{3,2,0,1:T(8,128)(2,1)} fusion(bf16[1,8,128,1024]{3,2,0,1:T(8,128)(2,1)} %bitcast.69, bf16[1,8,128,1024]{3,2,0,1:T(8,128)(2,1)} %bitcast.70), kind=kLoop, calls=%fused_computation.24 | loop fusion | flops 2097152 | bytes 8388608 | tf_op jit(solution)/shard_map/stack | solution.py:24
  11.5 4.7 %all-to-all-start = ((bf16[2,8,128,1024]{3,2,0,1:T(8,128)(2,1)}), bf16[2,8,128,1024]{3,2,0,1:T(8,128)(2,1)}, u32[]{:S(2)}, u32[]{:S(2)}) async-start(bf16[2,8,128,1024]{3,2,0,1:T(8,128)(2,1)} %pad_maximum_fusion), calls=%async_computation | async-start | bytes 8388608 | tf_op jit(solution)/shard_map/all_to_all | solution.py:43
  16.3 3.3 %constant_dynamic-slice_fusion.1 = (bf16[1,256,1024]{2,1,0:T(8,128)(2,1)}, bf16[1,256,1024]{2,1,0:T(8,128)(2,1)S(1)}, bf16[1,256,1024]{2,1,0:T(8,128)(2,1)S(1)},...) fusion(bf16[4,256,1024]{2,1,0:T(8,128)(2,1)S(1)} %copy-done.1, ...), kind=kLoop, calls=%fused_computation.97 | loop fusion | bytes 8388624 | tf_op jit(solution)/shard_map/jit(dynamic_index_in_dim)/dynamic_slice | solution.py:27
  27.2 2.0 collective-permute-start.2
  29.3 2.3 %collective-permute-start.3 = (f32[2,1024]{1,0:T(2,128)S(1)}, f32[2,1024]{1,0:T(2,128)S(1)}, u32[]{:S(2)}, u32[]{:S(2)}) collective-permute-start(f32[2,1024]{1,0:T(2,128)S(1)} %pad_maximum_fusion.6), channel_id=1, source_target_pairs={{0,0},{1,4},{2,8},{3,12},{4,16},{5,20},{6,24},{7,28},{8,1},{9,5},{... | collective-permute-start | bytes 24584 | tf_op jit(solution)/shard_map/ppermute | solution.py:62
  37.1 2.3 %fusion.11 = f32[4,256,256]{2,1,0:T(8,128)} fusion(bf16[4,256,1024]{2,1,0:T(8,128)(2,1)S(1)} %get-tuple-element.61, bf16[4,256,1024]{2,1,0:T(8,128)(2,1)S(1)} %get-tuple-element.60, bf16[4,256,1024]{2,1,0:T(8,128)(2,1)S(1)} %copy-done.3, bf16[4,256,1024]{2,1,0:T(8,128)(2,1)S(1)} %copy-done.1), kind=kOutput, calls=%fused_computation.25 | convolution fusion | flops 1090519040 | bytes 9437184 | tf_op jit(solution)/shard_map/sik,sjk->sij/dot_general | solution.py:54
  39.5 19.3 %collective-permute-done.3 = f32[2,1024]{1,0:T(2,128)S(1)} collective-permute-done((f32[2,1024]{1,0:T(2,128)S(1)}, f32[2,1024]{1,0:T(2,128)S(1)}, u32[]{:S(2)}, u32[]{:S(2)}) %collective-permute-start.3) | collective-permute-done | bytes 8224 | tf_op jit(solution)/shard_map/ppermute | solution.py:62
  58.9 6.5 %all-to-all-done = bf16[2,8,128,1024]{3,2,0,1:T(8,128)(2,1)} async-done(((bf16[2,8,128,1024]{3,2,0,1:T(8,128)(2,1)}), bf16[2,8,128,1024]{3,2,0,1:T(8,128)(2,1)}, u32[]{:S(2)}, u32[]{:S(2)}) %all-to-all-start) | async-done | bytes 4194336 | tf_op jit(solution)/shard_map/all_to_all | solution.py:43
  65.4 2.8 %broadcast_multiply_fusion.2 = (bf16[1,8,128,1024]{3,2,0,1:T(8,128)(2,1)S(1)}, bf16[1,8,128,1024]{3,2,0,1:T(8,128)(2,1)S(1)}, bf16[1,8,128,1024]{3,2,0,1:T(8,128)(2,1)S(1)}, bf16[1,8,128,1024]{3,2,0,1:T(8,128)(2,1)S(1)}) fusion(bf16[1024]{0:T(1024)(128)(2,1)S(1)} %fusion.43, bf16[2,8,128,1024]{3,2,0,1:T(8,128)(2,1)} %all-to-all-done), kind=kLoop, calls=%fused_computation.66 | loop fusion | flops 2097152 | bytes 12584960 | tf_op jit(solution)/shard_map/mul | solution.py:69
  68.2 2.3 %fusion.60 = f32[1024,1024]{1,0:T(8,128)S(1)} fusion(bf16[1024,1024]{1,0:T(8,128)(2,1)S(1)} %bitcast.74, bf16[1024,1024]{1,0:T(8,128)(2,1)S(1)} %bitcast.75), kind=kOutput, calls=%fused_computation.138 | convolution fusion | flops 2147483648 | bytes 8388608 | tf_op jit(solution)/shard_map/dot_general | solution.py:68
  70.5 3.7 %multiply_convert_fusion = bf16[1024,1024]{1,0:T(8,128)(2,1)} fusion(f32[1024,1024]{1,0:T(8,128)S(1)} %fusion.60, f32[1024]{0:T(1024)S(1)} %bitcast.76, bf16[1024,1024]{1,0:T(8,128)(2,1)S(1)} %bitcast.72, bf16[1024,1024]{1,0:T(8,128)(2,1)S(1)} %bitcast.73), kind=kOutput, calls=%fused_computation.40 | convolution fusion | flops 2150629376 | bytes 10489856 | tf_op jit(solution)/shard_map/dot_general | solution.py:69
  75.1 2.1 copy.46
  77.2 3.3 %reshape.134 = bf16[8,128,4,256]{3,2,1,0:T(4,128)(2,1)S(1)} reshape(bf16[1024,1024]{1,0:T(8,128)(2,1)} %multiply_convert_fusion) | data formatting | bytes 4194304 | tf_op jit(solution)/shard_map/reshape | solution.py:89
  92.7 9.2 %all-to-all-start.1 = ((bf16[32,128,256]{2,1,0:T(8,128)(2,1)}), bf16[32,128,256]{2,1,0:T(8,128)(2,1)S(1)}, u32[]{:S(2)}, u32[]{:S(2)}) async-start(bf16[32,128,256]{2,1,0:T(8,128)(2,1)} %bitcast.68), calls=%async_computation.1 | async-start | bytes 4194304 | tf_op jit(solution)/shard_map/all_to_all | solution.py:90
  101.9 12.5 %maximum_maximum_fusion = bf16[2,1024,1024]{2,1,0:T(8,128)(2,1)S(1)} fusion(bf16[2,256,256]{2,1,0:T(8,128)(2,1)S(1)} %slice.96, bf16[2,256,256]{2,1,0:T(8,128)(2,1)} %copy.50, bf16[2,256,256]{2,1,0:T(8,128)(2,1)} %copy.49, bf16[2,256,256]{2,1,0:T(8,128)(2,1)} %get-tuple-element.22, bf16[2,256,512]{2,1,0:T(8,128)(2,1)} %collective-permute-done.1, ...), kind=kLoop, calls=%fused_computation.32 | loop fusion | flops 46137344 | bytes 8388608 | tf_op jit(solution)/shard_map/concatenate | solution.py:82
  115.1 4.5 %fusion.18 = f32[1024,1024]{0,1:T(8,128)S(1)} fusion(bf16[1024,1024]{1,0:T(8,128)(2,1)S(1)} %get-tuple-element.30, bf16[1024,1024]{1,0:T(8,128)(2,1)S(1)} %get-tuple-element.29, bf16[1024,1024]{1,0:T(8,128)(2,1)S(1)} %get-tuple-element.38, bf16[1024,1024]{1,0:T(8,128)(2,1)S(1)} %get-tuple-element.37), kind=kOutput, calls=%fused_computation.33 | convolution fusion | flops 4311744512 | bytes 12582912 | tf_op jit(solution)/shard_map/dot_general | solution.py:85
  122.9 2.4 %collective-permute-start.5 = (f32[256,768]{0,1:T(8,128)}, f32[256,768]{0,1:T(8,128)}, u32[]{:S(2)}, u32[]{:S(2)}) collective-permute-start(f32[256,768]{0,1:T(8,128)} %pad_maximum_fusion.2), channel_id=1, source_target_pairs={{0,2},{1,3},{2,0},{3,1},{4,6},{5,7},{6,4},{7,5},{8,10},{9,11},{10,... | collective-permute-start | bytes 2359304 | tf_op jit(solution)/shard_map/ppermute | solution.py:102
  130.0 68.6 %collective-permute-done.5 = f32[256,768]{0,1:T(8,128)} collective-permute-done((f32[256,768]{0,1:T(8,128)}, f32[256,768]{0,1:T(8,128)}, u32[]{:S(2)}, u32[]{:S(2)}) %collective-permute-start.5) | collective-permute-done | bytes 786464 | tf_op jit(solution)/shard_map/ppermute | solution.py:102
  198.6 19.0 %collective-permute-done.6 = f32[256,768]{0,1:T(8,128)} collective-permute-done((f32[256,768]{0,1:T(8,128)}, f32[256,768]{0,1:T(8,128)}, u32[]{:S(2)}, u32[]{:S(2)}) %collective-permute-start.6) | collective-permute-done | bytes 786464 | tf_op jit(solution)/shard_map/ppermute | solution.py:102
  217.6 3.7 %select_bitcast_fusion = (f32[1,256,768]{1,2,0:T(8,128)}, f32[1,256,768]{1,2,0:T(8,128)}, f32[1,256,768]{1,2,0:T(8,128)}, f32[1,256,768]{1,2,0:T(8,128)}) fusion(f32[256,768]{0,1:T(8,128)} %collective-permute-done.5, f32[256,768]{0,1:T(8,128)} %collective-permute-done.6, f32[256,768]{0,1:T(8,128)} %collective-permute-done.4, f32[1024,1024]{0,1:T(8,128)} %copy-done.9, ...), kind=kLoop, calls=%fused_computation.72 | loop fusion | flops 2359296 | bytes 6291468 | tf_op jit(solution)/shard_map/stack | solution.py:103
  225.1 2.5 %fusion.7 = bf16[4,256,1024]{1,2,0:T(8,128)(2,1)S(1)} fusion(s32[]{:T(128)S(6)} %select_n.316, f32[1,256,768]{1,2,0:T(8,128)S(1)} %copy-done.8, f32[1,256,768]{1,2,0:T(8,128)S(1)} %copy-done.7, f32[1,256,768]{1,2,0:T(8,128)S(1)} %copy-done.6, f32[1,256,768]{1,2,0:T(8,128)S(1)} %copy-done.5, f32[4,256,256]{1,2,0:T(8,128)S(1)} %copy.52, ...), kind=kLoop, calls=%fused_computation.20 | loop fusion | flops 11534336 | bytes 10485764 | tf_op jit(solution)/shard_map/convert_element_type | solution.py:113
  227.6 2.4 %copy.58 = bf16[4,256,1024]{2,1,0:T(8,128)(2,1)} copy(bf16[4,256,1024]{1,2,0:T(8,128)(2,1)S(1)} %fusion.7) | data formatting | bytes 4194304 | tf_op jit(solution)/shard_map/convert_element_type | solution.py:113
  (79 shorter events, 39.8 us)
Async XLA Ops:
  0.0 0.7 copy-start
  0.0 4.9 %copy-start.2 = (bf16[4,256,1024]{2,1,0:T(8,128)(2,1)S(1)}, bf16[4,256,1024]{2,1,0:T(8,128)(2,1)}, u32[]{:S(2)}) copy-start(bf16[4,256,1024]{2,1,0:T(8,128)(2,1)} %param.7) | copy-start | bytes 6291460
  11.5 4.8 %copy-start.1 = (bf16[4,256,1024]{2,1,0:T(8,128)(2,1)S(1)}, bf16[4,256,1024]{2,1,0:T(8,128)(2,1)}, u32[]{:S(2)}) copy-start(bf16[4,256,1024]{2,1,0:T(8,128)(2,1)} %param.8) | copy-start | bytes 6291460
  11.5 53.8 %all-to-all-start = ((bf16[2,8,128,1024]{3,2,0,1:T(8,128)(2,1)}), bf16[2,8,128,1024]{3,2,0,1:T(8,128)(2,1)}, u32[]{:S(2)}, u32[]{:S(2)}) async-start(bf16[2,8,128,1024]{3,2,0,1:T(8,128)(2,1)} %pad_maximum_fusion), calls=%async_computation | async-start | bytes 8388608 | tf_op jit(solution)/shard_map/all_to_all | solution.py:43
  19.7 9.6 %copy-start.12 = (s32[1,1024]{1,0:T(1,128)S(1)}, s32[1,1024]{1,0:T(1,128)}, u32[]{:S(2)}) copy-start(s32[1,1024]{1,0:T(1,128)} %param.10) | copy-start | bytes 12292
  19.7 9.6 %copy-start.13 = (f32[1,1024]{1,0:T(1,128)S(1)}, f32[1,1024]{1,0:T(1,128)}, u32[]{:S(2)}) copy-start(f32[1,1024]{1,0:T(1,128)} %param.11) | copy-start | bytes 12292
  19.7 14.0 %copy-start.10 = (s32[4,1024]{1,0:T(4,128)S(1)}, s32[4,1024]{1,0:T(4,128)}, u32[]{:S(2)}) copy-start(s32[4,1024]{1,0:T(4,128)} %param.9) | copy-start | bytes 49156
  20.6 53.6 %collective-permute-start = (bf16[2,256,512]{2,1,0:T(8,128)(2,1)}, bf16[2,256,512]{2,1,0:T(8,128)(2,1)}, u32[]{:S(2)}, u32[]{:S(2)}) collective-permute-start(bf16[2,256,512]{2,1,0:T(8,128)(2,1)} %pad_maximum_fusion.3), channel_id=1, source_target_pairs={{0,1},{1,2},{2,3},{3,0},{4,5},{5,6},{6,7},{7,4},{8,9},{9,10},{10,1... | collective-permute-start | bytes 1572872 | tf_op jit(solution)/shard_map/ppermute | solution.py:36
  23.3 12.4 %copy-start.11 = (bf16[2]{0:T(256)(128)(2,1)S(1)}, bf16[2]{0:T(256)(128)(2,1)}, u32[]{:S(2)}) copy-start(bf16[2]{0:T(256)(128)(2,1)} %constant.158.clone) | copy-start | bytes 16
  24.2 50.0 %collective-permute-start.1 = (bf16[2,256,512]{2,1,0:T(8,128)(2,1)}, bf16[2,256,512]{2,1,0:T(8,128)(2,1)}, u32[]{:S(2)}, u32[]{:S(2)}) collective-permute-start(bf16[2,256,512]{2,1,0:T(8,128)(2,1)} %pad_maximum_fusion.4), channel_id=1, source_target_pairs={{0,2},{1,3},{2,0},{3,1},{4,6},{5,7},{6,4},{7,5},{8,10},{9,11},{10,... | collective-permute-start | bytes 1572872 | tf_op jit(solution)/shard_map/ppermute | solution.py:36
  27.2 47.0 %collective-permute-start.2 = (bf16[2,256,512]{2,1,0:T(8,128)(2,1)}, bf16[2,256,512]{2,1,0:T(8,128)(2,1)}, u32[]{:S(2)}, u32[]{:S(2)}) collective-permute-start(bf16[2,256,512]{2,1,0:T(8,128)(2,1)} %pad_maximum_fusion.5), channel_id=1, source_target_pairs={{0,3},{1,0},{2,1},{3,2},{4,7},{5,4},{6,5},{7,6},{8,11},{9,8},{10,9... | collective-permute-start | bytes 1572872 | tf_op jit(solution)/shard_map/ppermute | solution.py:36
  29.3 29.6 %collective-permute-start.3 = (f32[2,1024]{1,0:T(2,128)S(1)}, f32[2,1024]{1,0:T(2,128)S(1)}, u32[]{:S(2)}, u32[]{:S(2)}) collective-permute-start(f32[2,1024]{1,0:T(2,128)S(1)} %pad_maximum_fusion.6), channel_id=1, source_target_pairs={{0,0},{1,4},{2,8},{3,12},{4,16},{5,20},{6,24},{7,28},{8,1},{9,5},{... | collective-permute-start | bytes 24584 | tf_op jit(solution)/shard_map/ppermute | solution.py:62
  33.7 3.0 %copy-start.3 = (bf16[4,256,1024]{2,1,0:T(8,128)(2,1)S(1)}, bf16[4,256,1024]{2,1,0:T(8,128)(2,1)}, u32[]{:S(2)}) copy-start(bf16[4,256,1024]{2,1,0:T(8,128)(2,1)} %param.7) | copy-start | bytes 6291460
  91.0 10.9 %copy-start.4 = (bf16[2,256,1024]{2,1,0:T(8,128)(2,1)S(1)}, bf16[2,256,1024]{2,1,0:T(8,128)(2,1)}, u32[]{:S(2)}) copy-start(bf16[2,256,1024]{2,1,0:T(8,128)(2,1)} %copy.51) | copy-start | bytes 3145732
  92.7 128.7 %all-to-all-start.1 = ((bf16[32,128,256]{2,1,0:T(8,128)(2,1)}), bf16[32,128,256]{2,1,0:T(8,128)(2,1)S(1)}, u32[]{:S(2)}, u32[]{:S(2)}) async-start(bf16[32,128,256]{2,1,0:T(8,128)(2,1)} %bitcast.68), calls=%async_computation.1 | async-start | bytes 4194304 | tf_op jit(solution)/shard_map/all_to_all | solution.py:90
  119.7 2.2 copy-start.9
  122.9 75.7 %collective-permute-start.5 = (f32[256,768]{0,1:T(8,128)}, f32[256,768]{0,1:T(8,128)}, u32[]{:S(2)}, u32[]{:S(2)}) collective-permute-start(f32[256,768]{0,1:T(8,128)} %pad_maximum_fusion.2), channel_id=1, source_target_pairs={{0,2},{1,3},{2,0},{3,1},{4,6},{5,7},{6,4},{7,5},{8,10},{9,11},{10,... | collective-permute-start | bytes 2359304 | tf_op jit(solution)/shard_map/ppermute | solution.py:102
  125.4 92.3 %collective-permute-start.6 = (f32[256,768]{0,1:T(8,128)}, f32[256,768]{0,1:T(8,128)}, u32[]{:S(2)}, u32[]{:S(2)}) collective-permute-start(f32[256,768]{0,1:T(8,128)} %slice.124), channel_id=1, source_target_pairs={{0,3},{1,0},{2,1},{3,2},{4,7},{5,4},{6,5},{7,6},{8,11},{9,8},{10,9... | collective-permute-start | bytes 2359304 | tf_op jit(solution)/shard_map/ppermute | solution.py:102
  126.8 90.8 %collective-permute-start.4 = (f32[256,768]{0,1:T(8,128)}, f32[256,768]{0,1:T(8,128)}, u32[]{:S(2)}, u32[]{:S(2)}) collective-permute-start(f32[256,768]{0,1:T(8,128)} %pad_maximum_fusion.1), channel_id=1, source_target_pairs={{0,1},{1,2},{2,3},{3,0},{4,5},{5,6},{6,7},{7,4},{8,9},{9,10},{10,1... | collective-permute-start | bytes 2359304 | tf_op jit(solution)/shard_map/ppermute | solution.py:102
  223.2 1.1 copy-start.5
  223.2 1.4 copy-start.6
  223.2 1.6 copy-start.7
  223.3 1.8 copy-start.8

commit v15 on v13

--- a/solution.py
+++ b/solution.py
@@ -95,9 +95,9 @@
         [lax.select_n((level - s) % n_rows, *returned) for s in range(n_rows)]
     )
     chosen = src_slot[:, mine].reshape(n_chan, ch_dev)
-    onehot = (chosen[:, :, None] == jnp.arange(ch_dev, dtype=jnp.int32)[None, None, :]).astype(bf16)
-    back = jnp.einsum("gts,gtwi->sigw", onehot, landed, preferred_element_type=f32)
-    back = back.reshape(ch_dev, rows, width)
+    picked = chosen[None, :, :] == jnp.arange(ch_dev, dtype=jnp.int32)[:, None, None]
+    back = jnp.where(picked[..., None, None], landed[None].astype(f32), 0.0).sum(axis=2)
+    back = back.transpose(0, 3, 1, 2).reshape(ch_dev, rows, width)
 
     local_d = pp_factor.astype(bf16)[:, None, :]
     left = jnp.concatenate([eta_pp * local_d, gamma_pp * local_d], axis=-1)

time: 225 us -> 227 us (level)
  other arithmetic: 23 us -> 33.6 us
  waiting for transfers between devices: 128 us -> 119 us
    ppermute x3, waiting for transfers between devices: 100 us -> 91.5 us  [per_device(): returned.append(lax.ppermute(sending[shift], 'row', pairs))]
    dot_general x1, matrix products: 2.32 us -> 5.14 us  [per_device(): diag = jnp.einsum('sik,sjk->sij', left, right, preferred_element_type=f32)]
    reduce_sum x0 -> x1, other arithmetic: none -> 2.75 us  [per_device(): jnp.where(picked[..., None, None], landed[None].astype(f32), 0.0)]
  transfers between devices with their start and end apart: 9 -> 9, of which waited for: 4 -> 4; matrix products, arithmetic and copies ran while one was open for 17% -> 21% of each run, Pallas kernels for 0% -> 0%
where the time goes in v15:
time: 227 us; the launch traced here: 226 us
  waiting for transfers between devices  119 us (52%)
  local copies, waits for them, and re-layouts  34.7 us (15%)
  other arithmetic  33.6 us (15%)
  starting transfers between devices  21.8 us (10%)
  matrix products  15.9 us (7%)
    ppermute x3, waiting for transfers between devices, per_device(): returned.append(lax.ppermute(sending[shift], 'row', pairs))  91.5 us
    all_to_all x1, waiting for transfers between devices, per_device(): lax.all_to_all(outgoing, 'ch', split_axis=1, concat_axis=1, tiled=True)  28 us
    reshape x2, local copies, waits for them, and re-layouts, per_device(): returning = term_t.reshape(n_chan, slab, n_rows, rows).transpose(0, 2, 1, 3)  7.95 us
    ppermute x3, starting transfers between devices, per_device(): lax.ppermute(jnp.concatenate([own_blk, next_blk], axis=-1), 'row', pairs)  6.07 us
    gather x2, local copies, waits for them, and re-layouts, per_device(): x.reshape(ch_dev, rows // slab, slab, width)[slot_dest, part_dest]  5.64 us
    another operation x3, other arithmetic, per_device(): pair = lambda f: jnp.stack([f(eta_pp), f(gamma_pp)])  5.43 us
    dot_general x1, matrix products, per_device(): diag = jnp.einsum('sik,sjk->sij', left, right, preferred_element_type=f32)  5.14 us
    dot_general x1, matrix products, per_device(): lax.dot_general(left, right, (((1,), (1,)), ((), ())), preferred_element_...  4.73 us
  transfers between devices with their start and end apart: 9, of which 4 were waited for; matrix products, arithmetic and copies ran while one was open for 21% of the time, Pallas kernels for 0%

profile of v15, /device:TPU:8, one launch (start us, length us, event | category | flops | bytes accessed | tf_op | source)
XLA Modules:
  0.0 225.8 jit_solution(16909420977105538553)
XLA Ops:
  1.3 3.6 %gather_fusion.1 = bf16[8,128,1024]{2,1,0:T(8,128)(2,1)} fusion(bf16[4,2,128,1024]{3,2,1,0:T(8,128)(2,1)} %bitcast.61, s32[8]{0:T(128)S(1)} %fusion.51), kind=kCustom, calls=%fused_computation.1 | custom fusion | bytes 4194368 | tf_op jit(solution)/shard_map/gather | solution.py:42
  7.0 4.5 %pad_maximum_fusion = bf16[2,8,128,1024]{3,2,0,1:T(8,128)(2,1)} fusion(bf16[1,8,128,1024]{3,2,0,1:T(8,128)(2,1)} %bitcast.66, bf16[1,8,128,1024]{3,2,0,1:T(8,128)(2,1)} %bitcast.65), kind=kLoop, calls=%fused_computation.25 | loop fusion | flops 2097152 | bytes 8388608 | tf_op jit(solution)/shard_map/stack | solution.py:24
  11.5 4.7 %all-to-all-start = ((bf16[2,8,128,1024]{3,2,0,1:T(8,128)(2,1)}), bf16[2,8,128,1024]{3,2,0,1:T(8,128)(2,1)}, u32[]{:S(2)}, u32[]{:S(2)}) async-start(bf16[2,8,128,1024]{3,2,0,1:T(8,128)(2,1)} %pad_maximum_fusion), calls=%async_computation | async-start | bytes 8388608 | tf_op jit(solution)/shard_map/all_to_all | solution.py:43
  18.4 2.6 %constant_dynamic-slice_fusion.8 = (bf16[1,256,1024]{2,1,0:T(8,128)(2,1)}, bf16[1,256,1024]{2,1,0:T(8,128)(2,1)S(1)}, bf16[1,256,1024]{2,1,0:T(8,128)(2,1)S(1)}, bf16[1,256,1024]{2,1,0:T(8,128)(2,1)S(1)}) fusion(bf16[4,256,1024]{2,1,0:T(8,128)(2,1)} %param.8, s32[]{:T(128)S(6)} %select_n.267, s32[]{:T(128)S(6)} %select_n.278, s32[]{:T(128)S(6)} %select_n.275, ...), kind=kLoop, calls=%fused_computation.103 | loop fusion | bytes 4194320 | tf_op jit(solution)/shard_map/jit(dynamic_index_in_dim)/dynamic_slice | solution.py:59
  26.3 4.2 %collective-permute-start.1 = (bf16[2,256,512]{1,2,0:T(8,128)(2,1)}, bf16[2,256,512]{1,2,0:T(8,128)(2,1)}, u32[]{:S(2)}, u32[]{:S(2)}) collective-permute-start(bf16[2,256,512]{1,2,0:T(8,128)(2,1)} %pad_maximum_fusion.4), channel_id=1, source_target_pairs={{0,2},{1,3},{2,0},{3,1},{4,6},{5,7},{6,4},{7,5},{8,10},{9,11},{10,... | collective-permute-start | bytes 1572872 | tf_op jit(solution)/shard_map/ppermute | solution.py:36
  37.4 28.0 %all-to-all-done = bf16[2,8,128,1024]{3,2,0,1:T(8,128)(2,1)} async-done(((bf16[2,8,128,1024]{3,2,0,1:T(8,128)(2,1)}), bf16[2,8,128,1024]{3,2,0,1:T(8,128)(2,1)}, u32[]{:S(2)}, u32[]{:S(2)}) %all-to-all-start) | async-done | bytes 4194336 | tf_op jit(solution)/shard_map/all_to_all | solution.py:43
  65.4 2.8 %broadcast_multiply_fusion.4 = (bf16[1,8,128,1024]{3,2,0,1:T(8,128)(2,1)S(1)}, bf16[1,8,128,1024]{3,2,0,1:T(8,128)(2,1)S(1)}, bf16[1,8,128,1024]{3,2,0,1:T(8,128)(2,1)S(1)}, bf16[1,8,128,1024]{3,2,0,1:T(8,128)(2,1)S(1)}) fusion(bf16[1024]{0:T(1024)(128)(2,1)S(1)} %fusion.39, bf16[2,8,128,1024]{3,2,0,1:T(8,128)(2,1)} %all-to-all-done), kind=kLoop, calls=%fused_computation.68 | loop fusion | flops 2097152 | bytes 12584960 | tf_op jit(solution)/shard_map/mul | solution.py:55
  68.1 2.3 %fusion.56 = f32[1024,1024]{1,0:T(8,128)S(1)} fusion(bf16[1024,1024]{1,0:T(8,128)(2,1)S(1)} %bitcast.69, bf16[1024,1024]{1,0:T(8,128)(2,1)S(1)} %bitcast.70), kind=kOutput, calls=%fused_computation.136 | convolution fusion | flops 2147483648 | bytes 8388608 | tf_op jit(solution)/shard_map/dot_general | solution.py:54
  70.5 3.7 %multiply_convert_fusion = bf16[1024,1024]{1,0:T(8,128)(2,1)} fusion(f32[1024,1024]{1,0:T(8,128)S(1)} %fusion.56, f32[1024]{0:T(1024)S(1)} %bitcast.71, bf16[1024,1024]{1,0:T(8,128)(2,1)S(1)} %bitcast.67, bf16[1024,1024]{1,0:T(8,128)(2,1)S(1)} %bitcast.68), kind=kOutput, calls=%fused_computation.42 | convolution fusion | flops 2150629376 | bytes 10489856 | tf_op jit(solution)/shard_map/dot_general | solution.py:55
  74.1 4.5 %reshape.143 = bf16[8,128,4,256]{3,2,1,0:T(4,128)(2,1)} reshape(bf16[1024,1024]{1,0:T(8,128)(2,1)} %multiply_convert_fusion) | data formatting | bytes 4194304 | tf_op jit(solution)/shard_map/reshape | solution.py:80
  82.5 2.4 %fusion.36 = (bf16[2,256,256]{1,2,0:T(8,128)(2,1)S(1)}, bf16[2,256,256]{1,2,0:T(8,128)(2,1)}, bf16[2,256,256]{1,2,0:T(8,128)(2,1)}, bf16[2,256,256]{2,1,0:T(8,12...) fusion(bf16[2,256,1024]{2,1,0:T(8,128)(2,1)S(1)} %fusion.26, ...), kind=kLoop, calls=%fused_computation.90 | loop fusion | flops 786432 | bytes 3932164 | tf_op jit(solution)/shard_map/mul | solution.py:67
  88.5 3.4 %copy.52 = bf16[8,128,4,256]{3,1,2,0:T(8,128)(2,1)} copy(bf16[8,128,4,256]{3,2,1,0:T(4,128)(2,1)} %reshape.143) | data formatting | bytes 4194304 | tf_op jit(solution)/shard_map/reshape | solution.py:80
  92.0 4.6 %all-to-all-start.1 = ((bf16[32,128,256]{2,1,0:T(8,128)(2,1)}), bf16[32,128,256]{2,1,0:T(8,128)(2,1)}, u32[]{:S(2)}, u32[]{:S(2)}) async-start(bf16[32,128,256]{2,1,0:T(8,128)(2,1)} %bitcast.64), calls=%async_computation.1 | async-start | bytes 4194304 | tf_op jit(solution)/shard_map/all_to_all | solution.py:81
  96.6 2.2 maximum_maximum_fusion
  99.5 4.7 %fusion.11 = f32[1024,1024]{0,1:T(8,128)S(1)} fusion(bf16[1024,1024]{0,1:T(8,128)(2,1)S(1)} %get-tuple-element.16, bf16[1024,1024]{0,1:T(8,128)(2,1)S(1)} %get-tuple-element.15, bf16[1024,1024]{0,1:T(8,128)(2,1)S(1)} %get-tuple-element.24, bf16[1024,1024]{0,1:T(8,128)(2,1)S(1)} %get-tuple-element.23), kind=kOutput, calls=%fused_computation.27 | convolution fusion | flops 4311744512 | bytes 12582912 | tf_op jit(solution)/shard_map/dot_general | solution.py:76
  113.1 2.4 %broadcast_multiply_fusion.1 = (bf16[4,256,1024]{2,1,0:T(8,128)(2,1)}, bf16[4,256,1024]{2,1,0:T(8,128)(2,1)}) fusion(bf16[4,256,1024]{2,1,0:T(8,128)(2,1)S(1)} %copy-done.1, bf16[4,1024]{1,0:T(4,128)(2,1)S(1)} %convert_element_type.41, bf16[4,256,1024]{2,1,0:T(8,128)(2,1)S(1)} %copy-done.3), kind=kLoop, calls=%fused_computation.65 | loop fusion | flops 2097152 | bytes 8396800 | tf_op jit(solution)/shard_map/mul | solution.py:103
  115.6 5.1 %fusion.18 = f32[4,256,256]{1,2,0:T(8,128)} fusion(bf16[4,256,1024]{2,1,0:T(8,128)(2,1)} %get-tuple-element.48, bf16[4,256,1024]{2,1,0:T(8,128)(2,1)} %get-tuple-element.47, bf16[4,256,1024]{2,1,0:T(8,128)(2,1)S(1)} %copy-done.1, bf16[4,256,1024]{2,1,0:T(8,128)(2,1)} %param.8), kind=kOutput, calls=%fused_computation.34 | convolution fusion | flops 1090519040 | bytes 9437184 | tf_op jit(solution)/shard_map/sik,sjk->sij/dot_general | solution.py:105
  120.7 72.5 %collective-permute-done.4 = f32[256,768]{0,1:T(8,128)S(1)} collective-permute-done((f32[256,768]{0,1:T(8,128)}, f32[256,768]{0,1:T(8,128)S(1)}, u32[]{:S(2)}, u32[]{:S(2)}) %collective-permute-start.4) | collective-permute-done | bytes 786464 | tf_op jit(solution)/shard_map/ppermute | solution.py:93
  193.2 16.4 %collective-permute-done.5 = f32[256,768]{0,1:T(8,128)} collective-permute-done((f32[256,768]{0,1:T(8,128)}, f32[256,768]{0,1:T(8,128)}, u32[]{:S(2)}, u32[]{:S(2)}) %collective-permute-start.5) | collective-permute-done | bytes 786464 | tf_op jit(solution)/shard_map/ppermute | solution.py:93
  209.6 2.6 %collective-permute-done.6 = f32[256,768]{0,1:T(8,128)} collective-permute-done((f32[256,768]{0,1:T(8,128)}, f32[256,768]{0,1:T(8,128)}, u32[]{:S(2)}, u32[]{:S(2)}) %collective-permute-start.6) | collective-permute-done | bytes 786464 | tf_op jit(solution)/shard_map/ppermute | solution.py:93
  212.2 3.5 %select_bitcast_fusion = (f32[1,256,768]{1,2,0:T(8,128)S(1)}, f32[1,256,768]{1,2,0:T(8,128)}, f32[1,256,768]{1,2,0:T(8,128)}, f32[1,256,768]{1,2,0:T(8,128)}) fusion(f32[256,768]{0,1:T(8,128)} %collective-permute-done.5, f32[256,768]{0,1:T(8,128)} %collective-permute-done.6, f32[256,768]{0,1:T(8,128)} %copy-done.10, f32[1024,1024]{0,1:T(8,128)} %copy-done.8, ...), kind=kLoop, calls=%fused_computation.72 | loop fusion | flops 2359296 | bytes 6291468 | tf_op jit(solution)/shard_map/stack | solution.py:94
  218.1 2.8 %select_reduce_fusion = f32[4,8,128,256]{3,2,1,0:T(8,128)S(1)} fusion(f32[8,4,128,256]{3,2,1,0:T(8,128)S(1)} %bitcast.63, pred[4,8,4]{2,1,0:T(8,128)(4,1)S(1)} %iota_compare_fusion), kind=kLoop, calls=%fused_computation.3 | loop fusion | flops 7340032 | bytes 8388736 | tf_op jit(solution)/shard_map/reduce_sum | solution.py:99
  220.9 2.5 %fusion.7 = bf16[4,256,1024]{1,2,0:T(8,128)(2,1)S(1)} fusion(s32[]{:T(128)S(6)} %select_n.320, f32[1,256,768]{1,2,0:T(8,128)S(1)} %copy-done.7, f32[1,256,768]{1,2,0:T(8,128)S(1)} %copy-done.6, f32[1,256,768]{1,2,0:T(8,128)S(1)} %copy-done.5, f32[1,256,768]{1,2,0:T(8,128)S(1)} %get-tuple-element.11, f32[4,256,256]{1,2,0:T(8,128)S(1)} %copy-done.9, ...), kind=kLoop, calls=%fused_computation.21 | loop fusion | flops 11534336 | bytes 10485764 | tf_op jit(solution)/shard_map/convert_element_type | solution.py:108
  223.4 2.4 %copy.54 = bf16[4,256,1024]{2,1,0:T(8,128)(2,1)} copy(bf16[4,256,1024]{1,2,0:T(8,128)(2,1)S(1)} %fusion.7) | data formatting | bytes 4194304 | tf_op jit(solution)/shard_map/convert_element_type | solution.py:108
  (79 shorter events, 37.0 us)
Async XLA Ops:
  0.0 0.7 copy-start
  0.0 5.0 %copy-start.2 = (bf16[4,256,1024]{2,1,0:T(8,128)(2,1)S(1)}, bf16[4,256,1024]{2,1,0:T(8,128)(2,1)}, u32[]{:S(2)}) copy-start(bf16[4,256,1024]{2,1,0:T(8,128)(2,1)} %param.8) | copy-start | bytes 6291460
  11.5 4.7 %copy-start.12 = (s32[1,1024]{1,0:T(1,128)S(1)}, s32[1,1024]{1,0:T(1,128)}, u32[]{:S(2)}) copy-start(s32[1,1024]{1,0:T(1,128)} %param.10) | copy-start | bytes 12292
  11.5 4.7 %copy-start.13 = (f32[1,1024]{1,0:T(1,128)S(1)}, f32[1,1024]{1,0:T(1,128)}, u32[]{:S(2)}) copy-start(f32[1,1024]{1,0:T(1,128)} %param.11) | copy-start | bytes 12292
  11.5 53.8 %all-to-all-start = ((bf16[2,8,128,1024]{3,2,0,1:T(8,128)(2,1)}), bf16[2,8,128,1024]{3,2,0,1:T(8,128)(2,1)}, u32[]{:S(2)}, u32[]{:S(2)}) async-start(bf16[2,8,128,1024]{3,2,0,1:T(8,128)(2,1)} %pad_maximum_fusion), calls=%async_computation | async-start | bytes 8388608 | tf_op jit(solution)/shard_map/all_to_all | solution.py:43
  16.2 4.8 %copy-start.1 = (bf16[4,256,1024]{2,1,0:T(8,128)(2,1)S(1)}, bf16[4,256,1024]{2,1,0:T(8,128)(2,1)}, u32[]{:S(2)}) copy-start(bf16[4,256,1024]{2,1,0:T(8,128)(2,1)} %param.7) | copy-start | bytes 6291460
  16.3 21.0 %collective-permute-start.3 = (f32[2,1024]{1,0:T(2,128)S(1)}, f32[2,1024]{1,0:T(2,128)S(1)}, u32[]{:S(2)}, u32[]{:S(2)}) collective-permute-start(f32[2,1024]{1,0:T(2,128)S(1)} %pad_maximum_fusion.6), channel_id=1, source_target_pairs={{0,0},{1,4},{2,8},{3,12},{4,16},{5,20},{6,24},{7,28},{8,1},{9,5},{... | collective-permute-start | bytes 24584 | tf_op jit(solution)/shard_map/ppermute | solution.py:48
  23.1 11.0 %copy-start.11 = (s32[4,1024]{1,0:T(4,128)S(1)}, s32[4,1024]{1,0:T(4,128)}, u32[]{:S(2)}) copy-start(s32[4,1024]{1,0:T(4,128)} %param.9) | copy-start | bytes 49156
  23.9 54.7 %collective-permute-start.2 = (bf16[2,256,512]{2,1,0:T(8,128)(2,1)}, bf16[2,256,512]{2,1,0:T(8,128)(2,1)}, u32[]{:S(2)}, u32[]{:S(2)}) collective-permute-start(bf16[2,256,512]{2,1,0:T(8,128)(2,1)} %pad_maximum_fusion.5), channel_id=1, source_target_pairs={{0,3},{1,0},{2,1},{3,2},{4,7},{5,4},{6,5},{7,6},{8,11},{9,8},{10,9... | collective-permute-start | bytes 1572872 | tf_op jit(solution)/shard_map/ppermute | solution.py:36
  26.3 52.4 %collective-permute-start.1 = (bf16[2,256,512]{1,2,0:T(8,128)(2,1)}, bf16[2,256,512]{1,2,0:T(8,128)(2,1)}, u32[]{:S(2)}, u32[]{:S(2)}) collective-permute-start(bf16[2,256,512]{1,2,0:T(8,128)(2,1)} %pad_maximum_fusion.4), channel_id=1, source_target_pairs={{0,2},{1,3},{2,0},{3,1},{4,6},{5,7},{6,4},{7,5},{8,10},{9,11},{10,... | collective-permute-start | bytes 1572872 | tf_op jit(solution)/shard_map/ppermute | solution.py:36
  32.3 46.4 %collective-permute-start = (bf16[2,256,512]{2,1,0:T(8,128)(2,1)}, bf16[2,256,512]{2,1,0:T(8,128)(2,1)}, u32[]{:S(2)}, u32[]{:S(2)}) collective-permute-start(bf16[2,256,512]{2,1,0:T(8,128)(2,1)} %pad_maximum_fusion.3), channel_id=1, source_target_pairs={{0,1},{1,2},{2,3},{3,0},{4,5},{5,6},{6,7},{7,4},{8,9},{9,10},{10,1... | collective-permute-start | bytes 1572872 | tf_op jit(solution)/shard_map/ppermute | solution.py:36
  74.1 8.4 %copy-start.14 = (bf16[2]{0:T(256)(128)(2,1)S(1)}, bf16[2]{0:T(256)(128)(2,1)}, u32[]{:S(2)}) copy-start(bf16[2]{0:T(256)(128)(2,1)} %constant.160.clone) | copy-start | bytes 16
  88.5 8.0 %copy-start.4 = (bf16[2,256,1024]{1,2,0:T(8,128)(2,1)S(1)}, bf16[2,256,1024]{1,2,0:T(8,128)(2,1)}, u32[]{:S(2)}) copy-start(bf16[2,256,1024]{1,2,0:T(8,128)(2,1)} %copy.51) | copy-start | bytes 3145732
  92.0 123.7 %all-to-all-start.1 = ((bf16[32,128,256]{2,1,0:T(8,128)(2,1)}), bf16[32,128,256]{2,1,0:T(8,128)(2,1)}, u32[]{:S(2)}, u32[]{:S(2)}) async-start(bf16[32,128,256]{2,1,0:T(8,128)(2,1)} %bitcast.64), calls=%async_computation.1 | async-start | bytes 4194304 | tf_op jit(solution)/shard_map/all_to_all | solution.py:81
  104.3 2.4 %copy-start.8 = (f32[1024,1024]{0,1:T(8,128)}, f32[1024,1024]{0,1:T(8,128)S(1)}, u32[]{:S(2)}) copy-start(f32[1024,1024]{0,1:T(8,128)S(1)} %fusion.11) | copy-start | bytes 12582916
  104.3 8.8 %copy-start.3 = (bf16[4,256,1024]{2,1,0:T(8,128)(2,1)S(1)}, bf16[4,256,1024]{2,1,0:T(8,128)(2,1)}, u32[]{:S(2)}) copy-start(bf16[4,256,1024]{2,1,0:T(8,128)(2,1)} %param.8) | copy-start | bytes 6291460
  107.7 85.6 %collective-permute-start.4 = (f32[256,768]{0,1:T(8,128)}, f32[256,768]{0,1:T(8,128)S(1)}, u32[]{:S(2)}, u32[]{:S(2)}) collective-permute-start(f32[256,768]{0,1:T(8,128)} %pad_maximum_fusion.1), channel_id=1, source_target_pairs={{0,1},{1,2},{2,3},{3,0},{4,5},{5,6},{6,7},{7,4},{8,9},{9,10},{10,1... | collective-permute-start | bytes 2359304 | tf_op jit(solution)/shard_map/ppermute | solution.py:93
  110.1 99.5 %collective-permute-start.5 = (f32[256,768]{0,1:T(8,128)}, f32[256,768]{0,1:T(8,128)}, u32[]{:S(2)}, u32[]{:S(2)}) collective-permute-start(f32[256,768]{0,1:T(8,128)} %pad_maximum_fusion.2), channel_id=1, source_target_pairs={{0,2},{1,3},{2,0},{3,1},{4,6},{5,7},{6,4},{7,5},{8,10},{9,11},{10,... | collective-permute-start | bytes 2359304 | tf_op jit(solution)/shard_map/ppermute | solution.py:93
  111.5 100.7 %collective-permute-start.6 = (f32[256,768]{0,1:T(8,128)}, f32[256,768]{0,1:T(8,128)}, u32[]{:S(2)}, u32[]{:S(2)}) collective-permute-start(f32[256,768]{0,1:T(8,128)} %slice.122), channel_id=1, source_target_pairs={{0,3},{1,0},{2,1},{3,2},{4,7},{5,4},{6,5},{7,6},{8,11},{9,8},{10,9... | collective-permute-start | bytes 2359304 | tf_op jit(solution)/shard_map/ppermute | solution.py:93
  193.2 16.4 %copy-start.10 = (f32[256,768]{0,1:T(8,128)}, f32[256,768]{0,1:T(8,128)S(1)}, u32[]{:S(2)}) copy-start(f32[256,768]{0,1:T(8,128)S(1)} %collective-permute-done.4) | copy-start | bytes 2359300
  218.0 2.8 %copy-start.5 = (f32[1,256,768]{1,2,0:T(8,128)S(1)}, f32[1,256,768]{1,2,0:T(8,128)}, u32[]{:S(2)}) copy-start(f32[1,256,768]{1,2,0:T(8,128)} %get-tuple-element.12) | copy-start | bytes 2359300
  218.1 2.8 %copy-start.6 = (f32[1,256,768]{1,2,0:T(8,128)S(1)}, f32[1,256,768]{1,2,0:T(8,128)}, u32[]{:S(2)}) copy-start(f32[1,256,768]{1,2,0:T(8,128)} %get-tuple-element.13) | copy-start | bytes 2359300
  218.1 2.8 %copy-start.7 = (f32[1,256,768]{1,2,0:T(8,128)S(1)}, f32[1,256,768]{1,2,0:T(8,128)}, u32[]{:S(2)}) copy-start(f32[1,256,768]{1,2,0:T(8,128)} %get-tuple-element.14) | copy-start | bytes 2359300
  218.1 2.8 %copy-start.9 = (f32[4,256,256]{1,2,0:T(8,128)S(1)}, f32[4,256,256]{1,2,0:T(8,128)}, u32[]{:S(2)}) copy-start(f32[4,256,256]{1,2,0:T(8,128)} %fusion.18) | copy-start | bytes 3145732

commit v16 on v13

--- a/solution.py
+++ b/solution.py
@@ -1,6 +1,7 @@
 import jax
 import jax.numpy as jnp
 from jax import lax
+from jax.experimental.layout import Layout, with_layout_constraint
 from jax.sharding import PartitionSpec as P
 
 
@@ -75,7 +76,8 @@
     right = jnp.concatenate([whole[1], whole[0]], axis=-1)
     ladder_c = lax.dot_general(
         left, right, (((1,), (1,)), ((), ())), preferred_element_type=f32
-    ).reshape(n_rows, rows, width)
+    )
+    ladder_c = with_layout_constraint(ladder_c, Layout((0, 1))).reshape(n_rows, rows, width)
     sending = jnp.stack([skip_block(ladder_c[a], a, rows) for a in range(n_rows)])
     returning = term_t.reshape(n_chan, slab, n_rows, rows).transpose(0, 2, 1, 3)
     landed = lax.all_to_all(

time: 225 us -> 230 us (1.022)
    ppermute x1, waiting for transfers between devices: 0.01 us -> 12.1 us  [per_device(): lax.ppermute(jnp.concatenate([ph_factor.astype(f32), recouple], axis=0),...]
    all_to_all x1, waiting for transfers between devices: 27.8 us -> 17.4 us  [per_device(): lax.all_to_all(outgoing, 'ch', split_axis=1, concat_axis=1, tiled=True)]
    reshape x0 -> x1, local copies, waits for them, and re-layouts: none -> 5.39 us  [per_device(): back = back.reshape(ch_dev, rows, width)]
    convert_element_type x1 -> x0, local copies, waits for them, and re-layouts: 2.38 us -> none  [per_device(): return (ladder + back).astype(bf16)]
    convert_element_type x1, other arithmetic: 2.5 us -> 4.8 us  [per_device(): return (ladder + back).astype(bf16)]
  transfers between devices with their start and end apart: 9 -> 9, of which waited for: 4 -> 5; matrix products, arithmetic and copies ran while one was open for 17% -> 15% of each run, Pallas kernels for 0% -> 0%
where the time goes in v16:
time: 230 us; the launch traced here: 229 us
  waiting for transfers between devices  130 us (57%)
  local copies, waits for them, and re-layouts  36 us (16%)
  other arithmetic  23.7 us (10%)
  starting transfers between devices  22.8 us (10%)
  matrix products  16.8 us (7%)
    ppermute x3, waiting for transfers between devices, per_device(): returned.append(lax.ppermute(sending[shift], 'row', pairs))  100 us
    all_to_all x1, waiting for transfers between devices, per_device(): lax.all_to_all(outgoing, 'ch', split_axis=1, concat_axis=1, tiled=True)  17.4 us
    ppermute x1, waiting for transfers between devices, per_device(): lax.ppermute(jnp.concatenate([ph_factor.astype(f32), recouple], axis=0),...  12.1 us
    reshape x2, local copies, waits for them, and re-layouts, per_device(): returning = term_t.reshape(n_chan, slab, n_rows, rows).transpose(0, 2, 1, 3)  7.9 us
    gather x2, local copies, waits for them, and re-layouts, per_device(): x.reshape(ch_dev, rows // slab, slab, width)[slot_dest, part_dest]  5.64 us
    ppermute x3, starting transfers between devices, per_device(): lax.ppermute(jnp.concatenate([own_blk, next_blk], axis=-1), 'row', pairs)  5.5 us
    reshape x1, local copies, waits for them, and re-layouts, per_device(): back = back.reshape(ch_dev, rows, width)  5.39 us
    convert_element_type x1, other arithmetic, per_device(): return (ladder + back).astype(bf16)  4.8 us
  transfers between devices with their start and end apart: 9, of which 5 were waited for; matrix products, arithmetic and copies ran while one was open for 15% of the time, Pallas kernels for 0%

profile of v16, /device:TPU:8, one launch (start us, length us, event | category | flops | bytes accessed | tf_op | source)
XLA Modules:
  0.0 229.3 jit_solution(13805969526585123697)
XLA Ops:
  1.3 3.6 %gather_fusion.1 = bf16[8,128,1024]{2,1,0:T(8,128)(2,1)} fusion(bf16[4,2,128,1024]{3,2,1,0:T(8,128)(2,1)} %bitcast.65, s32[8]{0:T(128)S(1)} %fusion.56), kind=kCustom, calls=%fused_computation.1 | custom fusion | bytes 4194368 | tf_op jit(solution)/shard_map/gather | solution.py:43
  7.0 4.5 %pad_maximum_fusion = bf16[2,8,128,1024]{3,2,0,1:T(8,128)(2,1)} fusion(bf16[1,8,128,1024]{3,2,0,1:T(8,128)(2,1)} %bitcast.69, bf16[1,8,128,1024]{3,2,0,1:T(8,128)(2,1)} %bitcast.68), kind=kLoop, calls=%fused_computation.24 | loop fusion | flops 2097152 | bytes 8388608 | tf_op jit(solution)/shard_map/stack | solution.py:25
  11.5 4.6 %all-to-all-start = ((bf16[2,8,128,1024]{3,2,0,1:T(8,128)(2,1)}), bf16[2,8,128,1024]{3,2,0,1:T(8,128)(2,1)}, u32[]{:S(2)}, u32[]{:S(2)}) async-start(bf16[2,8,128,1024]{3,2,0,1:T(8,128)(2,1)} %pad_maximum_fusion), calls=%async_computation | async-start | bytes 8388608 | tf_op jit(solution)/shard_map/all_to_all | solution.py:44
  23.0 3.6 %collective-permute-start.3 = (f32[2,1024]{1,0:T(2,128)S(1)}, f32[2,1024]{1,0:T(2,128)S(1)}, u32[]{:S(2)}, u32[]{:S(2)}) collective-permute-start(f32[2,1024]{1,0:T(2,128)S(1)} %pad_maximum_fusion.6), channel_id=1, source_target_pairs={{0,0},{1,4},{2,8},{3,12},{4,16},{5,20},{6,24},{7,28},{8,1},{9,5},{... | collective-permute-start | bytes 24584 | tf_op jit(solution)/shard_map/ppermute | solution.py:49
  28.9 3.5 %collective-permute-start.1 = (bf16[2,256,512]{1,2,0:T(8,128)(2,1)}, bf16[2,256,512]{1,2,0:T(8,128)(2,1)}, u32[]{:S(2)}, u32[]{:S(2)}) collective-permute-start(bf16[2,256,512]{1,2,0:T(8,128)(2,1)} %pad_maximum_fusion.4), channel_id=1, source_target_pairs={{0,2},{1,3},{2,0},{3,1},{4,6},{5,7},{6,4},{7,5},{8,10},{9,11},{10,... | collective-permute-start | bytes 1572872 | tf_op jit(solution)/shard_map/ppermute | solution.py:37
  35.7 12.1 %collective-permute-done.3 = f32[2,1024]{1,0:T(2,128)S(1)} collective-permute-done((f32[2,1024]{1,0:T(2,128)S(1)}, f32[2,1024]{1,0:T(2,128)S(1)}, u32[]{:S(2)}, u32[]{:S(2)}) %collective-permute-start.3) | collective-permute-done | bytes 8224 | tf_op jit(solution)/shard_map/ppermute | solution.py:49
  47.8 17.4 %all-to-all-done = bf16[2,8,128,1024]{3,2,0,1:T(8,128)(2,1)} async-done(((bf16[2,8,128,1024]{3,2,0,1:T(8,128)(2,1)}), bf16[2,8,128,1024]{3,2,0,1:T(8,128)(2,1)}, u32[]{:S(2)}, u32[]{:S(2)}) %all-to-all-start) | async-done | bytes 4194336 | tf_op jit(solution)/shard_map/all_to_all | solution.py:44
  65.2 2.8 %broadcast_multiply_fusion.4 = (bf16[1,8,128,1024]{3,2,0,1:T(8,128)(2,1)S(1)}, bf16[1,8,128,1024]{3,2,0,1:T(8,128)(2,1)S(1)}, bf16[1,8,128,1024]{3,2,0,1:T(8,128)(2,1)S(1)}, bf16[1,8,128,1024]{3,2,0,1:T(8,128)(2,1)S(1)}) fusion(bf16[1024]{0:T(1024)(128)(2,1)S(1)} %fusion.44, bf16[2,8,128,1024]{3,2,0,1:T(8,128)(2,1)} %all-to-all-done), kind=kLoop, calls=%fused_computation.68 | loop fusion | flops 2097152 | bytes 12584960 | tf_op jit(solution)/shard_map/mul | solution.py:56
  68.0 2.3 %fusion.61 = f32[1024,1024]{1,0:T(8,128)S(1)} fusion(bf16[1024,1024]{1,0:T(8,128)(2,1)S(1)} %bitcast.73, bf16[1024,1024]{1,0:T(8,128)(2,1)S(1)} %bitcast.74), kind=kOutput, calls=%fused_computation.138 | convolution fusion | flops 2147483648 | bytes 8388608 | tf_op jit(solution)/shard_map/dot_general | solution.py:55
  70.3 3.7 %multiply_convert_fusion = bf16[1024,1024]{1,0:T(8,128)(2,1)} fusion(f32[1024,1024]{1,0:T(8,128)S(1)} %fusion.61, f32[1024]{0:T(1024)S(1)} %bitcast.75, bf16[1024,1024]{1,0:T(8,128)(2,1)S(1)} %bitcast.71, bf16[1024,1024]{1,0:T(8,128)(2,1)S(1)} %bitcast.72), kind=kOutput, calls=%fused_computation.40 | convolution fusion | flops 2150629376 | bytes 10489856 | tf_op jit(solution)/shard_map/dot_general | solution.py:56
  74.0 4.5 %reshape.134 = bf16[8,128,4,256]{3,2,1,0:T(4,128)(2,1)} reshape(bf16[1024,1024]{1,0:T(8,128)(2,1)} %multiply_convert_fusion) | data formatting | bytes 4194304 | tf_op jit(solution)/shard_map/reshape | solution.py:82
  80.3 2.1 copy.33
  82.4 2.4 %fusion.38 = (bf16[2,256,256]{1,2,0:T(8,128)(2,1)S(1)}, bf16[2,256,256]{1,2,0:T(8,128)(2,1)}, bf16[2,256,256]{1,2,0:T(8,128)(2,1)}, bf16[2,256,256]{2,1,0:T(8,12...) fusion(bf16[2,256,1024]{2,1,0:T(8,128)(2,1)S(1)} %fusion.28, ...), kind=kLoop, calls=%fused_computation.90 | loop fusion | flops 786432 | bytes 3932164 | tf_op jit(solution)/shard_map/mul | solution.py:68
  88.4 3.4 %copy.40 = bf16[8,128,4,256]{3,1,2,0:T(8,128)(2,1)} copy(bf16[8,128,4,256]{3,2,1,0:T(4,128)(2,1)} %reshape.134) | data formatting | bytes 4194304 | tf_op jit(solution)/shard_map/reshape | solution.py:82
  91.8 4.6 %all-to-all-start.1 = ((bf16[32,128,256]{2,1,0:T(8,128)(2,1)}), bf16[32,128,256]{2,1,0:T(8,128)(2,1)}, u32[]{:S(2)}, u32[]{:S(2)}) async-start(bf16[32,128,256]{2,1,0:T(8,128)(2,1)} %bitcast.67), calls=%async_computation.1 | async-start | bytes 4194304 | tf_op jit(solution)/shard_map/all_to_all | solution.py:83
  96.4 2.2 maximum_maximum_fusion
  99.4 4.7 %fusion.11 = f32[1024,1024]{1,0:T(8,128)S(1)} fusion(bf16[1024,1024]{0,1:T(8,128)(2,1)S(1)} %get-tuple-element.16, bf16[1024,1024]{0,1:T(8,128)(2,1)S(1)} %get-tuple-element.15, bf16[1024,1024]{0,1:T(8,128)(2,1)S(1)} %get-tuple-element.24, bf16[1024,1024]{0,1:T(8,128)(2,1)S(1)} %get-tuple-element.23), kind=kOutput, calls=%fused_computation.26 | convolution fusion | flops 4311744512 | bytes 12582912 | tf_op jit(solution)/shard_map/dot_general | solution.py:77
  109.4 2.3 %fusion.18 = f32[4,256,256]{2,1,0:T(8,128)} fusion(bf16[4,256,1024]{2,1,0:T(8,128)(2,1)S(1)} %get-tuple-element.48, bf16[4,256,1024]{2,1,0:T(8,128)(2,1)S(1)} %get-tuple-element.47, bf16[4,256,1024]{2,1,0:T(8,128)(2,1)S(1)} %copy-done.4, bf16[4,256,1024]{2,1,0:T(8,128)(2,1)S(1)} %copy-done.2), kind=kOutput, calls=%fused_computation.33 | convolution fusion | flops 1090519040 | bytes 9437184 | tf_op jit(solution)/shard_map/sik,sjk->sij/dot_general | solution.py:107
  111.7 81.3 %collective-permute-done.4 = f32[256,768]{1,0:T(8,128)S(1)} collective-permute-done((f32[256,768]{1,0:T(8,128)S(1)}, f32[256,768]{1,0:T(8,128)S(1)}, u32[]{:S(2)}, u32[]{:S(2)}) %collective-permute-start.4) | collective-permute-done | bytes 786464 | tf_op jit(solution)/shard_map/ppermute | solution.py:95
  193.0 16.4 %collective-permute-done.5 = f32[256,768]{1,0:T(8,128)S(1)} collective-permute-done((f32[256,768]{1,0:T(8,128)S(1)}, f32[256,768]{1,0:T(8,128)S(1)}, u32[]{:S(2)}, u32[]{:S(2)}) %collective-permute-start.5) | collective-permute-done | bytes 786464 | tf_op jit(solution)/shard_map/ppermute | solution.py:95
  209.3 2.6 %collective-permute-done.6 = f32[256,768]{1,0:T(8,128)S(1)} collective-permute-done((f32[256,768]{1,0:T(8,128)S(1)}, f32[256,768]{1,0:T(8,128)S(1)}, u32[]{:S(2)}, u32[]{:S(2)}) %collective-permute-start.6) | collective-permute-done | bytes 786464 | tf_op jit(solution)/shard_map/ppermute | solution.py:95
  215.3 3.7 %fusion.25 = f32[8,128,256,4]{2,3,1,0:T(4,128)} fusion(bf16[8,4,128,256]{3,2,1,0:T(8,128)(2,1)S(1)} %bitcast.70, s32[8,4]{1,0:T(8,128)S(1)} %eq.36), kind=kOutput, calls=%fused_computation.47 | convolution fusion | flops 8388736 | bytes 6291584 | tf_op jit(solution)/shard_map/gts,gtwi->sigw/dot_general | solution.py:101
  219.1 5.4 %copy.46 = f32[4,256,1024]{2,1,0:T(8,128)} copy(f32[4,256,1024]{1,0,2:T(4,128)} %bitcast.66) | data formatting | bytes 8388608 | tf_op jit(solution)/shard_map/reshape | solution.py:102
  224.5 4.8 %fusion.7 = bf16[4,256,1024]{2,1,0:T(8,128)(2,1)} fusion(f32[4,256,1024]{2,1,0:T(8,128)} %copy.46, s32[]{:T(128)S(6)} %select_n.316, f32[1,256,768]{2,1,0:T(8,128)} %get-tuple-element.14, f32[1,256,768]{2,1,0:T(8,128)S(1)} %copy-done.7, f32[1,256,768]{2,1,0:T(8,128)S(1)} %copy-done.6, f32[1,256,768]{2,1,0:T(8,128)S(1)} %get-tuple-element.11, ...), kind=kLoop, calls=%fused_computation.20 | loop fusion | flops 11534336 | bytes 10485764 | tf_op jit(solution)/shard_map/convert_element_type | solution.py:110
  (71 shorter events, 30.7 us)
Async XLA Ops:
  0.0 0.7 copy-start
  0.0 5.0 %copy-start.2 = (bf16[4,256,1024]{2,1,0:T(8,128)(2,1)S(1)}, bf16[4,256,1024]{2,1,0:T(8,128)(2,1)}, u32[]{:S(2)}) copy-start(bf16[4,256,1024]{2,1,0:T(8,128)(2,1)} %param.8) | copy-start | bytes 6291460
  11.5 53.7 %all-to-all-start = ((bf16[2,8,128,1024]{3,2,0,1:T(8,128)(2,1)}), bf16[2,8,128,1024]{3,2,0,1:T(8,128)(2,1)}, u32[]{:S(2)}, u32[]{:S(2)}) async-start(bf16[2,8,128,1024]{3,2,0,1:T(8,128)(2,1)} %pad_maximum_fusion), calls=%async_computation | async-start | bytes 8388608 | tf_op jit(solution)/shard_map/all_to_all | solution.py:44
  16.2 2.0 copy-start.3
  18.1 4.8 %copy-start.9 = (s32[1,1024]{1,0:T(1,128)S(1)}, s32[1,1024]{1,0:T(1,128)}, u32[]{:S(2)}) copy-start(s32[1,1024]{1,0:T(1,128)} %param.10) | copy-start | bytes 12292
  18.1 4.8 %copy-start.10 = (f32[1,1024]{1,0:T(1,128)S(1)}, f32[1,1024]{1,0:T(1,128)}, u32[]{:S(2)}) copy-start(f32[1,1024]{1,0:T(1,128)} %param.11) | copy-start | bytes 12292
  19.2 13.1 %copy-start.8 = (s32[4,1024]{1,0:T(4,128)S(1)}, s32[4,1024]{1,0:T(4,128)}, u32[]{:S(2)}) copy-start(s32[4,1024]{1,0:T(4,128)} %param.9) | copy-start | bytes 49156
  20.1 58.4 %collective-permute-start = (bf16[2,256,512]{2,1,0:T(8,128)(2,1)}, bf16[2,256,512]{2,1,0:T(8,128)(2,1)}, u32[]{:S(2)}, u32[]{:S(2)}) collective-permute-start(bf16[2,256,512]{2,1,0:T(8,128)(2,1)} %pad_maximum_fusion.3), channel_id=1, source_target_pairs={{0,1},{1,2},{2,3},{3,0},{4,5},{5,6},{6,7},{7,4},{8,9},{9,10},{10,1... | collective-permute-start | bytes 1572872 | tf_op jit(solution)/shard_map/ppermute | solution.py:37
  22.5 56.0 %collective-permute-start.2 = (bf16[2,256,512]{2,1,0:T(8,128)(2,1)}, bf16[2,256,512]{2,1,0:T(8,128)(2,1)}, u32[]{:S(2)}, u32[]{:S(2)}) collective-permute-start(bf16[2,256,512]{2,1,0:T(8,128)(2,1)} %pad_maximum_fusion.5), channel_id=1, source_target_pairs={{0,3},{1,0},{2,1},{3,2},{4,7},{5,4},{6,5},{7,6},{8,11},{9,8},{10,9... | collective-permute-start | bytes 1572872 | tf_op jit(solution)/shard_map/ppermute | solution.py:37
  23.0 24.8 %collective-permute-start.3 = (f32[2,1024]{1,0:T(2,128)S(1)}, f32[2,1024]{1,0:T(2,128)S(1)}, u32[]{:S(2)}, u32[]{:S(2)}) collective-permute-start(f32[2,1024]{1,0:T(2,128)S(1)} %pad_maximum_fusion.6), channel_id=1, source_target_pairs={{0,0},{1,4},{2,8},{3,12},{4,16},{5,20},{6,24},{7,28},{8,1},{9,5},{... | collective-permute-start | bytes 24584 | tf_op jit(solution)/shard_map/ppermute | solution.py:49
  28.9 49.6 %collective-permute-start.1 = (bf16[2,256,512]{1,2,0:T(8,128)(2,1)}, bf16[2,256,512]{1,2,0:T(8,128)(2,1)}, u32[]{:S(2)}, u32[]{:S(2)}) collective-permute-start(bf16[2,256,512]{1,2,0:T(8,128)(2,1)} %pad_maximum_fusion.4), channel_id=1, source_target_pairs={{0,2},{1,3},{2,0},{3,1},{4,6},{5,7},{6,4},{7,5},{8,10},{9,11},{10,... | collective-permute-start | bytes 1572872 | tf_op jit(solution)/shard_map/ppermute | solution.py:37
  74.0 8.4 %copy-start.11 = (bf16[2]{0:T(256)(128)(2,1)S(1)}, bf16[2]{0:T(256)(128)(2,1)}, u32[]{:S(2)}) copy-start(bf16[2]{0:T(256)(128)(2,1)} %constant.158.clone) | copy-start | bytes 16
  88.4 8.0 %copy-start.5 = (bf16[2,256,1024]{1,2,0:T(8,128)(2,1)S(1)}, bf16[2,256,1024]{1,2,0:T(8,128)(2,1)}, u32[]{:S(2)}) copy-start(bf16[2,256,1024]{1,2,0:T(8,128)(2,1)} %copy.37) | copy-start | bytes 3145732
  91.8 121.7 %all-to-all-start.1 = ((bf16[32,128,256]{2,1,0:T(8,128)(2,1)}), bf16[32,128,256]{2,1,0:T(8,128)(2,1)}, u32[]{:S(2)}, u32[]{:S(2)}) async-start(bf16[32,128,256]{2,1,0:T(8,128)(2,1)} %bitcast.67), calls=%async_computation.1 | async-start | bytes 4194304 | tf_op jit(solution)/shard_map/all_to_all | solution.py:83
  104.1 4.9 %copy-start.4 = (bf16[4,256,1024]{2,1,0:T(8,128)(2,1)S(1)}, bf16[4,256,1024]{2,1,0:T(8,128)(2,1)}, u32[]{:S(2)}) copy-start(bf16[4,256,1024]{2,1,0:T(8,128)(2,1)} %param.7) | copy-start | bytes 6291460
  104.3 88.6 %collective-permute-start.4 = (f32[256,768]{1,0:T(8,128)S(1)}, f32[256,768]{1,0:T(8,128)S(1)}, u32[]{:S(2)}, u32[]{:S(2)}) collective-permute-start(f32[256,768]{1,0:T(8,128)S(1)} %pad_maximum_fusion.1), channel_id=1, source_target_pairs={{0,1},{1,2},{2,3},{3,0},{4,5},{5,6},{6,7},{7,4},{8,9},{9,10},{10,1... | collective-permute-start | bytes 2359304 | tf_op jit(solution)/shard_map/ppermute | solution.py:95
  105.9 103.4 %collective-permute-start.5 = (f32[256,768]{1,0:T(8,128)S(1)}, f32[256,768]{1,0:T(8,128)S(1)}, u32[]{:S(2)}, u32[]{:S(2)}) collective-permute-start(f32[256,768]{1,0:T(8,128)S(1)} %pad_maximum_fusion.2), channel_id=1, source_target_pairs={{0,2},{1,3},{2,0},{3,1},{4,6},{5,7},{6,4},{7,5},{8,10},{9,11},{10,... | collective-permute-start | bytes 2359304 | tf_op jit(solution)/shard_map/ppermute | solution.py:95
  107.4 104.6 %collective-permute-start.6 = (f32[256,768]{1,0:T(8,128)S(1)}, f32[256,768]{1,0:T(8,128)S(1)}, u32[]{:S(2)}, u32[]{:S(2)}) collective-permute-start(f32[256,768]{1,0:T(8,128)S(1)} %slice.122), channel_id=1, source_target_pairs={{0,3},{1,0},{2,1},{3,2},{4,7},{5,4},{6,5},{7,6},{8,11},{9,8},{10,9... | collective-permute-start | bytes 2359304 | tf_op jit(solution)/shard_map/ppermute | solution.py:95
  219.1 5.4 %copy-start.6 = (f32[1,256,768]{2,1,0:T(8,128)S(1)}, f32[1,256,768]{2,1,0:T(8,128)}, u32[]{:S(2)}) copy-start(f32[1,256,768]{2,1,0:T(8,128)} %get-tuple-element.12) | copy-start | bytes 2359300
  219.1 5.4 %copy-start.7 = (f32[1,256,768]{2,1,0:T(8,128)S(1)}, f32[1,256,768]{2,1,0:T(8,128)}, u32[]{:S(2)}) copy-start(f32[1,256,768]{2,1,0:T(8,128)} %get-tuple-element.13) | copy-start | bytes 2359300
  224.5 4.8 %copy-start.1 = (s32[32,8]{0,1:T(8,128)S(1)}, s32[32,8]{0,1:T(8,128)}, u32[]{:S(2)}) copy-start(s32[32,8]{0,1:T(8,128)} %param.12) | copy-start | bytes 3076

commit v17 on v13

--- a/solution.py
+++ b/solution.py
@@ -51,9 +51,15 @@
     weight = coefs[0].astype(bf16)[None, :]
     coef = coefs[1]
 
-    ph_t = jnp.dot(a_eta * weight, b_gamma, preferred_element_type=f32)
-    ph_t = ph_t - jnp.dot(b_gamma * weight, a_eta, preferred_element_type=f32)
-    term_t = (ph_t * coef[:, None]).astype(bf16)
+    a_w = a_eta * weight
+    b_w = b_gamma * weight
+    parts = []
+    for r in range(n_rows):
+        cut = slice(r * rows, (r + 1) * rows)
+        part = jnp.dot(a_w, b_gamma[:, cut], preferred_element_type=f32)
+        part = part - jnp.dot(b_w, a_eta[:, cut], preferred_element_type=f32)
+        parts.append((part * coef[:, None]).astype(bf16).reshape(n_chan, slab, rows))
+    term_t = jnp.stack(parts, axis=1)
     ladder_in, _ = lax.optimization_barrier((ladder_in, term_t))
     sign = jnp.array([-1, 1], bf16)[:, None, None]
     own = pair(lambda x: lax.dynamic_index_in_dim(x, level, 0, False))
@@ -77,7 +83,7 @@
         left, right, (((1,), (1,)), ((), ())), preferred_element_type=f32
     ).reshape(n_rows, rows, width)
     sending = jnp.stack([skip_block(ladder_c[a], a, rows) for a in range(n_rows)])
-    returning = term_t.reshape(n_chan, slab, n_rows, rows).transpose(0, 2, 1, 3)
+    returning = term_t
     landed = lax.all_to_all(
         returning.reshape(n_chan * n_rows, slab, rows),
         ("ch", "row"),

time: 225 us -> 218 us (0.969)
  local copies, waits for them, and re-layouts: 35.8 us -> 30.9 us
    reshape x2 -> x0, local copies, waits for them, and re-layouts: 7.91 us -> none  [per_device(): returning = term_t.reshape(n_chan, slab, n_rows, rows).transpose(0, 2, 1, 3)]
    mul x1 -> x0, other arithmetic: 2.76 us -> none  [per_device(): ph_t = ph_t - jnp.dot(b_gamma * weight, a_eta, preferred_element_type=f32)]
    slice x0 -> x1, local copies, waits for them, and re-layouts: none -> 2.7 us  [per_device(): b_gamma = arrived[1].reshape(width, width)]
    dot_general x2 -> x8, matrix products: 6 us -> 5.73 us  [the longest x4 2.87 us: per_device(): part = part - jnp.dot(b_w, a_eta[:, cut], preferred_element_type=f32)]
  transfers between devices with their start and end apart: 9 -> 9, of which waited for: 4 -> 4; matrix products, arithmetic and copies ran while one was open for 17% -> 16% of each run, Pallas kernels for 0% -> 0%
where the time goes in v17:
time: 218 us
  waiting for transfers between devices  129 us (59%)
  local copies, waits for them, and re-layouts  30.9 us (14%)
  starting transfers between devices  21.8 us (10%)
  other arithmetic  21 us (10%)
  matrix products  14.6 us (7%)
    ppermute x3, waiting for transfers between devices, per_device(): returned.append(lax.ppermute(sending[shift], 'row', pairs))  100 us
    all_to_all x1, waiting for transfers between devices, per_device(): lax.all_to_all(outgoing, 'ch', split_axis=1, concat_axis=1, tiled=True)  28.7 us
    ppermute x3, starting transfers between devices, per_device(): lax.ppermute(jnp.concatenate([own_blk, next_blk], axis=-1), 'row', pairs)  6.07 us
    gather x2, local copies, waits for them, and re-layouts, per_device(): x.reshape(ch_dev, rows // slab, slab, width)[slot_dest, part_dest]  5.79 us
    another operation x3, other arithmetic, per_device(): pair = lambda f: jnp.stack([f(eta_pp), f(gamma_pp)])  5.46 us
    dot_general x1, matrix products, per_device(): lax.dot_general(left, right, (((1,), (1,)), ((), ())), preferred_element_...  4.81 us
    all_to_all x1, starting transfers between devices, per_device(): lax.all_to_all(outgoing, 'ch', split_axis=1, concat_axis=1, tiled=True)  4.7 us
    all_to_all x1, starting transfers between devices, per_device(): lax.all_to_all(returning.reshape(n_chan * n_rows, slab, rows), ('ch', 'ro...  4.57 us
  transfers between devices with their start and end apart: 9, of which 4 were waited for; matrix products, arithmetic and copies ran while one was open for 16% of the time, Pallas kernels for 0%

profile of v17, /device:TPU:8, one launch (start us, length us, event | category | flops | bytes accessed | tf_op | source)
XLA Modules:
  0.0 217.7 jit_solution(1867925137313285293)
XLA Ops:
  1.4 3.8 %gather_fusion.1 = bf16[8,128,1024]{2,1,0:T(8,128)(2,1)} fusion(bf16[4,2,128,1024]{3,2,1,0:T(8,128)(2,1)} %bitcast.69, s32[8]{0:T(128)S(1)} %fusion.99), kind=kCustom, calls=%fused_computation.1 | custom fusion | bytes 4194368 | tf_op jit(solution)/shard_map/gather | solution.py:42
  5.1 2.0 gather_fusion.2
  7.1 4.6 %pad_maximum_fusion = bf16[2,8,128,1024]{3,2,0,1:T(8,128)(2,1)} fusion(bf16[1,8,128,1024]{3,2,0,1:T(8,128)(2,1)} %bitcast.73, bf16[1,8,128,1024]{3,2,0,1:T(8,128)(2,1)} %bitcast.72), kind=kLoop, calls=%fused_computation.24 | loop fusion | flops 2097152 | bytes 8388608 | tf_op jit(solution)/shard_map/stack | solution.py:24
  11.7 4.7 %all-to-all-start = ((bf16[2,8,128,1024]{3,2,0,1:T(8,128)(2,1)}), bf16[2,8,128,1024]{3,2,0,1:T(8,128)(2,1)}, u32[]{:S(2)}, u32[]{:S(2)}) async-start(bf16[2,8,128,1024]{3,2,0,1:T(8,128)(2,1)} %pad_maximum_fusion), calls=%async_computation | async-start | bytes 8388608 | tf_op jit(solution)/shard_map/all_to_all | solution.py:43
  16.5 1.9 collective-permute-start.3
  18.5 2.8 %constant_dynamic-slice_fusion.8 = (bf16[1,256,1024]{2,1,0:T(8,128)(2,1)}, bf16[1,256,1024]{2,1,0:T(8,128)(2,1)S(1)}, bf16[1,256,1024]{2,1,0:T(8,128)(2,1)S(1)}, bf16[1,256,1024]{2,1,0:T(8,128)(2,1)S(1)}) fusion(bf16[4,256,1024]{2,1,0:T(8,128)(2,1)} %param.8, s32[]{:T(128)S(6)} %select_n.263, s32[]{:T(128)S(6)} %select_n.274, s32[]{:T(128)S(6)} %select_n.271, ...), kind=kLoop, calls=%fused_computation.142 | loop fusion | bytes 4194320 | tf_op jit(solution)/shard_map/jit(dynamic_index_in_dim)/dynamic_slice | solution.py:65
  26.5 4.2 %collective-permute-start.1 = (bf16[2,256,512]{1,2,0:T(8,128)(2,1)}, bf16[2,256,512]{1,2,0:T(8,128)(2,1)}, u32[]{:S(2)}, u32[]{:S(2)}) collective-permute-start(bf16[2,256,512]{1,2,0:T(8,128)(2,1)} %pad_maximum_fusion.5), channel_id=1, source_target_pairs={{0,2},{1,3},{2,0},{3,1},{4,6},{5,7},{6,4},{7,5},{8,10},{9,11},{10,... | collective-permute-start | bytes 1572872 | tf_op jit(solution)/shard_map/ppermute | solution.py:36
  31.6 1.8 collective-permute-start
  36.8 28.7 %all-to-all-done = bf16[2,8,128,1024]{3,2,0,1:T(8,128)(2,1)} async-done(((bf16[2,8,128,1024]{3,2,0,1:T(8,128)(2,1)}), bf16[2,8,128,1024]{3,2,0,1:T(8,128)(2,1)}, u32[]{:S(2)}, u32[]{:S(2)}) %all-to-all-start) | async-done | bytes 4194336 | tf_op jit(solution)/shard_map/all_to_all | solution.py:43
  65.5 2.7 %fusion.104 = (bf16[1,8,128,1024]{3,2,0,1:T(8,128)(2,1)S(1)}, bf16[1,8,128,1024]{3,2,0,1:T(8,128)(2,1)S(1)}) fusion(bf16[2,8,128,1024]{3,2,0,1:T(8,128)(2,1)} %all-to-all-done), kind=kLoop, calls=%fused_computation.176 | loop fusion | bytes 8388608 | tf_op jit(solution)/shard_map/slice | solution.py:45
  77.5 2.1 copy.38
  79.5 2.4 %fusion.81 = (bf16[2,256,256]{1,2,0:T(8,128)(2,1)S(1)}, bf16[2,256,256]{1,2,0:T(8,128)(2,1)}, bf16[2,256,256]{1,2,0:T(8,128)(2,1)}, bf16[2,256,256]{2,1,0:T(8,12...) fusion(bf16[2,256,1024]{2,1,0:T(8,128)(2,1)S(1)} %fusion.55, ...), kind=kLoop, calls=%fused_computation.128 | loop fusion | flops 786432 | bytes 3932164 | tf_op jit(solution)/shard_map/mul | solution.py:73
  82.0 1.8 copy.40
  83.7 1.8 copy.41
  85.5 4.6 %all-to-all-start.1 = ((bf16[32,128,256]{2,1,0:T(8,128)(2,1)}), bf16[32,128,256]{2,1,0:T(8,128)(2,1)}, u32[]{:S(2)}, u32[]{:S(2)}) async-start(bf16[32,128,256]{2,1,0:T(8,128)(2,1)} %bitcast.71), calls=%async_computation.1 | async-start | bytes 4194304 | tf_op jit(solution)/shard_map/all_to_all | solution.py:87
  90.1 2.2 maximum_maximum_fusion
  93.1 4.8 %fusion.11 = f32[1024,1024]{0,1:T(8,128)S(1)} fusion(bf16[1024,1024]{0,1:T(8,128)(2,1)S(1)} %get-tuple-element.16, bf16[1024,1024]{0,1:T(8,128)(2,1)S(1)} %get-tuple-element.15, bf16[1024,1024]{0,1:T(8,128)(2,1)S(1)} %get-tuple-element.22, bf16[1024,1024]{0,1:T(8,128)(2,1)S(1)} %get-tuple-element.21), kind=kOutput, calls=%fused_computation.26 | convolution fusion | flops 4311744512 | bytes 12582912 | tf_op jit(solution)/shard_map/dot_general | solution.py:82
  103.1 2.3 %fusion.18 = f32[4,256,256]{1,2,0:T(8,128)} fusion(bf16[4,256,1024]{2,1,0:T(8,128)(2,1)S(1)} %get-tuple-element.46, bf16[4,256,1024]{2,1,0:T(8,128)(2,1)S(1)} %get-tuple-element.45, bf16[4,256,1024]{2,1,0:T(8,128)(2,1)S(1)} %copy-done.2, bf16[4,256,1024]{2,1,0:T(8,128)(2,1)S(1)} %copy-done.4), kind=kOutput, calls=%fused_computation.33 | convolution fusion | flops 1090519040 | bytes 9437184 | tf_op jit(solution)/shard_map/sik,sjk->sij/dot_general | solution.py:111
  105.4 81.3 %collective-permute-done.4 = f32[256,768]{0,1:T(8,128)S(1)} collective-permute-done((f32[256,768]{0,1:T(8,128)S(1)}, f32[256,768]{0,1:T(8,128)S(1)}, u32[]{:S(2)}, u32[]{:S(2)}) %collective-permute-start.4) | collective-permute-done | bytes 786464 | tf_op jit(solution)/shard_map/ppermute | solution.py:99
  186.7 16.4 %collective-permute-done.5 = f32[256,768]{0,1:T(8,128)S(1)} collective-permute-done((f32[256,768]{0,1:T(8,128)S(1)}, f32[256,768]{0,1:T(8,128)S(1)}, u32[]{:S(2)}, u32[]{:S(2)}) %collective-permute-start.5) | collective-permute-done | bytes 786464 | tf_op jit(solution)/shard_map/ppermute | solution.py:99
  203.1 2.6 %collective-permute-done.6 = f32[256,768]{0,1:T(8,128)S(1)} collective-permute-done((f32[256,768]{0,1:T(8,128)S(1)}, f32[256,768]{0,1:T(8,128)S(1)}, u32[]{:S(2)}, u32[]{:S(2)}) %collective-permute-start.6) | collective-permute-done | bytes 786464 | tf_op jit(solution)/shard_map/ppermute | solution.py:99
  207.3 1.8 copy.43
  212.8 2.5 %fusion.7 = bf16[4,256,1024]{1,2,0:T(8,128)(2,1)S(1)} fusion(s32[]{:T(128)S(6)} %select_n.316, f32[1,256,768]{1,2,0:T(8,128)S(1)} %copy-done.8, f32[1,256,768]{1,2,0:T(8,128)S(1)} %copy-done.7, f32[1,256,768]{1,2,0:T(8,128)S(1)} %copy-done.6, f32[1,256,768]{1,2,0:T(8,128)S(1)} %get-tuple-element.11, f32[4,256,256]{1,2,0:T(8,128)S(1)} %copy-done.10, ...), kind=kLoop, calls=%fused_computation.20 | loop fusion | flops 11534336 | bytes 10485764 | tf_op jit(solution)/shard_map/convert_element_type | solution.py:114
  215.3 2.4 %copy.46 = bf16[4,256,1024]{2,1,0:T(8,128)(2,1)} copy(bf16[4,256,1024]{1,2,0:T(8,128)(2,1)S(1)} %fusion.7) | data formatting | bytes 4194304 | tf_op jit(solution)/shard_map/convert_element_type | solution.py:114
  (83 shorter events, 31.1 us)
Async XLA Ops:
  0.0 0.7 copy-start
  1.3 3.8 %copy-start.3 = (bf16[4,256,1024]{2,1,0:T(8,128)(2,1)S(1)}, bf16[4,256,1024]{2,1,0:T(8,128)(2,1)}, u32[]{:S(2)}) copy-start(bf16[4,256,1024]{2,1,0:T(8,128)(2,1)} %param.8) | copy-start | bytes 6291460
  11.7 4.7 %copy-start.12 = (s32[1,1024]{1,0:T(1,128)S(1)}, s32[1,1024]{1,0:T(1,128)}, u32[]{:S(2)}) copy-start(s32[1,1024]{1,0:T(1,128)} %param.10) | copy-start | bytes 12292
  11.7 4.7 %copy-start.13 = (f32[1,1024]{1,0:T(1,128)S(1)}, f32[1,1024]{1,0:T(1,128)}, u32[]{:S(2)}) copy-start(f32[1,1024]{1,0:T(1,128)} %param.11) | copy-start | bytes 12292
  11.7 53.8 %all-to-all-start = ((bf16[2,8,128,1024]{3,2,0,1:T(8,128)(2,1)}), bf16[2,8,128,1024]{3,2,0,1:T(8,128)(2,1)}, u32[]{:S(2)}, u32[]{:S(2)}) async-start(bf16[2,8,128,1024]{3,2,0,1:T(8,128)(2,1)} %pad_maximum_fusion), calls=%async_computation | async-start | bytes 8388608 | tf_op jit(solution)/shard_map/all_to_all | solution.py:43
  16.5 20.3 %collective-permute-start.3 = (f32[2,1024]{1,0:T(2,128)S(1)}, f32[2,1024]{1,0:T(2,128)S(1)}, u32[]{:S(2)}, u32[]{:S(2)}) collective-permute-start(f32[2,1024]{1,0:T(2,128)S(1)} %pad_maximum_fusion.7), channel_id=1, source_target_pairs={{0,0},{1,4},{2,8},{3,12},{4,16},{5,20},{6,24},{7,28},{8,1},{9,5},{... | collective-permute-start | bytes 24584 | tf_op jit(solution)/shard_map/ppermute | solution.py:48
  18.5 2.8 %copy-start.2 = (bf16[4,256,1024]{2,1,0:T(8,128)(2,1)S(1)}, bf16[4,256,1024]{2,1,0:T(8,128)(2,1)}, u32[]{:S(2)}) copy-start(bf16[4,256,1024]{2,1,0:T(8,128)(2,1)} %param.7) | copy-start | bytes 6291460
  24.1 51.5 %collective-permute-start.2 = (bf16[2,256,512]{2,1,0:T(8,128)(2,1)}, bf16[2,256,512]{2,1,0:T(8,128)(2,1)}, u32[]{:S(2)}, u32[]{:S(2)}) collective-permute-start(bf16[2,256,512]{2,1,0:T(8,128)(2,1)} %pad_maximum_fusion.6), channel_id=1, source_target_pairs={{0,3},{1,0},{2,1},{3,2},{4,7},{5,4},{6,5},{7,6},{8,11},{9,8},{10,9... | collective-permute-start | bytes 1572872 | tf_op jit(solution)/shard_map/ppermute | solution.py:36
  25.6 5.1 %copy-start.9 = (bf16[2,256,256]{2,1,0:T(8,128)(2,1)S(1)}, bf16[2,256,256]{2,1,0:T(8,128)(2,1)}, u32[]{:S(2)}) copy-start(bf16[2,256,256]{2,1,0:T(8,128)(2,1)} %get-tuple-element.53) | copy-start | bytes 786436
  25.6 7.8 %copy-start.11 = (s32[4,1024]{1,0:T(4,128)S(1)}, s32[4,1024]{1,0:T(4,128)}, u32[]{:S(2)}) copy-start(s32[4,1024]{1,0:T(4,128)} %param.9) | copy-start | bytes 49156
  26.5 49.1 %collective-permute-start.1 = (bf16[2,256,512]{1,2,0:T(8,128)(2,1)}, bf16[2,256,512]{1,2,0:T(8,128)(2,1)}, u32[]{:S(2)}, u32[]{:S(2)}) collective-permute-start(bf16[2,256,512]{1,2,0:T(8,128)(2,1)} %pad_maximum_fusion.5), channel_id=1, source_target_pairs={{0,2},{1,3},{2,0},{3,1},{4,6},{5,7},{6,4},{7,5},{8,10},{9,11},{10,... | collective-permute-start | bytes 1572872 | tf_op jit(solution)/shard_map/ppermute | solution.py:36
  31.6 44.0 %collective-permute-start = (bf16[2,256,512]{2,1,0:T(8,128)(2,1)}, bf16[2,256,512]{2,1,0:T(8,128)(2,1)}, u32[]{:S(2)}, u32[]{:S(2)}) collective-permute-start(bf16[2,256,512]{2,1,0:T(8,128)(2,1)} %pad_maximum_fusion.4), channel_id=1, source_target_pairs={{0,1},{1,2},{2,3},{3,0},{4,5},{5,6},{6,7},{7,4},{8,9},{9,10},{10,1... | collective-permute-start | bytes 1572872 | tf_op jit(solution)/shard_map/ppermute | solution.py:36
  75.6 3.9 %copy-start.14 = (bf16[2]{0:T(256)(128)(2,1)S(1)}, bf16[2]{0:T(256)(128)(2,1)}, u32[]{:S(2)}) copy-start(bf16[2]{0:T(256)(128)(2,1)} %constant.158.clone) | copy-start | bytes 16
  85.5 4.6 %copy-start.5 = (bf16[2,256,1024]{1,2,0:T(8,128)(2,1)S(1)}, bf16[2,256,1024]{1,2,0:T(8,128)(2,1)}, u32[]{:S(2)}) copy-start(bf16[2,256,1024]{1,2,0:T(8,128)(2,1)} %copy.42) | copy-start | bytes 3145732
  85.5 121.8 %all-to-all-start.1 = ((bf16[32,128,256]{2,1,0:T(8,128)(2,1)}), bf16[32,128,256]{2,1,0:T(8,128)(2,1)}, u32[]{:S(2)}, u32[]{:S(2)}) async-start(bf16[32,128,256]{2,1,0:T(8,128)(2,1)} %bitcast.71), calls=%async_computation.1 | async-start | bytes 4194304 | tf_op jit(solution)/shard_map/all_to_all | solution.py:87
  98.1 4.7 %copy-start.4 = (bf16[4,256,1024]{2,1,0:T(8,128)(2,1)S(1)}, bf16[4,256,1024]{2,1,0:T(8,128)(2,1)}, u32[]{:S(2)}) copy-start(bf16[4,256,1024]{2,1,0:T(8,128)(2,1)} %param.8) | copy-start | bytes 6291460
  98.2 88.5 %collective-permute-start.4 = (f32[256,768]{0,1:T(8,128)S(1)}, f32[256,768]{0,1:T(8,128)S(1)}, u32[]{:S(2)}, u32[]{:S(2)}) collective-permute-start(f32[256,768]{0,1:T(8,128)S(1)} %pad_maximum_fusion.2), channel_id=1, source_target_pairs={{0,1},{1,2},{2,3},{3,0},{4,5},{5,6},{6,7},{7,4},{8,9},{9,10},{10,1... | collective-permute-start | bytes 2359304 | tf_op jit(solution)/shard_map/ppermute | solution.py:99
  99.8 103.3 %collective-permute-start.5 = (f32[256,768]{0,1:T(8,128)S(1)}, f32[256,768]{0,1:T(8,128)S(1)}, u32[]{:S(2)}, u32[]{:S(2)}) collective-permute-start(f32[256,768]{0,1:T(8,128)S(1)} %pad_maximum_fusion.3), channel_id=1, source_target_pairs={{0,2},{1,3},{2,0},{3,1},{4,6},{5,7},{6,4},{7,5},{8,10},{9,11},{10,... | collective-permute-start | bytes 2359304 | tf_op jit(solution)/shard_map/ppermute | solution.py:99
  101.2 104.4 %collective-permute-start.6 = (f32[256,768]{0,1:T(8,128)S(1)}, f32[256,768]{0,1:T(8,128)S(1)}, u32[]{:S(2)}, u32[]{:S(2)}) collective-permute-start(f32[256,768]{0,1:T(8,128)S(1)} %slice.162), channel_id=1, source_target_pairs={{0,3},{1,0},{2,1},{3,2},{4,7},{5,4},{6,5},{7,6},{8,11},{9,8},{10,9... | collective-permute-start | bytes 2359304 | tf_op jit(solution)/shard_map/ppermute | solution.py:99
  210.8 1.1 copy-start.6
  210.9 1.4 copy-start.7
  210.9 1.6 copy-start.8
  210.9 1.9 copy-start.10
  212.8 4.9 %copy-start.1 = (s32[32,8]{0,1:T(8,128)S(1)}, s32[32,8]{0,1:T(8,128)}, u32[]{:S(2)}) copy-start(s32[32,8]{0,1:T(8,128)} %param.12) | copy-start | bytes 3076

commit v18 on v17

--- a/solution.py
+++ b/solution.py
@@ -60,7 +60,6 @@
         part = part - jnp.dot(b_w, a_eta[:, cut], preferred_element_type=f32)
         parts.append((part * coef[:, None]).astype(bf16).reshape(n_chan, slab, rows))
     term_t = jnp.stack(parts, axis=1)
-    ladder_in, _ = lax.optimization_barrier((ladder_in, term_t))
     sign = jnp.array([-1, 1], bf16)[:, None, None]
     own = pair(lambda x: lax.dynamic_index_in_dim(x, level, 0, False))
     own = jnp.roll(own, -level * rows, axis=-1)

time: 218 us -> 233 us (1.069)
  starting transfers between devices: 21.8 us -> 31.5 us
  other arithmetic: 21 us -> 26.4 us
  waiting for transfers between devices: 129 us -> 125 us
  local copies, waits for them, and re-layouts: 30.9 us -> 34.3 us
    all_to_all x1, waiting for transfers between devices: 28.7 us -> 0.01 us  [per_device(): lax.all_to_all(outgoing, 'ch', split_axis=1, concat_axis=1, tiled=True)]
    ppermute x1, waiting for transfers between devices: 0.01 us -> 24.6 us  [per_device(): lax.ppermute(jnp.concatenate([ph_factor.astype(f32), recouple], axis=0),...]
    all_to_all x1, starting transfers between devices: 4.57 us -> 15.7 us  [per_device(): lax.all_to_all(returning.reshape(n_chan * n_rows, slab, rows), ('ch', 'ro...]
    slice x4 -> x0, local copies, waits for them, and re-layouts: 5.39 us -> none  [the longest x2 1.82 us: per_device(): grid[d][succ] = piece[..., rows:]]
    unnamed x32 -> x34, local copies, waits for them, and re-layouts: 3.27 us -> 7.91 us
    mul x0 -> x2, local copies, waits for them, and re-layouts: none -> 3.59 us  [per_device(): grid[d][0] = sign * jnp.swapaxes(grid[0][d], -1, -2)]
    dynamic_slice x3 -> x1, local copies, waits for them, and re-layouts: 5.32 us -> 3.59 us  [per_device(): lax.dynamic_index_in_dim(x, (level + shift) % n_rows, 0, False)]
    another operation x3 -> x4, other arithmetic: 5.46 us -> 6.98 us  [per_device(): pair = lambda f: jnp.stack([f(eta_pp), f(gamma_pp)])]
  transfers between devices with their start and end apart: 9 -> 9, of which waited for: 4 -> 3; matrix products, arithmetic and copies ran while one was open for 16% -> 19% of each run, Pallas kernels for 0% -> 0%
where the time goes in v18:
time: 233 us; the launch traced here: 232 us
  waiting for transfers between devices  125 us (54%)
  local copies, waits for them, and re-layouts  34.3 us (15%)
  starting transfers between devices  31.5 us (14%)
  other arithmetic  26.4 us (11%)
  matrix products  14.6 us (6%)
    ppermute x3, waiting for transfers between devices, per_device(): returned.append(lax.ppermute(sending[shift], 'row', pairs))  100 us
    ppermute x1, waiting for transfers between devices, per_device(): lax.ppermute(jnp.concatenate([ph_factor.astype(f32), recouple], axis=0),...  24.6 us
    all_to_all x1, starting transfers between devices, per_device(): lax.all_to_all(returning.reshape(n_chan * n_rows, slab, rows), ('ch', 'ro...  15.7 us
    unnamed x34, local copies, waits for them, and re-layouts  7.91 us
    another operation x4, other arithmetic, per_device(): pair = lambda f: jnp.stack([f(eta_pp), f(gamma_pp)])  6.98 us
    gather x2, local copies, waits for them, and re-layouts, per_device(): x.reshape(ch_dev, rows // slab, slab, width)[slot_dest, part_dest]  5.78 us
    dot_general x1, matrix products, per_device(): lax.dot_general(left, right, (((1,), (1,)), ((), ())), preferred_element_...  4.84 us
    all_to_all x1, starting transfers between devices, per_device(): lax.all_to_all(outgoing, 'ch', split_axis=1, concat_axis=1, tiled=True)  4.71 us
  transfers between devices with their start and end apart: 9, of which 3 were waited for; matrix products, arithmetic and copies ran while one was open for 19% of the time, Pallas kernels for 0%

profile of v18, /device:TPU:8, one launch (start us, length us, event | category | flops | bytes accessed | tf_op | source)
XLA Modules:
  0.0 232.1 jit_solution(13917542901757526474)
XLA Ops:
  1.4 3.7 %gather_fusion.2 = bf16[8,128,1024]{2,1,0:T(8,128)(2,1)} fusion(bf16[4,2,128,1024]{3,2,1,0:T(8,128)(2,1)} %bitcast.69, s32[8]{0:T(128)S(1)} %fusion.101), kind=kCustom, calls=%fused_computation.2 | custom fusion | bytes 4194368 | tf_op jit(solution)/shard_map/gather | solution.py:42
  5.1 2.0 gather_fusion.1
  7.1 4.6 %pad_maximum_fusion = bf16[2,8,128,1024]{3,2,0,1:T(8,128)(2,1)} fusion(bf16[1,8,128,1024]{3,2,0,1:T(8,128)(2,1)} %bitcast.72, bf16[1,8,128,1024]{3,2,0,1:T(8,128)(2,1)} %bitcast.73), kind=kLoop, calls=%fused_computation.39 | loop fusion | flops 2097152 | bytes 8388608 | tf_op jit(solution)/shard_map/stack | solution.py:24
  11.7 4.7 %all-to-all-start = ((bf16[2,8,128,1024]{3,2,0,1:T(8,128)(2,1)}), bf16[2,8,128,1024]{3,2,0,1:T(8,128)(2,1)}, u32[]{:S(2)}, u32[]{:S(2)}) async-start(bf16[2,8,128,1024]{3,2,0,1:T(8,128)(2,1)} %pad_maximum_fusion), calls=%async_computation | async-start | bytes 8388608 | tf_op jit(solution)/shard_map/all_to_all | solution.py:43
  16.5 3.6 %constant_dynamic-slice_fusion.6 = (bf16[1,256,1024]{2,1,0:T(8,128)(2,1)}, bf16[1,256,1024]{2,1,0:T(8,128)(2,1)S(1)}, bf16[1,256,1024]{2,1,0:T(8,128)(2,1)}, bf1...) fusion(bf16[4,256,1024]{2,1,0:T(8,128)(2,1)S(1)} %copy-done.2, ...), kind=kLoop, calls=%fused_computation.143 | loop fusion | bytes 8388624 | tf_op jit(solution)/shard_map/jit(dynamic_index_in_dim)/dynamic_slice | solution.py:27
  20.1 2.0 copy.59
  22.1 2.0 copy.60
  31.2 2.6 %collective-permute-start.2 = (bf16[2,256,512]{2,1,0:T(8,128)(2,1)}, bf16[2,256,512]{2,1,0:T(8,128)(2,1)}, u32[]{:S(2)}, u32[]{:S(2)}) collective-permute-start(bf16[2,256,512]{2,1,0:T(8,128)(2,1)} %pad_maximum_fusion.7), channel_id=1, source_target_pairs={{0,2},{1,3},{2,0},{3,1},{4,6},{5,7},{6,4},{7,5},{8,10},{9,11},{10,... | collective-permute-start | bytes 1572872 | tf_op jit(solution)/shard_map/ppermute | solution.py:36
  39.8 24.6 %collective-permute-done.6 = f32[2,1024]{1,0:T(2,128)S(1)} collective-permute-done((f32[2,1024]{1,0:T(2,128)S(1)}, f32[2,1024]{1,0:T(2,128)S(1)}, u32[]{:S(2)}, u32[]{:S(2)}) %collective-permute-start.6) | collective-permute-done | bytes 8224 | tf_op jit(solution)/shard_map/ppermute | solution.py:48
  64.4 2.1 fusion.83
  70.1 2.3 pad_maximum_fusion.2
  72.4 2.3 copy.47
  74.7 2.0 copy.44
  76.7 1.9 fusion.81
  78.7 2.7 %fusion.104 = (bf16[1,8,128,1024]{3,2,0,1:T(8,128)(2,1)S(1)}, bf16[1,8,128,1024]{3,2,0,1:T(8,128)(2,1)S(1)}) fusion(bf16[2,8,128,1024]{3,2,0,1:T(8,128)(2,1)} %all-to-all-done), kind=kLoop, calls=%fused_computation.177 | loop fusion | bytes 8388608 | tf_op jit(solution)/shard_map/slice | solution.py:45
  88.7 15.7 %all-to-all-start.1 = ((bf16[32,128,256]{2,1,0:T(8,128)(2,1)}), bf16[32,128,256]{2,1,0:T(8,128)(2,1)}, u32[]{:S(2)}, u32[]{:S(2)}) async-start(bf16[32,128,256]{2,1,0:T(8,128)(2,1)} %bitcast.71), calls=%async_computation.1 | async-start | bytes 4194304 | tf_op jit(solution)/shard_map/all_to_all | solution.py:86
  104.5 2.1 maximum_maximum_fusion
  107.4 4.8 %fusion.11 = f32[1024,1024]{0,1:T(8,128)S(1)} fusion(bf16[1024,1024]{0,1:T(8,128)(2,1)S(1)} %get-tuple-element.10, bf16[1024,1024]{0,1:T(8,128)(2,1)S(1)} %get-tuple-element.9, bf16[1024,1024]{0,1:T(8,128)(2,1)S(1)} %get-tuple-element.18, bf16[1024,1024]{0,1:T(8,128)(2,1)S(1)} %get-tuple-element.17), kind=kOutput, calls=%fused_computation.25 | convolution fusion | flops 4311744512 | bytes 12582912 | tf_op jit(solution)/shard_map/dot_general | solution.py:81
  112.6 2.5 %collective-permute-start.4 = (f32[256,768]{0,1:T(8,128)S(1)}, f32[256,768]{0,1:T(8,128)S(1)}, u32[]{:S(2)}, u32[]{:S(2)}) collective-permute-start(f32[256,768]{0,1:T(8,128)S(1)} %pad_maximum_fusion.4), channel_id=1, source_target_pairs={{0,2},{1,3},{2,0},{3,1},{4,6},{5,7},{6,4},{7,5},{8,10},{9,11},{10,... | collective-permute-start | bytes 2359304 | tf_op jit(solution)/shard_map/ppermute | solution.py:98
  117.5 2.3 fusion.18
  119.8 81.2 %collective-permute-done.4 = f32[256,768]{0,1:T(8,128)S(1)} collective-permute-done((f32[256,768]{0,1:T(8,128)S(1)}, f32[256,768]{0,1:T(8,128)S(1)}, u32[]{:S(2)}, u32[]{:S(2)}) %collective-permute-start.4) | collective-permute-done | bytes 786464 | tf_op jit(solution)/shard_map/ppermute | solution.py:98
  201.0 19.0 %collective-permute-done.5 = f32[256,768]{0,1:T(8,128)S(1)} collective-permute-done((f32[256,768]{0,1:T(8,128)S(1)}, f32[256,768]{0,1:T(8,128)S(1)}, u32[]{:S(2)}, u32[]{:S(2)}) %collective-permute-start.5) | collective-permute-done | bytes 786464 | tf_op jit(solution)/shard_map/ppermute | solution.py:98
  227.2 2.5 %fusion.7 = bf16[4,256,1024]{1,2,0:T(8,128)(2,1)S(1)} fusion(s32[]{:T(128)S(6)} %select_n.311, f32[1,256,768]{1,2,0:T(8,128)S(1)} %copy-done.7, f32[1,256,768]{1,2,0:T(8,128)S(1)} %copy-done.6, f32[1,256,768]{1,2,0:T(8,128)S(1)} %copy-done.5, f32[1,256,768]{1,2,0:T(8,128)S(1)} %get-tuple-element.5, f32[4,256,256]{1,2,0:T(8,128)S(1)} %copy-done.10, ...), kind=kLoop, calls=%fused_computation.20 | loop fusion | flops 11534336 | bytes 10485764 | tf_op jit(solution)/shard_map/convert_element_type | solution.py:113
  229.7 2.4 %copy.55 = bf16[4,256,1024]{2,1,0:T(8,128)(2,1)} copy(bf16[4,256,1024]{1,2,0:T(8,128)(2,1)S(1)} %fusion.7) | data formatting | bytes 4194304 | tf_op jit(solution)/shard_map/convert_element_type | solution.py:113
  (85 shorter events, 35.8 us)
Async XLA Ops:
  0.0 0.7 copy-start
  1.3 3.8 %copy-start.3 = (bf16[4,256,1024]{2,1,0:T(8,128)(2,1)S(1)}, bf16[4,256,1024]{2,1,0:T(8,128)(2,1)}, u32[]{:S(2)}) copy-start(bf16[4,256,1024]{2,1,0:T(8,128)(2,1)} %param.7) | copy-start | bytes 6291460
  11.7 4.8 %copy-start.2 = (bf16[4,256,1024]{2,1,0:T(8,128)(2,1)S(1)}, bf16[4,256,1024]{2,1,0:T(8,128)(2,1)}, u32[]{:S(2)}) copy-start(bf16[4,256,1024]{2,1,0:T(8,128)(2,1)} %param.8) | copy-start | bytes 6291460
  11.7 67.0 %all-to-all-start = ((bf16[2,8,128,1024]{3,2,0,1:T(8,128)(2,1)}), bf16[2,8,128,1024]{3,2,0,1:T(8,128)(2,1)}, u32[]{:S(2)}, u32[]{:S(2)}) async-start(bf16[2,8,128,1024]{3,2,0,1:T(8,128)(2,1)} %pad_maximum_fusion), calls=%async_computation | async-start | bytes 8388608 | tf_op jit(solution)/shard_map/all_to_all | solution.py:43
  26.1 38.3 %collective-permute-start.1 = (bf16[2,256,512]{1,2,0:T(8,128)(2,1)}, bf16[2,256,512]{1,2,0:T(8,128)(2,1)}, u32[]{:S(2)}, u32[]{:S(2)}) collective-permute-start(bf16[2,256,512]{1,2,0:T(8,128)(2,1)} %pad_maximum_fusion.6), channel_id=1, source_target_pairs={{0,1},{1,2},{2,3},{3,0},{4,5},{5,6},{6,7},{7,4},{8,9},{9,10},{10,1... | collective-permute-start | bytes 1572872 | tf_op jit(solution)/shard_map/ppermute | solution.py:36
  27.7 2.5 %copy-start.8 = (bf16[1,256,1024]{2,1,0:T(8,128)(2,1)S(1)}, bf16[1,256,1024]{2,1,0:T(8,128)(2,1)}, u32[]{:S(2)}) copy-start(bf16[1,256,1024]{2,1,0:T(8,128)(2,1)} %get-tuple-element.21) | copy-start | bytes 1572868
  27.7 2.5 %copy-start.9 = (bf16[1,256,1024]{2,1,0:T(8,128)(2,1)S(1)}, bf16[1,256,1024]{2,1,0:T(8,128)(2,1)}, u32[]{:S(2)}) copy-start(bf16[1,256,1024]{2,1,0:T(8,128)(2,1)} %get-tuple-element.47) | copy-start | bytes 1572868
  28.9 4.8 %copy-start.12 = (s32[1,1024]{1,0:T(1,128)S(1)}, s32[1,1024]{1,0:T(1,128)}, u32[]{:S(2)}) copy-start(s32[1,1024]{1,0:T(1,128)} %param.10) | copy-start | bytes 12292
  28.9 4.8 %copy-start.13 = (f32[1,1024]{1,0:T(1,128)S(1)}, f32[1,1024]{1,0:T(1,128)}, u32[]{:S(2)}) copy-start(f32[1,1024]{1,0:T(1,128)} %param.11) | copy-start | bytes 12292
  29.8 40.3 %collective-permute-start = (bf16[2,256,512]{2,1,0:T(8,128)(2,1)}, bf16[2,256,512]{2,1,0:T(8,128)(2,1)}, u32[]{:S(2)}, u32[]{:S(2)}) collective-permute-start(bf16[2,256,512]{2,1,0:T(8,128)(2,1)} %pad_maximum_fusion.5), channel_id=1, source_target_pairs={{0,3},{1,0},{2,1},{3,2},{4,7},{5,4},{6,5},{7,6},{8,11},{9,8},{10,9... | collective-permute-start | bytes 1572872 | tf_op jit(solution)/shard_map/ppermute | solution.py:36
  31.2 43.5 %collective-permute-start.2 = (bf16[2,256,512]{2,1,0:T(8,128)(2,1)}, bf16[2,256,512]{2,1,0:T(8,128)(2,1)}, u32[]{:S(2)}, u32[]{:S(2)}) collective-permute-start(bf16[2,256,512]{2,1,0:T(8,128)(2,1)} %pad_maximum_fusion.7), channel_id=1, source_target_pairs={{0,2},{1,3},{2,0},{3,1},{4,6},{5,7},{6,4},{7,5},{8,10},{9,11},{10,... | collective-permute-start | bytes 1572872 | tf_op jit(solution)/shard_map/ppermute | solution.py:36
  33.8 30.6 %collective-permute-start.6 = (f32[2,1024]{1,0:T(2,128)S(1)}, f32[2,1024]{1,0:T(2,128)S(1)}, u32[]{:S(2)}, u32[]{:S(2)}) collective-permute-start(f32[2,1024]{1,0:T(2,128)S(1)} %pad_maximum_fusion.8), channel_id=1, source_target_pairs={{0,0},{1,4},{2,8},{3,12},{4,16},{5,20},{6,24},{7,28},{8,1},{9,5},{... | collective-permute-start | bytes 24584 | tf_op jit(solution)/shard_map/ppermute | solution.py:48
  35.7 3.8 %copy-start.11 = (s32[4,1024]{1,0:T(4,128)S(1)}, s32[4,1024]{1,0:T(4,128)}, u32[]{:S(2)}) copy-start(s32[4,1024]{1,0:T(4,128)} %param.9) | copy-start | bytes 49156
  35.7 28.7 %copy-start.14 = (bf16[2]{0:T(256)(128)(2,1)S(1)}, bf16[2]{0:T(256)(128)(2,1)}, u32[]{:S(2)}) copy-start(bf16[2]{0:T(256)(128)(2,1)} %constant.158.clone) | copy-start | bytes 16
  88.7 133.0 %all-to-all-start.1 = ((bf16[32,128,256]{2,1,0:T(8,128)(2,1)}), bf16[32,128,256]{2,1,0:T(8,128)(2,1)}, u32[]{:S(2)}, u32[]{:S(2)}) async-start(bf16[32,128,256]{2,1,0:T(8,128)(2,1)} %bitcast.71), calls=%async_computation.1 | async-start | bytes 4194304 | tf_op jit(solution)/shard_map/all_to_all | solution.py:86
  112.5 4.7 %copy-start.4 = (bf16[4,256,1024]{2,1,0:T(8,128)(2,1)S(1)}, bf16[4,256,1024]{2,1,0:T(8,128)(2,1)}, u32[]{:S(2)}) copy-start(bf16[4,256,1024]{2,1,0:T(8,128)(2,1)} %param.7) | copy-start | bytes 6291460
  112.6 88.4 %collective-permute-start.4 = (f32[256,768]{0,1:T(8,128)S(1)}, f32[256,768]{0,1:T(8,128)S(1)}, u32[]{:S(2)}, u32[]{:S(2)}) collective-permute-start(f32[256,768]{0,1:T(8,128)S(1)} %pad_maximum_fusion.4), channel_id=1, source_target_pairs={{0,2},{1,3},{2,0},{3,1},{4,6},{5,7},{6,4},{7,5},{8,10},{9,11},{10,... | collective-permute-start | bytes 2359304 | tf_op jit(solution)/shard_map/ppermute | solution.py:98
  115.1 105.0 %collective-permute-start.5 = (f32[256,768]{0,1:T(8,128)S(1)}, f32[256,768]{0,1:T(8,128)S(1)}, u32[]{:S(2)}, u32[]{:S(2)}) collective-permute-start(f32[256,768]{0,1:T(8,128)S(1)} %slice.154), channel_id=1, source_target_pairs={{0,3},{1,0},{2,1},{3,2},{4,7},{5,4},{6,5},{7,6},{8,11},{9,8},{10,9... | collective-permute-start | bytes 2359304 | tf_op jit(solution)/shard_map/ppermute | solution.py:98
  115.6 104.4 %collective-permute-start.3 = (f32[256,768]{0,1:T(8,128)S(1)}, f32[256,768]{0,1:T(8,128)S(1)}, u32[]{:S(2)}, u32[]{:S(2)}) collective-permute-start(f32[256,768]{0,1:T(8,128)S(1)} %pad_maximum_fusion.3), channel_id=1, source_target_pairs={{0,1},{1,2},{2,3},{3,0},{4,5},{5,6},{6,7},{7,4},{8,9},{9,10},{10,1... | collective-permute-start | bytes 2359304 | tf_op jit(solution)/shard_map/ppermute | solution.py:98
  225.2 1.1 copy-start.5
  225.2 1.4 copy-start.6
  225.3 1.6 copy-start.7
  225.3 1.9 copy-start.10
  227.2 4.9 %copy-start.1 = (s32[32,8]{0,1:T(8,128)S(1)}, s32[32,8]{0,1:T(8,128)}, u32[]{:S(2)}) copy-start(s32[32,8]{0,1:T(8,128)} %param.12) | copy-start | bytes 3076

commit v19 on v17

--- a/solution.py
+++ b/solution.py
@@ -51,13 +51,11 @@
     weight = coefs[0].astype(bf16)[None, :]
     coef = coefs[1]
 
-    a_w = a_eta * weight
-    b_w = b_gamma * weight
+    lhs = jnp.concatenate([a_eta * weight, b_gamma * weight], axis=1)
+    rhs = jnp.concatenate([b_gamma, -a_eta], axis=0)
     parts = []
     for r in range(n_rows):
-        cut = slice(r * rows, (r + 1) * rows)
-        part = jnp.dot(a_w, b_gamma[:, cut], preferred_element_type=f32)
-        part = part - jnp.dot(b_w, a_eta[:, cut], preferred_element_type=f32)
+        part = jnp.dot(lhs, rhs[:, r * rows : (r + 1) * rows], preferred_element_type=f32)
         parts.append((part * coef[:, None]).astype(bf16).reshape(n_chan, slab, rows))
     term_t = jnp.stack(parts, axis=1)
     ladder_in, _ = lax.optimization_barrier((ladder_in, term_t))

time: 218 us -> 218 us (level)
    dot_general x8 -> x4, matrix products: 5.73 us -> 5.03 us  [per_device(): jnp.dot(lhs, rhs[:, r * rows:(r + 1) * rows], preferred_element_type=f32)]
where the time goes in v19:
time: 218 us
  waiting for transfers between devices  128 us (59%)
  local copies, waits for them, and re-layouts  30.7 us (14%)
  other arithmetic  22.6 us (10%)
  starting transfers between devices  22 us (10%)
  matrix products  13.8 us (6%)
    ppermute x3, waiting for transfers between devices, per_device(): returned.append(lax.ppermute(sending[shift], 'row', pairs))  100 us
    all_to_all x1, waiting for transfers between devices, per_device(): lax.all_to_all(outgoing, 'ch', split_axis=1, concat_axis=1, tiled=True)  27.8 us
    ppermute x3, starting transfers between devices, per_device(): lax.ppermute(jnp.concatenate([own_blk, next_blk], axis=-1), 'row', pairs)  6.06 us
    gather x2, local copies, waits for them, and re-layouts, per_device(): x.reshape(ch_dev, rows // slab, slab, width)[slot_dest, part_dest]  5.64 us
    another operation x3, other arithmetic, per_device(): pair = lambda f: jnp.stack([f(eta_pp), f(gamma_pp)])  5.46 us
    dot_general x4, matrix products, per_device(): jnp.dot(lhs, rhs[:, r * rows:(r + 1) * rows], preferred_element_type=f32)  5.03 us
    dot_general x1, matrix products, per_device(): lax.dot_general(left, right, (((1,), (1,)), ((), ())), preferred_element_...  4.81 us
    all_to_all x1, starting transfers between devices, per_device(): lax.all_to_all(outgoing, 'ch', split_axis=1, concat_axis=1, tiled=True)  4.7 us
  transfers between devices with their start and end apart: 9, of which 4 were waited for; matrix products, arithmetic and copies ran while one was open for 16% of the time, Pallas kernels for 0%

profile of v19, /device:TPU:8, one launch (start us, length us, event | category | flops | bytes accessed | tf_op | source)
XLA Modules:
  0.0 217.5 jit_solution(705587635114739604)
XLA Ops:
  1.3 3.6 %gather_fusion.1 = bf16[8,128,1024]{2,1,0:T(8,128)(2,1)} fusion(bf16[4,2,128,1024]{3,2,1,0:T(8,128)(2,1)} %bitcast.72, s32[8]{0:T(128)S(1)} %fusion.66), kind=kCustom, calls=%fused_computation.1 | custom fusion | bytes 4194368 | tf_op jit(solution)/shard_map/gather | solution.py:42
  5.0 2.0 gather_fusion.2
  7.0 4.6 %pad_maximum_fusion = bf16[2,8,128,1024]{3,2,0,1:T(8,128)(2,1)} fusion(bf16[1,8,128,1024]{3,2,0,1:T(8,128)(2,1)} %bitcast.76, bf16[1,8,128,1024]{3,2,0,1:T(8,128)(2,1)} %bitcast.75), kind=kLoop, calls=%fused_computation.30 | loop fusion | flops 2097152 | bytes 8388608 | tf_op jit(solution)/shard_map/stack | solution.py:24
  11.6 4.7 %all-to-all-start = ((bf16[2,8,128,1024]{3,2,0,1:T(8,128)(2,1)}), bf16[2,8,128,1024]{3,2,0,1:T(8,128)(2,1)}, u32[]{:S(2)}, u32[]{:S(2)}) async-start(bf16[2,8,128,1024]{3,2,0,1:T(8,128)(2,1)} %pad_maximum_fusion), calls=%async_computation | async-start | bytes 8388608 | tf_op jit(solution)/shard_map/all_to_all | solution.py:43
  16.3 2.1 collective-permute-start.3
  18.4 2.6 %constant_dynamic-slice_fusion.8 = (bf16[1,256,1024]{2,1,0:T(8,128)(2,1)}, bf16[1,256,1024]{2,1,0:T(8,128)(2,1)S(1)}, bf16[1,256,1024]{2,1,0:T(8,128)(2,1)S(1)}, bf16[1,256,1024]{2,1,0:T(8,128)(2,1)S(1)}) fusion(bf16[4,256,1024]{2,1,0:T(8,128)(2,1)} %param.8, s32[]{:T(128)S(6)} %select_n.263, s32[]{:T(128)S(6)} %select_n.274, s32[]{:T(128)S(6)} %select_n.271, ...), kind=kLoop, calls=%fused_computation.125 | loop fusion | bytes 4194320 | tf_op jit(solution)/shard_map/jit(dynamic_index_in_dim)/dynamic_slice | solution.py:63
  26.3 4.2 %collective-permute-start.1 = (bf16[2,256,512]{1,2,0:T(8,128)(2,1)}, bf16[2,256,512]{1,2,0:T(8,128)(2,1)}, u32[]{:S(2)}, u32[]{:S(2)}) collective-permute-start(bf16[2,256,512]{1,2,0:T(8,128)(2,1)} %pad_maximum_fusion.8), channel_id=1, source_target_pairs={{0,2},{1,3},{2,0},{3,1},{4,6},{5,7},{6,4},{7,5},{8,10},{9,11},{10,... | collective-permute-start | bytes 1572872 | tf_op jit(solution)/shard_map/ppermute | solution.py:36
  30.5 1.8 pad_maximum_fusion.7
  32.3 1.8 collective-permute-start
  37.6 27.8 %all-to-all-done = bf16[2,8,128,1024]{3,2,0,1:T(8,128)(2,1)} async-done(((bf16[2,8,128,1024]{3,2,0,1:T(8,128)(2,1)}), bf16[2,8,128,1024]{3,2,0,1:T(8,128)(2,1)}, u32[]{:S(2)}, u32[]{:S(2)}) %all-to-all-start) | async-done | bytes 4194336 | tf_op jit(solution)/shard_map/all_to_all | solution.py:43
  65.4 2.7 %fusion.75 = (bf16[1,8,128,1024]{3,2,0,1:T(8,128)(2,1)S(1)}, bf16[1,8,128,1024]{3,2,0,1:T(8,128)(2,1)S(1)}) fusion(bf16[2,8,128,1024]{3,2,0,1:T(8,128)(2,1)} %all-to-all-done), kind=kLoop, calls=%fused_computation.163 | loop fusion | bytes 8388608 | tf_op jit(solution)/shard_map/slice | solution.py:45
  77.2 2.1 copy.38
  79.3 2.4 %fusion.48 = (bf16[2,256,256]{1,2,0:T(8,128)(2,1)S(1)}, bf16[2,256,256]{1,2,0:T(8,128)(2,1)}, bf16[2,256,256]{1,2,0:T(8,128)(2,1)}, bf16[2,256,256]{2,1,0:T(8,12...) fusion(bf16[2,256,1024]{2,1,0:T(8,128)(2,1)S(1)} %fusion.31, ...), kind=kLoop, calls=%fused_computation.111 | loop fusion | flops 786432 | bytes 3932164 | tf_op jit(solution)/shard_map/mul | solution.py:71
  81.7 1.9 copy.40
  85.4 4.6 %all-to-all-start.1 = ((bf16[32,128,256]{2,1,0:T(8,128)(2,1)}), bf16[32,128,256]{2,1,0:T(8,128)(2,1)}, u32[]{:S(2)}, u32[]{:S(2)}) async-start(bf16[32,128,256]{2,1,0:T(8,128)(2,1)} %bitcast.74), calls=%async_computation.1 | async-start | bytes 4194304 | tf_op jit(solution)/shard_map/all_to_all | solution.py:85
  90.0 2.2 maximum_maximum_fusion
  93.0 4.8 %fusion.11 = f32[1024,1024]{0,1:T(8,128)S(1)} fusion(bf16[1024,1024]{0,1:T(8,128)(2,1)S(1)} %get-tuple-element.16, bf16[1024,1024]{0,1:T(8,128)(2,1)S(1)} %get-tuple-element.15, bf16[1024,1024]{0,1:T(8,128)(2,1)S(1)} %get-tuple-element.22, bf16[1024,1024]{0,1:T(8,128)(2,1)S(1)} %get-tuple-element.21), kind=kOutput, calls=%fused_computation.33 | convolution fusion | flops 4311744512 | bytes 12582912 | tf_op jit(solution)/shard_map/dot_general | solution.py:80
  103.0 2.3 %fusion.18 = f32[4,256,256]{1,2,0:T(8,128)} fusion(bf16[4,256,1024]{2,1,0:T(8,128)(2,1)S(1)} %get-tuple-element.48, bf16[4,256,1024]{2,1,0:T(8,128)(2,1)S(1)} %get-tuple-element.47, bf16[4,256,1024]{2,1,0:T(8,128)(2,1)S(1)} %copy-done.2, bf16[4,256,1024]{2,1,0:T(8,128)(2,1)S(1)} %copy-done.4), kind=kOutput, calls=%fused_computation.40 | convolution fusion | flops 1090519040 | bytes 9437184 | tf_op jit(solution)/shard_map/sik,sjk->sij/dot_general | solution.py:109
  105.3 81.3 %collective-permute-done.4 = f32[256,768]{0,1:T(8,128)S(1)} collective-permute-done((f32[256,768]{0,1:T(8,128)S(1)}, f32[256,768]{0,1:T(8,128)S(1)}, u32[]{:S(2)}, u32[]{:S(2)}) %collective-permute-start.4) | collective-permute-done | bytes 786464 | tf_op jit(solution)/shard_map/ppermute | solution.py:97
  186.6 16.4 %collective-permute-done.5 = f32[256,768]{0,1:T(8,128)S(1)} collective-permute-done((f32[256,768]{0,1:T(8,128)S(1)}, f32[256,768]{0,1:T(8,128)S(1)}, u32[]{:S(2)}, u32[]{:S(2)}) %collective-permute-start.5) | collective-permute-done | bytes 786464 | tf_op jit(solution)/shard_map/ppermute | solution.py:97
  202.9 2.6 %collective-permute-done.6 = f32[256,768]{0,1:T(8,128)S(1)} collective-permute-done((f32[256,768]{0,1:T(8,128)S(1)}, f32[256,768]{0,1:T(8,128)S(1)}, u32[]{:S(2)}, u32[]{:S(2)}) %collective-permute-start.6) | collective-permute-done | bytes 786464 | tf_op jit(solution)/shard_map/ppermute | solution.py:97
  207.2 1.8 copy.43
  212.7 2.5 %fusion.7 = bf16[4,256,1024]{1,2,0:T(8,128)(2,1)S(1)} fusion(s32[]{:T(128)S(6)} %select_n.316, f32[1,256,768]{1,2,0:T(8,128)S(1)} %copy-done.8, f32[1,256,768]{1,2,0:T(8,128)S(1)} %copy-done.7, f32[1,256,768]{1,2,0:T(8,128)S(1)} %copy-done.6, f32[1,256,768]{1,2,0:T(8,128)S(1)} %get-tuple-element.11, f32[4,256,256]{1,2,0:T(8,128)S(1)} %copy-done.9, ...), kind=kLoop, calls=%fused_computation.26 | loop fusion | flops 11534336 | bytes 10485764 | tf_op jit(solution)/shard_map/convert_element_type | solution.py:112
  215.2 2.4 %copy.46 = bf16[4,256,1024]{2,1,0:T(8,128)(2,1)} copy(bf16[4,256,1024]{1,2,0:T(8,128)(2,1)S(1)} %fusion.7) | data formatting | bytes 4194304 | tf_op jit(solution)/shard_map/convert_element_type | solution.py:112
  (78 shorter events, 32.0 us)
Async XLA Ops:
  0.0 0.7 copy-start
  0.0 5.0 %copy-start.3 = (bf16[4,256,1024]{2,1,0:T(8,128)(2,1)S(1)}, bf16[4,256,1024]{2,1,0:T(8,128)(2,1)}, u32[]{:S(2)}) copy-start(bf16[4,256,1024]{2,1,0:T(8,128)(2,1)} %param.8) | copy-start | bytes 6291460
  11.6 4.7 %copy-start.11 = (s32[1,1024]{1,0:T(1,128)S(1)}, s32[1,1024]{1,0:T(1,128)}, u32[]{:S(2)}) copy-start(s32[1,1024]{1,0:T(1,128)} %param.10) | copy-start | bytes 12292
  11.6 4.7 %copy-start.12 = (f32[1,1024]{1,0:T(1,128)S(1)}, f32[1,1024]{1,0:T(1,128)}, u32[]{:S(2)}) copy-start(f32[1,1024]{1,0:T(1,128)} %param.11) | copy-start | bytes 12292
  11.6 53.8 %all-to-all-start = ((bf16[2,8,128,1024]{3,2,0,1:T(8,128)(2,1)}), bf16[2,8,128,1024]{3,2,0,1:T(8,128)(2,1)}, u32[]{:S(2)}, u32[]{:S(2)}) async-start(bf16[2,8,128,1024]{3,2,0,1:T(8,128)(2,1)} %pad_maximum_fusion), calls=%async_computation | async-start | bytes 8388608 | tf_op jit(solution)/shard_map/all_to_all | solution.py:43
  16.3 4.8 %copy-start.2 = (bf16[4,256,1024]{2,1,0:T(8,128)(2,1)S(1)}, bf16[4,256,1024]{2,1,0:T(8,128)(2,1)}, u32[]{:S(2)}) copy-start(bf16[4,256,1024]{2,1,0:T(8,128)(2,1)} %param.7) | copy-start | bytes 6291460
  16.3 21.2 %collective-permute-start.3 = (f32[2,1024]{1,0:T(2,128)S(1)}, f32[2,1024]{1,0:T(2,128)S(1)}, u32[]{:S(2)}, u32[]{:S(2)}) collective-permute-start(f32[2,1024]{1,0:T(2,128)S(1)} %pad_maximum_fusion.10), channel_id=1, source_target_pairs={{0,0},{1,4},{2,8},{3,12},{4,16},{5,20},{6,24},{7,28},{8,1},{9,5},{... | collective-permute-start | bytes 24584 | tf_op jit(solution)/shard_map/ppermute | solution.py:48
  23.1 11.1 %copy-start.10 = (s32[4,1024]{1,0:T(4,128)S(1)}, s32[4,1024]{1,0:T(4,128)}, u32[]{:S(2)}) copy-start(s32[4,1024]{1,0:T(4,128)} %param.9) | copy-start | bytes 49156
  24.0 51.4 %collective-permute-start.2 = (bf16[2,256,512]{2,1,0:T(8,128)(2,1)}, bf16[2,256,512]{2,1,0:T(8,128)(2,1)}, u32[]{:S(2)}, u32[]{:S(2)}) collective-permute-start(bf16[2,256,512]{2,1,0:T(8,128)(2,1)} %pad_maximum_fusion.9), channel_id=1, source_target_pairs={{0,3},{1,0},{2,1},{3,2},{4,7},{5,4},{6,5},{7,6},{8,11},{9,8},{10,9... | collective-permute-start | bytes 1572872 | tf_op jit(solution)/shard_map/ppermute | solution.py:36
  26.3 49.1 %collective-permute-start.1 = (bf16[2,256,512]{1,2,0:T(8,128)(2,1)}, bf16[2,256,512]{1,2,0:T(8,128)(2,1)}, u32[]{:S(2)}, u32[]{:S(2)}) collective-permute-start(bf16[2,256,512]{1,2,0:T(8,128)(2,1)} %pad_maximum_fusion.8), channel_id=1, source_target_pairs={{0,2},{1,3},{2,0},{3,1},{4,6},{5,7},{6,4},{7,5},{8,10},{9,11},{10,... | collective-permute-start | bytes 1572872 | tf_op jit(solution)/shard_map/ppermute | solution.py:36
  32.3 43.0 %collective-permute-start = (bf16[2,256,512]{2,1,0:T(8,128)(2,1)}, bf16[2,256,512]{2,1,0:T(8,128)(2,1)}, u32[]{:S(2)}, u32[]{:S(2)}) collective-permute-start(bf16[2,256,512]{2,1,0:T(8,128)(2,1)} %pad_maximum_fusion.7), channel_id=1, source_target_pairs={{0,1},{1,2},{2,3},{3,0},{4,5},{5,6},{6,7},{7,4},{8,9},{9,10},{10,1... | collective-permute-start | bytes 1572872 | tf_op jit(solution)/shard_map/ppermute | solution.py:36
  73.8 5.5 %copy-start.13 = (bf16[2]{0:T(256)(128)(2,1)S(1)}, bf16[2]{0:T(256)(128)(2,1)}, u32[]{:S(2)}) copy-start(bf16[2]{0:T(256)(128)(2,1)} %constant.158.clone) | copy-start | bytes 16
  81.7 8.3 %copy-start.5 = (bf16[2,256,1024]{1,2,0:T(8,128)(2,1)S(1)}, bf16[2,256,1024]{1,2,0:T(8,128)(2,1)}, u32[]{:S(2)}) copy-start(bf16[2,256,1024]{1,2,0:T(8,128)(2,1)} %copy.42) | copy-start | bytes 3145732
  85.4 121.8 %all-to-all-start.1 = ((bf16[32,128,256]{2,1,0:T(8,128)(2,1)}), bf16[32,128,256]{2,1,0:T(8,128)(2,1)}, u32[]{:S(2)}, u32[]{:S(2)}) async-start(bf16[32,128,256]{2,1,0:T(8,128)(2,1)} %bitcast.74), calls=%async_computation.1 | async-start | bytes 4194304 | tf_op jit(solution)/shard_map/all_to_all | solution.py:85
  97.8 4.9 %copy-start.4 = (bf16[4,256,1024]{2,1,0:T(8,128)(2,1)S(1)}, bf16[4,256,1024]{2,1,0:T(8,128)(2,1)}, u32[]{:S(2)}) copy-start(bf16[4,256,1024]{2,1,0:T(8,128)(2,1)} %param.8) | copy-start | bytes 6291460
  98.1 88.5 %collective-permute-start.4 = (f32[256,768]{0,1:T(8,128)S(1)}, f32[256,768]{0,1:T(8,128)S(1)}, u32[]{:S(2)}, u32[]{:S(2)}) collective-permute-start(f32[256,768]{0,1:T(8,128)S(1)} %pad_maximum_fusion.5), channel_id=1, source_target_pairs={{0,1},{1,2},{2,3},{3,0},{4,5},{5,6},{6,7},{7,4},{8,9},{9,10},{10,1... | collective-permute-start | bytes 2359304 | tf_op jit(solution)/shard_map/ppermute | solution.py:97
  99.6 103.3 %collective-permute-start.5 = (f32[256,768]{0,1:T(8,128)S(1)}, f32[256,768]{0,1:T(8,128)S(1)}, u32[]{:S(2)}, u32[]{:S(2)}) collective-permute-start(f32[256,768]{0,1:T(8,128)S(1)} %pad_maximum_fusion.6), channel_id=1, source_target_pairs={{0,2},{1,3},{2,0},{3,1},{4,6},{5,7},{6,4},{7,5},{8,10},{9,11},{10,... | collective-permute-start | bytes 2359304 | tf_op jit(solution)/shard_map/ppermute | solution.py:97
  101.1 104.4 %collective-permute-start.6 = (f32[256,768]{0,1:T(8,128)S(1)}, f32[256,768]{0,1:T(8,128)S(1)}, u32[]{:S(2)}, u32[]{:S(2)}) collective-permute-start(f32[256,768]{0,1:T(8,128)S(1)} %slice.144), channel_id=1, source_target_pairs={{0,3},{1,0},{2,1},{3,2},{4,7},{5,4},{6,5},{7,6},{8,11},{9,8},{10,9... | collective-permute-start | bytes 2359304 | tf_op jit(solution)/shard_map/ppermute | solution.py:97
  210.7 1.1 copy-start.6
  210.7 1.4 copy-start.7
  210.7 1.6 copy-start.8
  210.7 1.9 copy-start.9
  212.7 4.9 %copy-start.1 = (s32[32,8]{0,1:T(8,128)S(1)}, s32[32,8]{0,1:T(8,128)}, u32[]{:S(2)}) copy-start(s32[32,8]{0,1:T(8,128)} %param.12) | copy-start | bytes 3076

commit v20 on v17

--- a/solution.py
+++ b/solution.py
@@ -39,10 +39,12 @@
     q_dest = level * n_chan + dest
     slot_dest = src_slot[q_dest, mine]
     part_dest = q_dest // ch_dev - level * (rows // slab)
-    outgoing = pair(lambda x: x.reshape(ch_dev, rows // slab, slab, width)[slot_dest, part_dest])
-    arrived = lax.all_to_all(outgoing, "ch", split_axis=1, concat_axis=1, tiled=True)
-    a_eta = arrived[0].reshape(width, width)
-    b_gamma = arrived[1].reshape(width, width)
+    slabs = lambda x: lax.all_to_all(
+        x.reshape(ch_dev, rows // slab, slab, width)[slot_dest, part_dest],
+        "ch", split_axis=0, concat_axis=0, tiled=True,
+    )
+    a_eta = slabs(eta_pp).reshape(width, width)
+    b_gamma = slabs(gamma_pp).reshape(width, width)
 
     perm = [(q, (q % n_chan) * n_rows + q // n_chan) for q in range(n_total)]
     coefs = lax.ppermute(

time: 218 us -> 242 us (1.11)
  matrix products: 14.6 us -> 27.9 us
  waiting for transfers between devices: 129 us -> 142 us
  starting transfers between devices: 21.8 us -> 26.6 us
  other arithmetic: 21 us -> 16.5 us
  local copies, waits for them, and re-layouts: 30.9 us -> 28.1 us
    ppermute x3, waiting for transfers between devices: 0.01 us -> 10.9 us  [per_device(): lax.ppermute(jnp.concatenate([own_blk, next_blk], axis=-1), 'row', pairs)]
    dot_general x4, matrix products: 2.86 us -> 9.55 us  [per_device(): part = jnp.dot(a_w, b_gamma[:, cut], preferred_element_type=f32)]
    dot_general x4, matrix products: 2.87 us -> 9.55 us  [per_device(): part = part - jnp.dot(b_w, a_eta[:, cut], preferred_element_type=f32)]
    another operation x3 -> x2, other arithmetic: 5.46 us -> 0.9 us  [per_device(): pair = lambda f: jnp.stack([f(eta_pp), f(gamma_pp)])]
    all_to_all x1 -> x2, starting transfers between devices: 4.7 us -> 8.84 us  [per_device(): lax.all_to_all(x.reshape(ch_dev, rows // slab, slab, width)[slot_dest, pa...]
    slice x1 -> x0, local copies, waits for them, and re-layouts: 2.7 us -> none  [per_device(): b_gamma = arrived[1].reshape(width, width)]
    all_to_all x1 -> x2, waiting for transfers between devices: 28.7 us -> 30.7 us  [per_device(): lax.all_to_all(x.reshape(ch_dev, rows // slab, slab, width)[slot_dest, pa...]
  transfers between devices with their start and end apart: 9 -> 10, of which waited for: 4 -> 6; matrix products, arithmetic and copies ran while one was open for 16% -> 20% of each run, Pallas kernels for 0% -> 0%
where the time goes in v20:
time: 242 us; the launch traced here: 241 us
  waiting for transfers between devices  142 us (59%)
  local copies, waits for them, and re-layouts  28.1 us (12%)
  matrix products  27.9 us (12%)
  starting transfers between devices  26.6 us (11%)
  other arithmetic  16.5 us (7%)
    ppermute x3, waiting for transfers between devices, per_device(): returned.append(lax.ppermute(sending[shift], 'row', pairs))  100 us
    all_to_all x2, waiting for transfers between devices, per_device(): lax.all_to_all(x.reshape(ch_dev, rows // slab, slab, width)[slot_dest, pa...  30.7 us
    ppermute x3, waiting for transfers between devices, per_device(): lax.ppermute(jnp.concatenate([own_blk, next_blk], axis=-1), 'row', pairs)  10.9 us
    dot_general x4, matrix products, per_device(): part = part - jnp.dot(b_w, a_eta[:, cut], preferred_element_type=f32)  9.55 us
    dot_general x4, matrix products, per_device(): part = jnp.dot(a_w, b_gamma[:, cut], preferred_element_type=f32)  9.55 us
    all_to_all x2, starting transfers between devices, per_device(): lax.all_to_all(x.reshape(ch_dev, rows // slab, slab, width)[slot_dest, pa...  8.84 us
    ppermute x3, starting transfers between devices, per_device(): lax.ppermute(jnp.concatenate([own_blk, next_blk], axis=-1), 'row', pairs)  6.26 us
    gather x2, local copies, waits for them, and re-layouts, per_device(): x.reshape(ch_dev, rows // slab, slab, width)[slot_dest, part_dest]  5.64 us
  transfers between devices with their start and end apart: 10, of which 6 were waited for; matrix products, arithmetic and copies ran while one was open for 20% of the time, Pallas kernels for 0%

profile of v20, /device:TPU:8, one launch (start us, length us, event | category | flops | bytes accessed | tf_op | source)
XLA Modules:
  0.0 241.4 jit_solution(6700594777579184235)
XLA Ops:
  1.3 3.6 %gather_fusion.1 = bf16[8,128,1024]{2,1,0:T(8,128)(2,1)} fusion(bf16[4,2,128,1024]{3,2,1,0:T(8,128)(2,1)} %bitcast.67, s32[8]{0:T(128)S(1)} %fusion.99), kind=kCustom, calls=%fused_computation.1 | custom fusion | bytes 4194368 | tf_op jit(solution)/shard_map/gather | solution.py:43
  4.9 4.5 %all-to-all-start = ((bf16[8,128,1024]{2,1,0:T(8,128)(2,1)}), bf16[8,128,1024]{2,1,0:T(8,128)(2,1)}, u32[]{:S(2)}, u32[]{:S(2)}) async-start(bf16[8,128,1024]{2,1,0:T(8,128)(2,1)} %gather_fusion.1), calls=%async_computation | async-start | bytes 4194304 | tf_op jit(solution)/shard_map/all_to_all | solution.py:42
  11.5 24.6 %all-to-all-done = bf16[8,128,1024]{2,1,0:T(8,128)(2,1)} async-done(((bf16[8,128,1024]{2,1,0:T(8,128)(2,1)}), bf16[8,128,1024]{2,1,0:T(8,128)(2,1)}, u32[]{:S(2)}, u32[]{:S(2)}) %all-to-all-start) | async-done | bytes 2097184 | tf_op jit(solution)/shard_map/all_to_all | solution.py:42
  36.1 4.4 %all-to-all-start.1 = ((bf16[8,128,1024]{2,1,0:T(8,128)(2,1)}), bf16[8,128,1024]{2,1,0:T(8,128)(2,1)}, u32[]{:S(2)}, u32[]{:S(2)}) async-start(bf16[8,128,1024]{2,1,0:T(8,128)(2,1)} %gather_fusion.2), calls=%async_computation.1 | async-start | bytes 4194304 | tf_op jit(solution)/shard_map/all_to_all | solution.py:42
  42.5 2.7 %constant_dynamic-slice_fusion.8 = (bf16[1,256,1024]{2,1,0:T(8,128)(2,1)}, bf16[1,256,1024]{2,1,0:T(8,128)(2,1)S(1)}, bf16[1,256,1024]{2,1,0:T(8,128)(2,1)S(1)}, bf16[1,256,1024]{2,1,0:T(8,128)(2,1)S(1)}) fusion(bf16[4,256,1024]{2,1,0:T(8,128)(2,1)} %param.8, s32[]{:T(128)S(6)} %select_n.263, s32[]{:T(128)S(6)} %select_n.274, s32[]{:T(128)S(6)} %select_n.271, ...), kind=kLoop, calls=%fused_computation.141 | loop fusion | bytes 4194320 | tf_op jit(solution)/shard_map/jit(dynamic_index_in_dim)/dynamic_slice | solution.py:67
  50.5 4.1 %collective-permute-start.1 = (bf16[2,256,512]{1,2,0:T(8,128)(2,1)}, bf16[2,256,512]{1,2,0:T(8,128)(2,1)}, u32[]{:S(2)}, u32[]{:S(2)}) collective-permute-start(bf16[2,256,512]{1,2,0:T(8,128)(2,1)} %pad_maximum_fusion.4), channel_id=1, source_target_pairs={{0,2},{1,3},{2,0},{3,1},{4,6},{5,7},{6,4},{7,5},{8,10},{9,11},{10,... | collective-permute-start | bytes 1572872 | tf_op jit(solution)/shard_map/ppermute | solution.py:36
  61.0 6.1 %all-to-all-done.1 = bf16[8,128,1024]{2,1,0:T(8,128)(2,1)} async-done(((bf16[8,128,1024]{2,1,0:T(8,128)(2,1)}), bf16[8,128,1024]{2,1,0:T(8,128)(2,1)}, u32[]{:S(2)}, u32[]{:S(2)}) %all-to-all-start.1) | async-done | bytes 2097184 | tf_op jit(solution)/shard_map/all_to_all | solution.py:42
  67.1 2.4 fusion.40
  69.5 2.4 fusion.38
  71.9 2.4 fusion.36
  74.3 2.4 fusion.34
  76.7 2.4 fusion.42
  79.1 2.4 fusion.45
  81.5 2.4 fusion.48
  83.9 2.4 fusion.51
  87.9 10.9 %collective-permute-done = bf16[2,256,512]{2,1,0:T(8,128)(2,1)} collective-permute-done((bf16[2,256,512]{2,1,0:T(8,128)(2,1)}, bf16[2,256,512]{2,1,0:T(8,128)(2,1)}, u32[]{:S(2)}, u32[]{:S(2)}) %collective-permute-start) | collective-permute-done | bytes 524320 | tf_op jit(solution)/shard_map/ppermute | solution.py:36
  102.7 2.5 %fusion.81 = (bf16[2,256,256]{1,2,0:T(8,128)(2,1)S(1)}, bf16[2,256,256]{1,2,0:T(8,128)(2,1)}, bf16[2,256,256]{1,2,0:T(8,128)(2,1)}, bf16[2,256,256]{2,1,0:T(8,12...) fusion(bf16[2,256,1024]{2,1,0:T(8,128)(2,1)S(1)} %fusion.55, ...), kind=kLoop, calls=%fused_computation.127 | loop fusion | flops 786432 | bytes 3932164 | tf_op jit(solution)/shard_map/mul | solution.py:75
  108.8 5.0 %all-to-all-start.2 = ((bf16[32,128,256]{2,1,0:T(8,128)(2,1)}), bf16[32,128,256]{2,1,0:T(8,128)(2,1)}, u32[]{:S(2)}, u32[]{:S(2)}) async-start(bf16[32,128,256]{2,1,0:T(8,128)(2,1)} %bitcast.69), calls=%async_computation.2 | async-start | bytes 4194304 | tf_op jit(solution)/shard_map/all_to_all | solution.py:89
  116.8 4.8 %fusion.11 = f32[1024,1024]{0,1:T(8,128)S(1)} fusion(bf16[1024,1024]{0,1:T(8,128)(2,1)S(1)} %get-tuple-element.16, bf16[1024,1024]{0,1:T(8,128)(2,1)S(1)} %get-tuple-element.15, bf16[1024,1024]{0,1:T(8,128)(2,1)S(1)} %get-tuple-element.22, bf16[1024,1024]{0,1:T(8,128)(2,1)S(1)} %get-tuple-element.21), kind=kOutput, calls=%fused_computation.25 | convolution fusion | flops 4311744512 | bytes 12582912 | tf_op jit(solution)/shard_map/dot_general | solution.py:84
  129.2 81.3 %collective-permute-done.4 = f32[256,768]{0,1:T(8,128)S(1)} collective-permute-done((f32[256,768]{0,1:T(8,128)S(1)}, f32[256,768]{0,1:T(8,128)S(1)}, u32[]{:S(2)}, u32[]{:S(2)}) %collective-permute-start.4) | collective-permute-done | bytes 786464 | tf_op jit(solution)/shard_map/ppermute | solution.py:101
  210.4 16.4 %collective-permute-done.5 = f32[256,768]{0,1:T(8,128)S(1)} collective-permute-done((f32[256,768]{0,1:T(8,128)S(1)}, f32[256,768]{0,1:T(8,128)S(1)}, u32[]{:S(2)}, u32[]{:S(2)}) %collective-permute-start.5) | collective-permute-done | bytes 786464 | tf_op jit(solution)/shard_map/ppermute | solution.py:101
  226.8 2.6 %collective-permute-done.6 = f32[256,768]{0,1:T(8,128)S(1)} collective-permute-done((f32[256,768]{0,1:T(8,128)S(1)}, f32[256,768]{0,1:T(8,128)S(1)}, u32[]{:S(2)}, u32[]{:S(2)}) %collective-permute-start.6) | collective-permute-done | bytes 786464 | tf_op jit(solution)/shard_map/ppermute | solution.py:101
  236.6 2.5 %fusion.7 = bf16[4,256,1024]{1,2,0:T(8,128)(2,1)S(1)} fusion(s32[]{:T(128)S(6)} %select_n.316, f32[1,256,768]{1,2,0:T(8,128)S(1)} %copy-done.8, f32[1,256,768]{1,2,0:T(8,128)S(1)} %copy-done.7, f32[1,256,768]{1,2,0:T(8,128)S(1)} %copy-done.6, f32[1,256,768]{1,2,0:T(8,128)S(1)} %get-tuple-element.11, f32[4,256,256]{1,2,0:T(8,128)S(1)} %copy-done.10, ...), kind=kLoop, calls=%fused_computation.20 | loop fusion | flops 11534336 | bytes 10485764 | tf_op jit(solution)/shard_map/convert_element_type | solution.py:116
  239.1 2.4 copy.31
  (83 shorter events, 43.5 us)
Async XLA Ops:
  4.9 4.5 %copy-start.3 = (bf16[4,256,1024]{2,1,0:T(8,128)(2,1)S(1)}, bf16[4,256,1024]{2,1,0:T(8,128)(2,1)}, u32[]{:S(2)}) copy-start(bf16[4,256,1024]{2,1,0:T(8,128)(2,1)} %param.8) | copy-start | bytes 6291460
  4.9 31.1 %all-to-all-start = ((bf16[8,128,1024]{2,1,0:T(8,128)(2,1)}), bf16[8,128,1024]{2,1,0:T(8,128)(2,1)}, u32[]{:S(2)}, u32[]{:S(2)}) async-start(bf16[8,128,1024]{2,1,0:T(8,128)(2,1)} %gather_fusion.1), calls=%async_computation | async-start | bytes 4194304 | tf_op jit(solution)/shard_map/all_to_all | solution.py:42
  11.5 29.0 %copy-start.12 = (s32[1,1024]{1,0:T(1,128)S(1)}, s32[1,1024]{1,0:T(1,128)}, u32[]{:S(2)}) copy-start(s32[1,1024]{1,0:T(1,128)} %param.10) | copy-start | bytes 12292
  11.5 29.0 %copy-start.13 = (f32[1,1024]{1,0:T(1,128)S(1)}, f32[1,1024]{1,0:T(1,128)}, u32[]{:S(2)}) copy-start(f32[1,1024]{1,0:T(1,128)} %param.11) | copy-start | bytes 12292
  36.1 31.0 %all-to-all-start.1 = ((bf16[8,128,1024]{2,1,0:T(8,128)(2,1)}), bf16[8,128,1024]{2,1,0:T(8,128)(2,1)}, u32[]{:S(2)}, u32[]{:S(2)}) async-start(bf16[8,128,1024]{2,1,0:T(8,128)(2,1)} %gather_fusion.2), calls=%async_computation.1 | async-start | bytes 4194304 | tf_op jit(solution)/shard_map/all_to_all | solution.py:42
  40.5 20.5 %collective-permute-start.3 = (f32[2,1024]{1,0:T(2,128)S(1)}, f32[2,1024]{1,0:T(2,128)S(1)}, u32[]{:S(2)}, u32[]{:S(2)}) collective-permute-start(f32[2,1024]{1,0:T(2,128)S(1)} %pad_maximum_fusion.6), channel_id=1, source_target_pairs={{0,0},{1,4},{2,8},{3,12},{4,16},{5,20},{6,24},{7,28},{8,1},{9,5},{... | collective-permute-start | bytes 24584 | tf_op jit(solution)/shard_map/ppermute | solution.py:50
  42.5 2.7 %copy-start.2 = (bf16[4,256,1024]{2,1,0:T(8,128)(2,1)S(1)}, bf16[4,256,1024]{2,1,0:T(8,128)(2,1)}, u32[]{:S(2)}) copy-start(bf16[4,256,1024]{2,1,0:T(8,128)(2,1)} %param.7) | copy-start | bytes 6291460
  48.2 39.7 %collective-permute-start.2 = (bf16[2,256,512]{2,1,0:T(8,128)(2,1)}, bf16[2,256,512]{2,1,0:T(8,128)(2,1)}, u32[]{:S(2)}, u32[]{:S(2)}) collective-permute-start(bf16[2,256,512]{2,1,0:T(8,128)(2,1)} %pad_maximum_fusion.5), channel_id=1, source_target_pairs={{0,3},{1,0},{2,1},{3,2},{4,7},{5,4},{6,5},{7,6},{8,11},{9,8},{10,9... | collective-permute-start | bytes 1572872 | tf_op jit(solution)/shard_map/ppermute | solution.py:36
  49.6 5.1 %copy-start.9 = (bf16[2,256,256]{2,1,0:T(8,128)(2,1)S(1)}, bf16[2,256,256]{2,1,0:T(8,128)(2,1)}, u32[]{:S(2)}) copy-start(bf16[2,256,256]{2,1,0:T(8,128)(2,1)} %get-tuple-element.51) | copy-start | bytes 786436
  49.6 8.0 %copy-start.11 = (s32[4,1024]{1,0:T(4,128)S(1)}, s32[4,1024]{1,0:T(4,128)}, u32[]{:S(2)}) copy-start(s32[4,1024]{1,0:T(4,128)} %param.9) | copy-start | bytes 49156
  50.5 37.3 %collective-permute-start.1 = (bf16[2,256,512]{1,2,0:T(8,128)(2,1)}, bf16[2,256,512]{1,2,0:T(8,128)(2,1)}, u32[]{:S(2)}, u32[]{:S(2)}) collective-permute-start(bf16[2,256,512]{1,2,0:T(8,128)(2,1)} %pad_maximum_fusion.4), channel_id=1, source_target_pairs={{0,2},{1,3},{2,0},{3,1},{4,6},{5,7},{6,4},{7,5},{8,10},{9,11},{10,... | collective-permute-start | bytes 1572872 | tf_op jit(solution)/shard_map/ppermute | solution.py:36
  55.6 43.2 %collective-permute-start = (bf16[2,256,512]{2,1,0:T(8,128)(2,1)}, bf16[2,256,512]{2,1,0:T(8,128)(2,1)}, u32[]{:S(2)}, u32[]{:S(2)}) collective-permute-start(bf16[2,256,512]{2,1,0:T(8,128)(2,1)} %pad_maximum_fusion.3), channel_id=1, source_target_pairs={{0,1},{1,2},{2,3},{3,0},{4,5},{5,6},{6,7},{7,4},{8,9},{9,10},{10,1... | collective-permute-start | bytes 1572872 | tf_op jit(solution)/shard_map/ppermute | solution.py:36
  87.8 14.8 %copy-start.14 = (bf16[2]{0:T(256)(128)(2,1)S(1)}, bf16[2]{0:T(256)(128)(2,1)}, u32[]{:S(2)}) copy-start(bf16[2]{0:T(256)(128)(2,1)} %constant.158.clone) | copy-start | bytes 16
  108.8 5.0 %copy-start.5 = (bf16[2,256,1024]{1,2,0:T(8,128)(2,1)S(1)}, bf16[2,256,1024]{1,2,0:T(8,128)(2,1)}, u32[]{:S(2)}) copy-start(bf16[2,256,1024]{1,2,0:T(8,128)(2,1)} %copy.27) | copy-start | bytes 3145732
  108.8 122.3 %all-to-all-start.2 = ((bf16[32,128,256]{2,1,0:T(8,128)(2,1)}), bf16[32,128,256]{2,1,0:T(8,128)(2,1)}, u32[]{:S(2)}, u32[]{:S(2)}) async-start(bf16[32,128,256]{2,1,0:T(8,128)(2,1)} %bitcast.69), calls=%async_computation.2 | async-start | bytes 4194304 | tf_op jit(solution)/shard_map/all_to_all | solution.py:89
  121.9 4.7 %copy-start.4 = (bf16[4,256,1024]{2,1,0:T(8,128)(2,1)S(1)}, bf16[4,256,1024]{2,1,0:T(8,128)(2,1)}, u32[]{:S(2)}) copy-start(bf16[4,256,1024]{2,1,0:T(8,128)(2,1)} %param.8) | copy-start | bytes 6291460
  122.0 88.5 %collective-permute-start.4 = (f32[256,768]{0,1:T(8,128)S(1)}, f32[256,768]{0,1:T(8,128)S(1)}, u32[]{:S(2)}, u32[]{:S(2)}) collective-permute-start(f32[256,768]{0,1:T(8,128)S(1)} %pad_maximum_fusion.1), channel_id=1, source_target_pairs={{0,1},{1,2},{2,3},{3,0},{4,5},{5,6},{6,7},{7,4},{8,9},{9,10},{10,1... | collective-permute-start | bytes 2359304 | tf_op jit(solution)/shard_map/ppermute | solution.py:101
  123.5 103.3 %collective-permute-start.5 = (f32[256,768]{0,1:T(8,128)S(1)}, f32[256,768]{0,1:T(8,128)S(1)}, u32[]{:S(2)}, u32[]{:S(2)}) collective-permute-start(f32[256,768]{0,1:T(8,128)S(1)} %pad_maximum_fusion.2), channel_id=1, source_target_pairs={{0,2},{1,3},{2,0},{3,1},{4,6},{5,7},{6,4},{7,5},{8,10},{9,11},{10,... | collective-permute-start | bytes 2359304 | tf_op jit(solution)/shard_map/ppermute | solution.py:101
  125.0 104.4 %collective-permute-start.6 = (f32[256,768]{0,1:T(8,128)S(1)}, f32[256,768]{0,1:T(8,128)S(1)}, u32[]{:S(2)}, u32[]{:S(2)}) collective-permute-start(f32[256,768]{0,1:T(8,128)S(1)} %slice.152), channel_id=1, source_target_pairs={{0,3},{1,0},{2,1},{3,2},{4,7},{5,4},{6,5},{7,6},{8,11},{9,8},{10,9... | collective-permute-start | bytes 2359304 | tf_op jit(solution)/shard_map/ppermute | solution.py:101
  234.6 1.1 copy-start.6
  234.6 1.4 copy-start.7
  234.6 1.6 copy-start.8
  234.6 1.9 copy-start.10
  236.6 4.9 %copy-start.1 = (s32[32,8]{0,1:T(8,128)S(1)}, s32[32,8]{0,1:T(8,128)}, u32[]{:S(2)}) copy-start(s32[32,8]{0,1:T(8,128)} %param.12) | copy-start | bytes 3076
  (1 other events, 0.7 us)
